TPU v7x, 256 devices: a whole 4x4x8 slice. The times are simulated.
256 devices in a mesh: group: 8 (over x, y_lo), tp: 32 (over z, y_hi, core).
Axes of the slice: x: 4, y: 4 (y_hi: 2, y_lo: 2; y = y_hi * 2 + y_lo), z: 8, core: 2. Of those that a mesh axis runs over, the one named last changes fastest.
Arguments:
- hidden: bfloat16 [2, 256, 8192], P(None, 'group', 'tp'), may hold values from -6 to 6
- query_weight: bfloat16 [8192, 4096], P(None, 'tp'), may hold values from -0.0625 to 0.0625
- key_value_weight: bfloat16 [8192, 1024], P('tp'), may hold values from -0.0625 to 0.0625
- output_weight: bfloat16 [4096, 8192], P('tp'), may hold values from -0.1875 to 0.1875
- adapter_down_weight: bfloat16 [32, 8192, 128], P('group', 'tp'), may hold values from -0.0625 to 0.0625
- adapter_up_query: bfloat16 [32, 64, 4096], P('group', None, 'tp'), may hold values from -0.75 to 0.75
- adapter_up_value: bfloat16 [32, 64, 512], P('group'), may hold values from -0.75 to 0.75
- key_value_pool: bfloat16 [8192, 16, 1024], P(('group', 'tp')), may hold values from -250 to 250
- lengths: int32 [256], P(('group', 'tp')), may hold values from 257 to 512
- request_page_table: int32 [256, 32], P(('group', 'tp')), may hold values from 0 to 63, as said below
- page_send_list: int32 [8, 32, 8, 4], P('group', 'tp'), may hold values from -1 to 31, as said below
- request_adapter_entry: int32 [256], P('group'), may hold values from 0 to 15, as said below
- read_rows_list: int32 [8, 8, 2], replicated, may hold values from -1 to 3, as said below
Outputs:
- layer_out: bfloat16 [2, 256, 8192], P(None, 'group', 'tp')
Inputs may be any that keep to these rules, and one draw needn't show every extreme that they name: `request_page_table`: the entries of one device's requests are distinct; an entry below 32 names a page of that device's pool, an entry 32 + g * 4 + c names slot c of what device (g, same column) lists for this group in page_send_list, and only listed slots are named. `page_send_list`: for each source device and target group the listed pages are distinct and fill the first slots, -1 marks an empty slot; a group lists nothing for itself; in every draw each device fills all 4 slots for some group. `request_adapter_entry`: entry e of a request of group h names slot e % 2 of read_rows_list[h, e // 2], never an empty one; every listed slot is named by some request of the group. `read_rows_list`: listed rows of one reading group and owner are distinct and fill the first slots, -1 marks an empty slot; every reading group reads 2 adapters from some owner.
All inputs are finite; a program needn't handle non-finite values.
Results may differ from a plain program's by a relative error of at most 0.0158.
The roundings to bfloat16 on the way count: a program that leaves them out, or rounds other values in their place, can miss the bound.
Values may be sent and summed in bfloat16 or wider, within the bound.
No kernel may reach another device: no remote copies, remote signals or barrier semaphores. Data moves between devices by JAX's collectives and lax.ppermute only.
A program may use at most 64 MiB of HBM per device.

v0:
```python
import math

import jax
import jax.numpy as jnp
from jax import lax
from jax.sharding import PartitionSpec as P

HEAD_SIZE = 128
QUERY_HEADS = 32
KEY_VALUE_HEADS = 4
ADAPTER_RANK = 64


ADAPTER_SCALE = 1.5


def attend(query_own, ctx_pages, keyval_new, lengths):
    key_span_width = KEY_VALUE_HEADS * HEAD_SIZE
    group_q = QUERY_HEADS // KEY_VALUE_HEADS
    step_count = query_own.shape[0]
    batch_own = query_own.shape[1]
    ctx_len = ctx_pages.shape[1]
    query_rows = query_own.reshape(step_count, batch_own, KEY_VALUE_HEADS, group_q, HEAD_SIZE)
    ctx_keys = ctx_pages[..., :key_span_width].reshape(
        batch_own, ctx_len, KEY_VALUE_HEADS, HEAD_SIZE
    )
    ctx_values = ctx_pages[..., key_span_width:].reshape(
        batch_own, ctx_len, KEY_VALUE_HEADS, HEAD_SIZE
    )
    new_keys = keyval_new[..., :key_span_width].reshape(
        batch_own, step_count, KEY_VALUE_HEADS, HEAD_SIZE
    )
    new_values = keyval_new[..., key_span_width:].reshape(
        batch_own, step_count, KEY_VALUE_HEADS, HEAD_SIZE
    )
    score_scale = 1.0 / math.sqrt(HEAD_SIZE)
    ctx_scores = (
        jnp.einsum("sbkgd,bckd->bkgsc", query_rows, ctx_keys, preferred_element_type=jnp.float32)
        * score_scale
    )
    new_scores = (
        jnp.einsum("sbkgd,btkd->bkgst", query_rows, new_keys, preferred_element_type=jnp.float32)
        * score_scale
    )
    ctx_mask = (jnp.arange(ctx_len)[None, :] < lengths[:, None])[:, None, None, None, :]
    new_mask = jnp.arange(step_count)[None, :] <= jnp.arange(step_count)[:, None]
    ctx_scores = jnp.where(ctx_mask, ctx_scores, -jnp.inf)
    new_scores = jnp.where(new_mask, new_scores, -jnp.inf)
    row_max = jnp.maximum(
        jnp.max(ctx_scores, -1, keepdims=True), jnp.max(new_scores, -1, keepdims=True)
    )
    ctx_weights = jnp.exp(ctx_scores - row_max)
    new_weights = jnp.exp(new_scores - row_max)
    totals = jnp.sum(ctx_weights, -1, keepdims=True) + jnp.sum(new_weights, -1, keepdims=True)
    context = jnp.einsum(
        "bkgsc,bckd->bkgsd",
        ctx_weights.astype(jnp.bfloat16),
        ctx_values,
        preferred_element_type=jnp.float32,
    )
    context = context + jnp.einsum(
        "bkgst,btkd->bkgsd",
        new_weights.astype(jnp.bfloat16),
        new_values,
        preferred_element_type=jnp.float32,
    )
    context = context / totals
    return (
        jnp.transpose(context, (3, 0, 1, 2, 4))
        .reshape(step_count, batch_own, QUERY_HEADS, HEAD_SIZE)
        .astype(jnp.bfloat16)
    )


def per_device(
    hidden,
    query_weight,
    key_value_weight,
    output_weight,
    adapter_down_weight,
    adapter_up_query,
    adapter_up_value,
    key_value_pool,
    lengths,
    request_page_table,
    page_send_list,
    request_adapter_entry,
    read_rows_list,
):
    group_number = lax.axis_index("group")
    column_id = lax.axis_index("tp")
    step_count, batch_rows, width_local = hidden.shape
    batch_own = lengths.shape[0]
    key_span_width = KEY_VALUE_HEADS * HEAD_SIZE
    cap_slots = read_rows_list.shape[2]
    holder_group = request_adapter_entry // cap_slots
    slot_column = request_adapter_entry % cap_slots
    own_start = column_id * batch_own
    whole_down, whole_upq, whole_upv = (
        lax.all_gather(adapter_down_weight, "group", axis=0, tiled=True),
        lax.all_gather(adapter_up_query, "group", axis=0, tiled=True),
        lax.all_gather(adapter_up_value, "group", axis=0, tiled=True),
    )
    storage_rows = (
        holder_group * adapter_down_weight.shape[0]
        + read_rows_list[group_number, holder_group, slot_column]
    )
    down_rows = jnp.take(whole_down, storage_rows, axis=0)
    upq_rows = jnp.take(whole_upq, storage_rows, axis=0)
    upv_rows = jnp.take(
        whole_upv, lax.dynamic_slice_in_dim(storage_rows, own_start, batch_own), axis=0
    )
    shrink_part = jnp.einsum("srd,rdk->srk", hidden, down_rows, preferred_element_type=jnp.float32)
    down_projected_low = lax.psum(shrink_part, "tp").astype(jnp.bfloat16)
    query_plain = jnp.einsum(
        "srd,dc->src",
        lax.all_gather(hidden, "tp", axis=2, tiled=True),
        query_weight,
        preferred_element_type=jnp.float32,
    )
    query_adapter_term = jnp.einsum(
        "srk,rkc->src",
        down_projected_low[..., :ADAPTER_RANK],
        upq_rows,
        preferred_element_type=jnp.float32,
    )
    query_rows = (query_plain + ADAPTER_SCALE * query_adapter_term).astype(jnp.bfloat16)
    key_value_plain = lax.psum_scatter(
        jnp.einsum("srd,dc->rsc", hidden, key_value_weight, preferred_element_type=jnp.float32),
        "tp",
        scatter_dimension=0,
        tiled=True,
    )
    shrink_own = lax.dynamic_slice_in_dim(down_projected_low, own_start, batch_own, 1)
    value_adapter_term = ADAPTER_SCALE * jnp.einsum(
        "srk,rkc->rsc", shrink_own[..., ADAPTER_RANK:], upv_rows, preferred_element_type=jnp.float32
    )
    keyval_new = jnp.concatenate(
        [
            key_value_plain[..., :key_span_width],
            key_value_plain[..., key_span_width:] + value_adapter_term,
        ],
        -1,
    ).astype(jnp.bfloat16)
    heads_local = query_rows.shape[2] // HEAD_SIZE
    query_own = lax.all_to_all(
        query_rows.reshape(step_count, batch_rows, heads_local, HEAD_SIZE),
        "tp",
        split_axis=1,
        concat_axis=2,
        tiled=True,
    )
    move_row = page_send_list[0, 0]
    present_pages = (move_row >= 0).reshape(-1)
    outgoing = (
        jnp.take(key_value_pool, jnp.maximum(move_row, 0).reshape(-1), axis=0)
        * present_pages.astype(key_value_pool.dtype)[:, None, None]
    )
    arrived_pages = lax.all_to_all(outgoing, "group", split_axis=0, concat_axis=0, tiled=True)
    combined = jnp.concatenate([key_value_pool, arrived_pages], 0)
    ctx_pages = jnp.take(combined, request_page_table.reshape(-1), axis=0).reshape(
        batch_own, -1, 2 * key_span_width
    )
    attended = attend(query_own, ctx_pages, keyval_new, lengths)
    heads_back = lax.all_to_all(attended, "tp", split_axis=2, concat_axis=1, tiled=True)
    projected = jnp.dot(
        heads_back.reshape(step_count * batch_rows, -1),
        output_weight,
        preferred_element_type=jnp.float32,
    )
    summed = lax.psum_scatter(
        projected.reshape(step_count, batch_rows, -1), "tp", scatter_dimension=2, tiled=True
    )
    return summed.astype(jnp.bfloat16)


def solution(mesh):
    placed = (
        P(None, "group", "tp"),
        P(None, "tp"),
        P("tp", None),
        P("tp", None),
        P("group", "tp", None),
        P("group", None, "tp"),
        P("group", None, None),
        P(("group", "tp"), None, None),
        P(("group", "tp")),
        P(("group", "tp"), None),
        P("group", "tp", None, None),
        P("group"),
        P(),
    )
    return jax.shard_map(
        per_device, mesh=mesh, in_specs=placed, out_specs=P(None, "group", "tp"), check_vma=False
    )
```

profile of v0, /device:TPU:2, one launch (start us, length us, event | category | flops | bytes accessed | tf_op | source)
XLA Modules:
  0.0 627.6 jit_solution(2606935624223614851)
XLA Ops:
  6.5 0.7 all-gather.6.cloned.1.call-update
  7.3 0.7 all-gather.4.cloned.1.call-update
  8.1 1.3 convolution_bitcast_fusion
  9.3 0.9 copy.70
  10.3 0.7 compare_convert_fusion
  11.0 0.7 broadcast_maximum_fusion
  11.6 0.1 copy.62
  11.7 0.1 reshape.312
  11.8 0.1 copy.60
  11.9 0.1 le.59
  12.0 0.1 copy.61
  12.1 0.1 reshape.322
  12.2 1.8 gather_fusion
  14.1 1.1 select_multiply_fusion
  15.2 6.5 %all-to-all-start = ((bf16[32,16,1024]{2,1,0:T(8,128)(2,1)}), bf16[32,16,1024]{2,1,0:T(8,128)(2,1)}, u32[]{:S(2)}, u32[]{:S(2)}) async-start(bf16[32,16,1024]{2,1,0:T(8,128)(2,1)} %select_multiply_fusion), calls=%async_computation | async-start | bytes 2097152 | tf_op jit(solution)/shard_map/all_to_all | solution.py:159
  21.8 0.6 all-gather.8.cloned.1.call-update
  22.4 0.8 gather_fusion.2
  23.2 0.1 broadcast_in_dim.98
  23.3 0.1 broadcast_in_dim.99
  24.0 0.6 dynamic_slice.7
  26.6 48.5 %all_gather.13 = bf16[32,64,128]{2,1,0:T(8,128)(2,1)} all-gather(bf16[4,64,128]{2,1,0:T(8,128)(2,1)S(1)} %copy-done.4), channel_id=1, replica_groups=mesh['group'=8,'tp'=32] {'group'}, dimensions={0}, use_global_device_ids=true | all-gather | bytes 589824 | tf_op jit(solution)/shard_map/all_gather | solution.py:101
  75.1 2.5 gather_fusion.3
  77.6 0.6 dynamic-slice.4
  78.2 2.7 pad_maximum_fusion
  81.0 2.2 gather_fusion.1
  83.2 1.3 copy.63
  84.5 1.3 broadcast_select_fusion
  85.9 0.1 fusion.82
  86.0 3.7 gather_fusion.4
  89.7 2.0 fusion.10
  91.7 133.7 %psum.7 = bf16[2,32,128]{2,0,1:T(2,128)(2,1)S(1)} all-reduce(f32[2,32,128]{2,0,1:T(2,128)S(1)} %fusion.10), channel_id=1, replica_groups=mesh['group'=8,'tp'=32] {'tp'}, use_global_device_ids=true, to_apply=%region_0.1 | all-reduce | flops 8192 | bytes 49152 | tf_op jit(solution)/shard_map/psum | solution.py:114
  225.4 1.3 fusion.31
  226.8 2.4 fusion.21
  229.2 0.6 copy.66
  229.8 3.8 all-to-all-start.1
  233.7 196.1 %all-reduce.3.cloned.1.call-done = f32[32,2,1024]{2,1,0:T(2,128)} async-done(((f32[32,2,1024]{2,1,0:T(2,128)}), f32[32,2,1024]{2,1,0:T(2,128)}) %all-reduce.3.cloned.1.call-update) | async-done | bytes 262160
  429.8 1.5 convolution_multiply_fusion.1
  431.3 0.1 fusion.81
  431.4 0.3 fusion.83
  431.7 0.2 fusion.35
  431.9 0.1 fusion.55
  432.0 0.3 fusion.38
  432.3 52.3 %all-gather.8.cloned.1.call-done = bf16[32,64,512]{2,1,0:T(8,128)(2,1)} async-done(((bf16[4,64,512]{2,1,0:T(8,128)(2,1)}), bf16[32,64,512]{2,1,0:T(8,128)(2,1)}) %all-gather.8.cloned.1.call-update) | async-done | bytes 2097168 | tf_op jit(solution)/shard_map/all_gather | solution.py:102
  484.5 1.8 fusion.24
  486.3 18.2 %all_to_all.23 = bf16[2,1,32,128]{3,0,1,2:T(2,128)(2,1)S(1)} all-to-all(bf16[2,1,32,128]{3,0,1,2:T(2,128)(2,1)S(1)} %copy.79), channel_id=1, replica_groups=mesh['group'=8,'tp'=32] {'tp'}, dimensions={2} | all-to-all | bytes 32768 | tf_op jit(solution)/shard_map/all_to_all | solution.py:165
  504.6 1.8 fusion
  506.4 113.2 %reduce-scatter.2.cloned.1.call-done = f32[2,32,256]{2,1,0:T(8,128)} async-done(((f32[2,32,8192]{2,1,0:T(8,128)}), f32[2,32,256]{2,1,0:T(8,128)}) %reduce-scatter.2.cloned.1.call-update) | async-done | bytes 65552 | tf_op jit(solution)/shard_map/reduce_scatter | solution.py:171
  619.6 1.5 convert_element_type.64
  (42 shorter events, 0.4 us)
Async XLA Ops:
  6.5 498.0 %copy-start = (bf16[128,8192]{1,0:T(8,128)(2,1)S(1)}, bf16[128,8192]{1,0:T(8,128)(2,1)}, u32[]{:S(2)}) copy-start(bf16[128,8192]{1,0:T(8,128)(2,1)} %param.16) | copy-start | bytes 6291460
  6.5 79.4 %all-gather.6.cloned.1.call-start = ((), (), s32[]{:S(2)}) async-start(), calls=%async_computation.5 | async-start | bytes 2359296 | tf_op jit(solution)/shard_map/all_gather | solution.py:100
  7.3 219.5 %all-gather.4.cloned.1.call-start = ((), (), s32[]{:S(2)}) async-start(), calls=%async_computation.4 | async-start | bytes 1081344 | tf_op jit(solution)/shard_map/all_gather | solution.py:117
  8.0 421.8 %all-reduce.3.cloned.1.call-start = ((), (), s32[]{:S(2)}) async-start(), calls=%async_computation.8 | async-start | bytes 524288
  14.0 8.3 %copy-start.5 = (s32[32]{0:T(128)S(1)}, s32[32]{0:T(128)}, u32[]{:S(2)}) copy-start(s32[32]{0:T(128)} %param.24) | copy-start | bytes 388
  14.0 8.3 %copy-start.1 = (s32[8,8,2]{1,2,0:T(2,128)S(1)}, s32[8,8,2]{1,2,0:T(2,128)}, u32[]{:S(2)}) copy-start(s32[8,8,2]{1,2,0:T(2,128)} %param.25) | copy-start | bytes 1540
  14.1 9.1 %copy-start.6 = (s32[1,32]{1,0:T(1,128)S(1)}, s32[1,32]{1,0:T(1,128)}, u32[]{:S(2)}) copy-start(s32[1,32]{1,0:T(1,128)} %param.22) | copy-start | bytes 388
  14.1 12.5 %copy-start.4 = (bf16[4,64,128]{2,1,0:T(8,128)(2,1)S(1)}, bf16[4,64,128]{2,1,0:T(8,128)(2,1)}, u32[]{:S(2)}) copy-start(bf16[4,64,128]{2,1,0:T(8,128)(2,1)} %param.18) | copy-start | bytes 196612
  15.2 62.3 %copy-start.7 = (u32[256]{0:T(256)S(1)}, u32[256]{0:T(256)}, u32[]{:S(2)}) copy-start(u32[256]{0:T(256)} %constant.176) | copy-start | bytes 3076
  15.2 63.0 %copy-start.2 = (bf16[32,16,1024]{2,1,0:T(8,128)(2,1)S(1)}, bf16[32,16,1024]{2,1,0:T(8,128)(2,1)}, u32[]{:S(2)}) copy-start(bf16[32,16,1024]{2,1,0:T(8,128)(2,1)} %param.20) | copy-start | bytes 3145732
  15.2 63.0 %all-to-all-start = ((bf16[32,16,1024]{2,1,0:T(8,128)(2,1)}), bf16[32,16,1024]{2,1,0:T(8,128)(2,1)}, u32[]{:S(2)}, u32[]{:S(2)}) async-start(bf16[32,16,1024]{2,1,0:T(8,128)(2,1)} %select_multiply_fusion), calls=%async_computation | async-start | bytes 2097152 | tf_op jit(solution)/shard_map/all_to_all | solution.py:159
  21.8 462.8 %all-gather.8.cloned.1.call-start = ((), (), s32[]{:S(2)}) async-start(), calls=%async_computation.6 | async-start | bytes 2359296 | tf_op jit(solution)/shard_map/all_gather | solution.py:102
  85.9 3.8 copy-start.3
  229.8 200.0 %all-to-all-start.1 = ((bf16[2,32,1,128]{3,0,2,1:T(2,128)(2,1)}), bf16[2,32,1,128]{3,0,2,1:T(2,128)(2,1)S(1)}, u32[]{:S(2)}, u32[]{:S(2)}) async-start(bf16[2,32,1,128]{3,0,2,1:T(2,128)(2,1)} %copy.66), calls=%async_computation.1 | async-start | bytes 32768 | tf_op jit(solution)/shard_map/all_to_all | solution.py:146
  233.7 385.9 %reduce-scatter.2.cloned.1.call-start = ((), (), s32[]{:S(2)}) async-start(), calls=%async_computation.7 | async-start | bytes 2162688 | tf_op jit(solution)/shard_map/reduce_scatter | solution.py:171
Sparse Core Ops, SparseCore 0:
  9.1 76.7 all-gather.5
  88.5 75.1 all-gather.3
  166.3 263.5 all-reduce.2
  431.6 52.8 all-gather.7
  506.5 113.0 reduce-scatter.1
where the time goes:
time: 628 us
  waiting for transfers between devices  364 us (58%)
  blocking collectives  200 us (32%)
  local copies, waits for them, and re-layouts  16 us (3%)
  between operations  16 us (3%)
  matrix products  12.6 us (2%)
  starting transfers between devices  10.5 us (2%)
  other arithmetic  8.49 us (1%)
    unnamed x6, waiting for transfers between devices  198 us
    psum x1, blocking collectives, per_device(): down_projected_low = lax.psum(shrink_part, 'tp').astype(jnp.bfloat16)  134 us
    reduce_scatter x1, waiting for transfers between devices, per_device(): lax.psum_scatter(projected.reshape(step_count, batch_rows, -1), 'tp', sca...  113 us
    all_gather x1, waiting for transfers between devices, per_device(): lax.all_gather(adapter_up_value, 'group', axis=0, tiled=True)  52.3 us
    all_gather x1, blocking collectives, per_device(): lax.all_gather(adapter_up_query, 'group', axis=0, tiled=True)  48.5 us
    all_to_all x1, blocking collectives, per_device(): lax.all_to_all(attended, 'tp', split_axis=2, concat_axis=1, tiled=True)  18.2 us
  transfers between devices with their start and end apart: 7, of which 3 were waited for; matrix products, arithmetic and copies ran while one was open for 5% of the time, Pallas kernels for 0%

commit v1 on v0

--- a/solution.py
+++ b/solution.py
@@ -89,34 +89,69 @@
 ):
     group_number = lax.axis_index("group")
     column_id = lax.axis_index("tp")
+    n_group = read_rows_list.shape[0]
+    n_tp = query_weight.shape[0] // hidden.shape[2]
     step_count, batch_rows, width_local = hidden.shape
     batch_own = lengths.shape[0]
     key_span_width = KEY_VALUE_HEADS * HEAD_SIZE
     cap_slots = read_rows_list.shape[2]
-    holder_group = request_adapter_entry // cap_slots
-    slot_column = request_adapter_entry % cap_slots
     own_start = column_id * batch_own
-    whole_down, whole_upq, whole_upv = (
-        lax.all_gather(adapter_down_weight, "group", axis=0, tiled=True),
-        lax.all_gather(adapter_up_query, "group", axis=0, tiled=True),
-        lax.all_gather(adapter_up_value, "group", axis=0, tiled=True),
-    )
-    storage_rows = (
-        holder_group * adapter_down_weight.shape[0]
-        + read_rows_list[group_number, holder_group, slot_column]
-    )
-    down_rows = jnp.take(whole_down, storage_rows, axis=0)
-    upq_rows = jnp.take(whole_upq, storage_rows, axis=0)
-    upv_rows = jnp.take(
-        whole_upv, lax.dynamic_slice_in_dim(storage_rows, own_start, batch_own), axis=0
-    )
+
+    send_rows = jnp.maximum(read_rows_list[:, group_number, :], 0)
+    down_send = jnp.take(adapter_down_weight, send_rows, axis=0)
+    upq_send = jnp.take(adapter_up_query, send_rows, axis=0)
+    upv_send = jnp.take(adapter_up_value, send_rows, axis=0)
+    down_size = down_send[0, 0].size
+    upq_size = upq_send[0, 0].size
+    panel_send = jnp.concatenate(
+        [
+            down_send.reshape(n_group, cap_slots, -1),
+            upq_send.reshape(n_group, cap_slots, -1),
+            upv_send.reshape(n_group, cap_slots, -1),
+        ],
+        -1,
+    )
+    panel_recv = lax.all_to_all(panel_send, "group", 0, 0, tiled=True).reshape(
+        n_group * cap_slots, -1
+    )
+    down_recv = panel_recv[:, :down_size].reshape((-1,) + adapter_down_weight.shape[1:])
+    upq_recv = panel_recv[:, down_size : down_size + upq_size].reshape(
+        (-1,) + adapter_up_query.shape[1:]
+    )
+    upv_recv = panel_recv[:, down_size + upq_size :].reshape((-1,) + adapter_up_value.shape[1:])
+    down_rows = jnp.take(down_recv, request_adapter_entry, axis=0)
+    upq_rows = jnp.take(upq_recv, request_adapter_entry, axis=0)
+    own_entry = lax.dynamic_slice_in_dim(request_adapter_entry, own_start, batch_own)
+    upv_rows = jnp.take(upv_recv, own_entry, axis=0)
+
+    hidden_sent = lax.all_to_all(
+        jnp.broadcast_to(hidden[None], (n_tp,) + hidden.shape), "tp", 0, 0, tiled=True
+    )
+    hidden_full = jnp.transpose(hidden_sent, (1, 2, 0, 3)).reshape(
+        step_count, batch_rows, n_tp * width_local
+    )
+
     shrink_part = jnp.einsum("srd,rdk->srk", hidden, down_rows, preferred_element_type=jnp.float32)
-    down_projected_low = lax.psum(shrink_part, "tp").astype(jnp.bfloat16)
+    key_value_part = jnp.einsum(
+        "srd,dc->rsc", hidden, key_value_weight, preferred_element_type=jnp.float32
+    ).reshape(n_tp, batch_own * step_count * 2 * key_span_width)
+    reduce_send = jnp.concatenate(
+        [
+            key_value_part,
+            jnp.broadcast_to(shrink_part.reshape(1, -1), (n_tp, shrink_part.size)),
+        ],
+        -1,
+    )
+    reduce_recv = jnp.sum(lax.all_to_all(reduce_send, "tp", 0, 0, tiled=True), 0)
+    key_value_plain = reduce_recv[: key_value_part.shape[1]].reshape(
+        batch_own, step_count, 2 * key_span_width
+    )
+    down_projected_low = (
+        reduce_recv[key_value_part.shape[1] :].reshape(shrink_part.shape).astype(jnp.bfloat16)
+    )
+
     query_plain = jnp.einsum(
-        "srd,dc->src",
-        lax.all_gather(hidden, "tp", axis=2, tiled=True),
-        query_weight,
-        preferred_element_type=jnp.float32,
+        "srd,dc->src", hidden_full, query_weight, preferred_element_type=jnp.float32
     )
     query_adapter_term = jnp.einsum(
         "srk,rkc->src",
@@ -125,12 +160,6 @@
         preferred_element_type=jnp.float32,
     )
     query_rows = (query_plain + ADAPTER_SCALE * query_adapter_term).astype(jnp.bfloat16)
-    key_value_plain = lax.psum_scatter(
-        jnp.einsum("srd,dc->rsc", hidden, key_value_weight, preferred_element_type=jnp.float32),
-        "tp",
-        scatter_dimension=0,
-        tiled=True,
-    )
     shrink_own = lax.dynamic_slice_in_dim(down_projected_low, own_start, batch_own, 1)
     value_adapter_term = ADAPTER_SCALE * jnp.einsum(
         "srk,rkc->rsc", shrink_own[..., ADAPTER_RANK:], upv_rows, preferred_element_type=jnp.float32
@@ -168,10 +197,14 @@
         output_weight,
         preferred_element_type=jnp.float32,
     )
-    summed = lax.psum_scatter(
-        projected.reshape(step_count, batch_rows, -1), "tp", scatter_dimension=2, tiled=True
-    )
-    return summed.astype(jnp.bfloat16)
+    out_cols = projected.shape[1] // n_tp
+    summed = jnp.sum(
+        lax.all_to_all(
+            projected.reshape(step_count * batch_rows, n_tp, out_cols), "tp", 1, 1, tiled=True
+        ),
+        1,
+    )
+    return summed.reshape(step_count, batch_rows, out_cols).astype(jnp.bfloat16)
 
 
 def solution(mesh):

time: 628 us -> 259 us (0.41)
  waiting for transfers between devices: 364 us -> 85.2 us
  blocking collectives: 200 us -> 55.7 us
  starting transfers between devices: 10.5 us -> 39.8 us
  local copies, waits for them, and re-layouts: 16 us -> 44.8 us
  between operations: 16 us -> 3.03 us
  other arithmetic: 8.49 us -> 17.8 us
    unnamed x6 -> x0, waiting for transfers between devices: 198 us -> none
    psum x1 -> x0, blocking collectives: 134 us -> none  [per_device(): down_projected_low = lax.psum(shrink_part, 'tp').astype(jnp.bfloat16)]
    reduce_scatter x1 -> x0, waiting for transfers between devices: 113 us -> none  [per_device(): lax.psum_scatter(projected.reshape(step_count, batch_rows, -1), 'tp', sca...]
    all_to_all x0 -> x4, waiting for transfers between devices: none -> 72.7 us  [the longest x1 27.1 us: per_device(): lax.all_to_all(panel_send, 'group', 0, 0, tiled=True)]
    all_gather x3 -> x0, waiting for transfers between devices: 52.3 us -> none  [the longest x1 52.3 us: per_device(): lax.all_gather(adapter_up_value, 'group', axis=0, tiled=True)]
    all_gather x1 -> x0, blocking collectives: 48.5 us -> none  [per_device(): lax.all_gather(adapter_up_query, 'group', axis=0, tiled=True)]
    all_to_all x1, blocking collectives: 18.2 us -> 55.7 us  [per_device(): lax.all_to_all(projected.reshape(step_count * batch_rows, n_tp, out_cols)...]
    all_to_all x0 -> x4, starting transfers between devices: none -> 27.4 us  [the longest x1 12 us: per_device(): lax.all_to_all(jnp.broadcast_to(hidden[None], (n_tp,) + hidden.shape), 't...]
  transfers between devices with their start and end apart: 7 -> 6, of which waited for: 3 -> 6; matrix products, arithmetic and copies ran while one was open for 5% -> 14% of each run, Pallas kernels for 0% -> 0%
where the time goes in v1:
time: 259 us; the launch traced here: 256 us
  waiting for transfers between devices  85.2 us (33%)
  blocking collectives  55.7 us (22%)
  local copies, waits for them, and re-layouts  44.8 us (17%)
  starting transfers between devices  39.8 us (15%)
  other arithmetic  17.8 us (7%)
  matrix products  9.68 us (4%)
  between operations  3.03 us (1%)
    all_to_all x1, blocking collectives, per_device(): lax.all_to_all(projected.reshape(step_count * batch_rows, n_tp, out_cols)...  55.7 us
    all_to_all x1, waiting for transfers between devices, per_device(): lax.all_to_all(panel_send, 'group', 0, 0, tiled=True)  27.1 us
    all_to_all x1, waiting for transfers between devices, per_device(): lax.all_to_all(jnp.broadcast_to(hidden[None], (n_tp,) + hidden.shape), 't...  27 us
    all_to_all x1, waiting for transfers between devices, per_device(): lax.all_to_all(reduce_send, 'tp', 0, 0, tiled=True)  13.1 us
    all_to_all x1, starting transfers between devices, per_device(): lax.all_to_all(jnp.broadcast_to(hidden[None], (n_tp,) + hidden.shape), 't...  12 us
    all_to_all x1, waiting for transfers between devices, per_device(): lax.all_to_all(query_rows.reshape(step_count, batch_rows, heads_local, HE...  9.56 us
    all_to_all x1, starting transfers between devices, per_device(): lax.all_to_all(outgoing, 'group', split_axis=0, concat_axis=0, tiled=True)  6.96 us
    all_to_all x1, starting transfers between devices, per_device(): lax.all_to_all(panel_send, 'group', 0, 0, tiled=True)  6.66 us
  transfers between devices with their start and end apart: 6, of which 6 were waited for; matrix products, arithmetic and copies ran while one was open for 14% of the time, Pallas kernels for 0%

profile of v1, /device:TPU:2, one launch (start us, length us, event | category | flops | bytes accessed | tf_op | source)
XLA Modules:
  0.0 256.1 jit_solution(15606275139865540157)
XLA Ops:
  0.0 1.1 fusion.54
  1.1 0.8 broadcast_compare_fusion
  2.2 1.4 gather_fusion.3
  3.7 0.8 gather.46
  4.4 2.6 %gather_fusion.4 = bf16[16,64,512]{2,1,0:T(8,128)(2,1)} fusion(bf16[4,64,512]{2,1,0:T(8,128)(2,1)} %param.19, s32[1024]{0:T(1024)S(1)} %pad_clamp_fusion.1), kind=kCustom, calls=%fused_computation.4 | custom fusion | bytes 2097216 | tf_op jit(solution)/shard_map/jit(_take)/gather | solution.py:103
  7.0 1.8 gather.48
  8.9 1.7 gather_fusion.2
  10.6 2.2 gather.44
  13.1 3.1 %broadcast_select_fusion.1 = (bf16[8,2,32768]{2,1,0:T(2,128)(2,1)S(1)}, bf16[8,2,32768]{2,1,0:T(2,128)(2,1)S(1)}) fusion(bf16[8,2,32768]{2,1,0:T(2,128)(2,1)} %gather.44, pred[8,2]{1,0:T(8,128)(4,1)S(1)} %copy.103, bf16[8,2,32768]{2,1,0:T(2,128)(2,1)S(1)} %gather.48), kind=kLoop, calls=%fused_computation.15 | loop fusion | flops 1048576 | bytes 4194320 | tf_op jit(solution)/shard_map/jit(_take)/select_n | solution.py:101
  16.2 3.3 %pad_maximum_fusion = bf16[8,2,73728]{2,1,0:T(2,128)(2,1)} fusion(bf16[8,2,32768]{2,1,0:T(2,128)(2,1)S(1)} %get-tuple-element.25, bf16[8,2,8192]{2,1,0:T(2,128)(2,1)S(1)} %broadcast_select_fusion.3, bf16[8,2,32768]{2,1,0:T(2,128)(2,1)S(1)} %get-tuple-element.24), kind=kLoop, calls=%fused_computation.7 | loop fusion | flops 7077888 | bytes 4718592 | tf_op jit(solution)/shard_map/concatenate | solution.py:106
  19.4 6.7 %all-to-all-start.2 = ((bf16[8,2,73728]{2,1,0:T(2,128)(2,1)}), bf16[8,2,73728]{2,1,0:T(2,128)(2,1)}, u32[]{:S(2)}, u32[]{:S(2)}) async-start(bf16[8,2,73728]{2,1,0:T(2,128)(2,1)} %pad_maximum_fusion), calls=%async_computation.2 | async-start | bytes 4718592 | tf_op jit(solution)/shard_map/all_to_all | solution.py:114
  26.9 1.8 gather_fusion
  28.8 1.2 select_multiply_fusion
  30.0 27.1 %all-to-all-done.2 = bf16[8,2,73728]{2,1,0:T(2,128)(2,1)} async-done(((bf16[8,2,73728]{2,1,0:T(2,128)(2,1)}), bf16[8,2,73728]{2,1,0:T(2,128)(2,1)}, u32[]{:S(2)}, u32[]{:S(2)}) %all-to-all-start.2) | async-done | bytes 2359328 | tf_op jit(solution)/shard_map/all_to_all | solution.py:114
  57.1 7.0 %all-to-all-start = ((bf16[32,16,1024]{2,1,0:T(8,128)(2,1)}), bf16[32,16,1024]{2,1,0:T(8,128)(2,1)}, u32[]{:S(2)}, u32[]{:S(2)}) async-start(bf16[32,16,1024]{2,1,0:T(8,128)(2,1)} %select_multiply_fusion), calls=%async_computation | async-start | bytes 2097152 | tf_op jit(solution)/shard_map/all_to_all | solution.py:188
  64.0 3.2 %reshape.349 = bf16[16,73728]{1,0:T(8,128)(2,1)} reshape(bf16[8,2,73728]{2,1,0:T(2,128)(2,1)} %all-to-all-done.2) | data formatting | bytes 4718592 | tf_op jit(solution)/shard_map/reshape | solution.py:114
  67.3 2.7 %fusion.71 = (bf16[16,32768]{1,0:T(8,128)(2,1)}, bf16[2,8,256,128]{3,1,2,0:T(8,128)(2,1)S(1)}) fusion(bf16[16,73728]{1,0:T(8,128)(2,1)} %reshape.349), kind=kLoop, calls=%fused_computation.102 | loop fusion | bytes 4194304 | tf_op jit(solution)/shard_map/slice | solution.py:121
  70.1 2.1 gather_fusion.6
  72.2 2.0 fusion.8
  74.3 3.0 %all-to-all-done = bf16[32,16,1024]{2,1,0:T(8,128)(2,1)} async-done(((bf16[32,16,1024]{2,1,0:T(8,128)(2,1)}), bf16[32,16,1024]{2,1,0:T(8,128)(2,1)}, u32[]{:S(2)}, u32[]{:S(2)}) %all-to-all-start) | async-done | bytes 1048608 | tf_op jit(solution)/shard_map/all_to_all | solution.py:188
  77.3 1.1 broadcast_in_dim.134
  78.4 12.0 %all-to-all-start.1 = ((bf16[32,2,32,256]{3,2,1,0:T(8,128)(2,1)}), bf16[32,2,32,256]{3,2,1,0:T(8,128)(2,1)S(1)}, u32[]{:S(2)}, u32[]{:S(2)}) async-start(bf16[32,2,32,256]{3,2,1,0:T(8,128)(2,1)} %broadcast_in_dim.134), calls=%async_computation.1 | async-start | bytes 2097152 | tf_op jit(solution)/shard_map/all_to_all | solution.py:127
  90.5 2.0 all_to_all.35
  92.5 27.0 %all-to-all-done.1 = bf16[32,2,32,256]{3,2,1,0:T(8,128)(2,1)S(1)} async-done(((bf16[32,2,32,256]{3,2,1,0:T(8,128)(2,1)}), bf16[32,2,32,256]{3,2,1,0:T(8,128)(2,1)S(1)}, u32[]{:S(2)}, u32[]{:S(2)}) %all-to-all-start.1) | async-done | bytes 1048608 | tf_op jit(solution)/shard_map/all_to_all | solution.py:127
  119.5 1.1 copy-done.1
  120.6 4.8 %all-to-all-start.3 = ((f32[32,1,10240]{2,1,0:T(1,128)}), f32[32,1,10240]{2,1,0:T(1,128)S(1)}, u32[]{:S(2)}, u32[]{:S(2)}) async-start(f32[32,1,10240]{2,1,0:T(1,128)} %all_to_all.35), calls=%async_computation.3 | async-start | bytes 2621440 | tf_op jit(solution)/shard_map/all_to_all | solution.py:145
  129.0 3.0 %pad_maximum_fusion.1 = bf16[64,16,1024]{2,1,0:T(8,128)(2,1)} fusion(bf16[32,16,1024]{2,1,0:T(8,128)(2,1)} %all-to-all-done, bf16[32,16,1024]{2,1,0:T(8,128)(2,1)} %param.20), kind=kLoop, calls=%fused_computation.8 | loop fusion | flops 1048576 | bytes 4194304 | tf_op jit(solution)/shard_map/concatenate | solution.py:189
  132.1 3.2 %gather_fusion.1 = bf16[32,16,1024]{2,1,0:T(8,128)(2,1)} fusion(bf16[64,16,1024]{2,1,0:T(8,128)(2,1)} %pad_maximum_fusion.1, s32[1024]{0:T(1024)S(1)} %pad_clamp_fusion.2), kind=kCustom, calls=%fused_computation.1 | custom fusion | bytes 2097280 | tf_op jit(solution)/shard_map/jit(_take)/gather | solution.py:190
  135.2 2.3 copy.100
  137.5 1.4 broadcast_select_fusion.2
  138.9 1.1 fusion.72
  140.0 1.0 copy.137
  141.0 1.3 copy.141
  142.3 1.0 slice_bitcast_fusion.1
  143.3 0.8 copy.139
  144.1 2.4 gather_fusion.5
  146.4 13.1 %all-to-all-done.3 = f32[32,1,10240]{2,1,0:T(1,128)S(1)} async-done(((f32[32,1,10240]{2,1,0:T(1,128)}), f32[32,1,10240]{2,1,0:T(1,128)S(1)}, u32[]{:S(2)}, u32[]{:S(2)}) %all-to-all-start.3) | async-done | bytes 1310752 | tf_op jit(solution)/shard_map/all_to_all | solution.py:145
  160.3 1.4 fusion.29
  161.7 1.8 fusion.19
  164.1 5.5 %all-to-all-start.4 = ((bf16[2,32,1,128]{3,0,2,1:T(2,128)(2,1)}), bf16[2,32,1,128]{3,0,2,1:T(2,128)(2,1)S(1)}, u32[]{:S(2)}, u32[]{:S(2)}) async-start(bf16[2,32,1,128]{3,0,2,1:T(2,128)(2,1)} %copy.110), calls=%async_computation.4 | async-start | bytes 32768 | tf_op jit(solution)/shard_map/all_to_all | solution.py:175
  169.7 9.6 %all-to-all-done.4 = bf16[2,32,1,128]{3,0,2,1:T(2,128)(2,1)S(1)} async-done(((bf16[2,32,1,128]{3,0,2,1:T(2,128)(2,1)}), bf16[2,32,1,128]{3,0,2,1:T(2,128)(2,1)S(1)}, u32[]{:S(2)}, u32[]{:S(2)}) %all-to-all-start.4) | async-done | bytes 16416 | tf_op jit(solution)/shard_map/all_to_all | solution.py:175
  180.4 1.1 fusion.22
  182.1 3.8 %all-to-all-start.5 = ((bf16[2,1,32,128]{3,0,1,2:T(2,128)(2,1)}), bf16[2,1,32,128]{3,0,1,2:T(2,128)(2,1)S(1)}, u32[]{:S(2)}, u32[]{:S(2)}) async-start(bf16[2,1,32,128]{3,0,1,2:T(2,128)(2,1)} %copy.121), calls=%async_computation.5 | async-start | bytes 32768 | tf_op jit(solution)/shard_map/all_to_all | solution.py:194
  186.0 4.1 %copy.134 = bf16[8192,128]{1,0:T(8,128)(2,1)} copy(bf16[8192,128]{0,1:T(8,128)(2,1)} %bitcast.152) | data formatting | bytes 4194304 | tf_op jit(solution)/shard_map/dot_general | solution.py:195
  190.1 5.6 %all-to-all-done.5 = bf16[2,1,32,128]{3,0,1,2:T(2,128)(2,1)S(1)} async-done(((bf16[2,1,32,128]{3,0,1,2:T(2,128)(2,1)}), bf16[2,1,32,128]{3,0,1,2:T(2,128)(2,1)S(1)}, u32[]{:S(2)}, u32[]{:S(2)}) %all-to-all-start.5) | async-done | bytes 16416 | tf_op jit(solution)/shard_map/all_to_all | solution.py:194
  195.6 2.4 fusion.74
  198.1 55.7 %all_to_all.47 = f32[64,32,256]{2,0,1:T(8,128)} all-to-all(f32[64,32,256]{2,0,1:T(8,128)S(1)} %fusion.74), channel_id=1, replica_groups=mesh['group'=8,'tp'=32] {'tp'}, dimensions={1} | all-to-all | bytes 4194304 | tf_op jit(solution)/shard_map/all_to_all | solution.py:202
  253.8 2.3 reduce_sum.39
  (73 shorter events, 5.8 us)
Async XLA Ops:
  0.0 161.7 %copy-start = (bf16[8192,128]{1,0:T(8,128)(2,1)S(1)}, bf16[8192,128]{1,0:T(8,128)(2,1)}, u32[]{:S(2)}) copy-start(bf16[8192,128]{1,0:T(8,128)(2,1)} %param.14) | copy-start | bytes 6291460
  4.4 4.4 %copy-start.3 = (bf16[4,256,128]{2,1,0:T(8,128)(2,1)S(1)}, bf16[4,256,128]{2,1,0:T(8,128)(2,1)}, u32[]{:S(2)}) copy-start(bf16[4,256,128]{2,1,0:T(8,128)(2,1)} %param.17) | copy-start | bytes 786436
  10.6 2.2 copy-start.7
  19.4 6.7 %copy-start.10 = (s32[1,1,8,4]{2,3,1,0:T(4,128)S(1)}, s32[1,1,8,4]{2,3,1,0:T(4,128)}, u32[]{:S(2)}) copy-start(s32[1,1,8,4]{2,3,1,0:T(4,128)} %param.23) | copy-start | bytes 388
  19.4 7.2 %copy-start.8 = (bf16[256,1024]{1,0:T(8,128)(2,1)S(1)}, bf16[256,1024]{1,0:T(8,128)(2,1)}, u32[]{:S(2)}) copy-start(bf16[256,1024]{1,0:T(8,128)(2,1)} %param.15) | copy-start | bytes 1572868
  19.4 7.2 %copy-start.9 = (bf16[2,32,256]{2,1,0:T(8,128)(2,1)S(1)}, bf16[2,32,256]{2,1,0:T(8,128)(2,1)}, u32[]{:S(2)}) copy-start(bf16[2,32,256]{2,1,0:T(8,128)(2,1)} %param.13) | copy-start | bytes 98308
  19.4 37.6 %all-to-all-start.2 = ((bf16[8,2,73728]{2,1,0:T(2,128)(2,1)}), bf16[8,2,73728]{2,1,0:T(2,128)(2,1)}, u32[]{:S(2)}, u32[]{:S(2)}) async-start(bf16[8,2,73728]{2,1,0:T(2,128)(2,1)} %pad_maximum_fusion), calls=%async_computation.2 | async-start | bytes 4718592 | tf_op jit(solution)/shard_map/all_to_all | solution.py:114
  26.1 2.7 %copy-start.11 = (s32[32]{0:T(128)S(1)}, s32[32]{0:T(128)}, u32[]{:S(2)}) copy-start(s32[32]{0:T(128)} %param.24) | copy-start | bytes 388
  57.1 20.2 %all-to-all-start = ((bf16[32,16,1024]{2,1,0:T(8,128)(2,1)}), bf16[32,16,1024]{2,1,0:T(8,128)(2,1)}, u32[]{:S(2)}, u32[]{:S(2)}) async-start(bf16[32,16,1024]{2,1,0:T(8,128)(2,1)} %select_multiply_fusion), calls=%async_computation | async-start | bytes 2097152 | tf_op jit(solution)/shard_map/all_to_all | solution.py:188
  78.4 41.2 %all-to-all-start.1 = ((bf16[32,2,32,256]{3,2,1,0:T(8,128)(2,1)}), bf16[32,2,32,256]{3,2,1,0:T(8,128)(2,1)S(1)}, u32[]{:S(2)}, u32[]{:S(2)}) async-start(bf16[32,2,32,256]{3,2,1,0:T(8,128)(2,1)} %broadcast_in_dim.134), calls=%async_computation.1 | async-start | bytes 2097152 | tf_op jit(solution)/shard_map/all_to_all | solution.py:127
  90.5 38.3 %copy-start.12 = (s32[1,32]{1,0:T(1,128)S(1)}, s32[1,32]{1,0:T(1,128)}, u32[]{:S(2)}) copy-start(s32[1,32]{1,0:T(1,128)} %param.22) | copy-start | bytes 388
  119.5 1.1 copy-start.1
  120.6 38.9 %all-to-all-start.3 = ((f32[32,1,10240]{2,1,0:T(1,128)}), f32[32,1,10240]{2,1,0:T(1,128)S(1)}, u32[]{:S(2)}, u32[]{:S(2)}) async-start(f32[32,1,10240]{2,1,0:T(1,128)} %all_to_all.35), calls=%async_computation.3 | async-start | bytes 2621440 | tf_op jit(solution)/shard_map/all_to_all | solution.py:145
  137.5 2.5 copy-start.2
  138.9 2.1 copy-start.4
  160.3 19.3 %copy-start.6 = (bf16[1,512,512]{1,2,0:T(8,128)(2,1)S(1)}, bf16[1,512,512]{1,2,0:T(8,128)(2,1)}, u32[]{:S(2)}) copy-start(bf16[1,512,512]{1,2,0:T(8,128)(2,1)} %get-tuple-element.18) | copy-start | bytes 1572868
  161.7 18.4 %copy-start.5 = (bf16[1,512,512]{1,2,0:T(8,128)(2,1)S(1)}, bf16[1,512,512]{1,2,0:T(8,128)(2,1)}, u32[]{:S(2)}) copy-start(bf16[1,512,512]{1,2,0:T(8,128)(2,1)} %get-tuple-element.19) | copy-start | bytes 1572868
  164.1 15.2 %all-to-all-start.4 = ((bf16[2,32,1,128]{3,0,2,1:T(2,128)(2,1)}), bf16[2,32,1,128]{3,0,2,1:T(2,128)(2,1)S(1)}, u32[]{:S(2)}, u32[]{:S(2)}) async-start(bf16[2,32,1,128]{3,0,2,1:T(2,128)(2,1)} %copy.110), calls=%async_computation.4 | async-start | bytes 32768 | tf_op jit(solution)/shard_map/all_to_all | solution.py:175
  182.1 13.5 %all-to-all-start.5 = ((bf16[2,1,32,128]{3,0,1,2:T(2,128)(2,1)}), bf16[2,1,32,128]{3,0,1,2:T(2,128)(2,1)S(1)}, u32[]{:S(2)}, u32[]{:S(2)}) async-start(bf16[2,1,32,128]{3,0,1,2:T(2,128)(2,1)} %copy.121), calls=%async_computation.5 | async-start | bytes 32768 | tf_op jit(solution)/shard_map/all_to_all | solution.py:194

commit v2 on v1

--- a/solution.py
+++ b/solution.py
@@ -97,23 +97,30 @@
     cap_slots = read_rows_list.shape[2]
     own_start = column_id * batch_own
 
-    send_rows = jnp.maximum(read_rows_list[:, group_number, :], 0)
-    down_send = jnp.take(adapter_down_weight, send_rows, axis=0)
-    upq_send = jnp.take(adapter_up_query, send_rows, axis=0)
-    upv_send = jnp.take(adapter_up_value, send_rows, axis=0)
-    down_size = down_send[0, 0].size
-    upq_size = upq_send[0, 0].size
-    panel_send = jnp.concatenate(
+    local_panels = jnp.concatenate(
         [
-            down_send.reshape(n_group, cap_slots, -1),
-            upq_send.reshape(n_group, cap_slots, -1),
-            upv_send.reshape(n_group, cap_slots, -1),
+            adapter_down_weight.reshape(adapter_down_weight.shape[0], -1),
+            adapter_up_query.reshape(adapter_up_query.shape[0], -1),
+            adapter_up_value.reshape(adapter_up_value.shape[0], -1),
         ],
         -1,
     )
-    panel_recv = lax.all_to_all(panel_send, "group", 0, 0, tiled=True).reshape(
-        n_group * cap_slots, -1
-    )
+    send_rows = jnp.maximum(read_rows_list[:, group_number, :], 0)
+    panel_send = jnp.take(local_panels, send_rows.reshape(-1), axis=0).reshape(n_group, -1)
+    move_row = page_send_list[0, 0]
+    present_pages = (move_row >= 0).reshape(-1)
+    outgoing = (
+        jnp.take(key_value_pool, jnp.maximum(move_row, 0).reshape(-1), axis=0)
+        * present_pages.astype(key_value_pool.dtype)[:, None, None]
+    )
+    panel_width = panel_send.shape[1]
+    group_recv = lax.all_to_all(
+        jnp.concatenate([panel_send, outgoing.reshape(n_group, -1)], -1), "group", 0, 0, tiled=True
+    )
+    panel_recv = group_recv[:, :panel_width].reshape(n_group * cap_slots, -1)
+    arrived_pages = group_recv[:, panel_width:].reshape((-1,) + key_value_pool.shape[1:])
+    down_size = adapter_down_weight[0].size
+    upq_size = adapter_up_query[0].size
     down_recv = panel_recv[:, :down_size].reshape((-1,) + adapter_down_weight.shape[1:])
     upq_recv = panel_recv[:, down_size : down_size + upq_size].reshape(
         (-1,) + adapter_up_query.shape[1:]
@@ -131,24 +138,25 @@
         step_count, batch_rows, n_tp * width_local
     )
 
-    shrink_part = jnp.einsum("srd,rdk->srk", hidden, down_rows, preferred_element_type=jnp.float32)
+    shrink_part = jnp.einsum("srd,rdk->rsk", hidden, down_rows, preferred_element_type=jnp.float32)
     key_value_part = jnp.einsum(
         "srd,dc->rsc", hidden, key_value_weight, preferred_element_type=jnp.float32
-    ).reshape(n_tp, batch_own * step_count * 2 * key_span_width)
+    )
     reduce_send = jnp.concatenate(
         [
-            key_value_part,
-            jnp.broadcast_to(shrink_part.reshape(1, -1), (n_tp, shrink_part.size)),
+            key_value_part.reshape(n_tp, -1),
+            shrink_part.reshape(n_tp, -1),
         ],
         -1,
     )
     reduce_recv = jnp.sum(lax.all_to_all(reduce_send, "tp", 0, 0, tiled=True), 0)
-    key_value_plain = reduce_recv[: key_value_part.shape[1]].reshape(
-        batch_own, step_count, 2 * key_span_width
-    )
-    down_projected_low = (
-        reduce_recv[key_value_part.shape[1] :].reshape(shrink_part.shape).astype(jnp.bfloat16)
-    )
+    kv_size = key_value_part[0].size * batch_own
+    key_value_plain = reduce_recv[:kv_size].reshape(batch_own, step_count, 2 * key_span_width)
+    shrink_own = reduce_recv[kv_size:].reshape(batch_own, step_count, -1).astype(jnp.bfloat16)
+    shrink_all = lax.all_to_all(
+        jnp.broadcast_to(shrink_own[None], (n_tp,) + shrink_own.shape), "tp", 0, 0, tiled=True
+    )
+    down_projected_low = jnp.transpose(shrink_all.reshape(batch_rows, step_count, -1), (1, 0, 2))
 
     query_plain = jnp.einsum(
         "srd,dc->src", hidden_full, query_weight, preferred_element_type=jnp.float32
@@ -160,9 +168,8 @@
         preferred_element_type=jnp.float32,
     )
     query_rows = (query_plain + ADAPTER_SCALE * query_adapter_term).astype(jnp.bfloat16)
-    shrink_own = lax.dynamic_slice_in_dim(down_projected_low, own_start, batch_own, 1)
     value_adapter_term = ADAPTER_SCALE * jnp.einsum(
-        "srk,rkc->rsc", shrink_own[..., ADAPTER_RANK:], upv_rows, preferred_element_type=jnp.float32
+        "rsk,rkc->rsc", shrink_own[..., ADAPTER_RANK:], upv_rows, preferred_element_type=jnp.float32
     )
     keyval_new = jnp.concatenate(
         [
@@ -179,13 +186,6 @@
         concat_axis=2,
         tiled=True,
     )
-    move_row = page_send_list[0, 0]
-    present_pages = (move_row >= 0).reshape(-1)
-    outgoing = (
-        jnp.take(key_value_pool, jnp.maximum(move_row, 0).reshape(-1), axis=0)
-        * present_pages.astype(key_value_pool.dtype)[:, None, None]
-    )
-    arrived_pages = lax.all_to_all(outgoing, "group", split_axis=0, concat_axis=0, tiled=True)
     combined = jnp.concatenate([key_value_pool, arrived_pages], 0)
     ctx_pages = jnp.take(combined, request_page_table.reshape(-1), axis=0).reshape(
         batch_own, -1, 2 * key_span_width

time: 259 us -> 292 us (1.13)
  local copies, waits for them, and re-layouts: 44.8 us -> 78.9 us
  waiting for transfers between devices: 85.2 us -> 58.5 us
  other arithmetic: 17.8 us -> 31.5 us
  starting transfers between devices: 39.8 us -> 49.7 us
    all_to_all x1, waiting for transfers between devices: 27 us -> 0.01 us  [per_device(): lax.all_to_all(jnp.broadcast_to(hidden[None], (n_tp,) + hidden.shape), 't...]
    unnamed x30 -> x25, local copies, waits for them, and re-layouts: 4.36 us -> 29.6 us
    all_to_all x2, waiting for transfers between devices: 30 us -> 51.1 us  [the longest x1 43.8 us: per_device(): lax.all_to_all(jnp.concatenate([panel_send, outgoing.reshape(n_group, -1)...]
    all_to_all x0 -> x3, other arithmetic: none -> 16.5 us  [the longest x2 16.5 us: per_device(): lax.all_to_all(jnp.concatenate([panel_send, outgoing.reshape(n_group, -1)...]
    all_to_all x1, waiting for transfers between devices: 13.1 us -> 0.01 us  [per_device(): lax.all_to_all(reduce_send, 'tp', 0, 0, tiled=True)]
    all_to_all x1, waiting for transfers between devices: 9.56 us -> 1.88 us  [per_device(): lax.all_to_all(query_rows.reshape(step_count, batch_rows, heads_local, HE...]
    slice x4, local copies, waits for them, and re-layouts: 0.11 us -> 5.81 us  [the longest x1 2.29 us: per_device(): group_recv[:, panel_width:].reshape((-1,) + key_value_pool.shape[1:])]
    all_to_all x1, starting transfers between devices: 4.82 us -> 9.49 us  [per_device(): lax.all_to_all(reduce_send, 'tp', 0, 0, tiled=True)]
  transfers between devices with their start and end apart: 6 -> 6, of which waited for: 6 -> 4; matrix products, arithmetic and copies ran while one was open for 14% -> 21% of each run, Pallas kernels for 0% -> 0%
where the time goes in v2:
time: 292 us; the launch traced here: 288 us
  local copies, waits for them, and re-layouts  78.9 us (27%)
  waiting for transfers between devices  58.5 us (20%)
  blocking collectives  55.7 us (19%)
  starting transfers between devices  49.7 us (17%)
  other arithmetic  31.5 us (11%)
  matrix products  10.5 us (4%)
  between operations  2.93 us (1%)
    all_to_all x1, blocking collectives, per_device(): lax.all_to_all(projected.reshape(step_count * batch_rows, n_tp, out_cols)...  55.7 us
    all_to_all x1, waiting for transfers between devices, per_device(): lax.all_to_all(jnp.concatenate([panel_send, outgoing.reshape(n_group, -1)...  43.8 us
    unnamed x25, local copies, waits for them, and re-layouts  29.6 us
    all_to_all x2, other arithmetic, per_device(): lax.all_to_all(jnp.concatenate([panel_send, outgoing.reshape(n_group, -1)...  16.5 us
    all_to_all x1, starting transfers between devices, per_device(): lax.all_to_all(jnp.broadcast_to(hidden[None], (n_tp,) + hidden.shape), 't...  12 us
    all_to_all x1, starting transfers between devices, per_device(): lax.all_to_all(jnp.broadcast_to(shrink_own[None], (n_tp,) + shrink_own.sh...  9.78 us
    all_to_all x1, starting transfers between devices, per_device(): lax.all_to_all(reduce_send, 'tp', 0, 0, tiled=True)  9.49 us
    all_to_all x1, starting transfers between devices, per_device(): lax.all_to_all(attended, 'tp', split_axis=2, concat_axis=1, tiled=True)  7.89 us
  transfers between devices with their start and end apart: 6, of which 4 were waited for; matrix products, arithmetic and copies ran while one was open for 21% of the time, Pallas kernels for 0%

profile of v2, /device:TPU:2, one launch (start us, length us, event | category | flops | bytes accessed | tf_op | source)
XLA Modules:
  0.0 287.8 jit_solution(1649858013308848770)
XLA Ops:
  3.4 1.2 copy.164
  4.5 1.2 copy.128
  6.9 3.5 %gather_fusion = bf16[16,73728]{1,0:T(8,128)(2,1)} fusion(bf16[4,73728]{1,0:T(4,128)(2,1)S(1)} %pad_maximum_fusion.1, s32[1024]{0:T(1024)S(1)} %pad_clamp_fusion.3), kind=kCustom, calls=%fused_computation | custom fusion | bytes 4718656 | tf_op jit(solution)/shard_map/jit(_take)/gather | solution.py:109
  10.4 4.0 %gather.29 = bf16[8,147456]{1,0:T(8,128)(2,1)} reshape(bf16[16,73728]{1,0:T(8,128)(2,1)} %gather_fusion) | data formatting | bytes 4718592 | tf_op jit(solution)/shard_map/jit(_take)/gather | solution.py:109
  15.1 1.8 gather_fusion.1
  16.9 1.1 select_multiply_fusion
  18.1 1.7 mul.54
  20.1 2.0 broadcast_select_fusion
  22.1 11.0 %maximum_bitcast_fusion = bf16[8,1,212992]{2,0,1:T(8,128)(2,1)} fusion(bf16[8,65536]{1,0:T(8,128)(2,1)S(1)} %mul.54, bf16[8,147456]{1,0:T(8,128)(2,1)S(1)} %broadcast_select_fusion), kind=kLoop, calls=%fused_computation.5 | loop fusion | flops 6815744 | bytes 6815744 | tf_op jit(solution)/shard_map/all_to_all | solution.py:117
  33.6 5.5 %reduce.7 = bf16[8,212992]{1,0:T(8,128)(2,1)} reduce(bf16[8,1,212992]{2,0,1:T(8,128)(2,1)} %maximum_bitcast_fusion, bf16[]{:T(256)} %broadcast.243), dimensions={1}, to_apply=%copy.90.reduce_sub_computation | reduce | bytes 6815746 | tf_op jit(solution)/shard_map/all_to_all | solution.py:117
  39.1 6.9 %reshape.486 = bf16[8,2,106496]{2,1,0:T(2,128)(2,1)} reshape(bf16[8,212992]{1,0:T(8,128)(2,1)} %reduce.7) | data formatting | bytes 6815744
  46.0 6.8 %all-to-all-start = ((bf16[8,2,106496]{2,1,0:T(2,128)(2,1)}), bf16[8,2,106496]{2,1,0:T(2,128)(2,1)}, u32[]{:S(2)}, u32[]{:S(2)}) async-start(bf16[8,2,106496]{2,1,0:T(2,128)(2,1)} %reshape.486), calls=%async_computation | async-start | bytes 6815744 | tf_op jit(solution)/shard_map/all_to_all | solution.py:117
  53.8 43.8 %all-to-all-done = bf16[8,2,106496]{2,1,0:T(2,128)(2,1)} async-done(((bf16[8,2,106496]{2,1,0:T(2,128)(2,1)}), bf16[8,2,106496]{2,1,0:T(2,128)(2,1)}, u32[]{:S(2)}, u32[]{:S(2)}) %all-to-all-start) | async-done | bytes 3407904 | tf_op jit(solution)/shard_map/all_to_all | solution.py:117
  98.7 12.0 %all-to-all-start.1 = ((bf16[32,2,32,256]{3,2,1,0:T(8,128)(2,1)}), bf16[32,2,32,256]{3,2,1,0:T(8,128)(2,1)}, u32[]{:S(2)}, u32[]{:S(2)}) async-start(bf16[32,2,32,256]{3,2,1,0:T(8,128)(2,1)} %broadcast_in_dim.122), calls=%async_computation.1 | async-start | bytes 2097152 | tf_op jit(solution)/shard_map/all_to_all | solution.py:134
  110.7 8.0 %reshape.487 = bf16[8,1,212992]{2,1,0:T(2,128)(2,1)} reshape(bf16[8,2,106496]{2,1,0:T(2,128)(2,1)} %all-to-all-done) | data formatting | bytes 6815744
  118.7 7.3 %copy.163 = bf16[8,1,212992]{2,0,1:T(8,128)(2,1)S(1)} copy(bf16[8,1,212992]{2,1,0:T(2,128)(2,1)} %reshape.487) | data formatting | bytes 6815744
  126.0 1.7 copy-done.1
  127.7 1.5 slice.88
  129.2 4.0 %reshape.388 = bf16[16,73728]{1,0:T(8,128)(2,1)} reshape(bf16[8,147456]{1,0:T(8,128)(2,1)} %slice.88) | data formatting | bytes 4718592 | tf_op jit(solution)/shard_map/reshape | solution.py:120
  133.2 2.8 fusion.70
  136.2 2.1 gather_fusion.4
  138.3 2.0 fusion.2
  141.4 9.5 %all-to-all-start.2 = ((f32[32,1,2304]{2,1,0:T(1,128)}), f32[32,1,2304]{2,1,0:T(1,128)S(1)}, u32[]{:S(2)}, u32[]{:S(2)}) async-start(f32[32,1,2304]{2,1,0:T(1,128)} %copy.95), calls=%async_computation.2 | async-start | bytes 589824 | tf_op jit(solution)/shard_map/all_to_all | solution.py:152
  153.7 1.3 copy.124
  155.0 2.3 slice.86
  157.3 2.7 reshape.384
  159.9 3.1 %pad_maximum_fusion = bf16[64,16,1024]{2,1,0:T(8,128)(2,1)} fusion(bf16[32,16,1024]{2,1,0:T(8,128)(2,1)} %reshape.384, bf16[32,16,1024]{2,1,0:T(8,128)(2,1)} %param.20), kind=kLoop, calls=%fused_computation.7 | loop fusion | flops 1048576 | bytes 4194304 | tf_op jit(solution)/shard_map/concatenate | solution.py:189
  163.0 3.2 %gather_fusion.2 = bf16[32,16,1024]{2,1,0:T(8,128)(2,1)} fusion(bf16[64,16,1024]{2,1,0:T(8,128)(2,1)} %pad_maximum_fusion, s32[1024]{0:T(1024)S(1)} %pad_clamp_fusion.1), kind=kCustom, calls=%fused_computation.2 | custom fusion | bytes 2097280 | tf_op jit(solution)/shard_map/jit(_take)/gather | solution.py:190
  166.1 2.4 bitcast_select_fusion
  169.3 9.8 %all-to-all-start.3 = ((bf16[32,1,2,128]{3,2,1,0:T(2,128)(2,1)}), bf16[32,1,2,128]{3,2,1,0:T(2,128)(2,1)S(1)}, u32[]{:S(2)}, u32[]{:S(2)}) async-start(bf16[32,1,2,128]{3,2,1,0:T(2,128)(2,1)} %broadcast_in_dim.128), calls=%async_computation.3 | async-start | bytes 32768 | tf_op jit(solution)/shard_map/all_to_all | solution.py:156
  180.2 1.4 gather_fusion.3
  181.6 7.2 %all-to-all-done.3 = bf16[32,1,2,128]{3,2,1,0:T(2,128)(2,1)S(1)} async-done(((bf16[32,1,2,128]{3,2,1,0:T(2,128)(2,1)}), bf16[32,1,2,128]{3,2,1,0:T(2,128)(2,1)S(1)}, u32[]{:S(2)}, u32[]{:S(2)}) %all-to-all-start.3) | async-done | bytes 16416 | tf_op jit(solution)/shard_map/all_to_all | solution.py:156
  188.8 1.3 fusion.26
  191.3 3.8 %all-to-all-start.4 = ((bf16[2,32,1,128]{3,0,2,1:T(2,128)(2,1)}), bf16[2,32,1,128]{3,0,2,1:T(2,128)(2,1)S(1)}, u32[]{:S(2)}, u32[]{:S(2)}) async-start(bf16[2,32,1,128]{3,0,2,1:T(2,128)(2,1)} %copy.97), calls=%async_computation.4 | async-start | bytes 32768 | tf_op jit(solution)/shard_map/all_to_all | solution.py:182
  195.1 2.3 fusion.71
  197.4 2.1 copy.91
  199.5 2.1 copy.103
  201.6 1.3 copy.132
  202.9 1.9 all-to-all-done.4
  205.0 1.3 fusion.72
  206.6 1.3 fusion.33
  208.0 1.1 fusion.19
  209.8 7.9 %all-to-all-start.5 = ((bf16[2,1,32,128]{3,0,1,2:T(2,128)(2,1)}), bf16[2,1,32,128]{3,0,1,2:T(2,128)(2,1)S(1)}, u32[]{:S(2)}, u32[]{:S(2)}) async-start(bf16[2,1,32,128]{3,0,1,2:T(2,128)(2,1)} %copy.109), calls=%async_computation.5 | async-start | bytes 32768 | tf_op jit(solution)/shard_map/all_to_all | solution.py:194
  217.6 4.1 %copy.122 = bf16[8192,128]{1,0:T(8,128)(2,1)} copy(bf16[8192,128]{0,1:T(8,128)(2,1)} %bitcast.181) | data formatting | bytes 4194304 | tf_op jit(solution)/shard_map/dot_general | solution.py:195
  221.7 5.6 %all-to-all-done.5 = bf16[2,1,32,128]{3,0,1,2:T(2,128)(2,1)S(1)} async-done(((bf16[2,1,32,128]{3,0,1,2:T(2,128)(2,1)}), bf16[2,1,32,128]{3,0,1,2:T(2,128)(2,1)S(1)}, u32[]{:S(2)}, u32[]{:S(2)}) %all-to-all-start.5) | async-done | bytes 16416 | tf_op jit(solution)/shard_map/all_to_all | solution.py:194
  227.3 2.4 fusion.73
  229.7 55.7 %all_to_all.54 = f32[64,32,256]{2,0,1:T(8,128)} all-to-all(f32[64,32,256]{2,0,1:T(8,128)S(1)} %fusion.73), channel_id=1, replica_groups=mesh['group'=8,'tp'=32] {'tp'}, dimensions={1} | all-to-all | bytes 4194304 | tf_op jit(solution)/shard_map/all_to_all | solution.py:202
  285.4 2.3 reduce_sum.39
  (69 shorter events, 13.6 us)
Async XLA Ops:
  0.0 190.1 %copy-start = (bf16[8192,128]{1,0:T(8,128)(2,1)S(1)}, bf16[8192,128]{1,0:T(8,128)(2,1)}, u32[]{:S(2)}) copy-start(bf16[8192,128]{1,0:T(8,128)(2,1)} %param.14) | copy-start | bytes 6291460
  46.0 6.8 %copy-start.3 = (bf16[256,1024]{1,0:T(8,128)(2,1)S(1)}, bf16[256,1024]{1,0:T(8,128)(2,1)}, u32[]{:S(2)}) copy-start(bf16[256,1024]{1,0:T(8,128)(2,1)} %param.15) | copy-start | bytes 1572868
  46.0 6.8 %copy-start.4 = (bf16[2,32,256]{2,1,0:T(8,128)(2,1)S(1)}, bf16[2,32,256]{2,1,0:T(8,128)(2,1)}, u32[]{:S(2)}) copy-start(bf16[2,32,256]{2,1,0:T(8,128)(2,1)} %param.13) | copy-start | bytes 98308
  46.0 7.7 %copy-start.6 = (s32[32]{0:T(128)S(1)}, s32[32]{0:T(128)}, u32[]{:S(2)}) copy-start(s32[32]{0:T(128)} %param.24) | copy-start | bytes 388
  46.0 7.8 %copy-start.5 = (s32[1,32]{1,0:T(1,128)S(1)}, s32[1,32]{1,0:T(1,128)}, u32[]{:S(2)}) copy-start(s32[1,32]{1,0:T(1,128)} %param.22) | copy-start | bytes 388
  46.0 51.6 %all-to-all-start = ((bf16[8,2,106496]{2,1,0:T(2,128)(2,1)}), bf16[8,2,106496]{2,1,0:T(2,128)(2,1)}, u32[]{:S(2)}, u32[]{:S(2)}) async-start(bf16[8,2,106496]{2,1,0:T(2,128)(2,1)} %reshape.486), calls=%async_computation | async-start | bytes 6815744 | tf_op jit(solution)/shard_map/all_to_all | solution.py:117
  98.7 42.7 %all-to-all-start.1 = ((bf16[32,2,32,256]{3,2,1,0:T(8,128)(2,1)}), bf16[32,2,32,256]{3,2,1,0:T(8,128)(2,1)}, u32[]{:S(2)}, u32[]{:S(2)}) async-start(bf16[32,2,32,256]{3,2,1,0:T(8,128)(2,1)} %broadcast_in_dim.122), calls=%async_computation.1 | async-start | bytes 2097152 | tf_op jit(solution)/shard_map/all_to_all | solution.py:134
  126.0 1.7 copy-start.1
  141.4 27.1 %all-to-all-start.2 = ((f32[32,1,2304]{2,1,0:T(1,128)}), f32[32,1,2304]{2,1,0:T(1,128)S(1)}, u32[]{:S(2)}, u32[]{:S(2)}) async-start(f32[32,1,2304]{2,1,0:T(1,128)} %copy.95), calls=%async_computation.2 | async-start | bytes 589824 | tf_op jit(solution)/shard_map/all_to_all | solution.py:152
  169.3 19.4 %all-to-all-start.3 = ((bf16[32,1,2,128]{3,2,1,0:T(2,128)(2,1)}), bf16[32,1,2,128]{3,2,1,0:T(2,128)(2,1)S(1)}, u32[]{:S(2)}, u32[]{:S(2)}) async-start(bf16[32,1,2,128]{3,2,1,0:T(2,128)(2,1)} %broadcast_in_dim.128), calls=%async_computation.3 | async-start | bytes 32768 | tf_op jit(solution)/shard_map/all_to_all | solution.py:156
  191.3 13.5 %all-to-all-start.4 = ((bf16[2,32,1,128]{3,0,2,1:T(2,128)(2,1)}), bf16[2,32,1,128]{3,0,2,1:T(2,128)(2,1)S(1)}, u32[]{:S(2)}, u32[]{:S(2)}) async-start(bf16[2,32,1,128]{3,0,2,1:T(2,128)(2,1)} %copy.97), calls=%async_computation.4 | async-start | bytes 32768 | tf_op jit(solution)/shard_map/all_to_all | solution.py:182
  195.1 6.5 %copy-start.2 = (bf16[16,32768]{1,0:T(8,128)(2,1)S(1)}, bf16[16,32768]{1,0:T(8,128)(2,1)}, u32[]{:S(2)}) copy-start(bf16[16,32768]{1,0:T(8,128)(2,1)} %get-tuple-element.16) | copy-start | bytes 3145732
  209.8 17.6 %all-to-all-start.5 = ((bf16[2,1,32,128]{3,0,1,2:T(2,128)(2,1)}), bf16[2,1,32,128]{3,0,1,2:T(2,128)(2,1)S(1)}, u32[]{:S(2)}, u32[]{:S(2)}) async-start(bf16[2,1,32,128]{3,0,1,2:T(2,128)(2,1)} %copy.109), calls=%async_computation.5 | async-start | bytes 32768 | tf_op jit(solution)/shard_map/all_to_all | solution.py:194

commit v3 on v1

--- a/solution.py
+++ b/solution.py
@@ -96,6 +96,9 @@
     key_span_width = KEY_VALUE_HEADS * HEAD_SIZE
     cap_slots = read_rows_list.shape[2]
     own_start = column_id * batch_own
+    core = column_id % 2
+    swap = [(t, t ^ 1) for t in range(n_tp)]
+    parity = [[t for t in range(n_tp) if t % 2 == p] for p in range(2)]
 
     send_rows = jnp.maximum(read_rows_list[:, group_number, :], 0)
     down_send = jnp.take(adapter_down_weight, send_rows, axis=0)
@@ -124,9 +127,20 @@
     own_entry = lax.dynamic_slice_in_dim(request_adapter_entry, own_start, batch_own)
     upv_rows = jnp.take(upv_recv, own_entry, axis=0)
 
-    hidden_sent = lax.all_to_all(
-        jnp.broadcast_to(hidden[None], (n_tp,) + hidden.shape), "tp", 0, 0, tiled=True
-    )
+    hidden_same = lax.all_to_all(
+        jnp.broadcast_to(hidden[None], (n_tp // 2,) + hidden.shape),
+        "tp",
+        0,
+        0,
+        tiled=True,
+        axis_index_groups=parity,
+    )
+    hidden_other = lax.ppermute(hidden_same, "tp", swap)
+    hidden_sent = jnp.where(
+        core == 0,
+        jnp.stack([hidden_same, hidden_other], 1),
+        jnp.stack([hidden_other, hidden_same], 1),
+    ).reshape((n_tp,) + hidden.shape)
     hidden_full = jnp.transpose(hidden_sent, (1, 2, 0, 3)).reshape(
         step_count, batch_rows, n_tp * width_local
     )
@@ -134,20 +148,33 @@
     shrink_part = jnp.einsum("srd,rdk->srk", hidden, down_rows, preferred_element_type=jnp.float32)
     key_value_part = jnp.einsum(
         "srd,dc->rsc", hidden, key_value_weight, preferred_element_type=jnp.float32
-    ).reshape(n_tp, batch_own * step_count * 2 * key_span_width)
+    ).reshape(n_tp // 2, 2, batch_own * step_count * 2 * key_span_width)
+    pair_send = jnp.concatenate(
+        [
+            jnp.where(core == 0, key_value_part[:, 1], key_value_part[:, 0]).reshape(-1),
+            shrink_part.reshape(-1),
+        ]
+    )
+    pair_recv = lax.ppermute(pair_send, "tp", swap)
+    kv_pair = jnp.where(core == 0, key_value_part[:, 0], key_value_part[:, 1]) + pair_recv[
+        : key_value_part.shape[0] * key_value_part.shape[2]
+    ].reshape(key_value_part.shape[0], -1)
+    shrink_pair = shrink_part.reshape(-1) + pair_recv[key_value_part.shape[0] * key_value_part.shape[2] :]
     reduce_send = jnp.concatenate(
         [
-            key_value_part,
-            jnp.broadcast_to(shrink_part.reshape(1, -1), (n_tp, shrink_part.size)),
+            kv_pair,
+            jnp.broadcast_to(shrink_pair[None], (n_tp // 2, shrink_part.size)),
         ],
         -1,
     )
-    reduce_recv = jnp.sum(lax.all_to_all(reduce_send, "tp", 0, 0, tiled=True), 0)
-    key_value_plain = reduce_recv[: key_value_part.shape[1]].reshape(
+    reduce_recv = jnp.sum(
+        lax.all_to_all(reduce_send, "tp", 0, 0, tiled=True, axis_index_groups=parity), 0
+    )
+    key_value_plain = reduce_recv[: key_value_part.shape[2]].reshape(
         batch_own, step_count, 2 * key_span_width
     )
     down_projected_low = (
-        reduce_recv[key_value_part.shape[1] :].reshape(shrink_part.shape).astype(jnp.bfloat16)
+        reduce_recv[key_value_part.shape[2] :].reshape(shrink_part.shape).astype(jnp.bfloat16)
     )
 
     query_plain = jnp.einsum(
@@ -198,11 +225,13 @@
         preferred_element_type=jnp.float32,
     )
     out_cols = projected.shape[1] // n_tp
+    projected = projected.reshape(step_count * batch_rows, n_tp // 2, 2, out_cols)
+    out_other = lax.ppermute(
+        jnp.where(core == 0, projected[:, :, 1], projected[:, :, 0]), "tp", swap
+    )
+    out_pair = jnp.where(core == 0, projected[:, :, 0], projected[:, :, 1]) + out_other
     summed = jnp.sum(
-        lax.all_to_all(
-            projected.reshape(step_count * batch_rows, n_tp, out_cols), "tp", 1, 1, tiled=True
-        ),
-        1,
+        lax.all_to_all(out_pair, "tp", 1, 1, tiled=True, axis_index_groups=parity), 1
     )
     return summed.reshape(step_count, batch_rows, out_cols).astype(jnp.bfloat16)
 

time: 259 us -> 216 us (0.83)
  waiting for transfers between devices: 85.2 us -> 62.1 us
  blocking collectives: 55.7 us -> 34.4 us
  starting transfers between devices: 39.8 us -> 43.6 us
  local copies, waits for them, and re-layouts: 44.8 us -> 41 us
    all_to_all x2, waiting for transfers between devices: 40.1 us -> 16.3 us  [the longest x1 16 us: per_device(): lax.all_to_all(jnp.broadcast_to(hidden[None], (n_tp // 2,) + hidden.shape...]
    all_to_all x1, blocking collectives: 55.7 us -> 34.4 us  [per_device(): lax.all_to_all(out_pair, 'tp', 1, 1, tiled=True, axis_index_groups=parity)]
    ppermute x0 -> x3, waiting for transfers between devices: none -> 4.29 us  [the longest x1 2.65 us: per_device(): lax.ppermute(jnp.where(core == 0, projected[:, :, 1], projected[:, :, 0])...]
    all_to_all x1, starting transfers between devices: 5.51 us -> 9.52 us  [per_device(): lax.all_to_all(query_rows.reshape(step_count, batch_rows, heads_local, HE...]
  transfers between devices with their start and end apart: 6 -> 9, of which waited for: 6 -> 9; matrix products, arithmetic and copies ran while one was open for 14% -> 17% of each run, Pallas kernels for 0% -> 0%
where the time goes in v3:
time: 216 us; the launch traced here: 214 us
  waiting for transfers between devices  62.1 us (29%)
  starting transfers between devices  43.6 us (20%)
  local copies, waits for them, and re-layouts  41 us (19%)
  blocking collectives  34.4 us (16%)
  other arithmetic  19.7 us (9%)
  matrix products  10.5 us (5%)
  between operations  3.09 us (1%)
    all_to_all x1, blocking collectives, per_device(): lax.all_to_all(out_pair, 'tp', 1, 1, tiled=True, axis_index_groups=parity)  34.4 us
    all_to_all x1, waiting for transfers between devices, per_device(): lax.all_to_all(panel_send, 'group', 0, 0, tiled=True)  25.7 us
    all_to_all x1, waiting for transfers between devices, per_device(): lax.all_to_all(jnp.broadcast_to(hidden[None], (n_tp // 2,) + hidden.shape...  16 us
    all_to_all x1, starting transfers between devices, per_device(): lax.all_to_all(jnp.broadcast_to(hidden[None], (n_tp // 2,) + hidden.shape...  11.9 us
    all_to_all x1, waiting for transfers between devices, per_device(): lax.all_to_all(query_rows.reshape(step_count, batch_rows, heads_local, HE...  9.56 us
    all_to_all x1, starting transfers between devices, per_device(): lax.all_to_all(query_rows.reshape(step_count, batch_rows, heads_local, HE...  9.52 us
    all_to_all x1, starting transfers between devices, per_device(): lax.all_to_all(outgoing, 'group', split_axis=0, concat_axis=0, tiled=True)  6.98 us
    all_to_all x1, starting transfers between devices, per_device(): lax.all_to_all(panel_send, 'group', 0, 0, tiled=True)  6.65 us
  transfers between devices with their start and end apart: 9, of which 9 were waited for; matrix products, arithmetic and copies ran while one was open for 17% of the time, Pallas kernels for 0%

profile of v3, /device:TPU:2, one launch (start us, length us, event | category | flops | bytes accessed | tf_op | source)
XLA Modules:
  0.0 214.4 jit_solution(1055302160274640195)
XLA Ops:
  0.0 1.1 fusion.56
  1.1 0.8 broadcast_compare_fusion
  2.0 2.7 %gather_fusion.2 = bf16[16,256,128]{2,1,0:T(8,128)(2,1)} fusion(bf16[4,256,128]{2,1,0:T(8,128)(2,1)} %param.17, s32[1024]{0:T(1024)S(1)} %pad_clamp_fusion.1), kind=kCustom, calls=%fused_computation.2 | custom fusion | bytes 2097216 | tf_op jit(solution)/shard_map/jit(_take)/gather | solution.py:104
  4.7 1.3 gather.44
  6.0 1.6 gather_fusion.4
  7.7 2.6 %gather.48 = bf16[8,2,32768]{2,1,0:T(2,128)(2,1)} reshape(bf16[16,64,512]{2,1,0:T(8,128)(2,1)} %gather_fusion.4) | data formatting | bytes 2097152 | tf_op jit(solution)/shard_map/jit(_take)/gather | solution.py:106
  11.1 0.8 gather.46
  11.9 1.2 broadcast_select_fusion.3
  13.1 3.1 %broadcast_select_fusion.1 = (bf16[8,2,32768]{2,1,0:T(2,128)(2,1)S(1)}, bf16[8,2,32768]{2,1,0:T(2,128)(2,1)S(1)}) fusion(bf16[8,2,32768]{2,1,0:T(2,128)(2,1)S(1)} %gather.44, pred[8,2]{1,0:T(8,128)(4,1)S(1)} %copy.150, bf16[8,2,32768]{2,1,0:T(2,128)(2,1)} %gather.48), kind=kLoop, calls=%fused_computation.15 | loop fusion | flops 1048576 | bytes 4194320 | tf_op jit(solution)/shard_map/jit(_take)/select_n | solution.py:104
  16.2 3.3 %pad_maximum_fusion = bf16[8,2,73728]{2,1,0:T(2,128)(2,1)} fusion(bf16[8,2,32768]{2,1,0:T(2,128)(2,1)S(1)} %get-tuple-element.27, bf16[8,2,8192]{2,1,0:T(2,128)(2,1)S(1)} %broadcast_select_fusion.3, bf16[8,2,32768]{2,1,0:T(2,128)(2,1)S(1)} %get-tuple-element.26), kind=kLoop, calls=%fused_computation.7 | loop fusion | flops 7077888 | bytes 4718592 | tf_op jit(solution)/shard_map/concatenate | solution.py:109
  19.5 6.7 %all-to-all-start.2 = ((bf16[8,2,73728]{2,1,0:T(2,128)(2,1)}), bf16[8,2,73728]{2,1,0:T(2,128)(2,1)}, u32[]{:S(2)}, u32[]{:S(2)}) async-start(bf16[8,2,73728]{2,1,0:T(2,128)(2,1)} %pad_maximum_fusion), calls=%async_computation.2 | async-start | bytes 4718592 | tf_op jit(solution)/shard_map/all_to_all | solution.py:117
  27.5 1.8 gather_fusion
  29.5 1.1 select_multiply_fusion
  30.6 0.8 broadcast_select_fusion.5
  31.4 25.7 %all-to-all-done.2 = bf16[8,2,73728]{2,1,0:T(2,128)(2,1)} async-done(((bf16[8,2,73728]{2,1,0:T(2,128)(2,1)}), bf16[8,2,73728]{2,1,0:T(2,128)(2,1)}, u32[]{:S(2)}, u32[]{:S(2)}) %all-to-all-start.2) | async-done | bytes 2359328 | tf_op jit(solution)/shard_map/all_to_all | solution.py:117
  57.2 7.0 %all-to-all-start = ((bf16[32,16,1024]{2,1,0:T(8,128)(2,1)}), bf16[32,16,1024]{2,1,0:T(8,128)(2,1)}, u32[]{:S(2)}, u32[]{:S(2)}) async-start(bf16[32,16,1024]{2,1,0:T(8,128)(2,1)} %select_multiply_fusion), calls=%async_computation | async-start | bytes 2097152 | tf_op jit(solution)/shard_map/all_to_all | solution.py:215
  64.1 3.2 %reshape.377 = bf16[16,73728]{1,0:T(8,128)(2,1)} reshape(bf16[8,2,73728]{2,1,0:T(2,128)(2,1)} %all-to-all-done.2) | data formatting | bytes 4718592 | tf_op jit(solution)/shard_map/reshape | solution.py:117
  67.3 2.7 %fusion.73 = (bf16[16,32768]{1,0:T(8,128)(2,1)}, bf16[2,8,256,128]{3,1,2,0:T(8,128)(2,1)S(1)}) fusion(bf16[16,73728]{1,0:T(8,128)(2,1)} %reshape.377), kind=kLoop, calls=%fused_computation.112 | loop fusion | bytes 4194304 | tf_op jit(solution)/shard_map/slice | solution.py:124
  70.3 2.1 gather_fusion.6
  72.4 2.1 fusion.8
  77.4 0.8 broadcast_in_dim.133
  78.2 11.9 %all-to-all-start.1 = ((bf16[16,2,32,256]{3,2,1,0:T(8,128)(2,1)}), bf16[16,2,32,256]{3,2,1,0:T(8,128)(2,1)}, u32[]{:S(2)}, u32[]{:S(2)}) async-start(bf16[16,2,32,256]{3,2,1,0:T(8,128)(2,1)} %broadcast_in_dim.133), calls=%async_computation.1 | async-start | bytes 1048576 | tf_op jit(solution)/shard_map/all_to_all | solution.py:130
  90.2 0.8 pad_maximum_fusion.2
  91.0 1.3 all_to_all.35
  92.3 16.0 %all-to-all-done.1 = bf16[16,2,32,256]{3,2,1,0:T(8,128)(2,1)} async-done(((bf16[16,2,32,256]{3,2,1,0:T(8,128)(2,1)}), bf16[16,2,32,256]{3,2,1,0:T(8,128)(2,1)}, u32[]{:S(2)}, u32[]{:S(2)}) %all-to-all-start.1) | async-done | bytes 524320 | tf_op jit(solution)/shard_map/all_to_all | solution.py:130
  108.3 4.3 %all-to-all-start.3 = ((f32[16,1,10240]{2,1,0:T(1,128)}), f32[16,1,10240]{2,1,0:T(1,128)}, u32[]{:S(2)}, u32[]{:S(2)}) async-start(f32[16,1,10240]{2,1,0:T(1,128)} %all_to_all.35), calls=%async_computation.3 | async-start | bytes 1310720 | tf_op jit(solution)/shard_map/all_to_all | solution.py:171
  115.3 2.7 %pad_maximum_fusion.1 = bf16[64,16,1024]{2,1,0:T(8,128)(2,1)} fusion(bf16[32,16,1024]{2,1,0:T(8,128)(2,1)} %all-to-all-done, bf16[32,16,1024]{2,1,0:T(8,128)(2,1)S(1)} %copy-done.2), kind=kLoop, calls=%fused_computation.8 | loop fusion | flops 1048576 | bytes 4194304 | tf_op jit(solution)/shard_map/concatenate | solution.py:216
  118.1 3.2 %gather_fusion.1 = bf16[32,16,1024]{2,1,0:T(8,128)(2,1)} fusion(bf16[64,16,1024]{2,1,0:T(8,128)(2,1)} %pad_maximum_fusion.1, s32[1024]{0:T(1024)S(1)} %pad_clamp_fusion.2), kind=kCustom, calls=%fused_computation.1 | custom fusion | bytes 2097280 | tf_op jit(solution)/shard_map/jit(_take)/gather | solution.py:217
  121.3 1.5 copy.146
  123.1 1.1 fusion.74
  124.2 0.9 collective-permute-done
  125.1 1.5 maximum_select_fusion
  126.8 1.0 slice_bitcast_fusion.1
  127.9 1.4 gather_fusion.5
  129.3 2.5 %copy.194 = bf16[2,8,64,512]{3,2,1,0:T(8,128)(2,1)} copy(bf16[2,8,64,512]{3,1,2,0:T(8,128)(2,1)} %bitcast.175) | data formatting | bytes 2097152
  132.1 1.5 reduce_sum.36
  133.6 1.3 fusion.31
  136.1 9.5 %all-to-all-start.4 = ((bf16[2,32,1,128]{3,0,2,1:T(2,128)(2,1)}), bf16[2,32,1,128]{3,0,2,1:T(2,128)(2,1)S(1)}, u32[]{:S(2)}, u32[]{:S(2)}) async-start(bf16[2,32,1,128]{3,0,2,1:T(2,128)(2,1)} %copy.157), calls=%async_computation.4 | async-start | bytes 32768 | tf_op jit(solution)/shard_map/all_to_all | solution.py:202
  145.7 9.6 %all-to-all-done.4 = bf16[2,32,1,128]{3,0,2,1:T(2,128)(2,1)S(1)} async-done(((bf16[2,32,1,128]{3,0,2,1:T(2,128)(2,1)}), bf16[2,32,1,128]{3,0,2,1:T(2,128)(2,1)S(1)}, u32[]{:S(2)}, u32[]{:S(2)}) %all-to-all-start.4) | async-done | bytes 16416 | tf_op jit(solution)/shard_map/all_to_all | solution.py:202
  155.5 1.3 fusion.75
  157.1 1.3 fusion.38
  158.5 1.1 fusion.22
  160.2 3.8 %all-to-all-start.5 = ((bf16[2,1,32,128]{3,0,1,2:T(2,128)(2,1)}), bf16[2,1,32,128]{3,0,1,2:T(2,128)(2,1)S(1)}, u32[]{:S(2)}, u32[]{:S(2)}) async-start(bf16[2,1,32,128]{3,0,1,2:T(2,128)(2,1)} %copy.168), calls=%async_computation.5 | async-start | bytes 32768 | tf_op jit(solution)/shard_map/all_to_all | solution.py:221
  164.1 4.1 %copy.186 = bf16[8192,128]{1,0:T(8,128)(2,1)} copy(bf16[8192,128]{0,1:T(8,128)(2,1)} %bitcast.177) | data formatting | bytes 4194304 | tf_op jit(solution)/shard_map/dot_general | solution.py:222
  168.1 5.6 %all-to-all-done.5 = bf16[2,1,32,128]{3,0,1,2:T(2,128)(2,1)S(1)} async-done(((bf16[2,1,32,128]{3,0,1,2:T(2,128)(2,1)}), bf16[2,1,32,128]{3,0,1,2:T(2,128)(2,1)S(1)}, u32[]{:S(2)}, u32[]{:S(2)}) %all-to-all-start.5) | async-done | bytes 16416 | tf_op jit(solution)/shard_map/all_to_all | solution.py:221
  173.7 2.4 %fusion.76 = f32[64,16,2,256]{3,0,2,1:T(8,128)S(1)} fusion(bf16[64,128,1,1]{1,0,3,2:T(8,128)(2,1)S(1)} %bitcast.185, bf16[16,2,256,128]{3,2,1,0:T(8,128)(2,1)} %bitcast.171), kind=kOutput, calls=%fused_computation.115 | convolution fusion | flops 134217728 | bytes 4210688 | tf_op jit(solution)/shard_map/dot_general | solution.py:222
  176.4 2.6 %collective-permute-done.2 = f32[64,16,256]{2,0,1:T(8,128)S(1)} collective-permute-done((f32[64,16,256]{2,0,1:T(8,128)S(1)}, f32[64,16,256]{2,0,1:T(8,128)S(1)}, u32[]{:S(2)}, u32[]{:S(2)}) %collective-permute-start.2) | collective-permute-done | bytes 1048608 | tf_op jit(solution)/shard_map/ppermute | solution.py:229
  179.3 34.4 %all_to_all.47 = f32[64,16,256]{2,0,1:T(8,128)S(1)} all-to-all(f32[64,16,256]{2,0,1:T(8,128)S(1)} %fusion.28), channel_id=1, replica_groups={{0,2,4,6,8,10,12,14,16,18,20,22,24,26,28,30},{1,3,5,7,9,11,13,15,17,19,..., dimensions={1} | all-to-all | bytes 2097152 | tf_op jit(solution)/shard_map/all_to_all | solution.py:234
  (93 shorter events, 9.8 us)
Async XLA Ops:
  0.0 135.0 %copy-start = (bf16[8192,128]{1,0:T(8,128)(2,1)S(1)}, bf16[8192,128]{1,0:T(8,128)(2,1)}, u32[]{:S(2)}) copy-start(bf16[8192,128]{1,0:T(8,128)(2,1)} %param.14) | copy-start | bytes 6291460
  2.0 4.0 %copy-start.1 = (bf16[4,64,512]{2,1,0:T(8,128)(2,1)S(1)}, bf16[4,64,512]{2,1,0:T(8,128)(2,1)}, u32[]{:S(2)}) copy-start(bf16[4,64,512]{2,1,0:T(8,128)(2,1)} %param.19) | copy-start | bytes 786436
  6.0 4.5 %copy-start.3 = (bf16[4,64,128]{2,1,0:T(8,128)(2,1)S(1)}, bf16[4,64,128]{2,1,0:T(8,128)(2,1)}, u32[]{:S(2)}) copy-start(bf16[4,64,128]{2,1,0:T(8,128)(2,1)} %param.18) | copy-start | bytes 196612
  19.5 6.7 %copy-start.5 = (bf16[256,1024]{1,0:T(8,128)(2,1)S(1)}, bf16[256,1024]{1,0:T(8,128)(2,1)}, u32[]{:S(2)}) copy-start(bf16[256,1024]{1,0:T(8,128)(2,1)} %param.15) | copy-start | bytes 1572868
  19.5 6.7 %copy-start.6 = (bf16[2,32,256]{2,1,0:T(8,128)(2,1)S(1)}, bf16[2,32,256]{2,1,0:T(8,128)(2,1)}, u32[]{:S(2)}) copy-start(bf16[2,32,256]{2,1,0:T(8,128)(2,1)} %param.13) | copy-start | bytes 98308
  19.5 7.4 %copy-start.9 = (s32[1,1,8,4]{2,3,1,0:T(4,128)S(1)}, s32[1,1,8,4]{2,3,1,0:T(4,128)}, u32[]{:S(2)}) copy-start(s32[1,1,8,4]{2,3,1,0:T(4,128)} %param.23) | copy-start | bytes 388
  19.5 37.6 %all-to-all-start.2 = ((bf16[8,2,73728]{2,1,0:T(2,128)(2,1)}), bf16[8,2,73728]{2,1,0:T(2,128)(2,1)}, u32[]{:S(2)}, u32[]{:S(2)}) async-start(bf16[8,2,73728]{2,1,0:T(2,128)(2,1)} %pad_maximum_fusion), calls=%async_computation.2 | async-start | bytes 4718592 | tf_op jit(solution)/shard_map/all_to_all | solution.py:117
  26.2 3.2 %copy-start.11 = (s32[32]{0:T(128)S(1)}, s32[32]{0:T(128)}, u32[]{:S(2)}) copy-start(s32[32]{0:T(128)} %param.24) | copy-start | bytes 388
  26.2 3.2 %copy-start.10 = (s32[1,32]{1,0:T(1,128)S(1)}, s32[1,32]{1,0:T(1,128)}, u32[]{:S(2)}) copy-start(s32[1,32]{1,0:T(1,128)} %param.22) | copy-start | bytes 388
  29.4 42.9 %copy-start.13 = (pred[32]{0:T(512)(128)(4,1)}, pred[32]{0:T(512)(128)(4,1)S(1)}, u32[]{:S(2)}) copy-start(pred[32]{0:T(512)(128)(4,1)S(1)} %get-tuple-element.30) | copy-start | bytes 100
  57.2 20.2 %all-to-all-start = ((bf16[32,16,1024]{2,1,0:T(8,128)(2,1)}), bf16[32,16,1024]{2,1,0:T(8,128)(2,1)}, u32[]{:S(2)}, u32[]{:S(2)}) async-start(bf16[32,16,1024]{2,1,0:T(8,128)(2,1)} %select_multiply_fusion), calls=%async_computation | async-start | bytes 2097152 | tf_op jit(solution)/shard_map/all_to_all | solution.py:215
  70.2 2.2 %copy-start.7 = (bf16[2,32,256]{2,1,0:T(8,128)(2,1)S(1)}, bf16[2,32,256]{2,1,0:T(8,128)(2,1)}, u32[]{:S(2)}) copy-start(bf16[2,32,256]{2,1,0:T(8,128)(2,1)} %param.13) | copy-start | bytes 98308
  72.4 2.1 copy-start.4
  72.4 5.0 %copy-start.8 = (bf16[2,32,256]{2,1,0:T(8,128)(2,1)S(1)}, bf16[2,32,256]{2,1,0:T(8,128)(2,1)}, u32[]{:S(2)}) copy-start(bf16[2,32,256]{2,1,0:T(8,128)(2,1)} %param.13) | copy-start | bytes 98308
  74.5 1.5 collective-permute-start.1
  78.2 34.5 %copy-start.12 = (s32[32]{0:T(128)S(1)}, s32[32]{0:T(128)}, u32[]{:S(2)}) copy-start(s32[32]{0:T(128)} %param.24) | copy-start | bytes 388
  78.2 37.1 %copy-start.2 = (bf16[32,16,1024]{2,1,0:T(8,128)(2,1)S(1)}, bf16[32,16,1024]{2,1,0:T(8,128)(2,1)}, u32[]{:S(2)}) copy-start(bf16[32,16,1024]{2,1,0:T(8,128)(2,1)} %param.20) | copy-start | bytes 3145732
  78.2 30.1 %all-to-all-start.1 = ((bf16[16,2,32,256]{3,2,1,0:T(8,128)(2,1)}), bf16[16,2,32,256]{3,2,1,0:T(8,128)(2,1)}, u32[]{:S(2)}, u32[]{:S(2)}) async-start(bf16[16,2,32,256]{3,2,1,0:T(8,128)(2,1)} %broadcast_in_dim.133), calls=%async_computation.1 | async-start | bytes 1048576 | tf_op jit(solution)/shard_map/all_to_all | solution.py:130
  108.3 23.8 %all-to-all-start.3 = ((f32[16,1,10240]{2,1,0:T(1,128)}), f32[16,1,10240]{2,1,0:T(1,128)}, u32[]{:S(2)}, u32[]{:S(2)}) async-start(f32[16,1,10240]{2,1,0:T(1,128)} %all_to_all.35), calls=%async_computation.3 | async-start | bytes 1310720 | tf_op jit(solution)/shard_map/all_to_all | solution.py:171
  122.8 2.4 %collective-permute-start = (bf16[16,2,32,256]{3,2,1,0:T(8,128)(2,1)}, bf16[16,2,32,256]{3,2,1,0:T(8,128)(2,1)S(1)}, u32[]{:S(2)}, u32[]{:S(2)}) collective-permute-start(bf16[16,2,32,256]{3,2,1,0:T(8,128)(2,1)} %all-to-all-done.1), channel_id=1, source_target_pairs={{0,1},{1,0},{2,3},{3,2},{4,5},{5,4},{6,7},{7,6},{8,9},{9,8},{10,11... | collective-permute-start | bytes 1572872 | tf_op jit(solution)/shard_map/ppermute | solution.py:138
  127.8 5.8 %copy-start.14 = (pred[32]{0:T(512)(128)(4,1)S(1)}, pred[32]{0:T(512)(128)(4,1)}, u32[]{:S(2)}) copy-start(pred[32]{0:T(512)(128)(4,1)} %copy-done.13) | copy-start | bytes 100
  136.1 19.2 %all-to-all-start.4 = ((bf16[2,32,1,128]{3,0,2,1:T(2,128)(2,1)}), bf16[2,32,1,128]{3,0,2,1:T(2,128)(2,1)S(1)}, u32[]{:S(2)}, u32[]{:S(2)}) async-start(bf16[2,32,1,128]{3,0,2,1:T(2,128)(2,1)} %copy.157), calls=%async_computation.4 | async-start | bytes 32768 | tf_op jit(solution)/shard_map/all_to_all | solution.py:202
  160.2 13.5 %all-to-all-start.5 = ((bf16[2,1,32,128]{3,0,1,2:T(2,128)(2,1)}), bf16[2,1,32,128]{3,0,1,2:T(2,128)(2,1)S(1)}, u32[]{:S(2)}, u32[]{:S(2)}) async-start(bf16[2,1,32,128]{3,0,1,2:T(2,128)(2,1)} %copy.168), calls=%async_computation.5 | async-start | bytes 32768 | tf_op jit(solution)/shard_map/all_to_all | solution.py:221
  176.3 2.7 %collective-permute-start.2 = (f32[64,16,256]{2,0,1:T(8,128)S(1)}, f32[64,16,256]{2,0,1:T(8,128)S(1)}, u32[]{:S(2)}, u32[]{:S(2)}) collective-permute-start(f32[64,16,256]{2,0,1:T(8,128)S(1)} %select_bitcast_fusion), channel_id=1, source_target_pairs={{0,1},{1,0},{2,3},{3,2},{4,5},{5,4},{6,7},{7,6},{8,9},{9,8},{10,11... | collective-permute-start | bytes 3145736 | tf_op jit(solution)/shard_map/ppermute | solution.py:229

commit v4 on v3

--- a/solution.py
+++ b/solution.py
@@ -100,32 +100,34 @@
     swap = [(t, t ^ 1) for t in range(n_tp)]
     parity = [[t for t in range(n_tp) if t % 2 == p] for p in range(2)]
 
+    value_cols = adapter_up_value.shape[2] // n_tp
     send_rows = jnp.maximum(read_rows_list[:, group_number, :], 0)
+    upv_cols = lax.dynamic_slice_in_dim(adapter_up_value, column_id * value_cols, value_cols, 2)
     down_send = jnp.take(adapter_down_weight, send_rows, axis=0)
     upq_send = jnp.take(adapter_up_query, send_rows, axis=0)
-    upv_send = jnp.take(adapter_up_value, send_rows, axis=0)
-    down_size = down_send[0, 0].size
-    upq_size = upq_send[0, 0].size
+    upv_send = jnp.take(upv_cols, send_rows, axis=0)
+    lane = adapter_down_weight.shape[2]
+    down_len = adapter_down_weight.shape[1]
+    upq_len = adapter_up_query.shape[1]
     panel_send = jnp.concatenate(
         [
-            down_send.reshape(n_group, cap_slots, -1),
-            upq_send.reshape(n_group, cap_slots, -1),
-            upv_send.reshape(n_group, cap_slots, -1),
-        ],
-        -1,
+            down_send,
+            upq_send,
+            upv_send.reshape(n_group, cap_slots, -1, lane),
+        ],
+        2,
     )
     panel_recv = lax.all_to_all(panel_send, "group", 0, 0, tiled=True).reshape(
-        n_group * cap_slots, -1
-    )
-    down_recv = panel_recv[:, :down_size].reshape((-1,) + adapter_down_weight.shape[1:])
-    upq_recv = panel_recv[:, down_size : down_size + upq_size].reshape(
-        (-1,) + adapter_up_query.shape[1:]
-    )
-    upv_recv = panel_recv[:, down_size + upq_size :].reshape((-1,) + adapter_up_value.shape[1:])
+        (n_group * cap_slots,) + panel_send.shape[2:]
+    )
+    down_recv = panel_recv[:, :down_len]
+    upq_recv = panel_recv[:, down_len : down_len + upq_len]
+    upv_recv = panel_recv[:, down_len + upq_len :].reshape(
+        n_group * cap_slots, adapter_up_value.shape[1], value_cols
+    )
     down_rows = jnp.take(down_recv, request_adapter_entry, axis=0)
     upq_rows = jnp.take(upq_recv, request_adapter_entry, axis=0)
-    own_entry = lax.dynamic_slice_in_dim(request_adapter_entry, own_start, batch_own)
-    upv_rows = jnp.take(upv_recv, own_entry, axis=0)
+    upv_rows = jnp.take(upv_recv, request_adapter_entry, axis=0)
 
     hidden_same = lax.all_to_all(
         jnp.broadcast_to(hidden[None], (n_tp // 2,) + hidden.shape),
@@ -187,25 +189,32 @@
         preferred_element_type=jnp.float32,
     )
     query_rows = (query_plain + ADAPTER_SCALE * query_adapter_term).astype(jnp.bfloat16)
-    shrink_own = lax.dynamic_slice_in_dim(down_projected_low, own_start, batch_own, 1)
     value_adapter_term = ADAPTER_SCALE * jnp.einsum(
-        "srk,rkc->rsc", shrink_own[..., ADAPTER_RANK:], upv_rows, preferred_element_type=jnp.float32
+        "srk,rkc->src",
+        down_projected_low[..., ADAPTER_RANK:],
+        upv_rows,
+        preferred_element_type=jnp.float32,
+    )
+    heads_local = query_rows.shape[2] // HEAD_SIZE
+    query_send = jnp.concatenate(
+        [
+            query_rows.astype(jnp.float32).reshape(step_count, batch_rows, heads_local, HEAD_SIZE),
+            value_adapter_term.reshape(step_count, batch_rows, heads_local, value_cols),
+        ],
+        -1,
+    )
+    query_recv = lax.all_to_all(query_send, "tp", split_axis=1, concat_axis=2, tiled=True)
+    query_own = query_recv[..., :HEAD_SIZE].astype(jnp.bfloat16)
+    value_own = jnp.transpose(query_recv[..., HEAD_SIZE:], (1, 0, 2, 3)).reshape(
+        batch_own, step_count, -1
     )
     keyval_new = jnp.concatenate(
         [
             key_value_plain[..., :key_span_width],
-            key_value_plain[..., key_span_width:] + value_adapter_term,
+            key_value_plain[..., key_span_width:] + value_own,
         ],
         -1,
     ).astype(jnp.bfloat16)
-    heads_local = query_rows.shape[2] // HEAD_SIZE
-    query_own = lax.all_to_all(
-        query_rows.reshape(step_count, batch_rows, heads_local, HEAD_SIZE),
-        "tp",
-        split_axis=1,
-        concat_axis=2,
-        tiled=True,
-    )
     move_row = page_send_list[0, 0]
     present_pages = (move_row >= 0).reshape(-1)
     outgoing = (

time: 216 us -> 186 us (0.86)
  waiting for transfers between devices: 62.1 us -> 51 us
  local copies, waits for them, and re-layouts: 41 us -> 31.3 us
  starting transfers between devices: 43.6 us -> 38.7 us
    all_to_all x1, waiting for transfers between devices: 25.7 us -> 7.33 us  [per_device(): lax.all_to_all(panel_send, 'group', 0, 0, tiled=True)]
    all_to_all x1, waiting for transfers between devices: 0.64 us -> 6.38 us  [per_device(): lax.all_to_all(outgoing, 'group', split_axis=0, concat_axis=0, tiled=True)]
    unnamed x34 -> x22, local copies, waits for them, and re-layouts: 3.8 us -> 0.05 us
    reshape x2 -> x3, local copies, waits for them, and re-layouts: 3.83 us -> 0.41 us  [the longest x2 0.33 us: per_device(): panel_recv[:, down_len + upq_len:]]
    gather x2 -> x3, local copies, waits for them, and re-layouts: 4.25 us -> 1.38 us  [the longest x2 0.78 us: per_device(): upv_send = jnp.take(upv_cols, send_rows, axis=0)]
    all_to_all x1, waiting for transfers between devices: 0.26 us -> 2.82 us  [per_device(): lax.all_to_all(reduce_send, 'tp', 0, 0, tiled=True, axis_index_groups=par...]
    all_to_all x1, starting transfers between devices: 9.52 us -> 7.06 us  [per_device(): lax.all_to_all(query_send, 'tp', split_axis=1, concat_axis=2, tiled=True)]
    gather x2 -> x1, local copies, waits for them, and re-layouts: 3.99 us -> 1.73 us  [per_device(): down_send = jnp.take(adapter_down_weight, send_rows, axis=0)]
  transfers between devices with their start and end apart: 9 -> 9, of which waited for: 9 -> 8; matrix products, arithmetic and copies ran while one was open for 17% -> 20% of each run, Pallas kernels for 0% -> 0%
where the time goes in v4:
time: 186 us; the launch traced here: 184 us
  waiting for transfers between devices  51 us (27%)
  starting transfers between devices  38.7 us (21%)
  blocking collectives  34.4 us (18%)
  local copies, waits for them, and re-layouts  31.3 us (17%)
  other arithmetic  18.8 us (10%)
  matrix products  8.79 us (5%)
    all_to_all x1, blocking collectives, per_device(): lax.all_to_all(out_pair, 'tp', 1, 1, tiled=True, axis_index_groups=parity)  34.4 us
    all_to_all x1, waiting for transfers between devices, per_device(): lax.all_to_all(jnp.broadcast_to(hidden[None], (n_tp // 2,) + hidden.shape...  16.2 us
    all_to_all x1, starting transfers between devices, per_device(): lax.all_to_all(jnp.broadcast_to(hidden[None], (n_tp // 2,) + hidden.shape...  11.1 us
    all_to_all x1, waiting for transfers between devices, per_device(): lax.all_to_all(query_send, 'tp', split_axis=1, concat_axis=2, tiled=True)  8.69 us
    all_to_all x1, waiting for transfers between devices, per_device(): lax.all_to_all(panel_send, 'group', 0, 0, tiled=True)  7.33 us
    all_to_all x1, starting transfers between devices, per_device(): lax.all_to_all(query_send, 'tp', split_axis=1, concat_axis=2, tiled=True)  7.06 us
    all_to_all x1, waiting for transfers between devices, per_device(): lax.all_to_all(outgoing, 'group', split_axis=0, concat_axis=0, tiled=True)  6.38 us
    all_to_all x1, starting transfers between devices, per_device(): lax.all_to_all(outgoing, 'group', split_axis=0, concat_axis=0, tiled=True)  6.23 us
  transfers between devices with their start and end apart: 9, of which 8 were waited for; matrix products, arithmetic and copies ran while one was open for 20% of the time, Pallas kernels for 0%

profile of v4, /device:TPU:2, one launch (start us, length us, event | category | flops | bytes accessed | tf_op | source)
XLA Modules:
  0.0 184.2 jit_solution(9487850778114330864)
XLA Ops:
  0.0 1.1 fusion.55
  1.1 0.8 broadcast_compare_fusion
  2.0 0.9 constant_dynamic-slice_fusion
  4.0 1.7 gather_fusion.2
  5.8 1.1 broadcast_select_fusion
  7.7 2.4 %pad_maximum_fusion.1 = bf16[8,2,328,128]{3,2,1,0:T(8,128)(2,1)} fusion(bf16[8,2,8,128]{3,2,1,0:T(8,128)(2,1)S(1)} %broadcast_select_fusion.5, bf16[8,2,64,128]{3,2,1,0:T(8,128)(2,1)S(1)} %broadcast_select_fusion.4, bf16[8,2,256,128]{3,2,1,0:T(8,128)(2,1)} %broadcast_select_fusion), kind=kLoop, calls=%fused_computation.14 | loop fusion | flops 4030464 | bytes 2686976 | tf_op jit(solution)/shard_map/concatenate | solution.py:112
  10.1 6.0 %all-to-all-start.2 = ((bf16[8,2,328,128]{3,2,1,0:T(8,128)(2,1)}), bf16[8,2,328,128]{3,2,1,0:T(8,128)(2,1)S(1)}, u32[]{:S(2)}, u32[]{:S(2)}) async-start(bf16[8,2,328,128]{3,2,1,0:T(8,128)(2,1)} %pad_maximum_fusion.1), calls=%async_computation.2 | async-start | bytes 2686976 | tf_op jit(solution)/shard_map/all_to_all | solution.py:120
  16.1 1.2 convolution_bitcast_fusion
  17.4 0.9 copy.207
  18.3 2.0 %reshape.348 = f32[16,2,2048]{2,1,0:T(2,128)} reshape(f32[32,2,1024]{2,1,0:T(2,128)} %copy.207) | data formatting | bytes 524288 | tf_op jit(solution)/shard_map/reshape | solution.py:153
  20.8 2.8 %gather_fusion = bf16[32,16,1024]{2,1,0:T(8,128)(2,1)} fusion(bf16[32,16,1024]{2,1,0:T(8,128)(2,1)} %param.20, s32[1024]{0:T(1024)S(1)} %pad_clamp_fusion.3), kind=kCustom, calls=%fused_computation | custom fusion | bytes 2097280 | tf_op jit(solution)/shard_map/jit(_take)/gather | solution.py:221
  23.7 2.4 %select_multiply_fusion = bf16[32,16,1024]{2,1,0:T(8,128)(2,1)} fusion(bf16[32,16,1024]{2,1,0:T(8,128)(2,1)} %gather_fusion, pred[32]{0:T(512)(128)(4,1)S(1)} %le.73, bf16[32]{0:T(256)(128)(2,1)S(1)} %reshape.361), kind=kLoop, calls=%fused_computation.36 | loop fusion | flops 1048576 | bytes 2097248 | tf_op jit(solution)/shard_map/mul | solution.py:221
  26.1 0.9 broadcast_select_fusion.3
  27.0 7.3 %all-to-all-done.2 = bf16[8,2,328,128]{3,2,1,0:T(8,128)(2,1)S(1)} async-done(((bf16[8,2,328,128]{3,2,1,0:T(8,128)(2,1)}), bf16[8,2,328,128]{3,2,1,0:T(8,128)(2,1)S(1)}, u32[]{:S(2)}, u32[]{:S(2)}) %all-to-all-start.2) | async-done | bytes 1343520 | tf_op jit(solution)/shard_map/all_to_all | solution.py:120
  34.4 6.2 %all-to-all-start = ((bf16[32,16,1024]{2,1,0:T(8,128)(2,1)}), bf16[32,16,1024]{2,1,0:T(8,128)(2,1)}, u32[]{:S(2)}, u32[]{:S(2)}) async-start(bf16[32,16,1024]{2,1,0:T(8,128)(2,1)} %select_multiply_fusion), calls=%async_computation | async-start | bytes 2097152 | tf_op jit(solution)/shard_map/all_to_all | solution.py:224
  40.6 1.3 slice.130
  41.9 2.1 %gather_fusion.6 = bf16[32,256,128]{2,1,0:T(8,128)(2,1)} fusion(bf16[16,256,128]{2,1,0:T(8,128)(2,1)S(1)} %slice.130, s32[1024]{0:T(1024)S(1)} %pad_clamp_fusion), kind=kCustom, calls=%fused_computation.6 | custom fusion | bytes 4194432 | tf_op jit(solution)/shard_map/jit(_take)/gather | solution.py:128
  44.0 2.1 %fusion.8 = f32[2,32,128]{2,0,1:T(2,128)S(1)} fusion(bf16[32,256,128]{2,1,0:T(8,128)(2,1)} %gather_fusion.6, pred[32]{0:T(512)(128)(4,1)S(1)} %get-tuple-element.17, bf16[2,32,256]{2,1,0:T(8,128)(2,1)S(1)} %copy-done.7), kind=kOutput, calls=%fused_computation.20 | convolution fusion | flops 5242880 | bytes 2162720 | tf_op jit(solution)/shard_map/srd,rdk->srk/dot_general | solution.py:150
  46.3 1.4 collective-permute-done.1
  47.8 6.4 %all-to-all-done = bf16[32,16,1024]{2,1,0:T(8,128)(2,1)} async-done(((bf16[32,16,1024]{2,1,0:T(8,128)(2,1)}), bf16[32,16,1024]{2,1,0:T(8,128)(2,1)}, u32[]{:S(2)}, u32[]{:S(2)}) %all-to-all-start) | async-done | bytes 1048608 | tf_op jit(solution)/shard_map/all_to_all | solution.py:224
  54.2 0.9 broadcast_in_dim.135
  55.0 11.1 %all-to-all-start.1 = ((bf16[16,2,32,256]{3,2,1,0:T(8,128)(2,1)}), bf16[16,2,32,256]{3,2,1,0:T(8,128)(2,1)}, u32[]{:S(2)}, u32[]{:S(2)}) async-start(bf16[16,2,32,256]{3,2,1,0:T(8,128)(2,1)} %broadcast_in_dim.135), calls=%async_computation.1 | async-start | bytes 1048576 | tf_op jit(solution)/shard_map/all_to_all | solution.py:132
  66.2 1.3 all_to_all.37
  67.5 16.2 %all-to-all-done.1 = bf16[16,2,32,256]{3,2,1,0:T(8,128)(2,1)} async-done(((bf16[16,2,32,256]{3,2,1,0:T(8,128)(2,1)}), bf16[16,2,32,256]{3,2,1,0:T(8,128)(2,1)}, u32[]{:S(2)}, u32[]{:S(2)}) %all-to-all-start.1) | async-done | bytes 524320 | tf_op jit(solution)/shard_map/all_to_all | solution.py:132
  83.7 4.3 %all-to-all-start.3 = ((f32[16,1,10240]{2,1,0:T(1,128)}), f32[16,1,10240]{2,1,0:T(1,128)}, u32[]{:S(2)}, u32[]{:S(2)}) async-start(f32[16,1,10240]{2,1,0:T(1,128)} %all_to_all.37), calls=%async_computation.3 | async-start | bytes 1310720 | tf_op jit(solution)/shard_map/all_to_all | solution.py:173
  88.9 2.7 %pad_maximum_fusion = bf16[64,16,1024]{2,1,0:T(8,128)(2,1)} fusion(bf16[32,16,1024]{2,1,0:T(8,128)(2,1)} %all-to-all-done, bf16[32,16,1024]{2,1,0:T(8,128)(2,1)S(1)} %copy-done.2), kind=kLoop, calls=%fused_computation.8 | loop fusion | flops 1048576 | bytes 4194304 | tf_op jit(solution)/shard_map/concatenate | solution.py:225
  91.7 2.2 %gather_fusion.1 = bf16[32,16,1024]{2,1,0:T(8,128)(2,1)S(1)} fusion(bf16[64,16,1024]{2,1,0:T(8,128)(2,1)} %pad_maximum_fusion, s32[1024]{0:T(1024)S(1)} %pad_clamp_fusion.2), kind=kCustom, calls=%fused_computation.1 | custom fusion | bytes 2097280 | tf_op jit(solution)/shard_map/jit(_take)/gather | solution.py:226
  93.9 1.3 copy.200
  95.2 2.3 %broadcast_select_fusion.1 = bf16[1,512,1024]{1,2,0:T(8,128)(2,1)} fusion(bf16[1,512,1024]{1,2,0:T(8,128)(2,1)} %copy.200, pred[512]{0:T(512)(128)(4,1)S(1)} %broadcast_in_dim.130), kind=kLoop, calls=%fused_computation.38 | loop fusion | flops 524288 | bytes 2097664 | tf_op jit(solution)/shard_map/jit(_take)/select_n | solution.py:226
  97.5 1.0 slice.127
  98.5 0.8 slice.135
  99.3 1.4 gather_fusion.5
  101.6 1.7 maximum_select_fusion
  103.5 2.8 %all-to-all-done.3 = f32[16,1,10240]{2,1,0:T(1,128)} async-done(((f32[16,1,10240]{2,1,0:T(1,128)}), f32[16,1,10240]{2,1,0:T(1,128)}, u32[]{:S(2)}, u32[]{:S(2)}) %all-to-all-start.3) | async-done | bytes 655392 | tf_op jit(solution)/shard_map/all_to_all | solution.py:173
  106.3 1.5 reduce_sum.36
  108.4 1.4 fusion.30
  110.2 0.7 copy.216
  110.9 7.1 %all-to-all-start.4 = ((f32[2,32,1,144]{3,0,2,1:T(2,128)}), f32[2,32,1,144]{3,0,2,1:T(2,128)S(1)}, u32[]{:S(2)}, u32[]{:S(2)}) async-start(f32[2,32,1,144]{3,0,2,1:T(2,128)} %copy.216), calls=%async_computation.4 | async-start | bytes 131072 | tf_op jit(solution)/shard_map/all_to_all | solution.py:206
  118.0 1.3 fusion.65
  119.3 8.7 %all-to-all-done.4 = f32[2,32,1,144]{3,0,2,1:T(2,128)S(1)} async-done(((f32[2,32,1,144]{3,0,2,1:T(2,128)}), f32[2,32,1,144]{3,0,2,1:T(2,128)S(1)}, u32[]{:S(2)}, u32[]{:S(2)}) %all-to-all-start.4) | async-done | bytes 36896 | tf_op jit(solution)/shard_map/all_to_all | solution.py:206
  129.4 0.6 copy.227
  130.0 3.8 %all-to-all-start.5 = ((bf16[2,1,32,128]{3,0,1,2:T(2,128)(2,1)}), bf16[2,1,32,128]{3,0,1,2:T(2,128)(2,1)S(1)}, u32[]{:S(2)}, u32[]{:S(2)}) async-start(bf16[2,1,32,128]{3,0,1,2:T(2,128)(2,1)} %copy.227), calls=%async_computation.5 | async-start | bytes 32768 | tf_op jit(solution)/shard_map/all_to_all | solution.py:230
  133.9 4.1 %copy.245 = bf16[8192,128]{1,0:T(8,128)(2,1)} copy(bf16[8192,128]{0,1:T(8,128)(2,1)} %bitcast.167) | data formatting | bytes 4194304 | tf_op jit(solution)/shard_map/dot_general | solution.py:231
  138.0 5.6 %all-to-all-done.5 = bf16[2,1,32,128]{3,0,1,2:T(2,128)(2,1)S(1)} async-done(((bf16[2,1,32,128]{3,0,1,2:T(2,128)(2,1)}), bf16[2,1,32,128]{3,0,1,2:T(2,128)(2,1)S(1)}, u32[]{:S(2)}, u32[]{:S(2)}) %all-to-all-start.5) | async-done | bytes 16416 | tf_op jit(solution)/shard_map/all_to_all | solution.py:230
  143.5 2.4 %fusion.68 = f32[64,16,2,256]{3,0,2,1:T(8,128)S(1)} fusion(bf16[64,128,1,1]{1,0,3,2:T(8,128)(2,1)S(1)} %bitcast.178, bf16[16,2,256,128]{3,2,1,0:T(8,128)(2,1)} %bitcast.159), kind=kOutput, calls=%fused_computation.112 | convolution fusion | flops 134217728 | bytes 4210688 | tf_op jit(solution)/shard_map/dot_general | solution.py:231
  146.2 2.6 %collective-permute-done.2 = f32[64,16,256]{2,0,1:T(8,128)S(1)} collective-permute-done((f32[64,16,256]{2,0,1:T(8,128)S(1)}, f32[64,16,256]{2,0,1:T(8,128)S(1)}, u32[]{:S(2)}, u32[]{:S(2)}) %collective-permute-start.2) | collective-permute-done | bytes 1048608 | tf_op jit(solution)/shard_map/ppermute | solution.py:238
  149.1 34.4 %all_to_all.50 = f32[64,16,256]{2,0,1:T(8,128)S(1)} all-to-all(f32[64,16,256]{2,0,1:T(8,128)S(1)} %fusion.27), channel_id=1, replica_groups={{0,2,4,6,8,10,12,14,16,18,20,22,24,26,28,30},{1,3,5,7,9,11,13,15,17,19,..., dimensions={1} | all-to-all | bytes 2097152 | tf_op jit(solution)/shard_map/all_to_all | solution.py:243
  183.5 0.7 reduce_sum.39
  (92 shorter events, 7.0 us)
Async XLA Ops:
  0.0 109.7 %copy-start = (bf16[8192,128]{1,0:T(8,128)(2,1)S(1)}, bf16[8192,128]{1,0:T(8,128)(2,1)}, u32[]{:S(2)}) copy-start(bf16[8192,128]{1,0:T(8,128)(2,1)} %param.14) | copy-start | bytes 6291460
  4.0 3.0 %copy-start.4 = (bf16[4,64,128]{2,1,0:T(8,128)(2,1)S(1)}, bf16[4,64,128]{2,1,0:T(8,128)(2,1)}, u32[]{:S(2)}) copy-start(bf16[4,64,128]{2,1,0:T(8,128)(2,1)} %param.18) | copy-start | bytes 196612
  7.6 8.4 %copy-start.8 = (s32[1,1,8,4]{2,3,1,0:T(4,128)S(1)}, s32[1,1,8,4]{2,3,1,0:T(4,128)}, u32[]{:S(2)}) copy-start(s32[1,1,8,4]{2,3,1,0:T(4,128)} %param.23) | copy-start | bytes 388
  7.6 8.4 %copy-start.7 = (bf16[2,32,256]{2,1,0:T(8,128)(2,1)S(1)}, bf16[2,32,256]{2,1,0:T(8,128)(2,1)}, u32[]{:S(2)}) copy-start(bf16[2,32,256]{2,1,0:T(8,128)(2,1)} %param.13) | copy-start | bytes 98308
  10.1 10.2 %copy-start.9 = (s32[32]{0:T(128)S(1)}, s32[32]{0:T(128)}, u32[]{:S(2)}) copy-start(s32[32]{0:T(128)} %param.24) | copy-start | bytes 388
  10.1 24.3 %all-to-all-start.2 = ((bf16[8,2,328,128]{3,2,1,0:T(8,128)(2,1)}), bf16[8,2,328,128]{3,2,1,0:T(8,128)(2,1)S(1)}, u32[]{:S(2)}, u32[]{:S(2)}) async-start(bf16[8,2,328,128]{3,2,1,0:T(8,128)(2,1)} %pad_maximum_fusion.1), calls=%async_computation.2 | async-start | bytes 2686976 | tf_op jit(solution)/shard_map/all_to_all | solution.py:120
  16.0 7.6 %copy-start.10 = (s32[1,32]{1,0:T(1,128)S(1)}, s32[1,32]{1,0:T(1,128)}, u32[]{:S(2)}) copy-start(s32[1,32]{1,0:T(1,128)} %param.22) | copy-start | bytes 388
  23.6 2.5 %copy-start.3 = (f32[16,2,2048]{2,1,0:T(2,128)S(1)}, f32[16,2,2048]{2,1,0:T(2,128)}, u32[]{:S(2)}) copy-start(f32[16,2,2048]{2,1,0:T(2,128)} %reshape.348) | copy-start | bytes 786436
  34.4 6.2 %copy-start.1 = (bf16[8,2,328,128]{3,2,1,0:T(8,128)(2,1)}, bf16[8,2,328,128]{3,2,1,0:T(8,128)(2,1)S(1)}, u32[]{:S(2)}) copy-start(bf16[8,2,328,128]{3,2,1,0:T(8,128)(2,1)S(1)} %all-to-all-done.2) | copy-start | bytes 4030468
  34.4 19.8 %all-to-all-start = ((bf16[32,16,1024]{2,1,0:T(8,128)(2,1)}), bf16[32,16,1024]{2,1,0:T(8,128)(2,1)}, u32[]{:S(2)}, u32[]{:S(2)}) async-start(bf16[32,16,1024]{2,1,0:T(8,128)(2,1)} %select_multiply_fusion), calls=%async_computation | async-start | bytes 2097152 | tf_op jit(solution)/shard_map/all_to_all | solution.py:224
  44.0 2.1 %copy-start.6 = (f32[16,1,2048]{2,1,0:T(1,128)S(1)}, f32[16,1,2048]{2,1,0:T(1,128)}, u32[]{:S(2)}) copy-start(f32[16,1,2048]{2,1,0:T(1,128)} %get-tuple-element.8) | copy-start | bytes 393220
  44.0 3.7 %copy-start.5 = (f32[16,1,2048]{2,1,0:T(1,128)S(1)}, f32[16,1,2048]{2,1,0:T(1,128)}, u32[]{:S(2)}) copy-start(f32[16,1,2048]{2,1,0:T(1,128)} %get-tuple-element.7) | copy-start | bytes 393220
  46.2 1.5 collective-permute-start.1
  55.0 33.9 %copy-start.2 = (bf16[32,16,1024]{2,1,0:T(8,128)(2,1)S(1)}, bf16[32,16,1024]{2,1,0:T(8,128)(2,1)}, u32[]{:S(2)}) copy-start(bf16[32,16,1024]{2,1,0:T(8,128)(2,1)} %param.20) | copy-start | bytes 3145732
  55.0 28.6 %all-to-all-start.1 = ((bf16[16,2,32,256]{3,2,1,0:T(8,128)(2,1)}), bf16[16,2,32,256]{3,2,1,0:T(8,128)(2,1)}, u32[]{:S(2)}, u32[]{:S(2)}) async-start(bf16[16,2,32,256]{3,2,1,0:T(8,128)(2,1)} %broadcast_in_dim.135), calls=%async_computation.1 | async-start | bytes 1048576 | tf_op jit(solution)/shard_map/all_to_all | solution.py:132
  83.7 22.7 %all-to-all-start.3 = ((f32[16,1,10240]{2,1,0:T(1,128)}), f32[16,1,10240]{2,1,0:T(1,128)}, u32[]{:S(2)}, u32[]{:S(2)}) async-start(f32[16,1,10240]{2,1,0:T(1,128)} %all_to_all.37), calls=%async_computation.3 | async-start | bytes 1310720 | tf_op jit(solution)/shard_map/all_to_all | solution.py:173
  88.8 12.8 %collective-permute-start = (bf16[16,2,32,256]{3,2,1,0:T(8,128)(2,1)}, bf16[16,2,32,256]{3,2,1,0:T(8,128)(2,1)}, u32[]{:S(2)}, u32[]{:S(2)}) collective-permute-start(bf16[16,2,32,256]{3,2,1,0:T(8,128)(2,1)} %all-to-all-done.1), channel_id=1, source_target_pairs={{0,1},{1,0},{2,3},{3,2},{4,5},{5,4},{6,7},{7,6},{8,9},{9,8},{10,11... | collective-permute-start | bytes 1572872 | tf_op jit(solution)/shard_map/ppermute | solution.py:140
  110.9 17.1 %all-to-all-start.4 = ((f32[2,32,1,144]{3,0,2,1:T(2,128)}), f32[2,32,1,144]{3,0,2,1:T(2,128)S(1)}, u32[]{:S(2)}, u32[]{:S(2)}) async-start(f32[2,32,1,144]{3,0,2,1:T(2,128)} %copy.216), calls=%async_computation.4 | async-start | bytes 131072 | tf_op jit(solution)/shard_map/all_to_all | solution.py:206
  130.0 13.5 %all-to-all-start.5 = ((bf16[2,1,32,128]{3,0,1,2:T(2,128)(2,1)}), bf16[2,1,32,128]{3,0,1,2:T(2,128)(2,1)S(1)}, u32[]{:S(2)}, u32[]{:S(2)}) async-start(bf16[2,1,32,128]{3,0,1,2:T(2,128)(2,1)} %copy.227), calls=%async_computation.5 | async-start | bytes 32768 | tf_op jit(solution)/shard_map/all_to_all | solution.py:230
  146.1 2.7 %collective-permute-start.2 = (f32[64,16,256]{2,0,1:T(8,128)S(1)}, f32[64,16,256]{2,0,1:T(8,128)S(1)}, u32[]{:S(2)}, u32[]{:S(2)}) collective-permute-start(f32[64,16,256]{2,0,1:T(8,128)S(1)} %select_bitcast_fusion), channel_id=1, source_target_pairs={{0,1},{1,0},{2,3},{3,2},{4,5},{5,4},{6,7},{7,6},{8,9},{9,8},{10,11... | collective-permute-start | bytes 3145736 | tf_op jit(solution)/shard_map/ppermute | solution.py:238

commit v5 on v4

--- a/solution.py
+++ b/solution.py
@@ -70,6 +70,16 @@
         .reshape(step_count, batch_own, QUERY_HEADS, HEAD_SIZE)
         .astype(jnp.bfloat16)
     )
+
+
+def shifted_exchange(outgoing, group_number, n_group):
+    arrived = [jnp.take(outgoing, group_number, axis=0)]
+    for shift in range(1, n_group):
+        block = jnp.take(outgoing, (group_number + shift) % n_group, axis=0)
+        arrived.append(
+            lax.ppermute(block, "group", [(g, (g + shift) % n_group) for g in range(n_group)])
+        )
+    return jnp.stack(arrived, 0)
 
 
 def per_device(
@@ -117,7 +127,7 @@
         ],
         2,
     )
-    panel_recv = lax.all_to_all(panel_send, "group", 0, 0, tiled=True).reshape(
+    panel_recv = shifted_exchange(panel_send, group_number, n_group).reshape(
         (n_group * cap_slots,) + panel_send.shape[2:]
     )
     down_recv = panel_recv[:, :down_len]
@@ -125,9 +135,12 @@
     upv_recv = panel_recv[:, down_len + upq_len :].reshape(
         n_group * cap_slots, adapter_up_value.shape[1], value_cols
     )
-    down_rows = jnp.take(down_recv, request_adapter_entry, axis=0)
-    upq_rows = jnp.take(upq_recv, request_adapter_entry, axis=0)
-    upv_rows = jnp.take(upv_recv, request_adapter_entry, axis=0)
+    entry_at = ((group_number - request_adapter_entry // cap_slots) % n_group) * cap_slots + (
+        request_adapter_entry % cap_slots
+    )
+    down_rows = jnp.take(down_recv, entry_at, axis=0)
+    upq_rows = jnp.take(upq_recv, entry_at, axis=0)
+    upv_rows = jnp.take(upv_recv, entry_at, axis=0)
 
     hidden_same = lax.all_to_all(
         jnp.broadcast_to(hidden[None], (n_tp // 2,) + hidden.shape),
@@ -221,9 +234,22 @@
         jnp.take(key_value_pool, jnp.maximum(move_row, 0).reshape(-1), axis=0)
         * present_pages.astype(key_value_pool.dtype)[:, None, None]
     )
-    arrived_pages = lax.all_to_all(outgoing, "group", split_axis=0, concat_axis=0, tiled=True)
+    move_cap = move_row.shape[1]
+    arrived_pages = shifted_exchange(
+        outgoing.reshape((n_group, move_cap) + outgoing.shape[1:]), group_number, n_group
+    ).reshape(outgoing.shape)
     combined = jnp.concatenate([key_value_pool, arrived_pages], 0)
-    ctx_pages = jnp.take(combined, request_page_table.reshape(-1), axis=0).reshape(
+    pool_pages = key_value_pool.shape[0]
+    page_ids = request_page_table.reshape(-1)
+    moved_at = page_ids - pool_pages
+    page_at = jnp.where(
+        page_ids < pool_pages,
+        page_ids,
+        pool_pages
+        + ((group_number - moved_at // move_cap) % n_group) * move_cap
+        + moved_at % move_cap,
+    )
+    ctx_pages = jnp.take(combined, page_at, axis=0).reshape(
         batch_own, -1, 2 * key_span_width
     )
     attended = attend(query_own, ctx_pages, keyval_new, lengths)

time: 186 us -> 191 us (1.027)
  waiting for transfers between devices: 51 us -> 27.9 us
  local copies, waits for them, and re-layouts: 31.3 us -> 45.1 us
  starting transfers between devices: 38.7 us -> 52 us
    ppermute x0 -> x14, starting transfers between devices: none -> 21.5 us  [shifted_exchange(): lax.ppermute(block, 'group', [(g, (g + shift) % n_group) for g in range(n...]
    all_to_all x1, waiting for transfers between devices: 16.2 us -> 0.01 us  [per_device(): lax.all_to_all(jnp.broadcast_to(hidden[None], (n_tp // 2,) + hidden.shape...]
    all_to_all x2 -> x0, waiting for transfers between devices: 13.7 us -> none  [the longest x1 7.33 us: per_device(): lax.all_to_all(panel_send, 'group', 0, 0, tiled=True)]
    unnamed x22 -> x34, local copies, waits for them, and re-layouts: 0.05 us -> 12.5 us
    all_to_all x2 -> x0, starting transfers between devices: 12.2 us -> none  [the longest x1 6.23 us: per_device(): lax.all_to_all(outgoing, 'group', split_axis=0, concat_axis=0, tiled=True)]
    ppermute x0 -> x14, waiting for transfers between devices: none -> 7.47 us  [shifted_exchange(): lax.ppermute(block, 'group', [(g, (g + shift) % n_group) for g in range(n...]
    all_to_all x1, starting transfers between devices: 4.26 us -> 11 us  [per_device(): lax.all_to_all(reduce_send, 'tp', 0, 0, tiled=True, axis_index_groups=par...]
    all_to_all x1, starting transfers between devices: 7.06 us -> 4.03 us  [per_device(): lax.all_to_all(query_send, 'tp', split_axis=1, concat_axis=2, tiled=True)]
  transfers between devices with their start and end apart: 9 -> 21, of which waited for: 8 -> 6; matrix products, arithmetic and copies ran while one was open for 20% -> 26% of each run, Pallas kernels for 0% -> 0%
where the time goes in v5:
time: 191 us; the launch traced here: 188 us
  starting transfers between devices  52 us (27%)
  local copies, waits for them, and re-layouts  45.1 us (24%)
  blocking collectives  34.4 us (18%)
  waiting for transfers between devices  27.9 us (15%)
  other arithmetic  18.5 us (10%)
  matrix products  8.8 us (5%)
    all_to_all x1, blocking collectives, per_device(): lax.all_to_all(out_pair, 'tp', 1, 1, tiled=True, axis_index_groups=parity)  34.4 us
    ppermute x14, starting transfers between devices, shifted_exchange(): lax.ppermute(block, 'group', [(g, (g + shift) % n_group) for g in range(n...  21.5 us
    unnamed x34, local copies, waits for them, and re-layouts  12.5 us
    all_to_all x1, starting transfers between devices, per_device(): lax.all_to_all(jnp.broadcast_to(hidden[None], (n_tp // 2,) + hidden.shape...  11.3 us
    all_to_all x1, starting transfers between devices, per_device(): lax.all_to_all(reduce_send, 'tp', 0, 0, tiled=True, axis_index_groups=par...  11 us
    ppermute x14, waiting for transfers between devices, shifted_exchange(): lax.ppermute(block, 'group', [(g, (g + shift) % n_group) for g in range(n...  7.47 us
    all_to_all x1, waiting for transfers between devices, per_device(): lax.all_to_all(query_send, 'tp', split_axis=1, concat_axis=2, tiled=True)  6.42 us
    all_to_all x1, waiting for transfers between devices, per_device(): lax.all_to_all(reduce_send, 'tp', 0, 0, tiled=True, axis_index_groups=par...  5.75 us
  transfers between devices with their start and end apart: 21, of which 6 were waited for; matrix products, arithmetic and copies ran while one was open for 26% of the time, Pallas kernels for 0%

profile of v5, /device:TPU:2, one launch (start us, length us, event | category | flops | bytes accessed | tf_op | source)
XLA Modules:
  0.0 187.9 jit_solution(13607226260366393943)
XLA Ops:
  4.7 1.7 gather_fusion.2
  6.5 1.2 broadcast_select_fusion
  8.4 1.3 pad_maximum_fusion.1
  9.7 1.2 select_bitcast_fusion.1
  10.9 1.6 collective-permute-start.8
  12.5 1.5 collective-permute-start.9
  14.0 2.7 %collective-permute-start.10 = (bf16[2,328,128]{2,1,0:T(8,128)(2,1)}, bf16[2,328,128]{2,1,0:T(8,128)(2,1)}, u32[]{:S(2)}, u32[]{:S(2)}) collective-permute-start(bf16[2,328,128]{2,1,0:T(8,128)(2,1)} %get-tuple-element.35), channel_id=1, source_target_pairs={{0,96},{32,128},{64,160},{96,192},{128,224},{160,0},{192,32},{224,... | collective-permute-start | bytes 503816 | tf_op jit(solution)/shard_map/ppermute | solution.py:80
  18.3 11.3 %all-to-all-start = ((bf16[16,2,32,256]{3,2,1,0:T(8,128)(2,1)}), bf16[16,2,32,256]{3,2,1,0:T(8,128)(2,1)}, u32[]{:S(2)}, u32[]{:S(2)}) async-start(bf16[16,2,32,256]{3,2,1,0:T(8,128)(2,1)} %broadcast_in_dim.153), calls=%async_computation | async-start | bytes 1048576 | tf_op jit(solution)/shard_map/all_to_all | solution.py:145
  30.0 1.8 gather_fusion
  33.9 1.2 convolution_bitcast_fusion
  36.0 2.0 %reshape.478 = f32[16,2,2048]{2,1,0:T(2,128)} reshape(f32[32,2,1024]{2,1,0:T(2,128)} %copy.211) | data formatting | bytes 524288 | tf_op jit(solution)/shard_map/reshape | solution.py:166
  38.6 2.0 %broadcast_select_fusion.2 = (f32[16,1,2048]{2,1,0:T(1,128)}, f32[16,1,2048]{2,1,0:T(1,128)}) fusion(pred[]{:T(512)S(6)} %eq.28, f32[16,2,2048]{2,1,0:T(2,128)} %reshape.478), kind=kLoop, calls=%fused_computation.46 | loop fusion | flops 65536 | bytes 524289 | tf_op jit(solution)/shard_map/jit(_where)/select_n | solution.py:174
  40.8 1.3 collective-permute-start.1
  42.1 1.6 bitcast_dynamic-update-slice_fusion.13
  43.7 2.4 %collective-permute-done.1 = bf16[4,16,1024]{2,1,0:T(8,128)(2,1)S(1)} collective-permute-done((bf16[4,16,1024]{2,1,0:T(8,128)(2,1)}, bf16[4,16,1024]{2,1,0:T(8,128)(2,1)S(1)}, u32[]{:S(2)}, u32[]{:S(2)}) %collective-permute-start.1) | collective-permute-done | bytes 131104 | tf_op jit(solution)/shard_map/ppermute | solution.py:80
  46.1 1.9 %collective-permute-start.2 = (bf16[4,16,1024]{2,1,0:T(8,128)(2,1)}, bf16[4,16,1024]{2,1,0:T(8,128)(2,1)S(1)}, u32[]{:S(2)}, u32[]{:S(2)}) collective-permute-start(bf16[4,16,1024]{2,1,0:T(8,128)(2,1)} %get-tuple-element.45), channel_id=1, source_target_pairs={{0,96},{32,128},{64,160},{96,192},{128,224},{160,0},{192,32},{224,... | collective-permute-start | bytes 393224 | tf_op jit(solution)/shard_map/ppermute | solution.py:80
  48.6 5.0 %collective-permute-done.2 = bf16[4,16,1024]{2,1,0:T(8,128)(2,1)S(1)} collective-permute-done((bf16[4,16,1024]{2,1,0:T(8,128)(2,1)}, bf16[4,16,1024]{2,1,0:T(8,128)(2,1)S(1)}, u32[]{:S(2)}, u32[]{:S(2)}) %collective-permute-start.2) | collective-permute-done | bytes 131104 | tf_op jit(solution)/shard_map/ppermute | solution.py:80
  53.7 1.9 %collective-permute-start.12 = (bf16[2,328,128]{2,1,0:T(8,128)(2,1)}, bf16[2,328,128]{2,1,0:T(8,128)(2,1)S(1)}, u32[]{:S(2)}, u32[]{:S(2)}) collective-permute-start(bf16[2,328,128]{2,1,0:T(8,128)(2,1)} %get-tuple-element.33), channel_id=1, source_target_pairs={{0,160},{32,192},{64,224},{96,0},{128,32},{160,64},{192,96},{224,1... | collective-permute-start | bytes 503816 | tf_op jit(solution)/shard_map/ppermute | solution.py:80
  56.3 1.8 collective-permute-start.13
  61.1 3.4 %collective-permute-start.3 = (bf16[4,16,1024]{2,1,0:T(8,128)(2,1)}, bf16[4,16,1024]{2,1,0:T(8,128)(2,1)}, u32[]{:S(2)}, u32[]{:S(2)}) collective-permute-start(bf16[4,16,1024]{2,1,0:T(8,128)(2,1)} %get-tuple-element.44), channel_id=1, source_target_pairs={{0,128},{32,160},{64,192},{96,224},{128,0},{160,32},{192,64},{224,... | collective-permute-start | bytes 393224 | tf_op jit(solution)/shard_map/ppermute | solution.py:80
  67.7 1.6 collective-permute-start.6
  70.5 1.3 slice.152
  71.8 2.1 %gather_fusion.6 = bf16[32,256,128]{2,1,0:T(8,128)(2,1)} fusion(bf16[16,256,128]{2,1,0:T(8,128)(2,1)S(1)} %slice.152, s32[1024]{0:T(1024)S(1)} %pad_clamp_fusion), kind=kCustom, calls=%fused_computation.6 | custom fusion | bytes 4194432 | tf_op jit(solution)/shard_map/jit(_take)/gather | solution.py:141
  73.9 2.1 %fusion.8 = f32[2,32,128]{2,0,1:T(2,128)S(1)} fusion(bf16[32,256,128]{2,1,0:T(8,128)(2,1)} %gather_fusion.6, pred[32]{0:T(512)(128)(4,1)S(1)} %get-tuple-element.29, bf16[2,32,256]{2,1,0:T(8,128)(2,1)S(1)} %copy-done.7), kind=kOutput, calls=%fused_computation.20 | convolution fusion | flops 5242880 | bytes 2162720 | tf_op jit(solution)/shard_map/srd,rdk->srk/dot_general | solution.py:163
  76.2 1.6 bitcast_dynamic-update-slice_fusion.10
  78.0 1.3 all_to_all.29
  79.2 11.0 %all-to-all-start.1 = ((f32[16,1,10240]{2,1,0:T(1,128)}), f32[16,1,10240]{2,1,0:T(1,128)}, u32[]{:S(2)}, u32[]{:S(2)}) async-start(f32[16,1,10240]{2,1,0:T(1,128)} %all_to_all.29), calls=%async_computation.1 | async-start | bytes 1310720 | tf_op jit(solution)/shard_map/all_to_all | solution.py:186
  90.3 1.6 bitcast_dynamic-update-slice_fusion.9
  91.9 1.6 bitcast_dynamic-update-slice_fusion.8
  93.6 1.6 bitcast_dynamic-update-slice_fusion.7
  95.2 2.7 %pad_maximum_fusion = bf16[64,16,1024]{2,1,0:T(8,128)(2,1)} fusion(bf16[32,16,1024]{2,1,0:T(8,128)(2,1)} %bitcast.20, bf16[32,16,1024]{2,1,0:T(8,128)(2,1)S(1)} %copy-done.1), kind=kLoop, calls=%fused_computation.8 | loop fusion | flops 1048576 | bytes 4194304 | tf_op jit(solution)/shard_map/concatenate | solution.py:241
  97.9 2.2 %gather_fusion.1 = bf16[32,16,1024]{2,1,0:T(8,128)(2,1)S(1)} fusion(bf16[64,16,1024]{2,1,0:T(8,128)(2,1)} %pad_maximum_fusion, s32[1024]{0:T(1024)S(1)} %get-tuple-element.61), kind=kCustom, calls=%fused_computation.1 | custom fusion | bytes 2097280 | tf_op jit(solution)/shard_map/jit(_take)/gather | solution.py:252
  100.1 1.2 bitcast_select_fusion.1
  103.1 1.4 gather_fusion.5
  105.4 1.7 maximum_select_fusion
  107.4 5.7 %all-to-all-done.1 = f32[16,1,10240]{2,1,0:T(1,128)} async-done(((f32[16,1,10240]{2,1,0:T(1,128)}), f32[16,1,10240]{2,1,0:T(1,128)}, u32[]{:S(2)}, u32[]{:S(2)}) %all-to-all-start.1) | async-done | bytes 655392 | tf_op jit(solution)/shard_map/all_to_all | solution.py:186
  113.1 1.5 reduce_sum.36
  115.1 1.4 fusion.30
  117.7 4.0 %all-to-all-start.2 = ((f32[2,32,1,144]{3,0,2,1:T(2,128)}), f32[2,32,1,144]{3,0,2,1:T(2,128)S(1)}, u32[]{:S(2)}, u32[]{:S(2)}) async-start(f32[2,32,1,144]{3,0,2,1:T(2,128)} %copy.220), calls=%async_computation.2 | async-start | bytes 131072 | tf_op jit(solution)/shard_map/all_to_all | solution.py:219
  121.7 2.1 %fusion.79 = (bf16[1,512,512]{2,1,0:T(8,128)(2,1)S(1)}, bf16[1,512,512]{2,1,0:T(8,128)(2,1)}) fusion(bf16[1,512,1024]{2,1,0:T(8,128)(2,1)} %bitcast_select_fusion.1), kind=kLoop, calls=%fused_computation.181 | loop fusion | bytes 2097152 | tf_op jit(solution)/shard_map/slice | solution.py:24
  124.0 1.3 copy.226
  125.3 6.4 %all-to-all-done.2 = f32[2,32,1,144]{3,0,2,1:T(2,128)S(1)} async-done(((f32[2,32,1,144]{3,0,2,1:T(2,128)}), f32[2,32,1,144]{3,0,2,1:T(2,128)S(1)}, u32[]{:S(2)}, u32[]{:S(2)}) %all-to-all-start.2) | async-done | bytes 36896 | tf_op jit(solution)/shard_map/all_to_all | solution.py:219
  133.8 3.8 %all-to-all-start.3 = ((bf16[2,1,32,128]{3,0,1,2:T(2,128)(2,1)}), bf16[2,1,32,128]{3,0,1,2:T(2,128)(2,1)S(1)}, u32[]{:S(2)}, u32[]{:S(2)}) async-start(bf16[2,1,32,128]{3,0,1,2:T(2,128)(2,1)} %copy.232), calls=%async_computation.3 | async-start | bytes 32768 | tf_op jit(solution)/shard_map/all_to_all | solution.py:256
  137.6 4.1 %copy.250 = bf16[8192,128]{1,0:T(8,128)(2,1)} copy(bf16[8192,128]{0,1:T(8,128)(2,1)} %bitcast.245) | data formatting | bytes 4194304 | tf_op jit(solution)/shard_map/dot_general | solution.py:257
  141.7 5.6 %all-to-all-done.3 = bf16[2,1,32,128]{3,0,1,2:T(2,128)(2,1)S(1)} async-done(((bf16[2,1,32,128]{3,0,1,2:T(2,128)(2,1)}), bf16[2,1,32,128]{3,0,1,2:T(2,128)(2,1)S(1)}, u32[]{:S(2)}, u32[]{:S(2)}) %all-to-all-start.3) | async-done | bytes 16416 | tf_op jit(solution)/shard_map/all_to_all | solution.py:256
  147.3 2.4 %fusion.82 = f32[64,16,2,256]{3,0,2,1:T(8,128)S(1)} fusion(bf16[64,128,1,1]{1,0,3,2:T(8,128)(2,1)S(1)} %bitcast.259, bf16[16,2,256,128]{3,2,1,0:T(8,128)(2,1)} %bitcast.239), kind=kOutput, calls=%fused_computation.184 | convolution fusion | flops 134217728 | bytes 4210688 | tf_op jit(solution)/shard_map/dot_general | solution.py:257
  150.0 2.6 %collective-permute-done.16 = f32[64,16,256]{2,0,1:T(8,128)S(1)} collective-permute-done((f32[64,16,256]{2,0,1:T(8,128)S(1)}, f32[64,16,256]{2,0,1:T(8,128)S(1)}, u32[]{:S(2)}, u32[]{:S(2)}) %collective-permute-start.16) | collective-permute-done | bytes 1048608 | tf_op jit(solution)/shard_map/ppermute | solution.py:264
  152.8 34.4 %all_to_all.40 = f32[64,16,256]{2,0,1:T(8,128)S(1)} all-to-all(f32[64,16,256]{2,0,1:T(8,128)S(1)} %fusion.27), channel_id=1, replica_groups={{0,2,4,6,8,10,12,14,16,18,20,22,24,26,28,30},{1,3,5,7,9,11,13,15,17,19,..., dimensions={1} | all-to-all | bytes 2097152 | tf_op jit(solution)/shard_map/all_to_all | solution.py:269
  (129 shorter events, 27.5 us)
Async XLA Ops:
  0.0 116.5 %copy-start = (bf16[8192,128]{1,0:T(8,128)(2,1)S(1)}, bf16[8192,128]{1,0:T(8,128)(2,1)}, u32[]{:S(2)}) copy-start(bf16[8192,128]{1,0:T(8,128)(2,1)} %param.18) | copy-start | bytes 6291460
  4.7 3.0 %copy-start.4 = (bf16[4,64,128]{2,1,0:T(8,128)(2,1)S(1)}, bf16[4,64,128]{2,1,0:T(8,128)(2,1)}, u32[]{:S(2)}) copy-start(bf16[4,64,128]{2,1,0:T(8,128)(2,1)} %param.22) | copy-start | bytes 196612
  8.4 9.0 %copy-start.7 = (bf16[2,32,256]{2,1,0:T(8,128)(2,1)S(1)}, bf16[2,32,256]{2,1,0:T(8,128)(2,1)}, u32[]{:S(2)}) copy-start(bf16[2,32,256]{2,1,0:T(8,128)(2,1)} %param.17) | copy-start | bytes 98308
  9.7 19.8 %copy-start.8 = (s32[1,1,8,4]{2,3,1,0:T(4,128)S(1)}, s32[1,1,8,4]{2,3,1,0:T(4,128)}, u32[]{:S(2)}) copy-start(s32[1,1,8,4]{2,3,1,0:T(4,128)} %param.27) | copy-start | bytes 388
  10.9 45.3 %collective-permute-start.8 = (bf16[2,328,128]{2,1,0:T(8,128)(2,1)}, bf16[2,328,128]{2,1,0:T(8,128)(2,1)}, u32[]{:S(2)}, u32[]{:S(2)}) collective-permute-start(bf16[2,328,128]{2,1,0:T(8,128)(2,1)} %get-tuple-element.37), channel_id=1, source_target_pairs={{0,32},{32,64},{64,96},{96,128},{128,160},{160,192},{192,224},{224... | collective-permute-start | bytes 503816 | tf_op jit(solution)/shard_map/ppermute | solution.py:80
  12.5 46.5 %collective-permute-start.9 = (bf16[2,328,128]{2,1,0:T(8,128)(2,1)}, bf16[2,328,128]{2,1,0:T(8,128)(2,1)}, u32[]{:S(2)}, u32[]{:S(2)}) collective-permute-start(bf16[2,328,128]{2,1,0:T(8,128)(2,1)} %get-tuple-element.36), channel_id=1, source_target_pairs={{0,64},{32,96},{64,128},{96,160},{128,192},{160,224},{192,0},{224,... | collective-permute-start | bytes 503816 | tf_op jit(solution)/shard_map/ppermute | solution.py:80
  14.0 47.1 %collective-permute-start.10 = (bf16[2,328,128]{2,1,0:T(8,128)(2,1)}, bf16[2,328,128]{2,1,0:T(8,128)(2,1)}, u32[]{:S(2)}, u32[]{:S(2)}) collective-permute-start(bf16[2,328,128]{2,1,0:T(8,128)(2,1)} %get-tuple-element.35), channel_id=1, source_target_pairs={{0,96},{32,128},{64,160},{96,192},{128,224},{160,0},{192,32},{224,... | collective-permute-start | bytes 503816 | tf_op jit(solution)/shard_map/ppermute | solution.py:80
  16.7 48.7 %collective-permute-start.11 = (bf16[2,328,128]{2,1,0:T(8,128)(2,1)}, bf16[2,328,128]{2,1,0:T(8,128)(2,1)}, u32[]{:S(2)}, u32[]{:S(2)}) collective-permute-start(bf16[2,328,128]{2,1,0:T(8,128)(2,1)} %get-tuple-element.34), channel_id=1, source_target_pairs={{0,128},{32,160},{64,192},{96,224},{128,0},{160,32},{192,64},{224,... | collective-permute-start | bytes 503816 | tf_op jit(solution)/shard_map/ppermute | solution.py:80
  18.3 60.9 %all-to-all-start = ((bf16[16,2,32,256]{3,2,1,0:T(8,128)(2,1)}), bf16[16,2,32,256]{3,2,1,0:T(8,128)(2,1)}, u32[]{:S(2)}, u32[]{:S(2)}) async-start(bf16[16,2,32,256]{3,2,1,0:T(8,128)(2,1)} %broadcast_in_dim.153), calls=%async_computation | async-start | bytes 1048576 | tf_op jit(solution)/shard_map/all_to_all | solution.py:145
  31.8 2.0 %copy-start.9 = (s32[32]{0:T(128)S(1)}, s32[32]{0:T(128)}, u32[]{:S(2)}) copy-start(s32[32]{0:T(128)} %param.28) | copy-start | bytes 388
  31.8 2.0 %copy-start.10 = (s32[1,32]{1,0:T(1,128)S(1)}, s32[1,32]{1,0:T(1,128)}, u32[]{:S(2)}) copy-start(s32[1,32]{1,0:T(1,128)} %param.26) | copy-start | bytes 388
  33.1 24.9 %copy-start.2 = (bf16[8,2,328,128]{3,2,1,0:T(8,128)(2,1)S(1)}, bf16[8,2,328,128]{3,2,1,0:T(8,128)(2,1)}, u32[]{:S(2)}) copy-start(bf16[8,2,328,128]{3,2,1,0:T(8,128)(2,1)} %get-tuple-element.38) | copy-start | bytes 4030468
  33.1 7.7 %collective-permute-start = (bf16[4,16,1024]{2,1,0:T(8,128)(2,1)}, bf16[4,16,1024]{2,1,0:T(8,128)(2,1)}, u32[]{:S(2)}, u32[]{:S(2)}) collective-permute-start(bf16[4,16,1024]{2,1,0:T(8,128)(2,1)} %get-tuple-element.47), channel_id=1, source_target_pairs={{0,32},{32,64},{64,96},{96,128},{128,160},{160,192},{192,224},{224... | collective-permute-start | bytes 393224 | tf_op jit(solution)/shard_map/ppermute | solution.py:80
  40.8 5.3 %collective-permute-start.1 = (bf16[4,16,1024]{2,1,0:T(8,128)(2,1)}, bf16[4,16,1024]{2,1,0:T(8,128)(2,1)S(1)}, u32[]{:S(2)}, u32[]{:S(2)}) collective-permute-start(bf16[4,16,1024]{2,1,0:T(8,128)(2,1)} %get-tuple-element.46), channel_id=1, source_target_pairs={{0,64},{32,96},{64,128},{96,160},{128,192},{160,224},{192,0},{224,... | collective-permute-start | bytes 393224 | tf_op jit(solution)/shard_map/ppermute | solution.py:80
  46.1 7.6 %collective-permute-start.2 = (bf16[4,16,1024]{2,1,0:T(8,128)(2,1)}, bf16[4,16,1024]{2,1,0:T(8,128)(2,1)S(1)}, u32[]{:S(2)}, u32[]{:S(2)}) collective-permute-start(bf16[4,16,1024]{2,1,0:T(8,128)(2,1)} %get-tuple-element.45), channel_id=1, source_target_pairs={{0,96},{32,128},{64,160},{96,192},{128,224},{160,0},{192,32},{224,... | collective-permute-start | bytes 393224 | tf_op jit(solution)/shard_map/ppermute | solution.py:80
  53.7 13.6 %collective-permute-start.12 = (bf16[2,328,128]{2,1,0:T(8,128)(2,1)}, bf16[2,328,128]{2,1,0:T(8,128)(2,1)S(1)}, u32[]{:S(2)}, u32[]{:S(2)}) collective-permute-start(bf16[2,328,128]{2,1,0:T(8,128)(2,1)} %get-tuple-element.33), channel_id=1, source_target_pairs={{0,160},{32,192},{64,224},{96,0},{128,32},{160,64},{192,96},{224,1... | collective-permute-start | bytes 503816 | tf_op jit(solution)/shard_map/ppermute | solution.py:80
  56.3 11.4 %collective-permute-start.13 = (bf16[2,328,128]{2,1,0:T(8,128)(2,1)}, bf16[2,328,128]{2,1,0:T(8,128)(2,1)S(1)}, u32[]{:S(2)}, u32[]{:S(2)}) collective-permute-start(bf16[2,328,128]{2,1,0:T(8,128)(2,1)} %get-tuple-element.32), channel_id=1, source_target_pairs={{0,192},{32,224},{64,0},{96,32},{128,64},{160,96},{192,128},{224,1... | collective-permute-start | bytes 503816 | tf_op jit(solution)/shard_map/ppermute | solution.py:80
  59.0 10.3 %collective-permute-start.14 = (bf16[2,328,128]{2,1,0:T(8,128)(2,1)}, bf16[2,328,128]{2,1,0:T(8,128)(2,1)S(1)}, u32[]{:S(2)}, u32[]{:S(2)}) collective-permute-start(bf16[2,328,128]{2,1,0:T(8,128)(2,1)} %get-tuple-element.31), channel_id=1, source_target_pairs={{0,224},{32,0},{64,32},{96,64},{128,96},{160,128},{192,160},{224,1... | collective-permute-start | bytes 503816 | tf_op jit(solution)/shard_map/ppermute | solution.py:80
  61.1 15.1 %collective-permute-start.3 = (bf16[4,16,1024]{2,1,0:T(8,128)(2,1)}, bf16[4,16,1024]{2,1,0:T(8,128)(2,1)}, u32[]{:S(2)}, u32[]{:S(2)}) collective-permute-start(bf16[4,16,1024]{2,1,0:T(8,128)(2,1)} %get-tuple-element.44), channel_id=1, source_target_pairs={{0,128},{32,160},{64,192},{96,224},{128,0},{160,32},{192,64},{224,... | collective-permute-start | bytes 393224 | tf_op jit(solution)/shard_map/ppermute | solution.py:80
  65.5 24.8 %collective-permute-start.4 = (bf16[4,16,1024]{2,1,0:T(8,128)(2,1)}, bf16[4,16,1024]{2,1,0:T(8,128)(2,1)}, u32[]{:S(2)}, u32[]{:S(2)}) collective-permute-start(bf16[4,16,1024]{2,1,0:T(8,128)(2,1)} %get-tuple-element.43), channel_id=1, source_target_pairs={{0,160},{32,192},{64,224},{96,0},{128,32},{160,64},{192,96},{224,1... | collective-permute-start | bytes 393224 | tf_op jit(solution)/shard_map/ppermute | solution.py:80
  67.3 24.6 %collective-permute-start.5 = (bf16[4,16,1024]{2,1,0:T(8,128)(2,1)}, bf16[4,16,1024]{2,1,0:T(8,128)(2,1)}, u32[]{:S(2)}, u32[]{:S(2)}) collective-permute-start(bf16[4,16,1024]{2,1,0:T(8,128)(2,1)} %get-tuple-element.42), channel_id=1, source_target_pairs={{0,192},{32,224},{64,0},{96,32},{128,64},{160,96},{192,128},{224,1... | collective-permute-start | bytes 393224 | tf_op jit(solution)/shard_map/ppermute | solution.py:80
  67.7 25.9 %collective-permute-start.6 = (bf16[4,16,1024]{2,1,0:T(8,128)(2,1)}, bf16[4,16,1024]{2,1,0:T(8,128)(2,1)}, u32[]{:S(2)}, u32[]{:S(2)}) collective-permute-start(bf16[4,16,1024]{2,1,0:T(8,128)(2,1)} %get-tuple-element.41), channel_id=1, source_target_pairs={{0,224},{32,0},{64,32},{96,64},{128,96},{160,128},{192,160},{224,1... | collective-permute-start | bytes 393224 | tf_op jit(solution)/shard_map/ppermute | solution.py:80
  69.4 1.1 copy-start.3
  73.9 2.1 %copy-start.6 = (f32[16,1,2048]{2,1,0:T(1,128)S(1)}, f32[16,1,2048]{2,1,0:T(1,128)}, u32[]{:S(2)}) copy-start(f32[16,1,2048]{2,1,0:T(1,128)} %get-tuple-element.50) | copy-start | bytes 393220
  73.9 3.9 %copy-start.5 = (f32[16,1,2048]{2,1,0:T(1,128)S(1)}, f32[16,1,2048]{2,1,0:T(1,128)}, u32[]{:S(2)}) copy-start(f32[16,1,2048]{2,1,0:T(1,128)} %get-tuple-element.49) | copy-start | bytes 393220
  76.1 1.7 collective-permute-start.15
  77.9 17.3 %copy-start.1 = (bf16[32,16,1024]{2,1,0:T(8,128)(2,1)S(1)}, bf16[32,16,1024]{2,1,0:T(8,128)(2,1)}, u32[]{:S(2)}) copy-start(bf16[32,16,1024]{2,1,0:T(8,128)(2,1)} %param.24) | copy-start | bytes 3145732
  79.2 33.9 %all-to-all-start.1 = ((f32[16,1,10240]{2,1,0:T(1,128)}), f32[16,1,10240]{2,1,0:T(1,128)}, u32[]{:S(2)}, u32[]{:S(2)}) async-start(f32[16,1,10240]{2,1,0:T(1,128)} %all_to_all.29), calls=%async_computation.1 | async-start | bytes 1310720 | tf_op jit(solution)/shard_map/all_to_all | solution.py:186
  93.4 12.0 %collective-permute-start.7 = (bf16[16,2,32,256]{3,2,1,0:T(8,128)(2,1)}, bf16[16,2,32,256]{3,2,1,0:T(8,128)(2,1)}, u32[]{:S(2)}, u32[]{:S(2)}) collective-permute-start(bf16[16,2,32,256]{3,2,1,0:T(8,128)(2,1)} %all-to-all-done), channel_id=1, source_target_pairs={{0,1},{1,0},{2,3},{3,2},{4,5},{5,4},{6,7},{7,6},{8,9},{9,8},{10,11... | collective-permute-start | bytes 1572872 | tf_op jit(solution)/shard_map/ppermute | solution.py:153
  117.7 14.0 %all-to-all-start.2 = ((f32[2,32,1,144]{3,0,2,1:T(2,128)}), f32[2,32,1,144]{3,0,2,1:T(2,128)S(1)}, u32[]{:S(2)}, u32[]{:S(2)}) async-start(f32[2,32,1,144]{3,0,2,1:T(2,128)} %copy.220), calls=%async_computation.2 | async-start | bytes 131072 | tf_op jit(solution)/shard_map/all_to_all | solution.py:219
  133.8 13.5 %all-to-all-start.3 = ((bf16[2,1,32,128]{3,0,1,2:T(2,128)(2,1)}), bf16[2,1,32,128]{3,0,1,2:T(2,128)(2,1)S(1)}, u32[]{:S(2)}, u32[]{:S(2)}) async-start(bf16[2,1,32,128]{3,0,1,2:T(2,128)(2,1)} %copy.232), calls=%async_computation.3 | async-start | bytes 32768 | tf_op jit(solution)/shard_map/all_to_all | solution.py:256
  149.9 2.7 %collective-permute-start.16 = (f32[64,16,256]{2,0,1:T(8,128)S(1)}, f32[64,16,256]{2,0,1:T(8,128)S(1)}, u32[]{:S(2)}, u32[]{:S(2)}) collective-permute-start(f32[64,16,256]{2,0,1:T(8,128)S(1)} %select_bitcast_fusion), channel_id=1, source_target_pairs={{0,1},{1,0},{2,3},{3,2},{4,5},{5,4},{6,7},{7,6},{8,9},{9,8},{10,11... | collective-permute-start | bytes 3145736 | tf_op jit(solution)/shard_map/ppermute | solution.py:264

commit v6 on v4

--- a/solution.py
+++ b/solution.py
@@ -70,6 +70,55 @@
         .reshape(step_count, batch_own, QUERY_HEADS, HEAD_SIZE)
         .astype(jnp.bfloat16)
     )
+
+
+SWAP_BITS = (1, 2)
+
+
+def stage_groups(n_tp):
+    span = 1 << len(SWAP_BITS)
+    return [[t for t in range(n_tp) if t % span == p] for p in range(span)]
+
+
+def reduce_scatter_tp(parts, shared, column_id, n_tp):
+    for bit in SWAP_BITS:
+        mine = (column_id // bit) % 2
+        split = parts.reshape((-1, 2) + parts.shape[1:])
+        keep = jnp.where(mine == 0, split[:, 0], split[:, 1])
+        give = jnp.where(mine == 0, split[:, 1], split[:, 0])
+        sent = jnp.concatenate([give.reshape(-1), shared.reshape(-1)])
+        got = lax.ppermute(sent, "tp", [(t, t ^ bit) for t in range(n_tp)])
+        parts = keep + got[: give.size].reshape(give.shape)
+        shared = shared + got[give.size :].reshape(shared.shape)
+    flat = parts.reshape(parts.shape[0], -1)
+    send = jnp.concatenate(
+        [flat, jnp.broadcast_to(shared.reshape(1, -1), (flat.shape[0], shared.size))], -1
+    )
+    total = jnp.sum(
+        lax.all_to_all(send, "tp", 0, 0, tiled=True, axis_index_groups=stage_groups(n_tp)), 0
+    )
+    return total[: flat.shape[1]], total[flat.shape[1] :].reshape(shared.shape)
+
+
+def all_gather_tp(block, column_id, n_tp):
+    rest = n_tp >> len(SWAP_BITS)
+    gathered = lax.all_to_all(
+        jnp.broadcast_to(block[None], (rest,) + block.shape),
+        "tp",
+        0,
+        0,
+        tiled=True,
+        axis_index_groups=stage_groups(n_tp),
+    )
+    for done, bit in enumerate(reversed(SWAP_BITS)):
+        mine = (column_id // bit) % 2
+        other = lax.ppermute(gathered, "tp", [(t, t ^ bit) for t in range(n_tp)])
+        gathered = jnp.where(
+            mine == 0,
+            jnp.stack([gathered, other], 1 + done),
+            jnp.stack([other, gathered], 1 + done),
+        )
+    return gathered.reshape((n_tp,) + block.shape)
 
 
 def per_device(
@@ -96,9 +145,6 @@
     key_span_width = KEY_VALUE_HEADS * HEAD_SIZE
     cap_slots = read_rows_list.shape[2]
     own_start = column_id * batch_own
-    core = column_id % 2
-    swap = [(t, t ^ 1) for t in range(n_tp)]
-    parity = [[t for t in range(n_tp) if t % 2 == p] for p in range(2)]
 
     value_cols = adapter_up_value.shape[2] // n_tp
     send_rows = jnp.maximum(read_rows_list[:, group_number, :], 0)
@@ -129,20 +175,7 @@
     upq_rows = jnp.take(upq_recv, request_adapter_entry, axis=0)
     upv_rows = jnp.take(upv_recv, request_adapter_entry, axis=0)
 
-    hidden_same = lax.all_to_all(
-        jnp.broadcast_to(hidden[None], (n_tp // 2,) + hidden.shape),
-        "tp",
-        0,
-        0,
-        tiled=True,
-        axis_index_groups=parity,
-    )
-    hidden_other = lax.ppermute(hidden_same, "tp", swap)
-    hidden_sent = jnp.where(
-        core == 0,
-        jnp.stack([hidden_same, hidden_other], 1),
-        jnp.stack([hidden_other, hidden_same], 1),
-    ).reshape((n_tp,) + hidden.shape)
+    hidden_sent = all_gather_tp(hidden, column_id, n_tp)
     hidden_full = jnp.transpose(hidden_sent, (1, 2, 0, 3)).reshape(
         step_count, batch_rows, n_tp * width_local
     )
@@ -150,34 +183,10 @@
     shrink_part = jnp.einsum("srd,rdk->srk", hidden, down_rows, preferred_element_type=jnp.float32)
     key_value_part = jnp.einsum(
         "srd,dc->rsc", hidden, key_value_weight, preferred_element_type=jnp.float32
-    ).reshape(n_tp // 2, 2, batch_own * step_count * 2 * key_span_width)
-    pair_send = jnp.concatenate(
-        [
-            jnp.where(core == 0, key_value_part[:, 1], key_value_part[:, 0]).reshape(-1),
-            shrink_part.reshape(-1),
-        ]
-    )
-    pair_recv = lax.ppermute(pair_send, "tp", swap)
-    kv_pair = jnp.where(core == 0, key_value_part[:, 0], key_value_part[:, 1]) + pair_recv[
-        : key_value_part.shape[0] * key_value_part.shape[2]
-    ].reshape(key_value_part.shape[0], -1)
-    shrink_pair = shrink_part.reshape(-1) + pair_recv[key_value_part.shape[0] * key_value_part.shape[2] :]
-    reduce_send = jnp.concatenate(
-        [
-            kv_pair,
-            jnp.broadcast_to(shrink_pair[None], (n_tp // 2, shrink_part.size)),
-        ],
-        -1,
-    )
-    reduce_recv = jnp.sum(
-        lax.all_to_all(reduce_send, "tp", 0, 0, tiled=True, axis_index_groups=parity), 0
-    )
-    key_value_plain = reduce_recv[: key_value_part.shape[2]].reshape(
-        batch_own, step_count, 2 * key_span_width
-    )
-    down_projected_low = (
-        reduce_recv[key_value_part.shape[2] :].reshape(shrink_part.shape).astype(jnp.bfloat16)
-    )
+    )
+    kv_total, shrink_total = reduce_scatter_tp(key_value_part, shrink_part, column_id, n_tp)
+    key_value_plain = kv_total.reshape(batch_own, step_count, 2 * key_span_width)
+    down_projected_low = shrink_total.astype(jnp.bfloat16)
 
     query_plain = jnp.einsum(
         "srd,dc->src", hidden_full, query_weight, preferred_element_type=jnp.float32
@@ -228,19 +237,15 @@
     )
     attended = attend(query_own, ctx_pages, keyval_new, lengths)
     heads_back = lax.all_to_all(attended, "tp", split_axis=2, concat_axis=1, tiled=True)
-    projected = jnp.dot(
+    out_cols = output_weight.shape[1] // n_tp
+    projected = jnp.einsum(
+        "rk,kdc->drc",
         heads_back.reshape(step_count * batch_rows, -1),
-        output_weight,
-        preferred_element_type=jnp.float32,
-    )
-    out_cols = projected.shape[1] // n_tp
-    projected = projected.reshape(step_count * batch_rows, n_tp // 2, 2, out_cols)
-    out_other = lax.ppermute(
-        jnp.where(core == 0, projected[:, :, 1], projected[:, :, 0]), "tp", swap
-    )
-    out_pair = jnp.where(core == 0, projected[:, :, 0], projected[:, :, 1]) + out_other
-    summed = jnp.sum(
-        lax.all_to_all(out_pair, "tp", 1, 1, tiled=True, axis_index_groups=parity), 1
+        output_weight.reshape(output_weight.shape[0], n_tp, out_cols),
+        preferred_element_type=jnp.float32,
+    )
+    summed, _ = reduce_scatter_tp(
+        projected, jnp.zeros((0,), jnp.float32), column_id, n_tp
     )
     return summed.reshape(step_count, batch_rows, out_cols).astype(jnp.bfloat16)
 

time: 186 us -> 181 us (0.973)
  waiting for transfers between devices: 51 us -> 35 us
  other arithmetic: 18.8 us -> 26.7 us
  starting transfers between devices: 38.7 us -> 43.5 us
  blocking collectives: 34.4 us -> 32.3 us
    all_to_all x3 -> x2, waiting for transfers between devices: 24.6 us -> 0.01 us  [the longest x1 0.01 us: all_gather_tp(): lax.all_to_all(jnp.broadcast_to(block[None], (rest,) + block.shape), 'tp'...]
    ppermute x3 -> x6, waiting for transfers between devices: 4.03 us -> 19.3 us  [the longest x4 19.3 us: reduce_scatter_tp(): got = lax.ppermute(sent, 'tp', [(t, t ^ bit) for t in range(n_tp)])]
    ppermute x3 -> x6, starting transfers between devices: 0.28 us -> 7.23 us  [the longest x4 3.87 us: reduce_scatter_tp(): got = lax.ppermute(sent, 'tp', [(t, t ^ bit) for t in range(n_tp)])]
    all_to_all x1, waiting for transfers between devices: 6.38 us -> 0.01 us  [per_device(): lax.all_to_all(outgoing, 'group', split_axis=0, concat_axis=0, tiled=True)]
    all_to_all x3 -> x2, starting transfers between devices: 19.2 us -> 15 us  [the longest x1 8.47 us: all_gather_tp(): lax.all_to_all(jnp.broadcast_to(block[None], (rest,) + block.shape), 'tp'...]
    dot_general x1, local copies, waits for them, and re-layouts: 4.08 us -> 0.01 us  [per_device(): jnp.einsum('srd,rdk->srk', hidden, down_rows, preferred_element_type=jnp....]
    select_n x3 -> x5, other arithmetic: 2.75 us -> 6.06 us  [the longest x3 5.81 us: all_gather_tp(): jnp.where(mine == 0, jnp.stack([gathered, other], 1 + done), jnp.stack([o...]
    unnamed x22 -> x33, local copies, waits for them, and re-layouts: 0.05 us -> 3.28 us
  transfers between devices with their start and end apart: 9 -> 11, of which waited for: 8 -> 5; matrix products, arithmetic and copies ran while one was open for 20% -> 27% of each run, Pallas kernels for 0% -> 0%
where the time goes in v6:
time: 181 us; the launch traced here: 180 us
  starting transfers between devices  43.5 us (24%)
  waiting for transfers between devices  35 us (19%)
  local copies, waits for them, and re-layouts  32.7 us (18%)
  blocking collectives  32.3 us (18%)
  other arithmetic  26.7 us (15%)
  matrix products  8.38 us (5%)
    all_to_all x1, blocking collectives, reduce_scatter_tp(): lax.all_to_all(send, 'tp', 0, 0, tiled=True, axis_index_groups=stage_grou...  19.7 us
    ppermute x4, waiting for transfers between devices, reduce_scatter_tp(): got = lax.ppermute(sent, 'tp', [(t, t ^ bit) for t in range(n_tp)])  19.3 us
    all_to_all x1, blocking collectives, per_device(): lax.all_to_all(attended, 'tp', split_axis=2, concat_axis=1, tiled=True)  12.7 us
    all_to_all x1, starting transfers between devices, per_device(): lax.all_to_all(query_send, 'tp', split_axis=1, concat_axis=2, tiled=True)  9.19 us
    all_to_all x1, waiting for transfers between devices, per_device(): lax.all_to_all(query_send, 'tp', split_axis=1, concat_axis=2, tiled=True)  8.69 us
    all_to_all x1, starting transfers between devices, all_gather_tp(): lax.all_to_all(jnp.broadcast_to(block[None], (rest,) + block.shape), 'tp'...  8.47 us
    all_to_all x1, waiting for transfers between devices, per_device(): lax.all_to_all(panel_send, 'group', 0, 0, tiled=True)  6.96 us
    all_to_all x1, starting transfers between devices, reduce_scatter_tp(): lax.all_to_all(send, 'tp', 0, 0, tiled=True, axis_index_groups=stage_grou...  6.57 us
  transfers between devices with their start and end apart: 11, of which 5 were waited for; matrix products, arithmetic and copies ran while one was open for 27% of the time, Pallas kernels for 0%

profile of v6, /device:TPU:2, one launch (start us, length us, event | category | flops | bytes accessed | tf_op | source)
XLA Modules:
  0.0 179.9 jit_solution(18256170927674613093)
XLA Ops:
  0.0 1.6 broadcast_in_dim.136
  1.6 8.5 %all-to-all-start.1 = ((bf16[8,2,32,256]{3,2,1,0:T(8,128)(2,1)}), bf16[8,2,32,256]{3,2,1,0:T(8,128)(2,1)}, u32[]{:S(2)}, u32[]{:S(2)}) async-start(bf16[8,2,32,256]{3,2,1,0:T(8,128)(2,1)} %broadcast_in_dim.136), calls=%async_computation.1 | async-start | bytes 524288 | tf_op jit(solution)/shard_map/all_to_all | solution.py:105
  10.1 1.0 fusion.54
  11.9 1.3 convolution_bitcast_fusion
  13.3 0.9 fusion.65
  14.2 0.9 constant_dynamic-slice_fusion
  17.6 1.5 broadcast_select_fusion.3
  19.0 1.1 broadcast_select_fusion
  20.1 1.5 gather_fusion.3
  21.9 2.4 %pad_maximum_fusion.1 = bf16[8,2,328,128]{3,2,1,0:T(8,128)(2,1)} fusion(bf16[8,2,8,128]{3,2,1,0:T(8,128)(2,1)} %broadcast_select_fusion.3, bf16[8,2,64,128]{3,2,1,0:T(8,128)(2,1)S(1)} %broadcast_select_fusion.2, bf16[8,2,256,128]{3,2,1,0:T(8,128)(2,1)} %broadcast_select_fusion), kind=kLoop, calls=%fused_computation.17 | loop fusion | flops 4030464 | bytes 2686976 | tf_op jit(solution)/shard_map/concatenate | solution.py:158
  24.4 0.8 select_bitcast_fusion
  25.2 6.0 %all-to-all-start.2 = ((bf16[8,2,328,128]{3,2,1,0:T(8,128)(2,1)}), bf16[8,2,328,128]{3,2,1,0:T(8,128)(2,1)S(1)}, u32[]{:S(2)}, u32[]{:S(2)}) async-start(bf16[8,2,328,128]{3,2,1,0:T(8,128)(2,1)} %pad_maximum_fusion.1), calls=%async_computation.2 | async-start | bytes 2686976 | tf_op jit(solution)/shard_map/all_to_all | solution.py:166
  31.2 1.6 copy.285
  33.8 2.9 %gather_fusion = bf16[32,16,1024]{2,1,0:T(8,128)(2,1)} fusion(bf16[32,16,1024]{2,1,0:T(8,128)(2,1)} %param.20, s32[1024]{0:T(1024)S(1)} %pad_clamp_fusion.3), kind=kCustom, calls=%fused_computation | custom fusion | bytes 2097280 | tf_op jit(solution)/shard_map/jit(_take)/gather | solution.py:230
  36.7 2.4 %select_multiply_fusion = bf16[32,16,1024]{2,1,0:T(8,128)(2,1)} fusion(bf16[32,16,1024]{2,1,0:T(8,128)(2,1)} %gather_fusion, pred[32]{0:T(512)(128)(4,1)S(1)} %le.73, bf16[32]{0:T(256)(128)(2,1)S(1)} %reshape.527), kind=kLoop, calls=%fused_computation.35 | loop fusion | flops 1048576 | bytes 2097248 | tf_op jit(solution)/shard_map/mul | solution.py:230
  39.2 2.9 %collective-permute-start = (bf16[8,2,32,256]{3,2,1,0:T(8,128)(2,1)}, bf16[8,2,32,256]{3,2,1,0:T(8,128)(2,1)}, u32[]{:S(2)}, u32[]{:S(2)}) collective-permute-start(bf16[8,2,32,256]{3,2,1,0:T(8,128)(2,1)} %all-to-all-done.1), channel_id=1, source_target_pairs={{0,2},{1,3},{2,0},{3,1},{4,6},{5,7},{6,4},{7,5},{8,10},{9,11},{10,... | collective-permute-start | bytes 786440 | tf_op jit(solution)/shard_map/ppermute | solution.py:115
  42.1 7.0 %all-to-all-done.2 = bf16[8,2,328,128]{3,2,1,0:T(8,128)(2,1)S(1)} async-done(((bf16[8,2,328,128]{3,2,1,0:T(8,128)(2,1)}), bf16[8,2,328,128]{3,2,1,0:T(8,128)(2,1)S(1)}, u32[]{:S(2)}, u32[]{:S(2)}) %all-to-all-start.2) | async-done | bytes 1343520 | tf_op jit(solution)/shard_map/all_to_all | solution.py:166
  49.0 6.1 %all-to-all-start = ((bf16[32,16,1024]{2,1,0:T(8,128)(2,1)}), bf16[32,16,1024]{2,1,0:T(8,128)(2,1)}, u32[]{:S(2)}, u32[]{:S(2)}) async-start(bf16[32,16,1024]{2,1,0:T(8,128)(2,1)} %select_multiply_fusion), calls=%async_computation | async-start | bytes 2097152 | tf_op jit(solution)/shard_map/all_to_all | solution.py:233
  55.1 1.3 slice.191
  56.4 2.2 %gather_fusion.6 = bf16[32,256,128]{2,1,0:T(8,128)(2,1)} fusion(bf16[16,256,128]{2,1,0:T(8,128)(2,1)S(1)} %slice.191, s32[1024]{0:T(1024)S(1)} %pad_clamp_fusion), kind=kCustom, calls=%fused_computation.6 | custom fusion | bytes 4194432 | tf_op jit(solution)/shard_map/jit(_take)/gather | solution.py:174
  58.6 2.1 %fusion.5 = f32[32,128,2]{1,2,0:T(2,128)S(1)} fusion(bf16[32,256,128]{2,1,0:T(8,128)(2,1)} %gather_fusion.6, pred[32]{0:T(512)(128)(4,1)S(1)} %get-tuple-element.21, bf16[2,32,256]{2,1,0:T(8,128)(2,1)S(1)} %copy-done.10), kind=kOutput, calls=%fused_computation.14 | convolution fusion | flops 5242880 | bytes 2162720 | tf_op jit(solution)/shard_map/srd,rdk->srk/dot_general | solution.py:183
  61.0 2.1 %maximum_select_fusion.2 = bf16[8,2,2,32,256]{4,3,2,0,1:T(8,128)(2,1)} fusion(bf16[8,1,2,32,256]{4,3,2,0,1:T(8,128)(2,1)} %bitcast.10, bf16[8,1,2,32,256]{4,3,2,0,1:T(8,128)(2,1)} %bitcast.9, pred[]{:T(512)S(6)} %eq.11), kind=kLoop, calls=%fused_computation.41 | loop fusion | flops 786432 | bytes 1048577 | tf_op jit(solution)/shard_map/jit(_where)/select_n | solution.py:116
  64.0 3.0 %collective-permute-start.3 = (f32[24576]{0:T(1024)S(1)}, f32[24576]{0:T(1024)S(1)}, u32[]{:S(2)}, u32[]{:S(2)}) collective-permute-start(f32[24576]{0:T(1024)S(1)} %pad_maximum_fusion.4), channel_id=1, source_target_pairs={{0,2},{1,3},{2,0},{3,1},{4,6},{5,7},{6,4},{7,5},{8,10},{9,11},{10,... | collective-permute-start | bytes 294920 | tf_op jit(solution)/shard_map/ppermute | solution.py:90
  67.0 2.1 %maximum_select_fusion.1 = bf16[8,2,1,2,32,256]{5,4,3,0,2,1:T(8,128)(2,1)} fusion(bf16[8,1,1,2,32,256]{5,4,3,0,2,1:T(8,128)(2,1)} %bitcast.8, bf16[8,1,1,2,32,256]{5,4,3,0,2,1:T(8,128)(2,1)} %bitcast.7, pred[]{:T(512)S(6)} %eq.11), kind=kLoop, calls=%fused_computation.40 | loop fusion | flops 786432 | bytes 1048577 | tf_op jit(solution)/shard_map/jit(_where)/select_n | solution.py:116
  69.1 2.0 %collective-permute-done.3 = f32[24576]{0:T(1024)S(1)} collective-permute-done((f32[24576]{0:T(1024)S(1)}, f32[24576]{0:T(1024)S(1)}, u32[]{:S(2)}, u32[]{:S(2)}) %collective-permute-start.3) | collective-permute-done | bytes 98336 | tf_op jit(solution)/shard_map/ppermute | solution.py:90
  71.3 0.9 all_to_all.38
  72.3 6.6 %all-to-all-start.3 = ((f32[8,1,10240]{2,1,0:T(1,128)}), f32[8,1,10240]{2,1,0:T(1,128)}, u32[]{:S(2)}, u32[]{:S(2)}) async-start(f32[8,1,10240]{2,1,0:T(1,128)} %all_to_all.38), calls=%async_computation.3 | async-start | bytes 655360 | tf_op jit(solution)/shard_map/all_to_all | solution.py:98
  78.9 2.7 %pad_maximum_fusion = bf16[64,16,1024]{2,1,0:T(8,128)(2,1)} fusion(bf16[32,16,1024]{2,1,0:T(8,128)(2,1)} %all-to-all-done, bf16[32,16,1024]{2,1,0:T(8,128)(2,1)S(1)} %copy-done.3), kind=kLoop, calls=%fused_computation.11 | loop fusion | flops 1048576 | bytes 4194304 | tf_op jit(solution)/shard_map/concatenate | solution.py:234
  81.6 2.2 %gather_fusion.1 = bf16[32,16,1024]{2,1,0:T(8,128)(2,1)S(1)} fusion(bf16[64,16,1024]{2,1,0:T(8,128)(2,1)} %pad_maximum_fusion, s32[1024]{0:T(1024)S(1)} %pad_clamp_fusion.2), kind=kCustom, calls=%fused_computation.1 | custom fusion | bytes 2097280 | tf_op jit(solution)/shard_map/jit(_take)/gather | solution.py:235
  83.8 1.3 copy.230
  85.2 2.3 %broadcast_select_fusion.1 = bf16[1,512,1024]{1,2,0:T(8,128)(2,1)} fusion(bf16[1,512,1024]{1,2,0:T(8,128)(2,1)} %copy.230, pred[512]{0:T(512)(128)(4,1)S(1)} %broadcast_in_dim.131), kind=kLoop, calls=%fused_computation.37 | loop fusion | flops 524288 | bytes 2097664 | tf_op jit(solution)/shard_map/jit(_take)/select_n | solution.py:235
  87.5 1.0 slice.188
  89.2 1.4 gather_fusion.5
  91.6 1.6 maximum_select_fusion
  93.4 1.2 reduce_sum.36
  95.1 1.4 fusion.28
  97.7 9.2 %all-to-all-start.4 = ((f32[2,32,1,144]{3,0,2,1:T(2,128)}), f32[2,32,1,144]{3,0,2,1:T(2,128)S(1)}, u32[]{:S(2)}, u32[]{:S(2)}) async-start(f32[2,32,1,144]{3,0,2,1:T(2,128)} %copy.252), calls=%async_computation.4 | async-start | bytes 131072 | tf_op jit(solution)/shard_map/all_to_all | solution.py:215
  106.9 1.3 fusion.64
  108.2 8.7 %all-to-all-done.4 = f32[2,32,1,144]{3,0,2,1:T(2,128)S(1)} async-done(((f32[2,32,1,144]{3,0,2,1:T(2,128)}), f32[2,32,1,144]{3,0,2,1:T(2,128)S(1)}, u32[]{:S(2)}, u32[]{:S(2)}) %all-to-all-start.4) | async-done | bytes 36896 | tf_op jit(solution)/shard_map/all_to_all | solution.py:215
  118.4 12.7 %all_to_all.51 = bf16[2,1,32,128]{3,0,1,2:T(2,128)(2,1)S(1)} all-to-all(bf16[2,1,32,128]{3,0,1,2:T(2,128)(2,1)S(1)} %copy.263), channel_id=1, replica_groups=mesh['group'=8,'tp'=32] {'tp'}, dimensions={2} | all-to-all | bytes 32768 | tf_op jit(solution)/shard_map/all_to_all | solution.py:239
  131.1 2.0 %fusion = f32[64,32,256]{2,0,1:T(8,128)S(1)} fusion(bf16[64,128,1]{1,0,2:T(8,128)(2,1)S(1)} %bitcast.222, bf16[16,32,8,256]{3,2,1,0:T(8,128)(2,1)} %bitcast.203), kind=kOutput, calls=%fused_computation.8 | convolution fusion | flops 134217728 | bytes 4210688 | tf_op jit(solution)/shard_map/rk,kdc->drc/dot_general | solution.py:241
  133.9 2.8 %collective-permute-done.4 = f32[262144]{0:T(1024)} collective-permute-done((f32[262144]{0:T(1024)S(1)}, f32[262144]{0:T(1024)}, u32[]{:S(2)}, u32[]{:S(2)}) %collective-permute-start.4) | collective-permute-done | bytes 1048608 | tf_op jit(solution)/shard_map/ppermute | solution.py:90
  136.7 2.5 %reshape.525 = f32[8,2,64,256]{3,2,1,0:T(8,128)} reshape(f32[262144]{0:T(1024)} %collective-permute-done.4) | data formatting | bytes 2097152 | tf_op jit(solution)/shard_map/reshape | solution.py:91
  139.2 1.4 bitcast_add_fusion
  140.7 1.1 copy.289
  143.0 14.5 %collective-permute-done.5 = f32[131072]{0:T(1024)} collective-permute-done((f32[131072]{0:T(1024)}, f32[131072]{0:T(1024)}, u32[]{:S(2)}, u32[]{:S(2)}) %collective-permute-start.5) | collective-permute-done | bytes 524320 | tf_op jit(solution)/shard_map/ppermute | solution.py:90
  157.5 1.6 add.133
  159.1 19.7 %all_to_all.52 = f32[8,1,16384]{2,1,0:T(1,128)S(1)} all-to-all(f32[8,1,16384]{2,1,0:T(1,128)S(1)} %add.133), channel_id=1, replica_groups={{0,4,8,12,16,20,24,28},{1,5,9,13,17,21,25,29},{2,6,10,14,18,22,26,30},{..., dimensions={0} | all-to-all | bytes 1048576 | tf_op jit(solution)/shard_map/all_to_all | solution.py:98
  (122 shorter events, 13.6 us)
Async XLA Ops:
  0.0 96.5 %copy-start = (bf16[8192,128]{1,0:T(8,128)(2,1)S(1)}, bf16[8192,128]{1,0:T(8,128)(2,1)}, u32[]{:S(2)}) copy-start(bf16[8192,128]{1,0:T(8,128)(2,1)} %param.14) | copy-start | bytes 6291460
  0.0 16.8 %copy-start.2 = (bf16[4,256,128]{2,1,0:T(8,128)(2,1)S(1)}, bf16[4,256,128]{2,1,0:T(8,128)(2,1)}, u32[]{:S(2)}) copy-start(bf16[4,256,128]{2,1,0:T(8,128)(2,1)} %param.17) | copy-start | bytes 786436
  1.6 23.6 %all-to-all-start.1 = ((bf16[8,2,32,256]{3,2,1,0:T(8,128)(2,1)}), bf16[8,2,32,256]{3,2,1,0:T(8,128)(2,1)}, u32[]{:S(2)}, u32[]{:S(2)}) async-start(bf16[8,2,32,256]{3,2,1,0:T(8,128)(2,1)} %broadcast_in_dim.136), calls=%async_computation.1 | async-start | bytes 524288 | tf_op jit(solution)/shard_map/all_to_all | solution.py:105
  14.1 10.2 %copy-start.5 = (f32[16,1,2,1024]{3,1,0,2:T(1,128)}, f32[16,1,2,1024]{3,1,0,2:T(1,128)S(1)}, u32[]{:S(2)}) copy-start(f32[16,1,2,1024]{3,1,0,2:T(1,128)S(1)} %get-tuple-element.11) | copy-start | bytes 393220
  17.6 4.2 %copy-start.11 = (s32[1,1,8,4]{2,3,1,0:T(4,128)S(1)}, s32[1,1,8,4]{2,3,1,0:T(4,128)}, u32[]{:S(2)}) copy-start(s32[1,1,8,4]{2,3,1,0:T(4,128)} %param.23) | copy-start | bytes 388
  20.1 4.2 %copy-start.7 = (f32[16,1,2,1024]{3,1,0,2:T(1,128)S(1)}, f32[16,1,2,1024]{3,1,0,2:T(1,128)}, u32[]{:S(2)}) copy-start(f32[16,1,2,1024]{3,1,0,2:T(1,128)} %get-tuple-element.12) | copy-start | bytes 393220
  25.2 11.5 %copy-start.13 = (s32[32]{0:T(128)S(1)}, s32[32]{0:T(128)}, u32[]{:S(2)}) copy-start(s32[32]{0:T(128)} %param.24) | copy-start | bytes 388
  25.2 11.5 %copy-start.12 = (s32[1,32]{1,0:T(1,128)S(1)}, s32[1,32]{1,0:T(1,128)}, u32[]{:S(2)}) copy-start(s32[1,32]{1,0:T(1,128)} %param.22) | copy-start | bytes 388
  25.2 23.8 %all-to-all-start.2 = ((bf16[8,2,328,128]{3,2,1,0:T(8,128)(2,1)}), bf16[8,2,328,128]{3,2,1,0:T(8,128)(2,1)S(1)}, u32[]{:S(2)}, u32[]{:S(2)}) async-start(bf16[8,2,328,128]{3,2,1,0:T(8,128)(2,1)} %pad_maximum_fusion.1), calls=%async_computation.2 | async-start | bytes 2686976 | tf_op jit(solution)/shard_map/all_to_all | solution.py:166
  39.2 21.9 %collective-permute-start = (bf16[8,2,32,256]{3,2,1,0:T(8,128)(2,1)}, bf16[8,2,32,256]{3,2,1,0:T(8,128)(2,1)}, u32[]{:S(2)}, u32[]{:S(2)}) collective-permute-start(bf16[8,2,32,256]{3,2,1,0:T(8,128)(2,1)} %all-to-all-done.1), channel_id=1, source_target_pairs={{0,2},{1,3},{2,0},{3,1},{4,6},{5,7},{6,4},{7,5},{8,10},{9,11},{10,... | collective-permute-start | bytes 786440 | tf_op jit(solution)/shard_map/ppermute | solution.py:115
  49.0 6.1 %copy-start.1 = (bf16[8,2,328,128]{3,2,1,0:T(8,128)(2,1)}, bf16[8,2,328,128]{3,2,1,0:T(8,128)(2,1)S(1)}, u32[]{:S(2)}) copy-start(bf16[8,2,328,128]{3,2,1,0:T(8,128)(2,1)S(1)} %all-to-all-done.2) | copy-start | bytes 4030468
  49.0 23.3 %all-to-all-start = ((bf16[32,16,1024]{2,1,0:T(8,128)(2,1)}), bf16[32,16,1024]{2,1,0:T(8,128)(2,1)}, u32[]{:S(2)}, u32[]{:S(2)}) async-start(bf16[32,16,1024]{2,1,0:T(8,128)(2,1)} %select_multiply_fusion), calls=%async_computation | async-start | bytes 2097152 | tf_op jit(solution)/shard_map/all_to_all | solution.py:233
  56.4 2.2 %copy-start.10 = (bf16[2,32,256]{2,1,0:T(8,128)(2,1)S(1)}, bf16[2,32,256]{2,1,0:T(8,128)(2,1)}, u32[]{:S(2)}) copy-start(bf16[2,32,256]{2,1,0:T(8,128)(2,1)} %param.13) | copy-start | bytes 98308
  58.6 2.1 %copy-start.9 = (f32[16,8,2,128]{3,1,2,0:T(8,128)S(1)}, f32[16,8,2,128]{3,1,2,0:T(8,128)}, u32[]{:S(2)}) copy-start(f32[16,8,2,128]{3,1,2,0:T(8,128)} %copy.285) | copy-start | bytes 393220
  60.6 3.1 %copy-start.6 = (f32[16,1,2,1024]{3,1,0,2:T(1,128)S(1)}, f32[16,1,2,1024]{3,1,0,2:T(1,128)}, u32[]{:S(2)}) copy-start(f32[16,1,2,1024]{3,1,0,2:T(1,128)} %copy-done.5) | copy-start | bytes 393220
  60.7 3.1 %copy-start.8 = (f32[16,1,2,1024]{3,1,0,2:T(1,128)S(1)}, f32[16,1,2,1024]{3,1,0,2:T(1,128)}, u32[]{:S(2)}) copy-start(f32[16,1,2,1024]{3,1,0,2:T(1,128)} %get-tuple-element.12) | copy-start | bytes 393220
  60.7 2.9 %collective-permute-start.2 = (f32[40960]{0:T(1024)S(1)}, f32[40960]{0:T(1024)S(1)}, u32[]{:S(2)}, u32[]{:S(2)}) collective-permute-start(f32[40960]{0:T(1024)S(1)} %pad_maximum_fusion.3), channel_id=1, source_target_pairs={{0,1},{1,0},{2,3},{3,2},{4,5},{5,4},{6,7},{7,6},{8,9},{9,8},{10,11... | collective-permute-start | bytes 491528 | tf_op jit(solution)/shard_map/ppermute | solution.py:90
  63.2 28.5 %collective-permute-start.1 = (bf16[8,2,2,32,256]{4,3,2,0,1:T(8,128)(2,1)}, bf16[8,2,2,32,256]{4,3,2,0,1:T(8,128)(2,1)}, u32[]{:S(2)}, u32[]{:S(2)}) collective-permute-start(bf16[8,2,2,32,256]{4,3,2,0,1:T(8,128)(2,1)} %maximum_select_fusion.2), channel_id=1, source_target_pairs={{0,1},{1,0},{2,3},{3,2},{4,5},{5,4},{6,7},{7,6},{8,9},{9,8},{10,11... | collective-permute-start | bytes 1572872 | tf_op jit(solution)/shard_map/ppermute | solution.py:115
  64.0 14.9 %copy-start.3 = (bf16[32,16,1024]{2,1,0:T(8,128)(2,1)S(1)}, bf16[32,16,1024]{2,1,0:T(8,128)(2,1)}, u32[]{:S(2)}) copy-start(bf16[32,16,1024]{2,1,0:T(8,128)(2,1)} %param.20) | copy-start | bytes 3145732
  64.0 7.1 %collective-permute-start.3 = (f32[24576]{0:T(1024)S(1)}, f32[24576]{0:T(1024)S(1)}, u32[]{:S(2)}, u32[]{:S(2)}) collective-permute-start(f32[24576]{0:T(1024)S(1)} %pad_maximum_fusion.4), channel_id=1, source_target_pairs={{0,2},{1,3},{2,0},{3,1},{4,6},{5,7},{6,4},{7,5},{8,10},{9,11},{10,... | collective-permute-start | bytes 294920 | tf_op jit(solution)/shard_map/ppermute | solution.py:90
  72.3 21.1 %all-to-all-start.3 = ((f32[8,1,10240]{2,1,0:T(1,128)}), f32[8,1,10240]{2,1,0:T(1,128)}, u32[]{:S(2)}, u32[]{:S(2)}) async-start(f32[8,1,10240]{2,1,0:T(1,128)} %all_to_all.38), calls=%async_computation.3 | async-start | bytes 655360 | tf_op jit(solution)/shard_map/all_to_all | solution.py:98
  87.5 4.2 %copy-start.4 = (bf16[8,2,1,2,32,256]{5,4,3,0,2,1:T(8,128)(2,1)S(1)}, bf16[8,2,1,2,32,256]{5,4,3,0,2,1:T(8,128)(2,1)}, u32[]{:S(2)}) copy-start(bf16[8,2,1,2,32,256]{5,4,3,0,2,1:T(8,128)(2,1)} %maximum_select_fusion.1) | copy-start | bytes 1572868
  97.7 19.2 %all-to-all-start.4 = ((f32[2,32,1,144]{3,0,2,1:T(2,128)}), f32[2,32,1,144]{3,0,2,1:T(2,128)S(1)}, u32[]{:S(2)}, u32[]{:S(2)}) async-start(f32[2,32,1,144]{3,0,2,1:T(2,128)} %copy.252), calls=%async_computation.4 | async-start | bytes 131072 | tf_op jit(solution)/shard_map/all_to_all | solution.py:215
  133.8 2.9 %collective-permute-start.4 = (f32[262144]{0:T(1024)S(1)}, f32[262144]{0:T(1024)}, u32[]{:S(2)}, u32[]{:S(2)}) collective-permute-start(f32[262144]{0:T(1024)S(1)} %bitcast.208), channel_id=1, source_target_pairs={{0,1},{1,0},{2,3},{3,2},{4,5},{5,4},{6,7},{7,6},{8,9},{9,8},{10,11... | collective-permute-start | bytes 3145736 | tf_op jit(solution)/shard_map/ppermute | solution.py:90
  141.7 15.8 %collective-permute-start.5 = (f32[131072]{0:T(1024)}, f32[131072]{0:T(1024)}, u32[]{:S(2)}, u32[]{:S(2)}) collective-permute-start(f32[131072]{0:T(1024)} %bitcast.102), channel_id=1, source_target_pairs={{0,2},{1,3},{2,0},{3,1},{4,6},{5,7},{6,4},{7,5},{8,10},{9,11},{10,... | collective-permute-start | bytes 1572872 | tf_op jit(solution)/shard_map/ppermute | solution.py:90

commit v7 on v6

--- a/solution.py
+++ b/solution.py
@@ -155,6 +155,17 @@
     lane = adapter_down_weight.shape[2]
     down_len = adapter_down_weight.shape[1]
     upq_len = adapter_up_query.shape[1]
+    pool_pages, page_len, page_width = key_value_pool.shape
+    pool_tiles = jnp.transpose(
+        key_value_pool.reshape(pool_pages, page_len, page_width // lane, lane), (0, 2, 1, 3)
+    )
+    move_row = page_send_list[0, 0]
+    move_cap = move_row.shape[1]
+    present_pages = (move_row >= 0).reshape(-1)
+    outgoing = (
+        jnp.take(pool_tiles, jnp.maximum(move_row, 0).reshape(-1), axis=0)
+        * present_pages.astype(key_value_pool.dtype)[:, None, None, None]
+    )
     panel_send = jnp.concatenate(
         [
             down_send,
@@ -162,9 +173,18 @@
             upv_send.reshape(n_group, cap_slots, -1, lane),
         ],
         2,
-    )
-    panel_recv = lax.all_to_all(panel_send, "group", 0, 0, tiled=True).reshape(
-        (n_group * cap_slots,) + panel_send.shape[2:]
+    ).reshape(n_group, -1, lane)
+    panel_rows = panel_send.shape[1]
+    group_recv = lax.all_to_all(
+        jnp.concatenate([panel_send, outgoing.reshape(n_group, -1, lane)], 1),
+        "group",
+        0,
+        0,
+        tiled=True,
+    )
+    arrived_tiles = group_recv[:, panel_rows:].reshape((-1,) + pool_tiles.shape[1:])
+    panel_recv = group_recv[:, :panel_rows].reshape(
+        (n_group * cap_slots, -1, lane)
     )
     down_recv = panel_recv[:, :down_len]
     upq_recv = panel_recv[:, down_len : down_len + upq_len]
@@ -224,15 +244,9 @@
         ],
         -1,
     ).astype(jnp.bfloat16)
-    move_row = page_send_list[0, 0]
-    present_pages = (move_row >= 0).reshape(-1)
-    outgoing = (
-        jnp.take(key_value_pool, jnp.maximum(move_row, 0).reshape(-1), axis=0)
-        * present_pages.astype(key_value_pool.dtype)[:, None, None]
-    )
-    arrived_pages = lax.all_to_all(outgoing, "group", split_axis=0, concat_axis=0, tiled=True)
-    combined = jnp.concatenate([key_value_pool, arrived_pages], 0)
-    ctx_pages = jnp.take(combined, request_page_table.reshape(-1), axis=0).reshape(
+    combined = jnp.concatenate([pool_tiles, arrived_tiles], 0)
+    ctx_tiles = jnp.take(combined, request_page_table.reshape(-1), axis=0)
+    ctx_pages = jnp.transpose(ctx_tiles, (0, 2, 1, 3)).reshape(
         batch_own, -1, 2 * key_span_width
     )
     attended = attend(query_own, ctx_pages, keyval_new, lengths)

time: 181 us -> 202 us (1.12)
  waiting for transfers between devices: 35 us -> 52.7 us
  local copies, waits for them, and re-layouts: 32.7 us -> 42.6 us
  starting transfers between devices: 43.5 us -> 38.6 us
  other arithmetic: 26.7 us -> 23.6 us
    all_to_all x2 -> x1, waiting for transfers between devices: 6.96 us -> 27 us  [per_device(): lax.all_to_all(jnp.concatenate([panel_send, outgoing.reshape(n_group, -1,...]
    all_to_all x2 -> x1, starting transfers between devices: 12 us -> 5.98 us  [per_device(): lax.all_to_all(jnp.concatenate([panel_send, outgoing.reshape(n_group, -1,...]
    slice x0 -> x3, local copies, waits for them, and re-layouts: none -> 3.01 us  [the longest x1 1.42 us: per_device(): group_recv[:, :panel_rows].reshape((n_group * cap_slots, -1, lane))]
    reshape x0 -> x2, local copies, waits for them, and re-layouts: none -> 2.57 us  [the longest x1 2.3 us: per_device(): jnp.transpose(ctx_tiles, (0, 2, 1, 3))]
    all_to_all x1, waiting for transfers between devices: 8.69 us -> 6.21 us  [per_device(): lax.all_to_all(query_send, 'tp', split_axis=1, concat_axis=2, tiled=True)]
    concatenate x1, other arithmetic: 2.43 us -> 0.1 us  [per_device(): jnp.concatenate([down_send, upq_send, upv_send.reshape(n_group, cap_slots...]
    slice x1 -> x2, local copies, waits for them, and re-layouts: 1.27 us -> 3.35 us  [attend(): ctx_pages[..., :key_span_width]]
    unnamed x33 -> x32, local copies, waits for them, and re-layouts: 3.28 us -> 4.31 us
  transfers between devices with their start and end apart: 11 -> 10, of which waited for: 5 -> 5; matrix products, arithmetic and copies ran while one was open for 27% -> 27% of each run, Pallas kernels for 0% -> 0%
where the time goes in v7:
time: 202 us; the launch traced here: 200 us
  waiting for transfers between devices  52.7 us (26%)
  local copies, waits for them, and re-layouts  42.6 us (21%)
  starting transfers between devices  38.6 us (19%)
  blocking collectives  32.6 us (16%)
  other arithmetic  23.6 us (12%)
  matrix products  8.23 us (4%)
    all_to_all x1, waiting for transfers between devices, per_device(): lax.all_to_all(jnp.concatenate([panel_send, outgoing.reshape(n_group, -1,...  27 us
    all_to_all x1, blocking collectives, reduce_scatter_tp(): lax.all_to_all(send, 'tp', 0, 0, tiled=True, axis_index_groups=stage_grou...  19.7 us
    ppermute x4, waiting for transfers between devices, reduce_scatter_tp(): got = lax.ppermute(sent, 'tp', [(t, t ^ bit) for t in range(n_tp)])  19.4 us
    all_to_all x1, blocking collectives, per_device(): lax.all_to_all(attended, 'tp', split_axis=2, concat_axis=1, tiled=True)  12.9 us
    all_to_all x1, starting transfers between devices, per_device(): lax.all_to_all(query_send, 'tp', split_axis=1, concat_axis=2, tiled=True)  10.1 us
    all_to_all x1, starting transfers between devices, all_gather_tp(): lax.all_to_all(jnp.broadcast_to(block[None], (rest,) + block.shape), 'tp'...  8.47 us
    all_to_all x1, starting transfers between devices, reduce_scatter_tp(): lax.all_to_all(send, 'tp', 0, 0, tiled=True, axis_index_groups=stage_grou...  6.79 us
    all_to_all x1, waiting for transfers between devices, per_device(): lax.all_to_all(query_send, 'tp', split_axis=1, concat_axis=2, tiled=True)  6.21 us
  transfers between devices with their start and end apart: 10, of which 5 were waited for; matrix products, arithmetic and copies ran while one was open for 27% of the time, Pallas kernels for 0%

profile of v7, /device:TPU:2, one launch (start us, length us, event | category | flops | bytes accessed | tf_op | source)
XLA Modules:
  0.0 199.7 jit_solution(14341516889304186253)
XLA Ops:
  0.0 1.6 broadcast_in_dim.142
  1.6 8.5 %all-to-all-start.1 = ((bf16[8,2,32,256]{3,2,1,0:T(8,128)(2,1)}), bf16[8,2,32,256]{3,2,1,0:T(8,128)(2,1)}, u32[]{:S(2)}, u32[]{:S(2)}) async-start(bf16[8,2,32,256]{3,2,1,0:T(8,128)(2,1)} %broadcast_in_dim.142), calls=%async_computation.1 | async-start | bytes 524288 | tf_op jit(solution)/shard_map/all_to_all | solution.py:105
  11.5 1.0 fusion.54
  13.2 1.5 copy.299
  15.0 1.7 gather_fusion.3
  16.7 2.5 %copy.244 = bf16[32,8,16,128]{3,2,1,0:T(8,128)(2,1)} copy(bf16[32,8,16,128]{3,1,2,0:T(8,128)(2,1)} %gather_fusion.3) | data formatting | bytes 2097152 | tf_op jit(solution)/shard_map/jit(_take)/gather | solution.py:166
  23.6 1.7 gather_fusion
  25.3 1.4 broadcast_select_fusion
  26.7 1.4 select_multiply_fusion
  28.2 1.6 pad_maximum_fusion
  29.8 6.0 %all-to-all-start = ((bf16[8,1168,128]{2,1,0:T(8,128)(2,1)}), bf16[8,1168,128]{2,1,0:T(8,128)(2,1)}, u32[]{:S(2)}, u32[]{:S(2)}) async-start(bf16[8,1168,128]{2,1,0:T(8,128)(2,1)} %pad_maximum_fusion), calls=%async_computation | async-start | bytes 4784128 | tf_op jit(solution)/shard_map/all_to_all | solution.py:178
  37.9 2.9 %collective-permute-start = (bf16[8,2,32,256]{3,2,1,0:T(8,128)(2,1)}, bf16[8,2,32,256]{3,2,1,0:T(8,128)(2,1)}, u32[]{:S(2)}, u32[]{:S(2)}) collective-permute-start(bf16[8,2,32,256]{3,2,1,0:T(8,128)(2,1)} %all-to-all-done.1), channel_id=1, source_target_pairs={{0,2},{1,3},{2,0},{3,1},{4,6},{5,7},{6,4},{7,5},{8,10},{9,11},{10,... | collective-permute-start | bytes 786440 | tf_op jit(solution)/shard_map/ppermute | solution.py:115
  40.8 27.0 %all-to-all-done = bf16[8,1168,128]{2,1,0:T(8,128)(2,1)} async-done(((bf16[8,1168,128]{2,1,0:T(8,128)(2,1)}), bf16[8,1168,128]{2,1,0:T(8,128)(2,1)}, u32[]{:S(2)}, u32[]{:S(2)}) %all-to-all-start) | async-done | bytes 2392096 | tf_op jit(solution)/shard_map/all_to_all | solution.py:178
  67.8 1.4 slice.197
  69.3 1.1 copy-done.3
  70.5 2.1 %gather_fusion.6 = bf16[32,256,128]{2,1,0:T(8,128)(2,1)} fusion(bf16[16,256,128]{2,1,0:T(8,128)(2,1)S(1)} %slice.201, s32[1024]{0:T(1024)S(1)} %pad_clamp_fusion), kind=kCustom, calls=%fused_computation.6 | custom fusion | bytes 4194432 | tf_op jit(solution)/shard_map/jit(_take)/gather | solution.py:194
  72.6 2.1 %fusion.5 = f32[32,128,2]{1,2,0:T(2,128)S(1)} fusion(bf16[32,256,128]{2,1,0:T(8,128)(2,1)} %gather_fusion.6, pred[32]{0:T(512)(128)(4,1)} %get-tuple-element.21, bf16[2,32,256]{2,1,0:T(8,128)(2,1)} %param.13), kind=kOutput, calls=%fused_computation.15 | convolution fusion | flops 5242880 | bytes 2162720 | tf_op jit(solution)/shard_map/srd,rdk->srk/dot_general | solution.py:203
  74.9 2.1 %maximum_select_fusion.2 = bf16[8,2,2,32,256]{4,3,2,0,1:T(8,128)(2,1)} fusion(bf16[8,1,2,32,256]{4,3,2,0,1:T(8,128)(2,1)} %bitcast.17, bf16[8,1,2,32,256]{4,3,2,0,1:T(8,128)(2,1)} %bitcast.16, pred[]{:T(512)S(6)} %eq.11), kind=kLoop, calls=%fused_computation.43 | loop fusion | flops 786432 | bytes 1048577 | tf_op jit(solution)/shard_map/jit(_where)/select_n | solution.py:116
  77.8 3.0 %collective-permute-start.3 = (f32[24576]{0:T(1024)S(1)}, f32[24576]{0:T(1024)S(1)}, u32[]{:S(2)}, u32[]{:S(2)}) collective-permute-start(f32[24576]{0:T(1024)S(1)} %pad_maximum_fusion.5), channel_id=1, source_target_pairs={{0,2},{1,3},{2,0},{3,1},{4,6},{5,7},{6,4},{7,5},{8,10},{9,11},{10,... | collective-permute-start | bytes 294920 | tf_op jit(solution)/shard_map/ppermute | solution.py:90
  80.8 1.3 maximum_select_fusion.1
  82.1 2.1 %collective-permute-done.3 = f32[24576]{0:T(1024)S(1)} collective-permute-done((f32[24576]{0:T(1024)S(1)}, f32[24576]{0:T(1024)S(1)}, u32[]{:S(2)}, u32[]{:S(2)}) %collective-permute-start.3) | collective-permute-done | bytes 98336 | tf_op jit(solution)/shard_map/ppermute | solution.py:90
  85.3 6.8 %all-to-all-start.2 = ((f32[8,1,10240]{2,1,0:T(1,128)}), f32[8,1,10240]{2,1,0:T(1,128)}, u32[]{:S(2)}, u32[]{:S(2)}) async-start(f32[8,1,10240]{2,1,0:T(1,128)} %all_to_all.34), calls=%async_computation.2 | async-start | bytes 655360 | tf_op jit(solution)/shard_map/all_to_all | solution.py:98
  92.1 1.5 maximum_select_fusion
  94.6 1.0 slice.198
  95.6 1.4 slice.195
  97.3 1.5 pad_maximum_fusion.1
  98.8 3.2 %gather_fusion.4 = bf16[32,8,16,128]{3,1,2,0:T(8,128)(2,1)} fusion(bf16[64,8,16,128]{3,1,2,0:T(8,128)(2,1)} %pad_maximum_fusion.1, s32[1024]{0:T(1024)S(1)} %pad_clamp_fusion.1), kind=kCustom, calls=%fused_computation.4 | custom fusion | bytes 2097280 | tf_op jit(solution)/shard_map/jit(_take)/gather | solution.py:248
  102.1 2.4 %select_bitcast_fusion = bf16[32,16,8,128]{3,2,1,0:T(8,128)(2,1)} fusion(bf16[32,8,16,128]{3,1,2,0:T(8,128)(2,1)} %gather_fusion.4, pred[32]{0:T(512)(128)(4,1)S(1)} %get-tuple-element.22), kind=kLoop, calls=%fused_computation.37 | loop fusion | flops 524288 | bytes 2097184 | tf_op jit(solution)/shard_map/jit(_take)/select_n | solution.py:248
  104.4 2.3 %reshape.490 = bf16[1,512,1024]{2,1,0:T(8,128)(2,1)} reshape(bf16[32,16,8,128]{3,2,1,0:T(8,128)(2,1)} %select_bitcast_fusion) | data formatting | bytes 2097152 | tf_op jit(solution)/shard_map/reshape | solution.py:249
  107.6 1.1 copy.261
  108.7 1.2 gather_fusion.7
  109.9 1.4 gather_fusion.5
  111.4 1.2 reduce_sum.36
  112.7 1.1 fusion.32
  114.0 1.4 fusion.28
  116.6 10.1 %all-to-all-start.3 = ((f32[2,32,1,144]{3,0,2,1:T(2,128)}), f32[2,32,1,144]{3,0,2,1:T(2,128)S(1)}, u32[]{:S(2)}, u32[]{:S(2)}) async-start(f32[2,32,1,144]{3,0,2,1:T(2,128)} %copy.265), calls=%async_computation.3 | async-start | bytes 131072 | tf_op jit(solution)/shard_map/all_to_all | solution.py:235
  126.7 2.1 %fusion.64 = (bf16[1,512,512]{2,1,0:T(8,128)(2,1)}, bf16[1,512,512]{2,1,0:T(8,128)(2,1)S(1)}) fusion(bf16[1,512,1024]{2,1,0:T(8,128)(2,1)} %reshape.490), kind=kLoop, calls=%fused_computation.122 | loop fusion | bytes 2097152 | tf_op jit(solution)/shard_map/slice | solution.py:24
  129.0 1.3 copy.247
  130.3 6.2 %all-to-all-done.3 = f32[2,32,1,144]{3,0,2,1:T(2,128)S(1)} async-done(((f32[2,32,1,144]{3,0,2,1:T(2,128)}), f32[2,32,1,144]{3,0,2,1:T(2,128)S(1)}, u32[]{:S(2)}, u32[]{:S(2)}) %all-to-all-start.3) | async-done | bytes 36896 | tf_op jit(solution)/shard_map/all_to_all | solution.py:235
  138.0 12.9 %all_to_all.46 = bf16[2,1,32,128]{3,0,1,2:T(2,128)(2,1)S(1)} all-to-all(bf16[2,1,32,128]{3,0,1,2:T(2,128)(2,1)S(1)} %copy.277), channel_id=1, replica_groups=mesh['group'=8,'tp'=32] {'tp'}, dimensions={2} | all-to-all | bytes 32768 | tf_op jit(solution)/shard_map/all_to_all | solution.py:253
  150.9 2.0 %fusion = f32[64,32,256]{2,0,1:T(8,128)S(1)} fusion(bf16[64,128,1]{1,0,2:T(8,128)(2,1)S(1)} %bitcast.240, bf16[16,32,8,256]{3,2,1,0:T(8,128)(2,1)} %bitcast.220), kind=kOutput, calls=%fused_computation.9 | convolution fusion | flops 134217728 | bytes 4210688 | tf_op jit(solution)/shard_map/rk,kdc->drc/dot_general | solution.py:255
  153.7 2.8 %collective-permute-done.4 = f32[262144]{0:T(1024)} collective-permute-done((f32[262144]{0:T(1024)S(1)}, f32[262144]{0:T(1024)}, u32[]{:S(2)}, u32[]{:S(2)}) %collective-permute-start.4) | collective-permute-done | bytes 1048608 | tf_op jit(solution)/shard_map/ppermute | solution.py:90
  156.5 2.5 %reshape.512 = f32[8,2,64,256]{3,2,1,0:T(8,128)} reshape(f32[262144]{0:T(1024)} %collective-permute-done.4) | data formatting | bytes 2097152 | tf_op jit(solution)/shard_map/reshape | solution.py:91
  159.0 1.4 bitcast_add_fusion
  160.5 1.1 copy.304
  162.8 14.5 %collective-permute-done.5 = f32[131072]{0:T(1024)} collective-permute-done((f32[131072]{0:T(1024)}, f32[131072]{0:T(1024)}, u32[]{:S(2)}, u32[]{:S(2)}) %collective-permute-start.5) | collective-permute-done | bytes 524320 | tf_op jit(solution)/shard_map/ppermute | solution.py:90
  177.3 1.6 add.133
  178.9 19.7 %all_to_all.47 = f32[8,1,16384]{2,1,0:T(1,128)S(1)} all-to-all(f32[8,1,16384]{2,1,0:T(1,128)S(1)} %add.133), channel_id=1, replica_groups={{0,4,8,12,16,20,24,28},{1,5,9,13,17,21,25,29},{2,6,10,14,18,22,26,30},{..., dimensions={0} | all-to-all | bytes 1048576 | tf_op jit(solution)/shard_map/all_to_all | solution.py:98
  (129 shorter events, 18.8 us)
Async XLA Ops:
  0.0 115.4 %copy-start = (bf16[8192,128]{1,0:T(8,128)(2,1)S(1)}, bf16[8192,128]{1,0:T(8,128)(2,1)}, u32[]{:S(2)}) copy-start(bf16[8192,128]{1,0:T(8,128)(2,1)} %param.14) | copy-start | bytes 6291460
  1.6 28.2 %all-to-all-start.1 = ((bf16[8,2,32,256]{3,2,1,0:T(8,128)(2,1)}), bf16[8,2,32,256]{3,2,1,0:T(8,128)(2,1)}, u32[]{:S(2)}, u32[]{:S(2)}) async-start(bf16[8,2,32,256]{3,2,1,0:T(8,128)(2,1)} %broadcast_in_dim.142), calls=%async_computation.1 | async-start | bytes 524288 | tf_op jit(solution)/shard_map/all_to_all | solution.py:105
  14.9 4.4 %copy-start.1 = (bf16[32,8,16,128]{3,1,2,0:T(8,128)(2,1)}, bf16[32,8,16,128]{3,1,2,0:T(8,128)(2,1)S(1)}, u32[]{:S(2)}) copy-start(bf16[32,8,16,128]{3,1,2,0:T(8,128)(2,1)S(1)} %bitcast_bitcast_fusion) | copy-start | bytes 3145732
  16.7 5.4 %copy-start.6 = (bf16[4,64,128]{2,1,0:T(8,128)(2,1)S(1)}, bf16[4,64,128]{2,1,0:T(8,128)(2,1)}, u32[]{:S(2)}) copy-start(bf16[4,64,128]{2,1,0:T(8,128)(2,1)} %param.18) | copy-start | bytes 196612
  16.7 6.9 %copy-start.5 = (bf16[4,256,128]{2,1,0:T(8,128)(2,1)S(1)}, bf16[4,256,128]{2,1,0:T(8,128)(2,1)}, u32[]{:S(2)}) copy-start(bf16[4,256,128]{2,1,0:T(8,128)(2,1)} %param.17) | copy-start | bytes 786436
  23.6 3.1 %copy-start.4 = (bf16[32,8,16,128]{3,2,1,0:T(8,128)(2,1)S(1)}, bf16[32,8,16,128]{3,2,1,0:T(8,128)(2,1)}, u32[]{:S(2)}) copy-start(bf16[32,8,16,128]{3,2,1,0:T(8,128)(2,1)} %copy.244) | copy-start | bytes 3145732
  25.3 2.8 %copy-start.7 = (bf16[8,2,64,128]{3,2,1,0:T(8,128)(2,1)S(1)}, bf16[8,2,64,128]{3,2,1,0:T(8,128)(2,1)}, u32[]{:S(2)}) copy-start(bf16[8,2,64,128]{3,2,1,0:T(8,128)(2,1)} %broadcast_select_fusion.1) | copy-start | bytes 786436
  29.8 6.7 %copy-start.8 = (bf16[256,1024]{1,0:T(8,128)(2,1)S(1)}, bf16[256,1024]{1,0:T(8,128)(2,1)}, u32[]{:S(2)}) copy-start(bf16[256,1024]{1,0:T(8,128)(2,1)} %param.15) | copy-start | bytes 1572868
  29.8 6.7 %copy-start.9 = (bf16[2,32,256]{2,1,0:T(8,128)(2,1)S(1)}, bf16[2,32,256]{2,1,0:T(8,128)(2,1)}, u32[]{:S(2)}) copy-start(bf16[2,32,256]{2,1,0:T(8,128)(2,1)} %param.13) | copy-start | bytes 98308
  29.8 38.0 %all-to-all-start = ((bf16[8,1168,128]{2,1,0:T(8,128)(2,1)}), bf16[8,1168,128]{2,1,0:T(8,128)(2,1)}, u32[]{:S(2)}, u32[]{:S(2)}) async-start(bf16[8,1168,128]{2,1,0:T(8,128)(2,1)} %pad_maximum_fusion), calls=%async_computation | async-start | bytes 4784128 | tf_op jit(solution)/shard_map/all_to_all | solution.py:178
  35.8 1.5 copy-start.10
  35.8 1.5 copy-start.11
  37.9 37.0 %collective-permute-start = (bf16[8,2,32,256]{3,2,1,0:T(8,128)(2,1)}, bf16[8,2,32,256]{3,2,1,0:T(8,128)(2,1)}, u32[]{:S(2)}, u32[]{:S(2)}) collective-permute-start(bf16[8,2,32,256]{3,2,1,0:T(8,128)(2,1)} %all-to-all-done.1), channel_id=1, source_target_pairs={{0,2},{1,3},{2,0},{3,1},{4,6},{5,7},{6,4},{7,5},{8,10},{9,11},{10,... | collective-permute-start | bytes 786440 | tf_op jit(solution)/shard_map/ppermute | solution.py:115
  69.3 1.1 copy-start.3
  74.7 2.7 %collective-permute-start.2 = (f32[40960]{0:T(1024)S(1)}, f32[40960]{0:T(1024)S(1)}, u32[]{:S(2)}, u32[]{:S(2)}) collective-permute-start(f32[40960]{0:T(1024)S(1)} %pad_maximum_fusion.4), channel_id=1, source_target_pairs={{0,1},{1,0},{2,3},{3,2},{4,5},{5,4},{6,7},{7,6},{8,9},{9,8},{10,11... | collective-permute-start | bytes 491528 | tf_op jit(solution)/shard_map/ppermute | solution.py:90
  77.0 15.2 %collective-permute-start.1 = (bf16[8,2,2,32,256]{4,3,2,0,1:T(8,128)(2,1)}, bf16[8,2,2,32,256]{4,3,2,0,1:T(8,128)(2,1)}, u32[]{:S(2)}, u32[]{:S(2)}) collective-permute-start(bf16[8,2,2,32,256]{4,3,2,0,1:T(8,128)(2,1)} %maximum_select_fusion.2), channel_id=1, source_target_pairs={{0,1},{1,0},{2,3},{3,2},{4,5},{5,4},{6,7},{7,6},{8,9},{9,8},{10,11... | collective-permute-start | bytes 1572872 | tf_op jit(solution)/shard_map/ppermute | solution.py:115
  77.8 6.4 %collective-permute-start.3 = (f32[24576]{0:T(1024)S(1)}, f32[24576]{0:T(1024)S(1)}, u32[]{:S(2)}, u32[]{:S(2)}) collective-permute-start(f32[24576]{0:T(1024)S(1)} %pad_maximum_fusion.5), channel_id=1, source_target_pairs={{0,2},{1,3},{2,0},{3,1},{4,6},{5,7},{6,4},{7,5},{8,10},{9,11},{10,... | collective-permute-start | bytes 294920 | tf_op jit(solution)/shard_map/ppermute | solution.py:90
  85.3 26.0 %all-to-all-start.2 = ((f32[8,1,10240]{2,1,0:T(1,128)}), f32[8,1,10240]{2,1,0:T(1,128)}, u32[]{:S(2)}, u32[]{:S(2)}) async-start(f32[8,1,10240]{2,1,0:T(1,128)} %all_to_all.34), calls=%async_computation.2 | async-start | bytes 655360 | tf_op jit(solution)/shard_map/all_to_all | solution.py:98
  95.6 1.7 copy-start.2
  106.7 6.0 %copy-start.12 = (pred[32]{0:T(512)(128)(4,1)S(1)}, pred[32]{0:T(512)(128)(4,1)}, u32[]{:S(2)}) copy-start(pred[32]{0:T(512)(128)(4,1)} %get-tuple-element.21) | copy-start | bytes 100
  116.6 19.9 %all-to-all-start.3 = ((f32[2,32,1,144]{3,0,2,1:T(2,128)}), f32[2,32,1,144]{3,0,2,1:T(2,128)S(1)}, u32[]{:S(2)}, u32[]{:S(2)}) async-start(f32[2,32,1,144]{3,0,2,1:T(2,128)} %copy.265), calls=%async_computation.3 | async-start | bytes 131072 | tf_op jit(solution)/shard_map/all_to_all | solution.py:235
  153.6 2.9 %collective-permute-start.4 = (f32[262144]{0:T(1024)S(1)}, f32[262144]{0:T(1024)}, u32[]{:S(2)}, u32[]{:S(2)}) collective-permute-start(f32[262144]{0:T(1024)S(1)} %bitcast.226), channel_id=1, source_target_pairs={{0,1},{1,0},{2,3},{3,2},{4,5},{5,4},{6,7},{7,6},{8,9},{9,8},{10,11... | collective-permute-start | bytes 3145736 | tf_op jit(solution)/shard_map/ppermute | solution.py:90
  161.6 15.8 %collective-permute-start.5 = (f32[131072]{0:T(1024)}, f32[131072]{0:T(1024)}, u32[]{:S(2)}, u32[]{:S(2)}) collective-permute-start(f32[131072]{0:T(1024)} %bitcast.111), channel_id=1, source_target_pairs={{0,2},{1,3},{2,0},{3,1},{4,6},{5,7},{6,4},{7,5},{8,10},{9,11},{10,... | collective-permute-start | bytes 1572872 | tf_op jit(solution)/shard_map/ppermute | solution.py:90

commit v8 on v6

--- a/solution.py
+++ b/solution.py
@@ -75,13 +75,13 @@
 SWAP_BITS = (1, 2)
 
 
-def stage_groups(n_tp):
-    span = 1 << len(SWAP_BITS)
+def stage_groups(n_tp, bits):
+    span = 1 << len(bits)
     return [[t for t in range(n_tp) if t % span == p] for p in range(span)]
 
 
-def reduce_scatter_tp(parts, shared, column_id, n_tp):
-    for bit in SWAP_BITS:
+def reduce_scatter_tp(parts, shared, column_id, n_tp, bits=SWAP_BITS):
+    for bit in bits:
         mine = (column_id // bit) % 2
         split = parts.reshape((-1, 2) + parts.shape[1:])
         keep = jnp.where(mine == 0, split[:, 0], split[:, 1])
@@ -95,7 +95,8 @@
         [flat, jnp.broadcast_to(shared.reshape(1, -1), (flat.shape[0], shared.size))], -1
     )
     total = jnp.sum(
-        lax.all_to_all(send, "tp", 0, 0, tiled=True, axis_index_groups=stage_groups(n_tp)), 0
+        lax.all_to_all(send, "tp", 0, 0, tiled=True, axis_index_groups=stage_groups(n_tp, bits)),
+        0,
     )
     return total[: flat.shape[1]], total[flat.shape[1] :].reshape(shared.shape)
 
@@ -108,7 +109,7 @@
         0,
         0,
         tiled=True,
-        axis_index_groups=stage_groups(n_tp),
+        axis_index_groups=stage_groups(n_tp, SWAP_BITS),
     )
     for done, bit in enumerate(reversed(SWAP_BITS)):
         mine = (column_id // bit) % 2
@@ -245,7 +246,7 @@
         preferred_element_type=jnp.float32,
     )
     summed, _ = reduce_scatter_tp(
-        projected, jnp.zeros((0,), jnp.float32), column_id, n_tp
+        projected, jnp.zeros((0,), jnp.float32), column_id, n_tp, SWAP_BITS[:1]
     )
     return summed.reshape(step_count, batch_rows, out_cols).astype(jnp.bfloat16)
 

time: 181 us -> 177 us (0.978)
  waiting for transfers between devices: 35 us -> 18.6 us
  blocking collectives: 32.3 us -> 46.6 us
    ppermute x4 -> x3, waiting for transfers between devices: 19.3 us -> 2.96 us  [reduce_scatter_tp(): got = lax.ppermute(sent, 'tp', [(t, t ^ bit) for t in range(n_tp)])]
    all_to_all x1, blocking collectives: 19.7 us -> 33.9 us  [reduce_scatter_tp(): lax.all_to_all(send, 'tp', 0, 0, tiled=True, axis_index_groups=stage_grou...]
    reshape x1 -> x0, local copies, waits for them, and re-layouts: 2.51 us -> none  [reduce_scatter_tp(): parts = keep + got[:give.size].reshape(give.shape)]
    ppermute x4 -> x3, starting transfers between devices: 3.87 us -> 3.08 us  [reduce_scatter_tp(): got = lax.ppermute(sent, 'tp', [(t, t ^ bit) for t in range(n_tp)])]
  transfers between devices with their start and end apart: 11 -> 10, of which waited for: 5 -> 4; matrix products, arithmetic and copies ran while one was open for 27% -> 29% of each run, Pallas kernels for 0% -> 0%
where the time goes in v8:
time: 177 us; the launch traced here: 176 us
  blocking collectives  46.6 us (26%)
  starting transfers between devices  42.7 us (24%)
  local copies, waits for them, and re-layouts  31.6 us (18%)
  other arithmetic  26.6 us (15%)
  waiting for transfers between devices  18.6 us (11%)
  matrix products  8.38 us (5%)
    all_to_all x1, blocking collectives, reduce_scatter_tp(): lax.all_to_all(send, 'tp', 0, 0, tiled=True, axis_index_groups=stage_grou...  33.9 us
    all_to_all x1, blocking collectives, per_device(): lax.all_to_all(attended, 'tp', split_axis=2, concat_axis=1, tiled=True)  12.7 us
    all_to_all x1, starting transfers between devices, per_device(): lax.all_to_all(query_send, 'tp', split_axis=1, concat_axis=2, tiled=True)  9.17 us
    all_to_all x1, waiting for transfers between devices, per_device(): lax.all_to_all(query_send, 'tp', split_axis=1, concat_axis=2, tiled=True)  8.69 us
    all_to_all x1, starting transfers between devices, all_gather_tp(): lax.all_to_all(jnp.broadcast_to(block[None], (rest,) + block.shape), 'tp'...  8.47 us
    all_to_all x1, waiting for transfers between devices, per_device(): lax.all_to_all(panel_send, 'group', 0, 0, tiled=True)  6.95 us
    all_to_all x1, starting transfers between devices, reduce_scatter_tp(): lax.all_to_all(send, 'tp', 0, 0, tiled=True, axis_index_groups=stage_grou...  6.58 us
    all_to_all x1, starting transfers between devices, per_device(): lax.all_to_all(outgoing, 'group', split_axis=0, concat_axis=0, tiled=True)  6.07 us
  transfers between devices with their start and end apart: 10, of which 4 were waited for; matrix products, arithmetic and copies ran while one was open for 29% of the time, Pallas kernels for 0%

profile of v8, /device:TPU:2, one launch (start us, length us, event | category | flops | bytes accessed | tf_op | source)
XLA Modules:
  0.0 175.8 jit_solution(8527562267882693829)
XLA Ops:
  0.0 1.6 broadcast_in_dim.136
  1.7 8.5 %all-to-all-start.1 = ((bf16[8,2,32,256]{3,2,1,0:T(8,128)(2,1)}), bf16[8,2,32,256]{3,2,1,0:T(8,128)(2,1)}, u32[]{:S(2)}, u32[]{:S(2)}) async-start(bf16[8,2,32,256]{3,2,1,0:T(8,128)(2,1)} %broadcast_in_dim.136), calls=%async_computation.1 | async-start | bytes 524288 | tf_op jit(solution)/shard_map/all_to_all | solution.py:106
  10.1 1.0 fusion.54
  11.9 1.3 convolution_bitcast_fusion
  13.3 0.9 fusion.65
  14.3 0.9 constant_dynamic-slice_fusion
  15.8 0.8 gather.42
  17.6 1.5 broadcast_select_fusion.3
  19.1 1.1 broadcast_select_fusion
  20.2 1.5 gather_fusion.3
  22.0 2.4 %pad_maximum_fusion.1 = bf16[8,2,328,128]{3,2,1,0:T(8,128)(2,1)} fusion(bf16[8,2,8,128]{3,2,1,0:T(8,128)(2,1)} %broadcast_select_fusion.3, bf16[8,2,64,128]{3,2,1,0:T(8,128)(2,1)S(1)} %broadcast_select_fusion.2, bf16[8,2,256,128]{3,2,1,0:T(8,128)(2,1)} %broadcast_select_fusion), kind=kLoop, calls=%fused_computation.17 | loop fusion | flops 4030464 | bytes 2686976 | tf_op jit(solution)/shard_map/concatenate | solution.py:159
  24.4 0.8 select_bitcast_fusion
  25.3 6.0 %all-to-all-start.2 = ((bf16[8,2,328,128]{3,2,1,0:T(8,128)(2,1)}), bf16[8,2,328,128]{3,2,1,0:T(8,128)(2,1)S(1)}, u32[]{:S(2)}, u32[]{:S(2)}) async-start(bf16[8,2,328,128]{3,2,1,0:T(8,128)(2,1)} %pad_maximum_fusion.1), calls=%async_computation.2 | async-start | bytes 2686976 | tf_op jit(solution)/shard_map/all_to_all | solution.py:167
  31.2 1.6 copy.282
  33.8 2.9 %gather_fusion = bf16[32,16,1024]{2,1,0:T(8,128)(2,1)} fusion(bf16[32,16,1024]{2,1,0:T(8,128)(2,1)} %param.20, s32[1024]{0:T(1024)S(1)} %pad_clamp_fusion.3), kind=kCustom, calls=%fused_computation | custom fusion | bytes 2097280 | tf_op jit(solution)/shard_map/jit(_take)/gather | solution.py:231
  36.8 2.4 %select_multiply_fusion = bf16[32,16,1024]{2,1,0:T(8,128)(2,1)} fusion(bf16[32,16,1024]{2,1,0:T(8,128)(2,1)} %gather_fusion, pred[32]{0:T(512)(128)(4,1)S(1)} %le.73, bf16[32]{0:T(256)(128)(2,1)S(1)} %reshape.512), kind=kLoop, calls=%fused_computation.34 | loop fusion | flops 1048576 | bytes 2097248 | tf_op jit(solution)/shard_map/mul | solution.py:231
  39.2 2.9 %collective-permute-start = (bf16[8,2,32,256]{3,2,1,0:T(8,128)(2,1)}, bf16[8,2,32,256]{3,2,1,0:T(8,128)(2,1)}, u32[]{:S(2)}, u32[]{:S(2)}) collective-permute-start(bf16[8,2,32,256]{3,2,1,0:T(8,128)(2,1)} %all-to-all-done.1), channel_id=1, source_target_pairs={{0,2},{1,3},{2,0},{3,1},{4,6},{5,7},{6,4},{7,5},{8,10},{9,11},{10,... | collective-permute-start | bytes 786440 | tf_op jit(solution)/shard_map/ppermute | solution.py:116
  42.1 6.9 %all-to-all-done.2 = bf16[8,2,328,128]{3,2,1,0:T(8,128)(2,1)S(1)} async-done(((bf16[8,2,328,128]{3,2,1,0:T(8,128)(2,1)}), bf16[8,2,328,128]{3,2,1,0:T(8,128)(2,1)S(1)}, u32[]{:S(2)}, u32[]{:S(2)}) %all-to-all-start.2) | async-done | bytes 1343520 | tf_op jit(solution)/shard_map/all_to_all | solution.py:167
  49.1 6.1 %all-to-all-start = ((bf16[32,16,1024]{2,1,0:T(8,128)(2,1)}), bf16[32,16,1024]{2,1,0:T(8,128)(2,1)}, u32[]{:S(2)}, u32[]{:S(2)}) async-start(bf16[32,16,1024]{2,1,0:T(8,128)(2,1)} %select_multiply_fusion), calls=%async_computation | async-start | bytes 2097152 | tf_op jit(solution)/shard_map/all_to_all | solution.py:234
  55.1 1.3 slice.181
  56.5 2.1 %gather_fusion.6 = bf16[32,256,128]{2,1,0:T(8,128)(2,1)} fusion(bf16[16,256,128]{2,1,0:T(8,128)(2,1)S(1)} %slice.181, s32[1024]{0:T(1024)S(1)} %pad_clamp_fusion), kind=kCustom, calls=%fused_computation.6 | custom fusion | bytes 4194432 | tf_op jit(solution)/shard_map/jit(_take)/gather | solution.py:175
  58.6 2.1 %fusion.5 = f32[32,128,2]{1,2,0:T(2,128)S(1)} fusion(bf16[32,256,128]{2,1,0:T(8,128)(2,1)} %gather_fusion.6, pred[32]{0:T(512)(128)(4,1)S(1)} %get-tuple-element.19, bf16[2,32,256]{2,1,0:T(8,128)(2,1)S(1)} %copy-done.10), kind=kOutput, calls=%fused_computation.14 | convolution fusion | flops 5242880 | bytes 2162720 | tf_op jit(solution)/shard_map/srd,rdk->srk/dot_general | solution.py:184
  61.1 2.1 %maximum_select_fusion.2 = bf16[8,2,2,32,256]{4,3,2,0,1:T(8,128)(2,1)} fusion(bf16[8,1,2,32,256]{4,3,2,0,1:T(8,128)(2,1)} %bitcast.10, bf16[8,1,2,32,256]{4,3,2,0,1:T(8,128)(2,1)} %bitcast.9, pred[]{:T(512)S(6)} %eq.19), kind=kLoop, calls=%fused_computation.40 | loop fusion | flops 786432 | bytes 1048577 | tf_op jit(solution)/shard_map/jit(_where)/select_n | solution.py:117
  64.1 3.0 %collective-permute-start.3 = (f32[24576]{0:T(1024)S(1)}, f32[24576]{0:T(1024)S(1)}, u32[]{:S(2)}, u32[]{:S(2)}) collective-permute-start(f32[24576]{0:T(1024)S(1)} %pad_maximum_fusion.4), channel_id=1, source_target_pairs={{0,2},{1,3},{2,0},{3,1},{4,6},{5,7},{6,4},{7,5},{8,10},{9,11},{10,... | collective-permute-start | bytes 294920 | tf_op jit(solution)/shard_map/ppermute | solution.py:90
  67.1 2.1 %maximum_select_fusion.1 = bf16[8,2,1,2,32,256]{5,4,3,0,2,1:T(8,128)(2,1)} fusion(bf16[8,1,1,2,32,256]{5,4,3,0,2,1:T(8,128)(2,1)} %bitcast.8, bf16[8,1,1,2,32,256]{5,4,3,0,2,1:T(8,128)(2,1)} %bitcast.7, pred[]{:T(512)S(6)} %eq.19), kind=kLoop, calls=%fused_computation.39 | loop fusion | flops 786432 | bytes 1048577 | tf_op jit(solution)/shard_map/jit(_where)/select_n | solution.py:117
  69.2 2.0 %collective-permute-done.3 = f32[24576]{0:T(1024)S(1)} collective-permute-done((f32[24576]{0:T(1024)S(1)}, f32[24576]{0:T(1024)S(1)}, u32[]{:S(2)}, u32[]{:S(2)}) %collective-permute-start.3) | collective-permute-done | bytes 98336 | tf_op jit(solution)/shard_map/ppermute | solution.py:90
  71.4 0.9 all_to_all.38
  72.3 6.6 %all-to-all-start.3 = ((f32[8,1,10240]{2,1,0:T(1,128)}), f32[8,1,10240]{2,1,0:T(1,128)}, u32[]{:S(2)}, u32[]{:S(2)}) async-start(f32[8,1,10240]{2,1,0:T(1,128)} %all_to_all.38), calls=%async_computation.3 | async-start | bytes 655360 | tf_op jit(solution)/shard_map/all_to_all | solution.py:98
  78.9 2.7 %pad_maximum_fusion = bf16[64,16,1024]{2,1,0:T(8,128)(2,1)} fusion(bf16[32,16,1024]{2,1,0:T(8,128)(2,1)} %all-to-all-done, bf16[32,16,1024]{2,1,0:T(8,128)(2,1)S(1)} %copy-done.3), kind=kLoop, calls=%fused_computation.11 | loop fusion | flops 1048576 | bytes 4194304 | tf_op jit(solution)/shard_map/concatenate | solution.py:235
  81.6 2.2 %gather_fusion.1 = bf16[32,16,1024]{2,1,0:T(8,128)(2,1)S(1)} fusion(bf16[64,16,1024]{2,1,0:T(8,128)(2,1)} %pad_maximum_fusion, s32[1024]{0:T(1024)S(1)} %pad_clamp_fusion.2), kind=kCustom, calls=%fused_computation.1 | custom fusion | bytes 2097280 | tf_op jit(solution)/shard_map/jit(_take)/gather | solution.py:236
  83.9 1.3 copy.228
  85.2 2.3 %broadcast_select_fusion.1 = bf16[1,512,1024]{1,2,0:T(8,128)(2,1)} fusion(bf16[1,512,1024]{1,2,0:T(8,128)(2,1)} %copy.228, pred[512]{0:T(512)(128)(4,1)S(1)} %broadcast_in_dim.131), kind=kLoop, calls=%fused_computation.36 | loop fusion | flops 524288 | bytes 2097664 | tf_op jit(solution)/shard_map/jit(_take)/select_n | solution.py:236
  87.5 1.0 slice.178
  89.3 1.4 gather_fusion.5
  91.7 1.6 maximum_select_fusion
  93.4 1.2 reduce_sum.36
  95.2 1.4 fusion.28
  97.7 9.2 %all-to-all-start.4 = ((f32[2,32,1,144]{3,0,2,1:T(2,128)}), f32[2,32,1,144]{3,0,2,1:T(2,128)S(1)}, u32[]{:S(2)}, u32[]{:S(2)}) async-start(f32[2,32,1,144]{3,0,2,1:T(2,128)} %copy.250), calls=%async_computation.4 | async-start | bytes 131072 | tf_op jit(solution)/shard_map/all_to_all | solution.py:216
  106.9 1.3 fusion.64
  108.2 8.7 %all-to-all-done.4 = f32[2,32,1,144]{3,0,2,1:T(2,128)S(1)} async-done(((f32[2,32,1,144]{3,0,2,1:T(2,128)}), f32[2,32,1,144]{3,0,2,1:T(2,128)S(1)}, u32[]{:S(2)}, u32[]{:S(2)}) %all-to-all-start.4) | async-done | bytes 36896 | tf_op jit(solution)/shard_map/all_to_all | solution.py:216
  118.4 12.7 %all_to_all.51 = bf16[2,1,32,128]{3,0,1,2:T(2,128)(2,1)S(1)} all-to-all(bf16[2,1,32,128]{3,0,1,2:T(2,128)(2,1)S(1)} %copy.261), channel_id=1, replica_groups=mesh['group'=8,'tp'=32] {'tp'}, dimensions={2} | all-to-all | bytes 32768 | tf_op jit(solution)/shard_map/all_to_all | solution.py:240
  131.1 2.0 %fusion = f32[64,32,256]{2,0,1:T(8,128)S(1)} fusion(bf16[64,128,1]{1,0,2:T(8,128)(2,1)S(1)} %bitcast.214, bf16[16,32,8,256]{3,2,1,0:T(8,128)(2,1)} %bitcast.196), kind=kOutput, calls=%fused_computation.8 | convolution fusion | flops 134217728 | bytes 4210688 | tf_op jit(solution)/shard_map/rk,kdc->drc/dot_general | solution.py:242
  133.3 1.5 copy.285
  134.8 2.0 %select_n.252 = f32[16,1,16384]{2,1,0:T(1,128)} reshape(f32[16,1,64,256]{3,2,1,0:T(8,128)S(1)} %get-tuple-element.6) | data formatting | bytes 2097152 | tf_op jit(solution)/shard_map/jit(_where)/select_n | solution.py:87
  136.8 1.0 collective-permute-done.4
  137.8 2.6 %add.127 = f32[16,1,16384]{2,1,0:T(1,128)S(1)} add(f32[16,1,16384]{2,1,0:T(1,128)} %select_n.252, f32[16,1,16384]{2,1,0:T(1,128)} %bitcast.59) | non-fusion elementwise | flops 262144 | bytes 3145728 | tf_op jit(solution)/shard_map/add | solution.py:91
  140.4 33.9 %all_to_all.52 = f32[16,1,16384]{2,1,0:T(1,128)S(1)} all-to-all(f32[16,1,16384]{2,1,0:T(1,128)S(1)} %add.127), channel_id=1, replica_groups={{0,2,4,6,8,10,12,14,16,18,20,22,24,26,28,30},{1,3,5,7,9,11,13,15,17,19,..., dimensions={0} | all-to-all | bytes 2097152 | tf_op jit(solution)/shard_map/all_to_all | solution.py:98
  174.3 0.8 reduce_sum.39
  (116 shorter events, 10.4 us)
Async XLA Ops:
  0.0 96.5 %copy-start = (bf16[8192,128]{1,0:T(8,128)(2,1)S(1)}, bf16[8192,128]{1,0:T(8,128)(2,1)}, u32[]{:S(2)}) copy-start(bf16[8192,128]{1,0:T(8,128)(2,1)} %param.14) | copy-start | bytes 6291460
  0.0 16.8 %copy-start.2 = (bf16[4,256,128]{2,1,0:T(8,128)(2,1)S(1)}, bf16[4,256,128]{2,1,0:T(8,128)(2,1)}, u32[]{:S(2)}) copy-start(bf16[4,256,128]{2,1,0:T(8,128)(2,1)} %param.17) | copy-start | bytes 786436
  1.7 23.6 %all-to-all-start.1 = ((bf16[8,2,32,256]{3,2,1,0:T(8,128)(2,1)}), bf16[8,2,32,256]{3,2,1,0:T(8,128)(2,1)}, u32[]{:S(2)}, u32[]{:S(2)}) async-start(bf16[8,2,32,256]{3,2,1,0:T(8,128)(2,1)} %broadcast_in_dim.136), calls=%async_computation.1 | async-start | bytes 524288 | tf_op jit(solution)/shard_map/all_to_all | solution.py:106
  14.2 10.2 %copy-start.5 = (f32[16,1,2,1024]{3,1,0,2:T(1,128)}, f32[16,1,2,1024]{3,1,0,2:T(1,128)S(1)}, u32[]{:S(2)}) copy-start(f32[16,1,2,1024]{3,1,0,2:T(1,128)S(1)} %get-tuple-element.9) | copy-start | bytes 393220
  17.6 4.2 %copy-start.11 = (s32[1,1,8,4]{2,3,1,0:T(4,128)S(1)}, s32[1,1,8,4]{2,3,1,0:T(4,128)}, u32[]{:S(2)}) copy-start(s32[1,1,8,4]{2,3,1,0:T(4,128)} %param.23) | copy-start | bytes 388
  20.2 4.2 %copy-start.7 = (f32[16,1,2,1024]{3,1,0,2:T(1,128)S(1)}, f32[16,1,2,1024]{3,1,0,2:T(1,128)}, u32[]{:S(2)}) copy-start(f32[16,1,2,1024]{3,1,0,2:T(1,128)} %get-tuple-element.10) | copy-start | bytes 393220
  25.3 11.5 %copy-start.13 = (s32[32]{0:T(128)S(1)}, s32[32]{0:T(128)}, u32[]{:S(2)}) copy-start(s32[32]{0:T(128)} %param.24) | copy-start | bytes 388
  25.3 11.5 %copy-start.12 = (s32[1,32]{1,0:T(1,128)S(1)}, s32[1,32]{1,0:T(1,128)}, u32[]{:S(2)}) copy-start(s32[1,32]{1,0:T(1,128)} %param.22) | copy-start | bytes 388
  25.3 23.8 %all-to-all-start.2 = ((bf16[8,2,328,128]{3,2,1,0:T(8,128)(2,1)}), bf16[8,2,328,128]{3,2,1,0:T(8,128)(2,1)S(1)}, u32[]{:S(2)}, u32[]{:S(2)}) async-start(bf16[8,2,328,128]{3,2,1,0:T(8,128)(2,1)} %pad_maximum_fusion.1), calls=%async_computation.2 | async-start | bytes 2686976 | tf_op jit(solution)/shard_map/all_to_all | solution.py:167
  39.2 21.8 %collective-permute-start = (bf16[8,2,32,256]{3,2,1,0:T(8,128)(2,1)}, bf16[8,2,32,256]{3,2,1,0:T(8,128)(2,1)}, u32[]{:S(2)}, u32[]{:S(2)}) collective-permute-start(bf16[8,2,32,256]{3,2,1,0:T(8,128)(2,1)} %all-to-all-done.1), channel_id=1, source_target_pairs={{0,2},{1,3},{2,0},{3,1},{4,6},{5,7},{6,4},{7,5},{8,10},{9,11},{10,... | collective-permute-start | bytes 786440 | tf_op jit(solution)/shard_map/ppermute | solution.py:116
  49.1 6.1 %copy-start.1 = (bf16[8,2,328,128]{3,2,1,0:T(8,128)(2,1)}, bf16[8,2,328,128]{3,2,1,0:T(8,128)(2,1)S(1)}, u32[]{:S(2)}) copy-start(bf16[8,2,328,128]{3,2,1,0:T(8,128)(2,1)S(1)} %all-to-all-done.2) | copy-start | bytes 4030468
  49.1 23.2 %all-to-all-start = ((bf16[32,16,1024]{2,1,0:T(8,128)(2,1)}), bf16[32,16,1024]{2,1,0:T(8,128)(2,1)}, u32[]{:S(2)}, u32[]{:S(2)}) async-start(bf16[32,16,1024]{2,1,0:T(8,128)(2,1)} %select_multiply_fusion), calls=%async_computation | async-start | bytes 2097152 | tf_op jit(solution)/shard_map/all_to_all | solution.py:234
  56.5 2.2 %copy-start.10 = (bf16[2,32,256]{2,1,0:T(8,128)(2,1)S(1)}, bf16[2,32,256]{2,1,0:T(8,128)(2,1)}, u32[]{:S(2)}) copy-start(bf16[2,32,256]{2,1,0:T(8,128)(2,1)} %param.13) | copy-start | bytes 98308
  58.6 2.1 %copy-start.9 = (f32[16,8,2,128]{3,1,2,0:T(8,128)S(1)}, f32[16,8,2,128]{3,1,2,0:T(8,128)}, u32[]{:S(2)}) copy-start(f32[16,8,2,128]{3,1,2,0:T(8,128)} %copy.282) | copy-start | bytes 393220
  60.7 3.1 %copy-start.6 = (f32[16,1,2,1024]{3,1,0,2:T(1,128)S(1)}, f32[16,1,2,1024]{3,1,0,2:T(1,128)}, u32[]{:S(2)}) copy-start(f32[16,1,2,1024]{3,1,0,2:T(1,128)} %copy-done.5) | copy-start | bytes 393220
  60.7 3.1 %copy-start.8 = (f32[16,1,2,1024]{3,1,0,2:T(1,128)S(1)}, f32[16,1,2,1024]{3,1,0,2:T(1,128)}, u32[]{:S(2)}) copy-start(f32[16,1,2,1024]{3,1,0,2:T(1,128)} %get-tuple-element.10) | copy-start | bytes 393220
  60.7 2.9 %collective-permute-start.2 = (f32[40960]{0:T(1024)S(1)}, f32[40960]{0:T(1024)S(1)}, u32[]{:S(2)}, u32[]{:S(2)}) collective-permute-start(f32[40960]{0:T(1024)S(1)} %pad_maximum_fusion.3), channel_id=1, source_target_pairs={{0,1},{1,0},{2,3},{3,2},{4,5},{5,4},{6,7},{7,6},{8,9},{9,8},{10,11... | collective-permute-start | bytes 491528 | tf_op jit(solution)/shard_map/ppermute | solution.py:90
  63.2 28.5 %collective-permute-start.1 = (bf16[8,2,2,32,256]{4,3,2,0,1:T(8,128)(2,1)}, bf16[8,2,2,32,256]{4,3,2,0,1:T(8,128)(2,1)}, u32[]{:S(2)}, u32[]{:S(2)}) collective-permute-start(bf16[8,2,2,32,256]{4,3,2,0,1:T(8,128)(2,1)} %maximum_select_fusion.2), channel_id=1, source_target_pairs={{0,1},{1,0},{2,3},{3,2},{4,5},{5,4},{6,7},{7,6},{8,9},{9,8},{10,11... | collective-permute-start | bytes 1572872 | tf_op jit(solution)/shard_map/ppermute | solution.py:116
  64.0 14.9 %copy-start.3 = (bf16[32,16,1024]{2,1,0:T(8,128)(2,1)S(1)}, bf16[32,16,1024]{2,1,0:T(8,128)(2,1)}, u32[]{:S(2)}) copy-start(bf16[32,16,1024]{2,1,0:T(8,128)(2,1)} %param.20) | copy-start | bytes 3145732
  64.1 7.1 %collective-permute-start.3 = (f32[24576]{0:T(1024)S(1)}, f32[24576]{0:T(1024)S(1)}, u32[]{:S(2)}, u32[]{:S(2)}) collective-permute-start(f32[24576]{0:T(1024)S(1)} %pad_maximum_fusion.4), channel_id=1, source_target_pairs={{0,2},{1,3},{2,0},{3,1},{4,6},{5,7},{6,4},{7,5},{8,10},{9,11},{10,... | collective-permute-start | bytes 294920 | tf_op jit(solution)/shard_map/ppermute | solution.py:90
  72.3 21.1 %all-to-all-start.3 = ((f32[8,1,10240]{2,1,0:T(1,128)}), f32[8,1,10240]{2,1,0:T(1,128)}, u32[]{:S(2)}, u32[]{:S(2)}) async-start(f32[8,1,10240]{2,1,0:T(1,128)} %all_to_all.38), calls=%async_computation.3 | async-start | bytes 655360 | tf_op jit(solution)/shard_map/all_to_all | solution.py:98
  87.5 4.2 %copy-start.4 = (bf16[8,2,1,2,32,256]{5,4,3,0,2,1:T(8,128)(2,1)S(1)}, bf16[8,2,1,2,32,256]{5,4,3,0,2,1:T(8,128)(2,1)}, u32[]{:S(2)}) copy-start(bf16[8,2,1,2,32,256]{5,4,3,0,2,1:T(8,128)(2,1)} %maximum_select_fusion.1) | copy-start | bytes 1572868
  97.7 19.2 %all-to-all-start.4 = ((f32[2,32,1,144]{3,0,2,1:T(2,128)}), f32[2,32,1,144]{3,0,2,1:T(2,128)S(1)}, u32[]{:S(2)}, u32[]{:S(2)}) async-start(f32[2,32,1,144]{3,0,2,1:T(2,128)} %copy.250), calls=%async_computation.4 | async-start | bytes 131072 | tf_op jit(solution)/shard_map/all_to_all | solution.py:216
  134.8 3.0 %collective-permute-start.4 = (f32[262144]{0:T(1024)}, f32[262144]{0:T(1024)}, u32[]{:S(2)}, u32[]{:S(2)}) collective-permute-start(f32[262144]{0:T(1024)} %bitcast.99), channel_id=1, source_target_pairs={{0,1},{1,0},{2,3},{3,2},{4,5},{5,4},{6,7},{7,6},{8,9},{9,8},{10,11... | collective-permute-start | bytes 3145736 | tf_op jit(solution)/shard_map/ppermute | solution.py:90

commit v9 on v8

--- a/solution.py
+++ b/solution.py
@@ -120,6 +120,19 @@
             jnp.stack([other, gathered], 1 + done),
         )
     return gathered.reshape((n_tp,) + block.shape)
+
+
+def scatter_tp(blocks, column_id, n_tp):
+    mine = column_id % 2
+    split = blocks.reshape((-1, 2) + blocks.shape[1:])
+    keep = jnp.where(mine == 0, split[:, 0], split[:, 1])
+    give = jnp.where(mine == 0, split[:, 1], split[:, 0])
+    got = lax.ppermute(give, "tp", [(t, t ^ 1) for t in range(n_tp)])
+    pair = jnp.where(mine == 0, jnp.stack([keep, got], 1), jnp.stack([got, keep], 1))
+    arrived = lax.all_to_all(
+        pair, "tp", 0, 0, tiled=True, axis_index_groups=stage_groups(n_tp, SWAP_BITS[:1])
+    )
+    return arrived.reshape((n_tp,) + blocks.shape[1:])
 
 
 def per_device(
@@ -213,7 +226,9 @@
         ],
         -1,
     )
-    query_recv = lax.all_to_all(query_send, "tp", split_axis=1, concat_axis=2, tiled=True)
+    query_recv = jnp.transpose(
+        scatter_tp(jnp.transpose(query_send, (1, 0, 2, 3)), column_id, n_tp), (1, 2, 0, 3)
+    )
     query_own = query_recv[..., :HEAD_SIZE].astype(jnp.bfloat16)
     value_own = jnp.transpose(query_recv[..., HEAD_SIZE:], (1, 0, 2, 3)).reshape(
         batch_own, step_count, -1
@@ -237,7 +252,9 @@
         batch_own, -1, 2 * key_span_width
     )
     attended = attend(query_own, ctx_pages, keyval_new, lengths)
-    heads_back = lax.all_to_all(attended, "tp", split_axis=2, concat_axis=1, tiled=True)
+    heads_back = jnp.transpose(
+        scatter_tp(jnp.transpose(attended, (2, 0, 1, 3)), column_id, n_tp), (1, 0, 2, 3)
+    )
     out_cols = output_weight.shape[1] // n_tp
     projected = jnp.einsum(
         "rk,kdc->drc",

time: 177 us -> 180 us (1.017)
  waiting for transfers between devices: 18.6 us -> 21.5 us
    ppermute x0 -> x2, waiting for transfers between devices: none -> 2.3 us  [scatter_tp(): got = lax.ppermute(give, 'tp', [(t, t ^ 1) for t in range(n_tp)])]
  transfers between devices with their start and end apart: 10 -> 12, of which waited for: 4 -> 6; matrix products, arithmetic and copies ran while one was open for 29% -> 28% of each run, Pallas kernels for 0% -> 0%
where the time goes in v9:
time: 180 us; the launch traced here: 179 us
  blocking collectives  46.5 us (26%)
  starting transfers between devices  42.8 us (24%)
  local copies, waits for them, and re-layouts  31.1 us (17%)
  other arithmetic  27.5 us (15%)
  waiting for transfers between devices  21.5 us (12%)
  matrix products  8.38 us (5%)
    all_to_all x1, blocking collectives, reduce_scatter_tp(): lax.all_to_all(send, 'tp', 0, 0, tiled=True, axis_index_groups=stage_grou...  33.9 us
    all_to_all x1, blocking collectives, scatter_tp(): lax.all_to_all(pair, 'tp', 0, 0, tiled=True, axis_index_groups=stage_grou...  12.6 us
    all_to_all x1, waiting for transfers between devices, scatter_tp(): lax.all_to_all(pair, 'tp', 0, 0, tiled=True, axis_index_groups=stage_grou...  9.25 us
    all_to_all x1, starting transfers between devices, scatter_tp(): lax.all_to_all(pair, 'tp', 0, 0, tiled=True, axis_index_groups=stage_grou...  8.9 us
    all_to_all x1, starting transfers between devices, all_gather_tp(): lax.all_to_all(jnp.broadcast_to(block[None], (rest,) + block.shape), 'tp'...  8.47 us
    all_to_all x1, waiting for transfers between devices, per_device(): lax.all_to_all(panel_send, 'group', 0, 0, tiled=True)  6.97 us
    all_to_all x1, starting transfers between devices, reduce_scatter_tp(): lax.all_to_all(send, 'tp', 0, 0, tiled=True, axis_index_groups=stage_grou...  6.57 us
    all_to_all x1, starting transfers between devices, per_device(): lax.all_to_all(outgoing, 'group', split_axis=0, concat_axis=0, tiled=True)  6.07 us
  transfers between devices with their start and end apart: 12, of which 6 were waited for; matrix products, arithmetic and copies ran while one was open for 28% of the time, Pallas kernels for 0%

profile of v9, /device:TPU:2, one launch (start us, length us, event | category | flops | bytes accessed | tf_op | source)
XLA Modules:
  0.0 179.0 jit_solution(7435641925931583880)
XLA Ops:
  0.0 1.6 broadcast_in_dim.136
  1.6 8.5 %all-to-all-start.1 = ((bf16[8,2,32,256]{3,2,1,0:T(8,128)(2,1)}), bf16[8,2,32,256]{3,2,1,0:T(8,128)(2,1)}, u32[]{:S(2)}, u32[]{:S(2)}) async-start(bf16[8,2,32,256]{3,2,1,0:T(8,128)(2,1)} %broadcast_in_dim.136), calls=%async_computation.1 | async-start | bytes 524288 | tf_op jit(solution)/shard_map/all_to_all | solution.py:106
  10.1 1.0 fusion.53
  11.9 1.3 convolution_bitcast_fusion
  13.3 0.9 fusion.64
  14.2 0.9 constant_dynamic-slice_fusion
  17.6 1.5 broadcast_select_fusion.3
  19.0 1.1 broadcast_select_fusion
  20.2 1.5 gather_fusion.3
  22.0 2.4 %pad_maximum_fusion.1 = bf16[8,2,328,128]{3,2,1,0:T(8,128)(2,1)} fusion(bf16[8,2,8,128]{3,2,1,0:T(8,128)(2,1)} %broadcast_select_fusion.3, bf16[8,2,64,128]{3,2,1,0:T(8,128)(2,1)S(1)} %broadcast_select_fusion.2, bf16[8,2,256,128]{3,2,1,0:T(8,128)(2,1)} %broadcast_select_fusion), kind=kLoop, calls=%fused_computation.17 | loop fusion | flops 4030464 | bytes 2686976 | tf_op jit(solution)/shard_map/concatenate | solution.py:172
  25.2 6.0 %all-to-all-start.2 = ((bf16[8,2,328,128]{3,2,1,0:T(8,128)(2,1)}), bf16[8,2,328,128]{3,2,1,0:T(8,128)(2,1)S(1)}, u32[]{:S(2)}, u32[]{:S(2)}) async-start(bf16[8,2,328,128]{3,2,1,0:T(8,128)(2,1)} %pad_maximum_fusion.1), calls=%async_computation.2 | async-start | bytes 2686976 | tf_op jit(solution)/shard_map/all_to_all | solution.py:180
  31.2 1.6 copy.339
  33.8 2.9 %gather_fusion = bf16[32,16,1024]{2,1,0:T(8,128)(2,1)} fusion(bf16[32,16,1024]{2,1,0:T(8,128)(2,1)} %param.20, s32[1024]{0:T(1024)S(1)} %pad_clamp_fusion.3), kind=kCustom, calls=%fused_computation | custom fusion | bytes 2097280 | tf_op jit(solution)/shard_map/jit(_take)/gather | solution.py:246
  36.8 2.4 %select_multiply_fusion = bf16[32,16,1024]{2,1,0:T(8,128)(2,1)} fusion(bf16[32,16,1024]{2,1,0:T(8,128)(2,1)} %gather_fusion, pred[32]{0:T(512)(128)(4,1)S(1)} %le.73, bf16[32]{0:T(256)(128)(2,1)S(1)} %reshape.695), kind=kLoop, calls=%fused_computation.34 | loop fusion | flops 1048576 | bytes 2097248 | tf_op jit(solution)/shard_map/mul | solution.py:246
  39.2 2.9 %collective-permute-start = (bf16[8,2,32,256]{3,2,1,0:T(8,128)(2,1)}, bf16[8,2,32,256]{3,2,1,0:T(8,128)(2,1)}, u32[]{:S(2)}, u32[]{:S(2)}) collective-permute-start(bf16[8,2,32,256]{3,2,1,0:T(8,128)(2,1)} %all-to-all-done.1), channel_id=1, source_target_pairs={{0,2},{1,3},{2,0},{3,1},{4,6},{5,7},{6,4},{7,5},{8,10},{9,11},{10,... | collective-permute-start | bytes 786440 | tf_op jit(solution)/shard_map/ppermute | solution.py:116
  42.1 7.0 %all-to-all-done.2 = bf16[8,2,328,128]{3,2,1,0:T(8,128)(2,1)S(1)} async-done(((bf16[8,2,328,128]{3,2,1,0:T(8,128)(2,1)}), bf16[8,2,328,128]{3,2,1,0:T(8,128)(2,1)S(1)}, u32[]{:S(2)}, u32[]{:S(2)}) %all-to-all-start.2) | async-done | bytes 1343520 | tf_op jit(solution)/shard_map/all_to_all | solution.py:180
  49.0 6.1 %all-to-all-start = ((bf16[32,16,1024]{2,1,0:T(8,128)(2,1)}), bf16[32,16,1024]{2,1,0:T(8,128)(2,1)}, u32[]{:S(2)}, u32[]{:S(2)}) async-start(bf16[32,16,1024]{2,1,0:T(8,128)(2,1)} %select_multiply_fusion), calls=%async_computation | async-start | bytes 2097152 | tf_op jit(solution)/shard_map/all_to_all | solution.py:249
  55.1 1.3 slice.201
  56.4 2.2 %gather_fusion.6 = bf16[32,256,128]{2,1,0:T(8,128)(2,1)} fusion(bf16[16,256,128]{2,1,0:T(8,128)(2,1)S(1)} %slice.201, s32[1024]{0:T(1024)S(1)} %pad_clamp_fusion), kind=kCustom, calls=%fused_computation.6 | custom fusion | bytes 4194432 | tf_op jit(solution)/shard_map/jit(_take)/gather | solution.py:188
  58.6 2.1 %fusion.5 = f32[32,128,2]{1,2,0:T(2,128)S(1)} fusion(bf16[32,256,128]{2,1,0:T(8,128)(2,1)} %gather_fusion.6, pred[32]{0:T(512)(128)(4,1)S(1)} %get-tuple-element.23, bf16[2,32,256]{2,1,0:T(8,128)(2,1)S(1)} %copy-done.10), kind=kOutput, calls=%fused_computation.14 | convolution fusion | flops 5242880 | bytes 2162720 | tf_op jit(solution)/shard_map/srd,rdk->srk/dot_general | solution.py:197
  61.0 2.1 %maximum_select_fusion.2 = bf16[8,2,2,32,256]{4,3,2,0,1:T(8,128)(2,1)} fusion(bf16[8,1,2,32,256]{4,3,2,0,1:T(8,128)(2,1)} %bitcast.11, bf16[8,1,2,32,256]{4,3,2,0,1:T(8,128)(2,1)} %bitcast.10, pred[]{:T(512)S(6)} %eq.13), kind=kLoop, calls=%fused_computation.40 | loop fusion | flops 786432 | bytes 1048577 | tf_op jit(solution)/shard_map/jit(_where)/select_n | solution.py:117
  64.1 3.0 %collective-permute-start.3 = (f32[24576]{0:T(1024)S(1)}, f32[24576]{0:T(1024)S(1)}, u32[]{:S(2)}, u32[]{:S(2)}) collective-permute-start(f32[24576]{0:T(1024)S(1)} %pad_maximum_fusion.4), channel_id=1, source_target_pairs={{0,2},{1,3},{2,0},{3,1},{4,6},{5,7},{6,4},{7,5},{8,10},{9,11},{10,... | collective-permute-start | bytes 294920 | tf_op jit(solution)/shard_map/ppermute | solution.py:90
  67.0 2.1 %maximum_select_fusion.1 = bf16[8,2,1,2,32,256]{5,4,3,0,2,1:T(8,128)(2,1)} fusion(bf16[8,1,1,2,32,256]{5,4,3,0,2,1:T(8,128)(2,1)} %bitcast.9, bf16[8,1,1,2,32,256]{5,4,3,0,2,1:T(8,128)(2,1)} %bitcast.8, pred[]{:T(512)S(6)} %eq.13), kind=kLoop, calls=%fused_computation.39 | loop fusion | flops 786432 | bytes 1048577 | tf_op jit(solution)/shard_map/jit(_where)/select_n | solution.py:117
  69.2 2.0 %collective-permute-done.3 = f32[24576]{0:T(1024)S(1)} collective-permute-done((f32[24576]{0:T(1024)S(1)}, f32[24576]{0:T(1024)S(1)}, u32[]{:S(2)}, u32[]{:S(2)}) %collective-permute-start.3) | collective-permute-done | bytes 98336 | tf_op jit(solution)/shard_map/ppermute | solution.py:90
  71.4 0.9 all_to_all.28
  72.3 6.6 %all-to-all-start.3 = ((f32[8,1,10240]{2,1,0:T(1,128)}), f32[8,1,10240]{2,1,0:T(1,128)}, u32[]{:S(2)}, u32[]{:S(2)}) async-start(f32[8,1,10240]{2,1,0:T(1,128)} %all_to_all.28), calls=%async_computation.3 | async-start | bytes 655360 | tf_op jit(solution)/shard_map/all_to_all | solution.py:98
  78.9 2.7 %pad_maximum_fusion = bf16[64,16,1024]{2,1,0:T(8,128)(2,1)} fusion(bf16[32,16,1024]{2,1,0:T(8,128)(2,1)} %all-to-all-done, bf16[32,16,1024]{2,1,0:T(8,128)(2,1)S(1)} %copy-done.3), kind=kLoop, calls=%fused_computation.11 | loop fusion | flops 1048576 | bytes 4194304 | tf_op jit(solution)/shard_map/concatenate | solution.py:250
  81.6 2.2 %gather_fusion.1 = bf16[32,16,1024]{2,1,0:T(8,128)(2,1)S(1)} fusion(bf16[64,16,1024]{2,1,0:T(8,128)(2,1)} %pad_maximum_fusion, s32[1024]{0:T(1024)S(1)} %pad_clamp_fusion.2), kind=kCustom, calls=%fused_computation.1 | custom fusion | bytes 2097280 | tf_op jit(solution)/shard_map/jit(_take)/gather | solution.py:251
  83.8 1.3 copy.275
  85.2 2.3 %broadcast_select_fusion.1 = bf16[1,512,1024]{1,2,0:T(8,128)(2,1)} fusion(bf16[1,512,1024]{1,2,0:T(8,128)(2,1)} %copy.275, pred[512]{0:T(512)(128)(4,1)S(1)} %broadcast_in_dim.131), kind=kLoop, calls=%fused_computation.36 | loop fusion | flops 524288 | bytes 2097664 | tf_op jit(solution)/shard_map/jit(_take)/select_n | solution.py:251
  87.5 1.0 slice.198
  89.3 1.4 gather_fusion.5
  91.7 1.6 maximum_select_fusion
  93.4 1.2 reduce_sum.36
  95.1 1.4 fusion.28
  97.4 1.1 collective-permute-done.4
  99.2 8.9 %all-to-all-start.4 = ((f32[16,2,2,1,144]{4,2,1,3,0:T(2,128)}), f32[16,2,2,1,144]{4,2,1,3,0:T(2,128)S(1)}, u32[]{:S(2)}, u32[]{:S(2)}) async-start(f32[16,2,2,1,144]{4,2,1,3,0:T(2,128)} %maximum_select_fusion.3), calls=%async_computation.4 | async-start | bytes 131072 | tf_op jit(solution)/shard_map/all_to_all | solution.py:132
  108.1 1.3 fusion.63
  109.4 9.3 %all-to-all-done.4 = f32[16,2,2,1,144]{4,2,1,3,0:T(2,128)S(1)} async-done(((f32[16,2,2,1,144]{4,2,1,3,0:T(2,128)}), f32[16,2,2,1,144]{4,2,1,3,0:T(2,128)S(1)}, u32[]{:S(2)}, u32[]{:S(2)}) %all-to-all-start.4) | async-done | bytes 36896 | tf_op jit(solution)/shard_map/all_to_all | solution.py:132
  120.4 1.2 collective-permute-done.5
  121.7 12.6 %all_to_all.40 = bf16[16,2,2,1,128]{4,1,2,3,0:T(2,128)(2,1)S(1)} all-to-all(bf16[16,2,2,1,128]{4,1,2,3,0:T(2,128)(2,1)S(1)} %copy.315), channel_id=1, replica_groups={{0,2,4,6,8,10,12,14,16,18,20,22,24,26,28,30},{1,3,5,7,9,11,13,15,17,19,..., dimensions={0} | all-to-all | bytes 32768 | tf_op jit(solution)/shard_map/all_to_all | solution.py:132
  134.3 2.0 %fusion = f32[64,32,256]{2,0,1:T(8,128)S(1)} fusion(bf16[64,128,1]{1,0,2:T(8,128)(2,1)S(1)} %bitcast.239, bf16[16,32,8,256]{3,2,1,0:T(8,128)(2,1)} %bitcast.221), kind=kOutput, calls=%fused_computation.8 | convolution fusion | flops 134217728 | bytes 4210688 | tf_op jit(solution)/shard_map/rk,kdc->drc/dot_general | solution.py:259
  136.5 1.5 copy.342
  138.1 2.1 %select_n.352 = f32[16,1,16384]{2,1,0:T(1,128)} reshape(f32[16,1,64,256]{3,2,1,0:T(8,128)S(1)} %get-tuple-element.6) | data formatting | bytes 2097152 | tf_op jit(solution)/shard_map/jit(_where)/select_n | solution.py:87
  140.1 0.9 collective-permute-done.6
  141.1 2.6 %add.129 = f32[16,1,16384]{2,1,0:T(1,128)S(1)} add(f32[16,1,16384]{2,1,0:T(1,128)} %select_n.352, f32[16,1,16384]{2,1,0:T(1,128)} %bitcast.74) | non-fusion elementwise | flops 262144 | bytes 3145728 | tf_op jit(solution)/shard_map/add | solution.py:91
  143.7 33.9 %all_to_all.41 = f32[16,1,16384]{2,1,0:T(1,128)S(1)} all-to-all(f32[16,1,16384]{2,1,0:T(1,128)S(1)} %add.129), channel_id=1, replica_groups={{0,2,4,6,8,10,12,14,16,18,20,22,24,26,28,30},{1,3,5,7,9,11,13,15,17,19,..., dimensions={0} | all-to-all | bytes 2097152 | tf_op jit(solution)/shard_map/all_to_all | solution.py:98
  177.5 0.8 reduce_sum.39
  (129 shorter events, 12.7 us)
Async XLA Ops:
  0.0 96.5 %copy-start = (bf16[8192,128]{1,0:T(8,128)(2,1)S(1)}, bf16[8192,128]{1,0:T(8,128)(2,1)}, u32[]{:S(2)}) copy-start(bf16[8192,128]{1,0:T(8,128)(2,1)} %param.14) | copy-start | bytes 6291460
  0.0 16.8 %copy-start.2 = (bf16[4,256,128]{2,1,0:T(8,128)(2,1)S(1)}, bf16[4,256,128]{2,1,0:T(8,128)(2,1)}, u32[]{:S(2)}) copy-start(bf16[4,256,128]{2,1,0:T(8,128)(2,1)} %param.17) | copy-start | bytes 786436
  1.6 23.6 %all-to-all-start.1 = ((bf16[8,2,32,256]{3,2,1,0:T(8,128)(2,1)}), bf16[8,2,32,256]{3,2,1,0:T(8,128)(2,1)}, u32[]{:S(2)}, u32[]{:S(2)}) async-start(bf16[8,2,32,256]{3,2,1,0:T(8,128)(2,1)} %broadcast_in_dim.136), calls=%async_computation.1 | async-start | bytes 524288 | tf_op jit(solution)/shard_map/all_to_all | solution.py:106
  14.1 10.2 %copy-start.5 = (f32[16,1,2,1024]{3,1,0,2:T(1,128)}, f32[16,1,2,1024]{3,1,0,2:T(1,128)S(1)}, u32[]{:S(2)}) copy-start(f32[16,1,2,1024]{3,1,0,2:T(1,128)S(1)} %get-tuple-element.9) | copy-start | bytes 393220
  17.6 4.2 %copy-start.11 = (s32[1,1,8,4]{2,3,1,0:T(4,128)S(1)}, s32[1,1,8,4]{2,3,1,0:T(4,128)}, u32[]{:S(2)}) copy-start(s32[1,1,8,4]{2,3,1,0:T(4,128)} %param.23) | copy-start | bytes 388
  20.2 4.2 %copy-start.7 = (f32[16,1,2,1024]{3,1,0,2:T(1,128)S(1)}, f32[16,1,2,1024]{3,1,0,2:T(1,128)}, u32[]{:S(2)}) copy-start(f32[16,1,2,1024]{3,1,0,2:T(1,128)} %get-tuple-element.10) | copy-start | bytes 393220
  25.2 11.5 %copy-start.13 = (s32[32]{0:T(128)S(1)}, s32[32]{0:T(128)}, u32[]{:S(2)}) copy-start(s32[32]{0:T(128)} %param.24) | copy-start | bytes 388
  25.2 11.5 %copy-start.12 = (s32[1,32]{1,0:T(1,128)S(1)}, s32[1,32]{1,0:T(1,128)}, u32[]{:S(2)}) copy-start(s32[1,32]{1,0:T(1,128)} %param.22) | copy-start | bytes 388
  25.2 23.8 %all-to-all-start.2 = ((bf16[8,2,328,128]{3,2,1,0:T(8,128)(2,1)}), bf16[8,2,328,128]{3,2,1,0:T(8,128)(2,1)S(1)}, u32[]{:S(2)}, u32[]{:S(2)}) async-start(bf16[8,2,328,128]{3,2,1,0:T(8,128)(2,1)} %pad_maximum_fusion.1), calls=%async_computation.2 | async-start | bytes 2686976 | tf_op jit(solution)/shard_map/all_to_all | solution.py:180
  39.2 21.9 %collective-permute-start = (bf16[8,2,32,256]{3,2,1,0:T(8,128)(2,1)}, bf16[8,2,32,256]{3,2,1,0:T(8,128)(2,1)}, u32[]{:S(2)}, u32[]{:S(2)}) collective-permute-start(bf16[8,2,32,256]{3,2,1,0:T(8,128)(2,1)} %all-to-all-done.1), channel_id=1, source_target_pairs={{0,2},{1,3},{2,0},{3,1},{4,6},{5,7},{6,4},{7,5},{8,10},{9,11},{10,... | collective-permute-start | bytes 786440 | tf_op jit(solution)/shard_map/ppermute | solution.py:116
  49.0 6.1 %copy-start.1 = (bf16[8,2,328,128]{3,2,1,0:T(8,128)(2,1)}, bf16[8,2,328,128]{3,2,1,0:T(8,128)(2,1)S(1)}, u32[]{:S(2)}) copy-start(bf16[8,2,328,128]{3,2,1,0:T(8,128)(2,1)S(1)} %all-to-all-done.2) | copy-start | bytes 4030468
  49.0 23.3 %all-to-all-start = ((bf16[32,16,1024]{2,1,0:T(8,128)(2,1)}), bf16[32,16,1024]{2,1,0:T(8,128)(2,1)}, u32[]{:S(2)}, u32[]{:S(2)}) async-start(bf16[32,16,1024]{2,1,0:T(8,128)(2,1)} %select_multiply_fusion), calls=%async_computation | async-start | bytes 2097152 | tf_op jit(solution)/shard_map/all_to_all | solution.py:249
  56.4 2.2 %copy-start.10 = (bf16[2,32,256]{2,1,0:T(8,128)(2,1)S(1)}, bf16[2,32,256]{2,1,0:T(8,128)(2,1)}, u32[]{:S(2)}) copy-start(bf16[2,32,256]{2,1,0:T(8,128)(2,1)} %param.13) | copy-start | bytes 98308
  58.6 2.1 %copy-start.9 = (f32[16,8,2,128]{3,1,2,0:T(8,128)S(1)}, f32[16,8,2,128]{3,1,2,0:T(8,128)}, u32[]{:S(2)}) copy-start(f32[16,8,2,128]{3,1,2,0:T(8,128)} %copy.339) | copy-start | bytes 393220
  60.7 3.1 %copy-start.6 = (f32[16,1,2,1024]{3,1,0,2:T(1,128)S(1)}, f32[16,1,2,1024]{3,1,0,2:T(1,128)}, u32[]{:S(2)}) copy-start(f32[16,1,2,1024]{3,1,0,2:T(1,128)} %copy-done.5) | copy-start | bytes 393220
  60.7 3.1 %copy-start.8 = (f32[16,1,2,1024]{3,1,0,2:T(1,128)S(1)}, f32[16,1,2,1024]{3,1,0,2:T(1,128)}, u32[]{:S(2)}) copy-start(f32[16,1,2,1024]{3,1,0,2:T(1,128)} %get-tuple-element.10) | copy-start | bytes 393220
  60.7 2.9 %collective-permute-start.2 = (f32[40960]{0:T(1024)S(1)}, f32[40960]{0:T(1024)S(1)}, u32[]{:S(2)}, u32[]{:S(2)}) collective-permute-start(f32[40960]{0:T(1024)S(1)} %pad_maximum_fusion.3), channel_id=1, source_target_pairs={{0,1},{1,0},{2,3},{3,2},{4,5},{5,4},{6,7},{7,6},{8,9},{9,8},{10,11... | collective-permute-start | bytes 491528 | tf_op jit(solution)/shard_map/ppermute | solution.py:90
  63.2 28.5 %collective-permute-start.1 = (bf16[8,2,2,32,256]{4,3,2,0,1:T(8,128)(2,1)}, bf16[8,2,2,32,256]{4,3,2,0,1:T(8,128)(2,1)}, u32[]{:S(2)}, u32[]{:S(2)}) collective-permute-start(bf16[8,2,2,32,256]{4,3,2,0,1:T(8,128)(2,1)} %maximum_select_fusion.2), channel_id=1, source_target_pairs={{0,1},{1,0},{2,3},{3,2},{4,5},{5,4},{6,7},{7,6},{8,9},{9,8},{10,11... | collective-permute-start | bytes 1572872 | tf_op jit(solution)/shard_map/ppermute | solution.py:116
  64.0 14.9 %copy-start.3 = (bf16[32,16,1024]{2,1,0:T(8,128)(2,1)S(1)}, bf16[32,16,1024]{2,1,0:T(8,128)(2,1)}, u32[]{:S(2)}) copy-start(bf16[32,16,1024]{2,1,0:T(8,128)(2,1)} %param.20) | copy-start | bytes 3145732
  64.1 7.1 %collective-permute-start.3 = (f32[24576]{0:T(1024)S(1)}, f32[24576]{0:T(1024)S(1)}, u32[]{:S(2)}, u32[]{:S(2)}) collective-permute-start(f32[24576]{0:T(1024)S(1)} %pad_maximum_fusion.4), channel_id=1, source_target_pairs={{0,2},{1,3},{2,0},{3,1},{4,6},{5,7},{6,4},{7,5},{8,10},{9,11},{10,... | collective-permute-start | bytes 294920 | tf_op jit(solution)/shard_map/ppermute | solution.py:90
  72.3 21.1 %all-to-all-start.3 = ((f32[8,1,10240]{2,1,0:T(1,128)}), f32[8,1,10240]{2,1,0:T(1,128)}, u32[]{:S(2)}, u32[]{:S(2)}) async-start(f32[8,1,10240]{2,1,0:T(1,128)} %all_to_all.28), calls=%async_computation.3 | async-start | bytes 655360 | tf_op jit(solution)/shard_map/all_to_all | solution.py:98
  87.5 4.2 %copy-start.4 = (bf16[8,2,1,2,32,256]{5,4,3,0,2,1:T(8,128)(2,1)S(1)}, bf16[8,2,1,2,32,256]{5,4,3,0,2,1:T(8,128)(2,1)}, u32[]{:S(2)}) copy-start(bf16[8,2,1,2,32,256]{5,4,3,0,2,1:T(8,128)(2,1)} %maximum_select_fusion.1) | copy-start | bytes 1572868
  97.2 1.3 collective-permute-start.4
  99.2 19.5 %all-to-all-start.4 = ((f32[16,2,2,1,144]{4,2,1,3,0:T(2,128)}), f32[16,2,2,1,144]{4,2,1,3,0:T(2,128)S(1)}, u32[]{:S(2)}, u32[]{:S(2)}) async-start(f32[16,2,2,1,144]{4,2,1,3,0:T(2,128)} %maximum_select_fusion.3), calls=%async_computation.4 | async-start | bytes 131072 | tf_op jit(solution)/shard_map/all_to_all | solution.py:132
  120.2 1.4 collective-permute-start.5
  138.1 3.0 %collective-permute-start.6 = (f32[262144]{0:T(1024)}, f32[262144]{0:T(1024)}, u32[]{:S(2)}, u32[]{:S(2)}) collective-permute-start(f32[262144]{0:T(1024)} %bitcast.119), channel_id=1, source_target_pairs={{0,1},{1,0},{2,3},{3,2},{4,5},{5,4},{6,7},{7,6},{8,9},{9,8},{10,11... | collective-permute-start | bytes 3145736 | tf_op jit(solution)/shard_map/ppermute | solution.py:90

commit v10 on v8

--- a/solution.py
+++ b/solution.py
@@ -119,6 +119,23 @@
             jnp.stack([gathered, other], 1 + done),
             jnp.stack([other, gathered], 1 + done),
         )
+    return gathered.reshape((n_tp,) + block.shape)
+
+
+def doubling_gather_tp(block, column_id, n_tp):
+    gathered = block
+    bit = n_tp // 2
+    stage = 0
+    while bit >= 1:
+        mine = (column_id // bit) % 2
+        other = lax.ppermute(gathered, "tp", [(t, t ^ bit) for t in range(n_tp)])
+        gathered = jnp.where(
+            mine == 0,
+            jnp.stack([gathered, other], stage),
+            jnp.stack([other, gathered], stage),
+        )
+        bit //= 2
+        stage += 1
     return gathered.reshape((n_tp,) + block.shape)
 
 
@@ -176,7 +193,7 @@
     upq_rows = jnp.take(upq_recv, request_adapter_entry, axis=0)
     upv_rows = jnp.take(upv_recv, request_adapter_entry, axis=0)
 
-    hidden_sent = all_gather_tp(hidden, column_id, n_tp)
+    hidden_sent = doubling_gather_tp(hidden, column_id, n_tp)
     hidden_full = jnp.transpose(hidden_sent, (1, 2, 0, 3)).reshape(
         step_count, batch_rows, n_tp * width_local
     )

time: 177 us -> 187 us (1.056); the launches traced: 176 us -> 184 us
  local copies, waits for them, and re-layouts: 31.6 us -> 35 us
  other arithmetic: 26.6 us -> 28.7 us
  waiting for transfers between devices: 18.6 us -> 20.7 us
    ppermute x2 -> x5, waiting for transfers between devices: 0.01 us -> 9.93 us  [doubling_gather_tp(): other = lax.ppermute(gathered, 'tp', [(t, t ^ bit) for t in range(n_tp)])]
    ppermute x2 -> x5, starting transfers between devices: 3.36 us -> 12.2 us  [doubling_gather_tp(): other = lax.ppermute(gathered, 'tp', [(t, t ^ bit) for t in range(n_tp)])]
    all_to_all x1 -> x0, starting transfers between devices: 8.47 us -> none  [all_gather_tp(): lax.all_to_all(jnp.broadcast_to(block[None], (rest,) + block.shape), 'tp'...]
    all_to_all x1, waiting for transfers between devices: 6.95 us -> 0.01 us  [per_device(): lax.all_to_all(panel_send, 'group', 0, 0, tiled=True)]
    all_to_all x1, starting transfers between devices: 6.58 us -> 4.07 us  [reduce_scatter_tp(): lax.all_to_all(send, 'tp', 0, 0, tiled=True, axis_index_groups=stage_grou...]
    another operation x1 -> x5, other arithmetic: 0.09 us -> 2.32 us  [the longest x4 2.22 us: doubling_gather_tp(): jnp.stack([gathered, other], stage)]
    select_n x3 -> x9, other arithmetic: 5.79 us -> 6.98 us  [doubling_gather_tp(): jnp.where(mine == 0, jnp.stack([gathered, other], stage), jnp.stack([othe...]
    unnamed x32 -> x38, local copies, waits for them, and re-layouts: 3.18 us -> 3.94 us
  transfers between devices with their start and end apart: 10 -> 12, of which waited for: 4 -> 6; matrix products, arithmetic and copies ran while one was open for 29% -> 31% of each run, Pallas kernels for 0% -> 0%
where the time goes in v10:
time: 187 us; the launch traced here: 184 us
  blocking collectives  46.6 us (25%)
  starting transfers between devices  41.7 us (22%)
  local copies, waits for them, and re-layouts  35 us (19%)
  other arithmetic  28.7 us (15%)
  waiting for transfers between devices  20.7 us (11%)
  matrix products  9.99 us (5%)
    all_to_all x1, blocking collectives, reduce_scatter_tp(): lax.all_to_all(send, 'tp', 0, 0, tiled=True, axis_index_groups=stage_grou...  33.9 us
    all_to_all x1, blocking collectives, per_device(): lax.all_to_all(attended, 'tp', split_axis=2, concat_axis=1, tiled=True)  12.7 us
    ppermute x5, starting transfers between devices, doubling_gather_tp(): other = lax.ppermute(gathered, 'tp', [(t, t ^ bit) for t in range(n_tp)])  12.2 us
    all_to_all x1, starting transfers between devices, per_device(): lax.all_to_all(query_send, 'tp', split_axis=1, concat_axis=2, tiled=True)  10.3 us
    ppermute x5, waiting for transfers between devices, doubling_gather_tp(): other = lax.ppermute(gathered, 'tp', [(t, t ^ bit) for t in range(n_tp)])  9.93 us
    all_to_all x1, waiting for transfers between devices, per_device(): lax.all_to_all(query_send, 'tp', split_axis=1, concat_axis=2, tiled=True)  8.51 us
    select_n x9, other arithmetic, doubling_gather_tp(): jnp.where(mine == 0, jnp.stack([gathered, other], stage), jnp.stack([othe...  6.98 us
    all_to_all x1, starting transfers between devices, per_device(): lax.all_to_all(panel_send, 'group', 0, 0, tiled=True)  5.84 us
  transfers between devices with their start and end apart: 12, of which 6 were waited for; matrix products, arithmetic and copies ran while one was open for 31% of the time, Pallas kernels for 0%

profile of v10, /device:TPU:2, one launch (start us, length us, event | category | flops | bytes accessed | tf_op | source)
XLA Modules:
  0.0 183.8 jit_solution(10391755852289747662)
XLA Ops:
  0.0 7.2 %collective-permute-start = (bf16[2,32,256]{2,1,0:T(8,128)(2,1)}, bf16[2,32,256]{2,1,0:T(8,128)(2,1)S(1)}, u32[]{:S(2)}, u32[]{:S(2)}) collective-permute-start(bf16[2,32,256]{2,1,0:T(8,128)(2,1)} %param.13), channel_id=1, source_target_pairs={{0,16},{1,17},{2,18},{3,19},{4,20},{5,21},{6,22},{7,23},{8,24},{9,... | collective-permute-start | bytes 98312 | tf_op jit(solution)/shard_map/ppermute | solution.py:131
  7.2 1.0 fusion.54
  11.0 1.4 gather_fusion.3
  15.1 1.2 pad_maximum_fusion.1
  16.2 5.8 %all-to-all-start.1 = ((bf16[8,2,328,128]{3,2,1,0:T(8,128)(2,1)}), bf16[8,2,328,128]{3,2,1,0:T(8,128)(2,1)S(1)}, u32[]{:S(2)}, u32[]{:S(2)}) async-start(bf16[8,2,328,128]{3,2,1,0:T(8,128)(2,1)} %pad_maximum_fusion.1), calls=%async_computation.1 | async-start | bytes 2686976 | tf_op jit(solution)/shard_map/all_to_all | solution.py:184
  23.4 2.0 %convolution_bitcast_fusion = f32[32,2,1024]{2,0,1:T(8,128)} fusion(bf16[2,32,256]{2,1,0:T(8,128)(2,1)S(1)} %copy-done.10, bf16[256,1024]{1,0:T(8,128)(2,1)} %param.15), kind=kOutput, calls=%fused_computation.18 | convolution fusion | flops 33554432 | bytes 819200 | tf_op jit(solution)/shard_map/srd,dc->rsc/dot_general | solution.py:202
  25.4 1.8 reshape.843
  27.2 2.0 %fusion.65 = (f32[16,1,2,1024]{3,1,0,2:T(1,128)}, f32[16,1,2,1024]{3,1,0,2:T(1,128)}) fusion(f32[16,2,2,1024]{3,1,0,2:T(2,128)} %reshape.843), kind=kLoop, calls=%fused_computation.129 | loop fusion | bytes 524288 | tf_op jit(solution)/shard_map/slice | solution.py:87
  29.1 2.9 %gather_fusion = bf16[32,16,1024]{2,1,0:T(8,128)(2,1)} fusion(bf16[32,16,1024]{2,1,0:T(8,128)(2,1)} %param.20, s32[1024]{0:T(1024)S(1)} %pad_clamp_fusion.3), kind=kCustom, calls=%fused_computation | custom fusion | bytes 2097280 | tf_op jit(solution)/shard_map/jit(_take)/gather | solution.py:248
  32.0 1.8 select_bitcast_fusion
  33.8 2.4 %select_multiply_fusion = bf16[32,16,1024]{2,1,0:T(8,128)(2,1)} fusion(bf16[32,16,1024]{2,1,0:T(8,128)(2,1)} %gather_fusion, pred[32]{0:T(512)(128)(4,1)S(1)} %le.73, bf16[32]{0:T(256)(128)(2,1)S(1)} %reshape.862), kind=kLoop, calls=%fused_computation.34 | loop fusion | flops 1048576 | bytes 2097248 | tf_op jit(solution)/shard_map/mul | solution.py:248
  36.9 1.6 copy.254
  38.5 1.6 collective-permute-start.1
  40.1 4.4 %collective-permute-done.1 = bf16[2,2,32,256]{3,2,1,0:T(8,128)(2,1)S(1)} collective-permute-done((bf16[2,2,32,256]{3,2,1,0:T(8,128)(2,1)S(1)}, bf16[2,2,32,256]{3,2,1,0:T(8,128)(2,1)S(1)}, u32[]{:S(2)}, u32[]{:S(2)}) %collective-permute-start.1) | collective-permute-done | bytes 65568 | tf_op jit(solution)/shard_map/ppermute | solution.py:131
  45.0 4.5 %collective-permute-done.2 = bf16[2,2,2,32,256]{4,3,2,1,0:T(8,128)(2,1)S(1)} collective-permute-done((bf16[2,2,2,32,256]{4,3,2,1,0:T(8,128)(2,1)S(1)}, bf16[2,2,2,32,256]{4,3,2,1,0:T(8,128)(2,1)S(1)}, u32[]{:S(2)}, u32[]{:S(2)}) %collective-permute-start.2) | collective-permute-done | bytes 131104 | tf_op jit(solution)/shard_map/ppermute | solution.py:131
  50.3 2.9 %collective-permute-start.3 = (bf16[2,2,2,2,32,256]{5,4,3,2,1,0:T(8,128)(2,1)}, bf16[2,2,2,2,32,256]{5,4,3,2,1,0:T(8,128)(2,1)}, u32[]{:S(2)}, u32[]{:S(2)}) collective-permute-start(bf16[2,2,2,2,32,256]{5,4,3,2,1,0:T(8,128)(2,1)} %maximum_select_fusion.2), channel_id=1, source_target_pairs={{0,2},{1,3},{2,0},{3,1},{4,6},{5,7},{6,4},{7,5},{8,10},{9,11},{10,... | collective-permute-start | bytes 786440 | tf_op jit(solution)/shard_map/ppermute | solution.py:131
  53.9 5.1 %all-to-all-start = ((bf16[32,16,1024]{2,1,0:T(8,128)(2,1)}), bf16[32,16,1024]{2,1,0:T(8,128)(2,1)}, u32[]{:S(2)}, u32[]{:S(2)}) async-start(bf16[32,16,1024]{2,1,0:T(8,128)(2,1)} %select_multiply_fusion), calls=%async_computation | async-start | bytes 2097152 | tf_op jit(solution)/shard_map/all_to_all | solution.py:251
  59.0 1.3 slice.181
  60.3 2.1 %gather_fusion.6 = bf16[32,256,128]{2,1,0:T(8,128)(2,1)} fusion(bf16[16,256,128]{2,1,0:T(8,128)(2,1)S(1)} %slice.181, s32[1024]{0:T(1024)S(1)} %pad_clamp_fusion), kind=kCustom, calls=%fused_computation.6 | custom fusion | bytes 4194432 | tf_op jit(solution)/shard_map/jit(_take)/gather | solution.py:192
  62.5 2.1 %fusion.5 = f32[32,128,2]{1,2,0:T(2,128)S(1)} fusion(bf16[32,256,128]{2,1,0:T(8,128)(2,1)} %gather_fusion.6, pred[32]{0:T(512)(128)(4,1)S(1)} %get-tuple-element.25, bf16[2,32,256]{2,1,0:T(8,128)(2,1)S(1)} %copy-done.10), kind=kOutput, calls=%fused_computation.14 | convolution fusion | flops 5242880 | bytes 2162720 | tf_op jit(solution)/shard_map/srd,rdk->srk/dot_general | solution.py:201
  64.7 1.1 collective-permute-done.3
  65.8 2.0 %maximum_select_fusion.1 = bf16[2,2,2,2,2,32,256]{6,5,4,3,2,1,0:T(8,128)(2,1)} fusion(bf16[2,2,2,1,2,32,256]{6,5,4,3,2,1,0:T(8,128)(2,1)} %bitcast.19, bf16[2,2,2,1,2,32,256]{6,5,4,3,2,1,0:T(8,128)(2,1)S(1)} %copy-done.4, pred[]{:T(512)S(6)} %eq.31), kind=kLoop, calls=%fused_computation.41 | loop fusion | flops 786432 | bytes 1048577 | tf_op jit(solution)/shard_map/jit(_where)/select_n | solution.py:132
  67.8 2.2 %pad_maximum_fusion.2 = (bf16[2,2,2,2,1,2,32,256]{7,6,5,2,1,0,4,3:T(8,128)(2,1)}, bf16[2,2,2,2,1,2,32,256]{7,6,5,2,1,0,4,3:T(8,128)(2,1)}) fusion(bf16[2,2,2,1,1,2,32,256]{7,6,5,2,1,0,4,3:T(8,128)(2,1)} %bitcast.18, bf16[2,2,2,1,1,2,32,256]{7,6,5,2,1,0,4,3:T(8,128)(2,1)S(1)} %bitcast.203), kind=kLoop, calls=%fused_computation.39 | loop fusion | flops 524288 | bytes 1572864 | tf_op jit(solution)/shard_map/stack | solution.py:134
  70.4 4.1 %collective-permute-start.6 = (f32[24576]{0:T(1024)S(1)}, f32[24576]{0:T(1024)S(1)}, u32[]{:S(2)}, u32[]{:S(2)}) collective-permute-start(f32[24576]{0:T(1024)S(1)} %pad_maximum_fusion.10), channel_id=1, source_target_pairs={{0,2},{1,3},{2,0},{3,1},{4,6},{5,7},{6,4},{7,5},{8,10},{9,11},{10,... | collective-permute-start | bytes 294920 | tf_op jit(solution)/shard_map/ppermute | solution.py:90
  74.4 2.1 %copy_select_fusion = bf16[2,2,2,2,1,2,32,256]{7,6,5,4,3,2,1,0:T(8,128)(2,1)} fusion(bf16[2,2,2,2,1,2,32,256]{7,6,5,2,1,0,4,3:T(8,128)(2,1)} %get-tuple-element.10, bf16[2,2,2,2,1,2,32,256]{7,6,5,2,1,0,4,3:T(8,128)(2,1)} %get-tuple-element.9, pred[]{:T(512)S(6)} %eq.31), kind=kLoop, calls=%fused_computation.43 | loop fusion | flops 262144 | bytes 1572865 | tf_op jit(solution)/shard_map/jit(_where)/select_n | solution.py:132
  76.6 1.3 collective-permute-done.6
  79.1 4.1 %all-to-all-start.2 = ((f32[8,1,10240]{2,1,0:T(1,128)}), f32[8,1,10240]{2,1,0:T(1,128)}, u32[]{:S(2)}, u32[]{:S(2)}) async-start(f32[8,1,10240]{2,1,0:T(1,128)} %all_to_all.34), calls=%async_computation.2 | async-start | bytes 655360 | tf_op jit(solution)/shard_map/all_to_all | solution.py:98
  83.2 2.7 %pad_maximum_fusion = bf16[64,16,1024]{2,1,0:T(8,128)(2,1)} fusion(bf16[32,16,1024]{2,1,0:T(8,128)(2,1)} %all-to-all-done, bf16[32,16,1024]{2,1,0:T(8,128)(2,1)S(1)} %copy-done.3), kind=kLoop, calls=%fused_computation.11 | loop fusion | flops 1048576 | bytes 4194304 | tf_op jit(solution)/shard_map/concatenate | solution.py:252
  85.9 2.2 %gather_fusion.1 = bf16[32,16,1024]{2,1,0:T(8,128)(2,1)S(1)} fusion(bf16[64,16,1024]{2,1,0:T(8,128)(2,1)} %pad_maximum_fusion, s32[1024]{0:T(1024)S(1)} %pad_clamp_fusion.2), kind=kCustom, calls=%fused_computation.1 | custom fusion | bytes 2097280 | tf_op jit(solution)/shard_map/jit(_take)/gather | solution.py:253
  88.1 1.3 copy.198
  89.4 2.4 %broadcast_select_fusion.1 = bf16[1,512,1024]{1,2,0:T(8,128)(2,1)} fusion(bf16[1,512,1024]{1,2,0:T(8,128)(2,1)} %copy.198, pred[512]{0:T(512)(128)(4,1)S(1)} %broadcast_in_dim.125), kind=kLoop, calls=%fused_computation.36 | loop fusion | flops 524288 | bytes 2097664 | tf_op jit(solution)/shard_map/jit(_take)/select_n | solution.py:253
  91.8 1.3 maximum_select_fusion
  94.0 1.0 slice.178
  95.9 1.1 copy.218
  97.0 1.3 gather_fusion.7
  98.2 1.4 gather_fusion.5
  99.6 1.2 reduce_sum.36
  100.9 1.1 fusion.32
  102.3 1.4 fusion.28
  104.8 10.3 %all-to-all-start.3 = ((f32[2,32,1,144]{3,0,2,1:T(2,128)}), f32[2,32,1,144]{3,0,2,1:T(2,128)S(1)}, u32[]{:S(2)}, u32[]{:S(2)}) async-start(f32[2,32,1,144]{3,0,2,1:T(2,128)} %copy.222), calls=%async_computation.3 | async-start | bytes 131072 | tf_op jit(solution)/shard_map/all_to_all | solution.py:233
  115.2 1.3 fusion.64
  116.5 8.5 %all-to-all-done.3 = f32[2,32,1,144]{3,0,2,1:T(2,128)S(1)} async-done(((f32[2,32,1,144]{3,0,2,1:T(2,128)}), f32[2,32,1,144]{3,0,2,1:T(2,128)S(1)}, u32[]{:S(2)}, u32[]{:S(2)}) %all-to-all-start.3) | async-done | bytes 36896 | tf_op jit(solution)/shard_map/all_to_all | solution.py:233
  126.4 12.7 %all_to_all.46 = bf16[2,1,32,128]{3,0,1,2:T(2,128)(2,1)S(1)} all-to-all(bf16[2,1,32,128]{3,0,1,2:T(2,128)(2,1)S(1)} %copy.233), channel_id=1, replica_groups=mesh['group'=8,'tp'=32] {'tp'}, dimensions={2} | all-to-all | bytes 32768 | tf_op jit(solution)/shard_map/all_to_all | solution.py:257
  139.1 2.0 %fusion = f32[64,32,256]{2,0,1:T(8,128)S(1)} fusion(bf16[64,128,1]{1,0,2:T(8,128)(2,1)S(1)} %bitcast.233, bf16[16,32,8,256]{3,2,1,0:T(8,128)(2,1)} %bitcast.204), kind=kOutput, calls=%fused_computation.8 | convolution fusion | flops 134217728 | bytes 4210688 | tf_op jit(solution)/shard_map/rk,kdc->drc/dot_general | solution.py:259
  141.3 1.5 copy.257
  142.8 2.1 %select_n.375 = f32[16,1,16384]{2,1,0:T(1,128)} reshape(f32[16,1,64,256]{3,2,1,0:T(8,128)S(1)} %get-tuple-element.6) | data formatting | bytes 2097152 | tf_op jit(solution)/shard_map/jit(_where)/select_n | solution.py:87
  145.8 2.6 %add.142 = f32[16,1,16384]{2,1,0:T(1,128)S(1)} add(f32[16,1,16384]{2,1,0:T(1,128)} %select_n.375, f32[16,1,16384]{2,1,0:T(1,128)} %bitcast.68) | non-fusion elementwise | flops 262144 | bytes 3145728 | tf_op jit(solution)/shard_map/add | solution.py:91
  148.5 33.9 %all_to_all.47 = f32[16,1,16384]{2,1,0:T(1,128)S(1)} all-to-all(f32[16,1,16384]{2,1,0:T(1,128)S(1)} %add.142), channel_id=1, replica_groups={{0,2,4,6,8,10,12,14,16,18,20,22,24,26,28,30},{1,3,5,7,9,11,13,15,17,19,..., dimensions={0} | all-to-all | bytes 2097152 | tf_op jit(solution)/shard_map/all_to_all | solution.py:98
  (134 shorter events, 17.6 us)
Async XLA Ops:
  0.0 103.6 %copy-start = (bf16[8192,128]{1,0:T(8,128)(2,1)S(1)}, bf16[8192,128]{1,0:T(8,128)(2,1)}, u32[]{:S(2)}) copy-start(bf16[8192,128]{1,0:T(8,128)(2,1)} %param.14) | copy-start | bytes 6291460
  0.0 13.3 %copy-start.2 = (bf16[4,256,128]{2,1,0:T(8,128)(2,1)S(1)}, bf16[4,256,128]{2,1,0:T(8,128)(2,1)}, u32[]{:S(2)}) copy-start(bf16[4,256,128]{2,1,0:T(8,128)(2,1)} %param.17) | copy-start | bytes 786436
  0.0 38.5 %collective-permute-start = (bf16[2,32,256]{2,1,0:T(8,128)(2,1)}, bf16[2,32,256]{2,1,0:T(8,128)(2,1)S(1)}, u32[]{:S(2)}, u32[]{:S(2)}) collective-permute-start(bf16[2,32,256]{2,1,0:T(8,128)(2,1)} %param.13), channel_id=1, source_target_pairs={{0,16},{1,17},{2,18},{3,19},{4,20},{5,21},{6,22},{7,23},{8,24},{9,... | collective-permute-start | bytes 98312 | tf_op jit(solution)/shard_map/ppermute | solution.py:131
  14.1 1.0 copy-start.8
  15.0 7.0 %copy-start.13 = (s32[1,32]{1,0:T(1,128)S(1)}, s32[1,32]{1,0:T(1,128)}, u32[]{:S(2)}) copy-start(s32[1,32]{1,0:T(1,128)} %param.22) | copy-start | bytes 388
  15.0 7.1 %copy-start.14 = (s32[32]{0:T(128)S(1)}, s32[32]{0:T(128)}, u32[]{:S(2)}) copy-start(s32[32]{0:T(128)} %param.24) | copy-start | bytes 388
  15.0 7.1 %copy-start.11 = (s32[1,1,8,4]{2,3,1,0:T(4,128)S(1)}, s32[1,1,8,4]{2,3,1,0:T(4,128)}, u32[]{:S(2)}) copy-start(s32[1,1,8,4]{2,3,1,0:T(4,128)} %param.23) | copy-start | bytes 388
  15.0 8.4 %copy-start.10 = (bf16[2,32,256]{2,1,0:T(8,128)(2,1)S(1)}, bf16[2,32,256]{2,1,0:T(8,128)(2,1)}, u32[]{:S(2)}) copy-start(bf16[2,32,256]{2,1,0:T(8,128)(2,1)} %param.13) | copy-start | bytes 98308
  16.2 37.7 %all-to-all-start.1 = ((bf16[8,2,328,128]{3,2,1,0:T(8,128)(2,1)}), bf16[8,2,328,128]{3,2,1,0:T(8,128)(2,1)S(1)}, u32[]{:S(2)}, u32[]{:S(2)}) async-start(bf16[8,2,328,128]{3,2,1,0:T(8,128)(2,1)} %pad_maximum_fusion.1), calls=%async_computation.1 | async-start | bytes 2686976 | tf_op jit(solution)/shard_map/all_to_all | solution.py:184
  22.1 40.3 %copy-start.15 = (pred[32]{0:T(512)(128)(4,1)}, pred[32]{0:T(512)(128)(4,1)S(1)}, u32[]{:S(2)}) copy-start(pred[32]{0:T(512)(128)(4,1)S(1)} %get-tuple-element.25) | copy-start | bytes 100
  38.5 6.0 %collective-permute-start.1 = (bf16[2,2,32,256]{3,2,1,0:T(8,128)(2,1)S(1)}, bf16[2,2,32,256]{3,2,1,0:T(8,128)(2,1)S(1)}, u32[]{:S(2)}, u32[]{:S(2)}) collective-permute-start(bf16[2,2,32,256]{3,2,1,0:T(8,128)(2,1)S(1)} %maximum_select_fusion.5), channel_id=1, source_target_pairs={{0,8},{1,9},{2,10},{3,11},{4,12},{5,13},{6,14},{7,15},{8,0},{9,1},... | collective-permute-start | bytes 196616 | tf_op jit(solution)/shard_map/ppermute | solution.py:131
  44.5 5.1 %collective-permute-start.2 = (bf16[2,2,2,32,256]{4,3,2,1,0:T(8,128)(2,1)S(1)}, bf16[2,2,2,32,256]{4,3,2,1,0:T(8,128)(2,1)S(1)}, u32[]{:S(2)}, u32[]{:S(2)}) collective-permute-start(bf16[2,2,2,32,256]{4,3,2,1,0:T(8,128)(2,1)S(1)} %maximum_select_fusion.3), channel_id=1, source_target_pairs={{0,4},{1,5},{2,6},{3,7},{4,0},{5,1},{6,2},{7,3},{8,12},{9,13},{10,... | collective-permute-start | bytes 393224 | tf_op jit(solution)/shard_map/ppermute | solution.py:131
  50.3 15.5 %collective-permute-start.3 = (bf16[2,2,2,2,32,256]{5,4,3,2,1,0:T(8,128)(2,1)}, bf16[2,2,2,2,32,256]{5,4,3,2,1,0:T(8,128)(2,1)}, u32[]{:S(2)}, u32[]{:S(2)}) collective-permute-start(bf16[2,2,2,2,32,256]{5,4,3,2,1,0:T(8,128)(2,1)} %maximum_select_fusion.2), channel_id=1, source_target_pairs={{0,2},{1,3},{2,0},{3,1},{4,6},{5,7},{6,4},{7,5},{8,10},{9,11},{10,... | collective-permute-start | bytes 786440 | tf_op jit(solution)/shard_map/ppermute | solution.py:131
  53.9 5.1 %copy-start.1 = (bf16[8,2,328,128]{3,2,1,0:T(8,128)(2,1)}, bf16[8,2,328,128]{3,2,1,0:T(8,128)(2,1)S(1)}, u32[]{:S(2)}) copy-start(bf16[8,2,328,128]{3,2,1,0:T(8,128)(2,1)S(1)} %all-to-all-done.1) | copy-start | bytes 4030468
  53.9 25.1 %all-to-all-start = ((bf16[32,16,1024]{2,1,0:T(8,128)(2,1)}), bf16[32,16,1024]{2,1,0:T(8,128)(2,1)}, u32[]{:S(2)}, u32[]{:S(2)}) async-start(bf16[32,16,1024]{2,1,0:T(8,128)(2,1)} %select_multiply_fusion), calls=%async_computation | async-start | bytes 2097152 | tf_op jit(solution)/shard_map/all_to_all | solution.py:251
  62.5 2.1 %copy-start.9 = (f32[16,8,2,128]{3,1,2,0:T(8,128)S(1)}, f32[16,8,2,128]{3,1,2,0:T(8,128)}, u32[]{:S(2)}) copy-start(f32[16,8,2,128]{3,1,2,0:T(8,128)} %copy.254) | copy-start | bytes 393220
  62.5 3.3 %copy-start.4 = (bf16[2,2,2,1,2,32,256]{6,5,4,3,2,1,0:T(8,128)(2,1)S(1)}, bf16[2,2,2,1,2,32,256]{6,5,4,3,2,1,0:T(8,128)(2,1)}, u32[]{:S(2)}) copy-start(bf16[2,2,2,1,2,32,256]{6,5,4,3,2,1,0:T(8,128)(2,1)} %copy_select_fusion.1) | copy-start | bytes 786436
  64.6 5.5 %copy-start.6 = (f32[16,1,2,1024]{3,1,0,2:T(1,128)S(1)}, f32[16,1,2,1024]{3,1,0,2:T(1,128)}, u32[]{:S(2)}) copy-start(f32[16,1,2,1024]{3,1,0,2:T(1,128)} %get-tuple-element.13) | copy-start | bytes 393220
  64.6 5.5 %copy-start.7 = (f32[16,1,2,1024]{3,1,0,2:T(1,128)S(1)}, f32[16,1,2,1024]{3,1,0,2:T(1,128)}, u32[]{:S(2)}) copy-start(f32[16,1,2,1024]{3,1,0,2:T(1,128)} %get-tuple-element.14) | copy-start | bytes 393220
  64.6 5.3 %collective-permute-start.5 = (f32[40960]{0:T(1024)S(1)}, f32[40960]{0:T(1024)S(1)}, u32[]{:S(2)}, u32[]{:S(2)}) collective-permute-start(f32[40960]{0:T(1024)S(1)} %pad_maximum_fusion.7), channel_id=1, source_target_pairs={{0,1},{1,0},{2,3},{3,2},{4,5},{5,4},{6,7},{7,6},{8,9},{9,8},{10,11... | collective-permute-start | bytes 491528 | tf_op jit(solution)/shard_map/ppermute | solution.py:90
  67.8 24.0 %collective-permute-start.4 = (bf16[2,2,2,2,2,32,256]{6,5,4,3,2,1,0:T(8,128)(2,1)}, bf16[2,2,2,2,2,32,256]{6,5,4,3,2,1,0:T(8,128)(2,1)}, u32[]{:S(2)}, u32[]{:S(2)}) collective-permute-start(bf16[2,2,2,2,2,32,256]{6,5,4,3,2,1,0:T(8,128)(2,1)} %maximum_select_fusion.1), channel_id=1, source_target_pairs={{0,1},{1,0},{2,3},{3,2},{4,5},{5,4},{6,7},{7,6},{8,9},{9,8},{10,11... | collective-permute-start | bytes 1572872 | tf_op jit(solution)/shard_map/ppermute | solution.py:131
  70.4 7.5 %collective-permute-start.6 = (f32[24576]{0:T(1024)S(1)}, f32[24576]{0:T(1024)S(1)}, u32[]{:S(2)}, u32[]{:S(2)}) collective-permute-start(f32[24576]{0:T(1024)S(1)} %pad_maximum_fusion.10), channel_id=1, source_target_pairs={{0,2},{1,3},{2,0},{3,1},{4,6},{5,7},{6,4},{7,5},{8,10},{9,11},{10,... | collective-permute-start | bytes 294920 | tf_op jit(solution)/shard_map/ppermute | solution.py:90
  74.4 8.7 %copy-start.3 = (bf16[32,16,1024]{2,1,0:T(8,128)(2,1)S(1)}, bf16[32,16,1024]{2,1,0:T(8,128)(2,1)}, u32[]{:S(2)}) copy-start(bf16[32,16,1024]{2,1,0:T(8,128)(2,1)} %param.20) | copy-start | bytes 3145732
  79.1 20.6 %all-to-all-start.2 = ((f32[8,1,10240]{2,1,0:T(1,128)}), f32[8,1,10240]{2,1,0:T(1,128)}, u32[]{:S(2)}, u32[]{:S(2)}) async-start(f32[8,1,10240]{2,1,0:T(1,128)} %all_to_all.34), calls=%async_computation.2 | async-start | bytes 655360 | tf_op jit(solution)/shard_map/all_to_all | solution.py:98
  89.4 2.4 %copy-start.5 = (bf16[2,2,2,2,1,2,32,256]{7,6,5,4,3,2,1,0:T(8,128)(2,1)S(1)}, bf16[2,2,2,2,1,2,32,256]{7,6,5,4,3,2,1,0:T(8,128)(2,1)}, u32[]{:S(2)}) copy-start(bf16[2,2,2,2,1,2,32,256]{7,6,5,4,3,2,1,0:T(8,128)(2,1)} %copy_select_fusion) | copy-start | bytes 1572868
  93.2 7.7 %copy-start.16 = (pred[32]{0:T(512)(128)(4,1)S(1)}, pred[32]{0:T(512)(128)(4,1)}, u32[]{:S(2)}) copy-start(pred[32]{0:T(512)(128)(4,1)} %copy-done.15) | copy-start | bytes 100
  104.1 21.1 %copy-start.12 = (pred[512]{0:T(512)(128)(4,1)S(1)}, pred[512]{0:T(512)(128)(4,1)}, u32[]{:S(2)}) copy-start(pred[512]{0:T(512)(128)(4,1)} %iota_compare_fusion) | copy-start | bytes 1540
  104.8 20.2 %all-to-all-start.3 = ((f32[2,32,1,144]{3,0,2,1:T(2,128)}), f32[2,32,1,144]{3,0,2,1:T(2,128)S(1)}, u32[]{:S(2)}, u32[]{:S(2)}) async-start(f32[2,32,1,144]{3,0,2,1:T(2,128)} %copy.222), calls=%async_computation.3 | async-start | bytes 131072 | tf_op jit(solution)/shard_map/all_to_all | solution.py:233
  142.8 3.0 %collective-permute-start.7 = (f32[262144]{0:T(1024)}, f32[262144]{0:T(1024)}, u32[]{:S(2)}, u32[]{:S(2)}) collective-permute-start(f32[262144]{0:T(1024)} %bitcast.108), channel_id=1, source_target_pairs={{0,1},{1,0},{2,3},{3,2},{4,5},{5,4},{6,7},{7,6},{8,9},{9,8},{10,11... | collective-permute-start | bytes 3145736 | tf_op jit(solution)/shard_map/ppermute | solution.py:90

commit v11 on v8

--- a/solution.py
+++ b/solution.py
@@ -239,14 +239,32 @@
     attended = attend(query_own, ctx_pages, keyval_new, lengths)
     heads_back = lax.all_to_all(attended, "tp", split_axis=2, concat_axis=1, tiled=True)
     out_cols = output_weight.shape[1] // n_tp
-    projected = jnp.einsum(
-        "rk,kdc->drc",
-        heads_back.reshape(step_count * batch_rows, -1),
-        output_weight.reshape(output_weight.shape[0], n_tp, out_cols),
-        preferred_element_type=jnp.float32,
-    )
-    summed, _ = reduce_scatter_tp(
-        projected, jnp.zeros((0,), jnp.float32), column_id, n_tp, SWAP_BITS[:1]
+    core = column_id % 2
+    weight_halves = output_weight.reshape(output_weight.shape[0], n_tp // 2, 2, out_cols)
+    head_rows = heads_back.reshape(step_count * batch_rows, -1)
+    give = jnp.einsum(
+        "rk,kjc->jrc",
+        head_rows,
+        lax.dynamic_index_in_dim(weight_halves, 1 - core, 2, keepdims=False),
+        preferred_element_type=jnp.float32,
+    )
+    got = lax.ppermute(give, "tp", [(t, t ^ 1) for t in range(n_tp)])
+    keep = jnp.einsum(
+        "rk,kjc->jrc",
+        head_rows,
+        lax.dynamic_index_in_dim(weight_halves, core, 2, keepdims=False),
+        preferred_element_type=jnp.float32,
+    )
+    summed = jnp.sum(
+        lax.all_to_all(
+            (keep + got).reshape(n_tp // 2, -1),
+            "tp",
+            0,
+            0,
+            tiled=True,
+            axis_index_groups=stage_groups(n_tp, SWAP_BITS[:1]),
+        ),
+        0,
     )
     return summed.reshape(step_count, batch_rows, out_cols).astype(jnp.bfloat16)
 

time: 177 us -> 189 us (1.068)
  local copies, waits for them, and re-layouts: 31.6 us -> 44.4 us
  blocking collectives: 46.6 us -> 40 us
  starting transfers between devices: 42.7 us -> 47.6 us
    dynamic_slice x0 -> x1, local copies, waits for them, and re-layouts: none -> 9.75 us  [per_device(): lax.dynamic_index_in_dim(weight_halves, core, 2, keepdims=False)]
    all_to_all x2 -> x1, blocking collectives: 46.6 us -> 40 us  [per_device(): lax.all_to_all((keep + got).reshape(n_tp // 2, -1), 'tp', 0, 0, tiled=Tru...]
    reshape x0 -> x1, local copies, waits for them, and re-layouts: none -> 4.52 us  [per_device(): output_weight.reshape(output_weight.shape[0], n_tp // 2, 2, out_cols)]
    all_to_all x0 -> x1, starting transfers between devices: none -> 4.01 us  [per_device(): lax.all_to_all(attended, 'tp', split_axis=2, concat_axis=1, tiled=True)]
    ppermute x0 -> x1, waiting for transfers between devices: none -> 2.65 us  [per_device(): got = lax.ppermute(give, 'tp', [(t, t ^ 1) for t in range(n_tp)])]
    add x2 -> x1, other arithmetic: 2.84 us -> 0.21 us  [reduce_scatter_tp(): parts = keep + got[:give.size].reshape(give.shape)]
    dot_general x1 -> x2, matrix products: 2.02 us -> 4.35 us  [per_device(): jnp.einsum('rk,kjc->jrc', head_rows, lax.dynamic_index_in_dim(weight_halv...]
    all_to_all x0 -> x1, local copies, waits for them, and re-layouts: none -> 2.08 us  [per_device(): lax.all_to_all((keep + got).reshape(n_tp // 2, -1), 'tp', 0, 0, tiled=Tru...]
  transfers between devices with their start and end apart: 10 -> 11, of which waited for: 4 -> 4; matrix products, arithmetic and copies ran while one was open for 29% -> 33% of each run, Pallas kernels for 0% -> 0%
where the time goes in v11:
time: 189 us; the launch traced here: 188 us
  starting transfers between devices  47.6 us (25%)
  local copies, waits for them, and re-layouts  44.4 us (23%)
  blocking collectives  40 us (21%)
  other arithmetic  25.5 us (13%)
  waiting for transfers between devices  19.6 us (10%)
  matrix products  9.65 us (5%)
    all_to_all x1, blocking collectives, per_device(): lax.all_to_all((keep + got).reshape(n_tp // 2, -1), 'tp', 0, 0, tiled=Tru...  40 us
    all_to_all x1, starting transfers between devices, per_device(): lax.all_to_all(query_send, 'tp', split_axis=1, concat_axis=2, tiled=True)  9.93 us
    dynamic_slice x1, local copies, waits for them, and re-layouts, per_device(): lax.dynamic_index_in_dim(weight_halves, core, 2, keepdims=False)  9.75 us
    all_to_all x1, waiting for transfers between devices, per_device(): lax.all_to_all(query_send, 'tp', split_axis=1, concat_axis=2, tiled=True)  8.69 us
    all_to_all x1, starting transfers between devices, all_gather_tp(): lax.all_to_all(jnp.broadcast_to(block[None], (rest,) + block.shape), 'tp'...  8.47 us
    all_to_all x1, waiting for transfers between devices, per_device(): lax.all_to_all(panel_send, 'group', 0, 0, tiled=True)  7.06 us
    all_to_all x1, starting transfers between devices, reduce_scatter_tp(): lax.all_to_all(send, 'tp', 0, 0, tiled=True, axis_index_groups=stage_grou...  6.56 us
    all_to_all x1, starting transfers between devices, per_device(): lax.all_to_all(outgoing, 'group', split_axis=0, concat_axis=0, tiled=True)  6.07 us
  transfers between devices with their start and end apart: 11, of which 4 were waited for; matrix products, arithmetic and copies ran while one was open for 33% of the time, Pallas kernels for 0%

profile of v11, /device:TPU:2, one launch (start us, length us, event | category | flops | bytes accessed | tf_op | source)
XLA Modules:
  0.0 187.9 jit_solution(12381087881398260229)
XLA Ops:
  0.0 1.6 broadcast_in_dim.136
  1.7 8.5 %all-to-all-start.1 = ((bf16[8,2,32,256]{3,2,1,0:T(8,128)(2,1)}), bf16[8,2,32,256]{3,2,1,0:T(8,128)(2,1)}, u32[]{:S(2)}, u32[]{:S(2)}) async-start(bf16[8,2,32,256]{3,2,1,0:T(8,128)(2,1)} %broadcast_in_dim.136), calls=%async_computation.1 | async-start | bytes 524288 | tf_op jit(solution)/shard_map/all_to_all | solution.py:106
  10.1 1.0 fusion.52
  13.1 0.9 constant_dynamic-slice_fusion.1
  14.8 1.4 gather_fusion.3
  17.0 0.8 broadcast_select_fusion.2
  18.2 0.9 fusion.63
  19.9 1.1 broadcast_select_fusion
  21.0 2.5 %pad_maximum_fusion.1 = bf16[8,2,328,128]{3,2,1,0:T(8,128)(2,1)} fusion(bf16[8,2,8,128]{3,2,1,0:T(8,128)(2,1)S(1)} %copy-done.12, bf16[8,2,64,128]{3,2,1,0:T(8,128)(2,1)} %broadcast_select_fusion.2, bf16[8,2,256,128]{3,2,1,0:T(8,128)(2,1)} %broadcast_select_fusion), kind=kLoop, calls=%fused_computation.17 | loop fusion | flops 4030464 | bytes 2686976 | tf_op jit(solution)/shard_map/concatenate | solution.py:159
  24.0 0.8 select_bitcast_fusion
  24.9 6.0 %all-to-all-start.2 = ((bf16[8,2,328,128]{3,2,1,0:T(8,128)(2,1)}), bf16[8,2,328,128]{3,2,1,0:T(8,128)(2,1)S(1)}, u32[]{:S(2)}, u32[]{:S(2)}) async-start(bf16[8,2,328,128]{3,2,1,0:T(8,128)(2,1)} %pad_maximum_fusion.1), calls=%async_computation.2 | async-start | bytes 2686976 | tf_op jit(solution)/shard_map/all_to_all | solution.py:167
  31.9 1.6 copy.293
  33.4 2.8 %gather_fusion = bf16[32,16,1024]{2,1,0:T(8,128)(2,1)} fusion(bf16[32,16,1024]{2,1,0:T(8,128)(2,1)} %param.20, s32[1024]{0:T(1024)S(1)} %pad_clamp_fusion.3), kind=kCustom, calls=%fused_computation | custom fusion | bytes 2097280 | tf_op jit(solution)/shard_map/jit(_take)/gather | solution.py:231
  36.3 2.4 %select_multiply_fusion = bf16[32,16,1024]{2,1,0:T(8,128)(2,1)} fusion(bf16[32,16,1024]{2,1,0:T(8,128)(2,1)} %gather_fusion, pred[32]{0:T(512)(128)(4,1)S(1)} %le.73, bf16[32]{0:T(256)(128)(2,1)S(1)} %reshape.468), kind=kLoop, calls=%fused_computation.36 | loop fusion | flops 1048576 | bytes 2097248 | tf_op jit(solution)/shard_map/mul | solution.py:231
  38.7 2.9 %collective-permute-start = (bf16[8,2,32,256]{3,2,1,0:T(8,128)(2,1)}, bf16[8,2,32,256]{3,2,1,0:T(8,128)(2,1)}, u32[]{:S(2)}, u32[]{:S(2)}) collective-permute-start(bf16[8,2,32,256]{3,2,1,0:T(8,128)(2,1)} %all-to-all-done.1), channel_id=1, source_target_pairs={{0,2},{1,3},{2,0},{3,1},{4,6},{5,7},{6,4},{7,5},{8,10},{9,11},{10,... | collective-permute-start | bytes 786440 | tf_op jit(solution)/shard_map/ppermute | solution.py:116
  41.6 7.1 %all-to-all-done.2 = bf16[8,2,328,128]{3,2,1,0:T(8,128)(2,1)S(1)} async-done(((bf16[8,2,328,128]{3,2,1,0:T(8,128)(2,1)}), bf16[8,2,328,128]{3,2,1,0:T(8,128)(2,1)S(1)}, u32[]{:S(2)}, u32[]{:S(2)}) %all-to-all-start.2) | async-done | bytes 1343520 | tf_op jit(solution)/shard_map/all_to_all | solution.py:167
  48.7 6.1 %all-to-all-start = ((bf16[32,16,1024]{2,1,0:T(8,128)(2,1)}), bf16[32,16,1024]{2,1,0:T(8,128)(2,1)}, u32[]{:S(2)}, u32[]{:S(2)}) async-start(bf16[32,16,1024]{2,1,0:T(8,128)(2,1)} %select_multiply_fusion), calls=%async_computation | async-start | bytes 2097152 | tf_op jit(solution)/shard_map/all_to_all | solution.py:234
  54.7 1.3 slice.171
  56.1 2.1 %gather_fusion.6 = bf16[32,256,128]{2,1,0:T(8,128)(2,1)} fusion(bf16[16,256,128]{2,1,0:T(8,128)(2,1)S(1)} %slice.171, s32[1024]{0:T(1024)S(1)} %pad_clamp_fusion), kind=kCustom, calls=%fused_computation.6 | custom fusion | bytes 4194432 | tf_op jit(solution)/shard_map/jit(_take)/gather | solution.py:175
  58.2 2.1 %fusion.2 = f32[32,128,2]{1,2,0:T(2,128)S(1)} fusion(bf16[32,256,128]{2,1,0:T(8,128)(2,1)} %gather_fusion.6, pred[32]{0:T(512)(128)(4,1)S(1)} %get-tuple-element.19, bf16[2,32,256]{2,1,0:T(8,128)(2,1)S(1)} %copy-done.14), kind=kOutput, calls=%fused_computation.11 | convolution fusion | flops 5242880 | bytes 2162720 | tf_op jit(solution)/shard_map/srd,rdk->srk/dot_general | solution.py:184
  61.1 4.5 %reshape.446 = bf16[128,16,2,256]{3,2,1,0:T(2,128)(2,1)} reshape(bf16[128,8192]{1,0:T(8,128)(2,1)} %param.16) | data formatting | bytes 4194304 | tf_op jit(solution)/shard_map/reshape | solution.py:243
  65.6 2.1 %maximum_select_fusion.2 = bf16[8,2,2,32,256]{4,3,2,0,1:T(8,128)(2,1)} fusion(bf16[8,1,2,32,256]{4,3,2,0,1:T(8,128)(2,1)} %bitcast.11, bf16[8,1,2,32,256]{4,3,2,0,1:T(8,128)(2,1)} %bitcast.10, pred[]{:T(512)S(6)} %eq.17), kind=kLoop, calls=%fused_computation.40 | loop fusion | flops 786432 | bytes 1048577 | tf_op jit(solution)/shard_map/jit(_where)/select_n | solution.py:117
  68.7 3.0 %collective-permute-start.3 = (f32[24576]{0:T(1024)S(1)}, f32[24576]{0:T(1024)S(1)}, u32[]{:S(2)}, u32[]{:S(2)}) collective-permute-start(f32[24576]{0:T(1024)S(1)} %pad_maximum_fusion.4), channel_id=1, source_target_pairs={{0,2},{1,3},{2,0},{3,1},{4,6},{5,7},{6,4},{7,5},{8,10},{9,11},{10,... | collective-permute-start | bytes 294920 | tf_op jit(solution)/shard_map/ppermute | solution.py:90
  71.6 2.1 %maximum_select_fusion.1 = bf16[8,2,1,2,32,256]{5,4,3,0,2,1:T(8,128)(2,1)} fusion(bf16[8,1,1,2,32,256]{5,4,3,0,2,1:T(8,128)(2,1)} %bitcast.9, bf16[8,1,1,2,32,256]{5,4,3,0,2,1:T(8,128)(2,1)} %bitcast.8, pred[]{:T(512)S(6)} %eq.17), kind=kLoop, calls=%fused_computation.39 | loop fusion | flops 786432 | bytes 1048577 | tf_op jit(solution)/shard_map/jit(_where)/select_n | solution.py:117
  73.8 1.2 collective-permute-done.3
  75.2 1.0 all_to_all.40
  76.1 6.6 %all-to-all-start.3 = ((f32[8,1,10240]{2,1,0:T(1,128)}), f32[8,1,10240]{2,1,0:T(1,128)}, u32[]{:S(2)}, u32[]{:S(2)}) async-start(f32[8,1,10240]{2,1,0:T(1,128)} %all_to_all.40), calls=%async_computation.3 | async-start | bytes 655360 | tf_op jit(solution)/shard_map/all_to_all | solution.py:98
  82.7 2.7 %pad_maximum_fusion = bf16[64,16,1024]{2,1,0:T(8,128)(2,1)} fusion(bf16[32,16,1024]{2,1,0:T(8,128)(2,1)} %all-to-all-done, bf16[32,16,1024]{2,1,0:T(8,128)(2,1)S(1)} %copy-done.4), kind=kLoop, calls=%fused_computation.8 | loop fusion | flops 1048576 | bytes 4194304 | tf_op jit(solution)/shard_map/concatenate | solution.py:235
  85.4 2.2 %gather_fusion.1 = bf16[32,16,1024]{2,1,0:T(8,128)(2,1)S(1)} fusion(bf16[64,16,1024]{2,1,0:T(8,128)(2,1)} %pad_maximum_fusion, s32[1024]{0:T(1024)S(1)} %pad_clamp_fusion.2), kind=kCustom, calls=%fused_computation.1 | custom fusion | bytes 2097280 | tf_op jit(solution)/shard_map/jit(_take)/gather | solution.py:236
  87.6 1.3 copy.237
  88.9 2.3 %broadcast_select_fusion.1 = bf16[1,512,1024]{1,2,0:T(8,128)(2,1)} fusion(bf16[1,512,1024]{1,2,0:T(8,128)(2,1)} %copy.237, pred[512]{0:T(512)(128)(4,1)S(1)} %broadcast_in_dim.131), kind=kLoop, calls=%fused_computation.38 | loop fusion | flops 524288 | bytes 2097664 | tf_op jit(solution)/shard_map/jit(_take)/select_n | solution.py:236
  91.2 0.8 slice.180
  92.1 1.0 slice.168
  94.0 1.4 gather_fusion.5
  95.4 1.6 maximum_select_fusion
  97.2 1.2 reduce_sum.36
  98.9 1.4 fusion.26
  101.5 9.9 %all-to-all-start.4 = ((f32[2,32,1,144]{3,0,2,1:T(2,128)}), f32[2,32,1,144]{3,0,2,1:T(2,128)S(1)}, u32[]{:S(2)}, u32[]{:S(2)}) async-start(f32[2,32,1,144]{3,0,2,1:T(2,128)} %copy.259), calls=%async_computation.4 | async-start | bytes 131072 | tf_op jit(solution)/shard_map/all_to_all | solution.py:216
  111.4 1.3 fusion.62
  112.7 8.7 %all-to-all-done.4 = f32[2,32,1,144]{3,0,2,1:T(2,128)S(1)} async-done(((f32[2,32,1,144]{3,0,2,1:T(2,128)}), f32[2,32,1,144]{3,0,2,1:T(2,128)S(1)}, u32[]{:S(2)}, u32[]{:S(2)}) %all-to-all-start.4) | async-done | bytes 36896 | tf_op jit(solution)/shard_map/all_to_all | solution.py:216
  123.5 4.0 %all-to-all-start.5 = ((bf16[2,1,32,128]{3,0,1,2:T(2,128)(2,1)}), bf16[2,1,32,128]{3,0,1,2:T(2,128)(2,1)S(1)}, u32[]{:S(2)}, u32[]{:S(2)}) async-start(bf16[2,1,32,128]{3,0,1,2:T(2,128)(2,1)} %copy.270), calls=%async_computation.5 | async-start | bytes 32768 | tf_op jit(solution)/shard_map/all_to_all | solution.py:240
  127.5 9.7 %constant_dynamic-slice_fusion.2 = (bf16[128,16,1,256]{3,2,1,0:T(2,128)(2,1)}, bf16[128,16,1,256]{3,2,1,0:T(2,128)(2,1)}) fusion(bf16[128,16,2,256]{3,2,1,0:T(2,128)(2,1)} %reshape.446, s32[]{:T(128)S(6)} %select_n.194, s32[]{:T(128)S(6)} %select_n.230), kind=kLoop, calls=%fused_computation.113 | loop fusion | bytes 4194312 | tf_op jit(solution)/shard_map/jit(dynamic_index_in_dim)/dynamic_slice | solution.py:255
  137.2 3.0 %convolution_bitcast_fusion = f32[16,64,256]{2,1,0:T(8,128)S(1)} fusion(bf16[64,128,1]{1,0,2:T(8,128)(2,1)S(1)} %bitcast.207, bf16[128,16,1,256]{3,2,1,0:T(2,128)(2,1)} %get-tuple-element.6), kind=kOutput, calls=%fused_computation.14 | convolution fusion | flops 67108864 | bytes 2113536 | tf_op jit(solution)/shard_map/rk,kjc->jrc/dot_general | solution.py:245
  140.4 2.6 %collective-permute-done.4 = f32[16,64,256]{2,1,0:T(8,128)S(1)} collective-permute-done((f32[16,64,256]{2,1,0:T(8,128)S(1)}, f32[16,64,256]{2,1,0:T(8,128)S(1)}, u32[]{:S(2)}, u32[]{:S(2)}) %collective-permute-start.4) | collective-permute-done | bytes 1048608 | tf_op jit(solution)/shard_map/ppermute | solution.py:251
  143.0 1.3 fusion.5
  144.3 2.1 %all_to_all.47 = f32[16,1,16384]{2,1,0:T(1,128)} reshape(f32[16,64,256]{2,1,0:T(8,128)S(1)} %fusion.5) | data formatting | bytes 2097152 | tf_op jit(solution)/shard_map/all_to_all | solution.py:259
  146.4 40.0 %all_to_all.55 = f32[16,1,16384]{2,1,0:T(1,128)S(1)} all-to-all(f32[16,1,16384]{2,1,0:T(1,128)} %all_to_all.47), channel_id=1, replica_groups={{0,2,4,6,8,10,12,14,16,18,20,22,24,26,28,30},{1,3,5,7,9,11,13,15,17,19,..., dimensions={0} | all-to-all | bytes 2097152 | tf_op jit(solution)/shard_map/all_to_all | solution.py:259
  186.4 0.8 reduce_sum.39
  (133 shorter events, 12.9 us)
Async XLA Ops:
  0.0 100.3 %copy-start = (bf16[8192,128]{1,0:T(8,128)(2,1)S(1)}, bf16[8192,128]{1,0:T(8,128)(2,1)}, u32[]{:S(2)}) copy-start(bf16[8192,128]{1,0:T(8,128)(2,1)} %param.14) | copy-start | bytes 6291460
  0.0 17.8 %copy-start.13 = (bf16[2,32,256]{2,1,0:T(8,128)(2,1)S(1)}, bf16[2,32,256]{2,1,0:T(8,128)(2,1)}, u32[]{:S(2)}) copy-start(bf16[2,32,256]{2,1,0:T(8,128)(2,1)} %param.13) | copy-start | bytes 98308
  0.0 17.8 %copy-start.10 = (bf16[256,1024]{1,0:T(8,128)(2,1)S(1)}, bf16[256,1024]{1,0:T(8,128)(2,1)}, u32[]{:S(2)}) copy-start(bf16[256,1024]{1,0:T(8,128)(2,1)} %param.15) | copy-start | bytes 1572868
  1.7 23.2 %all-to-all-start.1 = ((bf16[8,2,32,256]{3,2,1,0:T(8,128)(2,1)}), bf16[8,2,32,256]{3,2,1,0:T(8,128)(2,1)}, u32[]{:S(2)}, u32[]{:S(2)}) async-start(bf16[8,2,32,256]{3,2,1,0:T(8,128)(2,1)} %broadcast_in_dim.136), calls=%async_computation.1 | async-start | bytes 524288 | tf_op jit(solution)/shard_map/all_to_all | solution.py:106
  10.1 8.9 %copy-start.3 = (bf16[4,256,128]{2,1,0:T(8,128)(2,1)S(1)}, bf16[4,256,128]{2,1,0:T(8,128)(2,1)}, u32[]{:S(2)}) copy-start(bf16[4,256,128]{2,1,0:T(8,128)(2,1)} %param.17) | copy-start | bytes 786436
  19.1 5.0 %copy-start.6 = (f32[16,1,2,1024]{3,1,0,2:T(1,128)}, f32[16,1,2,1024]{3,1,0,2:T(1,128)S(1)}, u32[]{:S(2)}) copy-start(f32[16,1,2,1024]{3,1,0,2:T(1,128)S(1)} %get-tuple-element.9) | copy-start | bytes 393220
  19.8 1.2 copy-start.12
  19.8 3.7 %copy-start.15 = (s32[1,1,8,4]{2,3,1,0:T(4,128)S(1)}, s32[1,1,8,4]{2,3,1,0:T(4,128)}, u32[]{:S(2)}) copy-start(s32[1,1,8,4]{2,3,1,0:T(4,128)} %param.23) | copy-start | bytes 388
  19.8 4.2 %copy-start.8 = (f32[16,1,2,1024]{3,1,0,2:T(1,128)S(1)}, f32[16,1,2,1024]{3,1,0,2:T(1,128)}, u32[]{:S(2)}) copy-start(f32[16,1,2,1024]{3,1,0,2:T(1,128)} %get-tuple-element.10) | copy-start | bytes 393220
  24.0 7.7 %copy-start.17 = (pred[1,1,8,4]{2,3,1,0:T(4,128)(4,1)S(1)}, pred[1,1,8,4]{2,3,1,0:T(4,128)(4,1)}, u32[]{:S(2)}) copy-start(pred[1,1,8,4]{2,3,1,0:T(4,128)(4,1)} %get-tuple-element.16) | copy-start | bytes 100
  24.8 11.4 %copy-start.19 = (s32[32]{0:T(128)S(1)}, s32[32]{0:T(128)}, u32[]{:S(2)}) copy-start(s32[32]{0:T(128)} %param.24) | copy-start | bytes 388
  24.8 11.4 %copy-start.18 = (s32[1,32]{1,0:T(1,128)S(1)}, s32[1,32]{1,0:T(1,128)}, u32[]{:S(2)}) copy-start(s32[1,32]{1,0:T(1,128)} %param.22) | copy-start | bytes 388
  24.9 23.8 %all-to-all-start.2 = ((bf16[8,2,328,128]{3,2,1,0:T(8,128)(2,1)}), bf16[8,2,328,128]{3,2,1,0:T(8,128)(2,1)S(1)}, u32[]{:S(2)}, u32[]{:S(2)}) async-start(bf16[8,2,328,128]{3,2,1,0:T(8,128)(2,1)} %pad_maximum_fusion.1), calls=%async_computation.2 | async-start | bytes 2686976 | tf_op jit(solution)/shard_map/all_to_all | solution.py:167
  36.3 21.9 %copy-start.20 = (pred[32]{0:T(512)(128)(4,1)}, pred[32]{0:T(512)(128)(4,1)S(1)}, u32[]{:S(2)}) copy-start(pred[32]{0:T(512)(128)(4,1)S(1)} %get-tuple-element.19) | copy-start | bytes 100
  38.7 26.9 %collective-permute-start = (bf16[8,2,32,256]{3,2,1,0:T(8,128)(2,1)}, bf16[8,2,32,256]{3,2,1,0:T(8,128)(2,1)}, u32[]{:S(2)}, u32[]{:S(2)}) collective-permute-start(bf16[8,2,32,256]{3,2,1,0:T(8,128)(2,1)} %all-to-all-done.1), channel_id=1, source_target_pairs={{0,2},{1,3},{2,0},{3,1},{4,6},{5,7},{6,4},{7,5},{8,10},{9,11},{10,... | collective-permute-start | bytes 786440 | tf_op jit(solution)/shard_map/ppermute | solution.py:116
  48.7 6.1 %copy-start.1 = (bf16[8,2,328,128]{3,2,1,0:T(8,128)(2,1)}, bf16[8,2,328,128]{3,2,1,0:T(8,128)(2,1)S(1)}, u32[]{:S(2)}) copy-start(bf16[8,2,328,128]{3,2,1,0:T(8,128)(2,1)S(1)} %all-to-all-done.2) | copy-start | bytes 4030468
  48.7 27.5 %all-to-all-start = ((bf16[32,16,1024]{2,1,0:T(8,128)(2,1)}), bf16[32,16,1024]{2,1,0:T(8,128)(2,1)}, u32[]{:S(2)}, u32[]{:S(2)}) async-start(bf16[32,16,1024]{2,1,0:T(8,128)(2,1)} %select_multiply_fusion), calls=%async_computation | async-start | bytes 2097152 | tf_op jit(solution)/shard_map/all_to_all | solution.py:234
  56.0 2.2 %copy-start.14 = (bf16[2,32,256]{2,1,0:T(8,128)(2,1)S(1)}, bf16[2,32,256]{2,1,0:T(8,128)(2,1)}, u32[]{:S(2)}) copy-start(bf16[2,32,256]{2,1,0:T(8,128)(2,1)} %param.13) | copy-start | bytes 98308
  58.2 2.1 %copy-start.11 = (f32[16,8,2,128]{3,1,2,0:T(8,128)S(1)}, f32[16,8,2,128]{3,1,2,0:T(8,128)}, u32[]{:S(2)}) copy-start(f32[16,8,2,128]{3,1,2,0:T(8,128)} %copy.293) | copy-start | bytes 393220
  60.3 7.9 %collective-permute-start.2 = (f32[40960]{0:T(1024)S(1)}, f32[40960]{0:T(1024)S(1)}, u32[]{:S(2)}, u32[]{:S(2)}) collective-permute-start(f32[40960]{0:T(1024)S(1)} %pad_maximum_fusion.3), channel_id=1, source_target_pairs={{0,1},{1,0},{2,3},{3,2},{4,5},{5,4},{6,7},{7,6},{8,9},{9,8},{10,11... | collective-permute-start | bytes 491528 | tf_op jit(solution)/shard_map/ppermute | solution.py:90
  61.1 7.2 %copy-start.7 = (f32[16,1,2,1024]{3,1,0,2:T(1,128)S(1)}, f32[16,1,2,1024]{3,1,0,2:T(1,128)}, u32[]{:S(2)}) copy-start(f32[16,1,2,1024]{3,1,0,2:T(1,128)} %copy-done.6) | copy-start | bytes 393220
  61.1 7.2 %copy-start.9 = (f32[16,1,2,1024]{3,1,0,2:T(1,128)S(1)}, f32[16,1,2,1024]{3,1,0,2:T(1,128)}, u32[]{:S(2)}) copy-start(f32[16,1,2,1024]{3,1,0,2:T(1,128)} %get-tuple-element.10) | copy-start | bytes 393220
  67.7 27.7 %collective-permute-start.1 = (bf16[8,2,2,32,256]{4,3,2,0,1:T(8,128)(2,1)}, bf16[8,2,2,32,256]{4,3,2,0,1:T(8,128)(2,1)}, u32[]{:S(2)}, u32[]{:S(2)}) collective-permute-start(bf16[8,2,2,32,256]{4,3,2,0,1:T(8,128)(2,1)} %maximum_select_fusion.2), channel_id=1, source_target_pairs={{0,1},{1,0},{2,3},{3,2},{4,5},{5,4},{6,7},{7,6},{8,9},{9,8},{10,11... | collective-permute-start | bytes 1572872 | tf_op jit(solution)/shard_map/ppermute | solution.py:116
  68.6 14.1 %copy-start.4 = (bf16[32,16,1024]{2,1,0:T(8,128)(2,1)S(1)}, bf16[32,16,1024]{2,1,0:T(8,128)(2,1)}, u32[]{:S(2)}) copy-start(bf16[32,16,1024]{2,1,0:T(8,128)(2,1)} %param.20) | copy-start | bytes 3145732
  68.7 6.3 %collective-permute-start.3 = (f32[24576]{0:T(1024)S(1)}, f32[24576]{0:T(1024)S(1)}, u32[]{:S(2)}, u32[]{:S(2)}) collective-permute-start(f32[24576]{0:T(1024)S(1)} %pad_maximum_fusion.4), channel_id=1, source_target_pairs={{0,2},{1,3},{2,0},{3,1},{4,6},{5,7},{6,4},{7,5},{8,10},{9,11},{10,... | collective-permute-start | bytes 294920 | tf_op jit(solution)/shard_map/ppermute | solution.py:90
  76.1 21.0 %all-to-all-start.3 = ((f32[8,1,10240]{2,1,0:T(1,128)}), f32[8,1,10240]{2,1,0:T(1,128)}, u32[]{:S(2)}, u32[]{:S(2)}) async-start(f32[8,1,10240]{2,1,0:T(1,128)} %all_to_all.40), calls=%async_computation.3 | async-start | bytes 655360 | tf_op jit(solution)/shard_map/all_to_all | solution.py:98
  91.2 4.2 %copy-start.5 = (bf16[8,2,1,2,32,256]{5,4,3,0,2,1:T(8,128)(2,1)S(1)}, bf16[8,2,1,2,32,256]{5,4,3,0,2,1:T(8,128)(2,1)}, u32[]{:S(2)}) copy-start(bf16[8,2,1,2,32,256]{5,4,3,0,2,1:T(8,128)(2,1)} %maximum_select_fusion.1) | copy-start | bytes 1572868
  97.0 1.5 copy-start.21
  100.8 21.0 %copy-start.16 = (pred[512]{0:T(512)(128)(4,1)S(1)}, pred[512]{0:T(512)(128)(4,1)}, u32[]{:S(2)}) copy-start(pred[512]{0:T(512)(128)(4,1)} %iota_compare_fusion) | copy-start | bytes 1540
  101.5 19.9 %all-to-all-start.4 = ((f32[2,32,1,144]{3,0,2,1:T(2,128)}), f32[2,32,1,144]{3,0,2,1:T(2,128)S(1)}, u32[]{:S(2)}, u32[]{:S(2)}) async-start(f32[2,32,1,144]{3,0,2,1:T(2,128)} %copy.259), calls=%async_computation.4 | async-start | bytes 131072 | tf_op jit(solution)/shard_map/all_to_all | solution.py:216
  123.5 13.8 %all-to-all-start.5 = ((bf16[2,1,32,128]{3,0,1,2:T(2,128)(2,1)}), bf16[2,1,32,128]{3,0,1,2:T(2,128)(2,1)S(1)}, u32[]{:S(2)}, u32[]{:S(2)}) async-start(bf16[2,1,32,128]{3,0,1,2:T(2,128)(2,1)} %copy.270), calls=%async_computation.5 | async-start | bytes 32768 | tf_op jit(solution)/shard_map/all_to_all | solution.py:240
  137.2 5.8 %copy-start.2 = (bf16[128,16,1,256]{3,2,1,0:T(2,128)(2,1)S(1)}, bf16[128,16,1,256]{3,2,1,0:T(2,128)(2,1)}, u32[]{:S(2)}) copy-start(bf16[128,16,1,256]{3,2,1,0:T(2,128)(2,1)} %get-tuple-element.5) | copy-start | bytes 3145732
  140.3 2.7 %collective-permute-start.4 = (f32[16,64,256]{2,1,0:T(8,128)S(1)}, f32[16,64,256]{2,1,0:T(8,128)S(1)}, u32[]{:S(2)}, u32[]{:S(2)}) collective-permute-start(f32[16,64,256]{2,1,0:T(8,128)S(1)} %convolution_bitcast_fusion), channel_id=1, source_target_pairs={{0,1},{1,0},{2,3},{3,2},{4,5},{5,4},{6,7},{7,6},{8,9},{9,8},{10,11... | collective-permute-start | bytes 3145736 | tf_op jit(solution)/shard_map/ppermute | solution.py:251

commit v12 on v8

--- a/solution.py
+++ b/solution.py
@@ -120,6 +120,45 @@
             jnp.stack([other, gathered], 1 + done),
         )
     return gathered.reshape((n_tp,) + block.shape)
+
+
+def hidden_and_key_values_tp(hidden, key_value_part, column_id, n_tp):
+    for bit in SWAP_BITS:
+        mine = (column_id // bit) % 2
+        split = key_value_part.reshape((-1, 2) + key_value_part.shape[1:])
+        keep = jnp.where(mine == 0, split[:, 0], split[:, 1])
+        give = jnp.where(mine == 0, split[:, 1], split[:, 0])
+        key_value_part = keep + lax.ppermute(give, "tp", [(t, t ^ bit) for t in range(n_tp)])
+    rest = key_value_part.shape[0]
+    send = jnp.concatenate(
+        [
+            jnp.broadcast_to(hidden.astype(jnp.float32).reshape(1, -1), (rest, hidden.size)),
+            key_value_part.reshape(rest, -1),
+        ],
+        -1,
+    ).reshape(rest, 1, -1)
+    arrived = lax.all_to_all(
+        send, "tp", 0, 0, tiled=True, axis_index_groups=stage_groups(n_tp, SWAP_BITS)
+    ).reshape(rest, -1)
+    key_value_total = jnp.sum(arrived[:, hidden.size :], 0)
+    gathered = arrived[:, : hidden.size].astype(hidden.dtype).reshape((rest,) + hidden.shape)
+    for done, bit in enumerate(reversed(SWAP_BITS)):
+        mine = (column_id // bit) % 2
+        other = lax.ppermute(gathered, "tp", [(t, t ^ bit) for t in range(n_tp)])
+        gathered = jnp.where(
+            mine == 0,
+            jnp.stack([gathered, other], 1 + done),
+            jnp.stack([other, gathered], 1 + done),
+        )
+    return gathered.reshape((n_tp,) + hidden.shape), key_value_total
+
+
+def all_reduce_tp(value, n_tp):
+    bit = 1
+    while bit < n_tp:
+        value = value + lax.ppermute(value, "tp", [(t, t ^ bit) for t in range(n_tp)])
+        bit *= 2
+    return value
 
 
 def per_device(
@@ -176,16 +215,16 @@
     upq_rows = jnp.take(upq_recv, request_adapter_entry, axis=0)
     upv_rows = jnp.take(upv_recv, request_adapter_entry, axis=0)
 
-    hidden_sent = all_gather_tp(hidden, column_id, n_tp)
+    key_value_part = jnp.einsum(
+        "srd,dc->rsc", hidden, key_value_weight, preferred_element_type=jnp.float32
+    )
+    hidden_sent, kv_total = hidden_and_key_values_tp(hidden, key_value_part, column_id, n_tp)
     hidden_full = jnp.transpose(hidden_sent, (1, 2, 0, 3)).reshape(
         step_count, batch_rows, n_tp * width_local
     )
 
     shrink_part = jnp.einsum("srd,rdk->srk", hidden, down_rows, preferred_element_type=jnp.float32)
-    key_value_part = jnp.einsum(
-        "srd,dc->rsc", hidden, key_value_weight, preferred_element_type=jnp.float32
-    )
-    kv_total, shrink_total = reduce_scatter_tp(key_value_part, shrink_part, column_id, n_tp)
+    shrink_total = all_reduce_tp(shrink_part, n_tp)
     key_value_plain = kv_total.reshape(batch_own, step_count, 2 * key_span_width)
     down_projected_low = shrink_total.astype(jnp.bfloat16)
 

time: 177 us -> 192 us (1.085)
  waiting for transfers between devices: 18.6 us -> 31.6 us
  local copies, waits for them, and re-layouts: 31.6 us -> 34.6 us
  other arithmetic: 26.6 us -> 24.5 us
    ppermute x2 -> x9, starting transfers between devices: 3.36 us -> 18 us  [the longest x5 12.2 us: all_reduce_tp(): lax.ppermute(value, 'tp', [(t, t ^ bit) for t in range(n_tp)])]
    ppermute x2 -> x9, waiting for transfers between devices: 0.01 us -> 12.6 us  [the longest x2 4.34 us: hidden_and_key_values_tp(): lax.ppermute(give, 'tp', [(t, t ^ bit) for t in range(n_tp)])]
    all_to_all x1, waiting for transfers between devices: 0.01 us -> 9.01 us  [per_device(): lax.all_to_all(outgoing, 'group', split_axis=0, concat_axis=0, tiled=True)]
    all_to_all x2 -> x1, starting transfers between devices: 15 us -> 7.66 us  [hidden_and_key_values_tp(): lax.all_to_all(send, 'tp', 0, 0, tiled=True, axis_index_groups=stage_grou...]
    all_to_all x1, waiting for transfers between devices: 6.95 us -> 0.01 us  [per_device(): lax.all_to_all(panel_send, 'group', 0, 0, tiled=True)]
    all_to_all x1, starting transfers between devices: 9.17 us -> 5.91 us  [per_device(): lax.all_to_all(query_send, 'tp', split_axis=1, concat_axis=2, tiled=True)]
    ppermute x3 -> x1, starting transfers between devices: 3.08 us -> 0.01 us  [reduce_scatter_tp(): got = lax.ppermute(sent, 'tp', [(t, t ^ bit) for t in range(n_tp)])]
    reshape x1 -> x4, local copies, waits for them, and re-layouts: 0.15 us -> 3.01 us  [the longest x2 1.78 us: hidden_and_key_values_tp(): split = key_value_part.reshape((-1, 2) + key_value_part.shape[1:])]
  transfers between devices with their start and end apart: 10 -> 14, of which waited for: 4 -> 7; matrix products, arithmetic and copies ran while one was open for 29% -> 26% of each run, Pallas kernels for 0% -> 0%
where the time goes in v12:
time: 192 us; the launch traced here: 191 us
  blocking collectives  46.6 us (24%)
  starting transfers between devices  43.5 us (23%)
  local copies, waits for them, and re-layouts  34.6 us (18%)
  waiting for transfers between devices  31.6 us (16%)
  other arithmetic  24.5 us (13%)
  matrix products  9.21 us (5%)
    all_to_all x1, blocking collectives, reduce_scatter_tp(): lax.all_to_all(send, 'tp', 0, 0, tiled=True, axis_index_groups=stage_grou...  33.9 us
    all_to_all x1, blocking collectives, per_device(): lax.all_to_all(attended, 'tp', split_axis=2, concat_axis=1, tiled=True)  12.7 us
    ppermute x5, starting transfers between devices, all_reduce_tp(): lax.ppermute(value, 'tp', [(t, t ^ bit) for t in range(n_tp)])  12.2 us
    all_to_all x1, waiting for transfers between devices, per_device(): lax.all_to_all(query_send, 'tp', split_axis=1, concat_axis=2, tiled=True)  9.11 us
    all_to_all x1, waiting for transfers between devices, per_device(): lax.all_to_all(outgoing, 'group', split_axis=0, concat_axis=0, tiled=True)  9.01 us
    all_to_all x1, starting transfers between devices, hidden_and_key_values_tp(): lax.all_to_all(send, 'tp', 0, 0, tiled=True, axis_index_groups=stage_grou...  7.66 us
    all_to_all x1, starting transfers between devices, per_device(): lax.all_to_all(outgoing, 'group', split_axis=0, concat_axis=0, tiled=True)  6.01 us
    all_to_all x1, starting transfers between devices, per_device(): lax.all_to_all(query_send, 'tp', split_axis=1, concat_axis=2, tiled=True)  5.91 us
  transfers between devices with their start and end apart: 14, of which 7 were waited for; matrix products, arithmetic and copies ran while one was open for 26% of the time, Pallas kernels for 0%

profile of v12, /device:TPU:2, one launch (start us, length us, event | category | flops | bytes accessed | tf_op | source)
XLA Modules:
  0.0 191.2 jit_solution(6613681475260947069)
XLA Ops:
  0.0 1.4 convolution_bitcast_fusion
  3.9 0.9 constant_dynamic-slice_fusion
  8.8 1.2 pad_maximum_fusion.1
  10.0 5.9 %all-to-all-start.2 = ((bf16[8,2,328,128]{3,2,1,0:T(8,128)(2,1)}), bf16[8,2,328,128]{3,2,1,0:T(8,128)(2,1)S(1)}, u32[]{:S(2)}, u32[]{:S(2)}) async-start(bf16[8,2,328,128]{3,2,1,0:T(8,128)(2,1)} %pad_maximum_fusion.1), calls=%async_computation.2 | async-start | bytes 2686976 | tf_op jit(solution)/shard_map/all_to_all | solution.py:206
  17.6 2.9 %gather_fusion = bf16[32,16,1024]{2,1,0:T(8,128)(2,1)} fusion(bf16[32,16,1024]{2,1,0:T(8,128)(2,1)} %param.20, s32[1024]{0:T(1024)S(1)} %pad_clamp_fusion.3), kind=kCustom, calls=%fused_computation | custom fusion | bytes 2097280 | tf_op jit(solution)/shard_map/jit(_take)/gather | solution.py:270
  20.5 2.4 %select_multiply_fusion = bf16[32,16,1024]{2,1,0:T(8,128)(2,1)} fusion(bf16[32,16,1024]{2,1,0:T(8,128)(2,1)} %gather_fusion, pred[32]{0:T(512)(128)(4,1)S(1)} %le.73, bf16[32]{0:T(256)(128)(2,1)S(1)} %reshape.464), kind=kLoop, calls=%fused_computation.35 | loop fusion | flops 1048576 | bytes 2097248 | tf_op jit(solution)/shard_map/mul | solution.py:270
  23.0 1.8 fusion.36
  24.7 1.6 reshape.442
  26.4 1.1 fusion.70
  27.5 3.0 %collective-permute-start.1 = (f32[8,2,1024]{2,0,1:T(8,128)S(1)}, f32[8,2,1024]{2,0,1:T(8,128)S(1)}, u32[]{:S(2)}, u32[]{:S(2)}) collective-permute-start(f32[8,2,1024]{2,0,1:T(8,128)S(1)} %select_bitcast_fusion), channel_id=1, source_target_pairs={{0,2},{1,3},{2,0},{3,1},{4,6},{5,7},{6,4},{7,5},{8,10},{9,11},{10,... | collective-permute-start | bytes 196616 | tf_op jit(solution)/shard_map/ppermute | solution.py:131
  31.1 4.3 %collective-permute-done.1 = f32[8,2,1024]{2,0,1:T(8,128)S(1)} collective-permute-done((f32[8,2,1024]{2,0,1:T(8,128)S(1)}, f32[8,2,1024]{2,0,1:T(8,128)S(1)}, u32[]{:S(2)}, u32[]{:S(2)}) %collective-permute-start.1) | collective-permute-done | bytes 65568 | tf_op jit(solution)/shard_map/ppermute | solution.py:131
  36.1 6.0 %all-to-all-start = ((bf16[32,16,1024]{2,1,0:T(8,128)(2,1)}), bf16[32,16,1024]{2,1,0:T(8,128)(2,1)}, u32[]{:S(2)}, u32[]{:S(2)}) async-start(bf16[32,16,1024]{2,1,0:T(8,128)(2,1)} %select_multiply_fusion), calls=%async_computation | async-start | bytes 2097152 | tf_op jit(solution)/shard_map/all_to_all | solution.py:273
  43.0 1.2 reshape.444
  44.2 1.3 slice.113
  45.5 2.1 %gather_fusion.6 = bf16[32,256,128]{2,1,0:T(8,128)(2,1)} fusion(bf16[16,256,128]{2,1,0:T(8,128)(2,1)S(1)} %slice.113, s32[1024]{0:T(1024)S(1)} %pad_clamp_fusion), kind=kCustom, calls=%fused_computation.6 | custom fusion | bytes 4194432 | tf_op jit(solution)/shard_map/jit(_take)/gather | solution.py:214
  47.7 9.0 %all-to-all-done = bf16[32,16,1024]{2,1,0:T(8,128)(2,1)} async-done(((bf16[32,16,1024]{2,1,0:T(8,128)(2,1)}), bf16[32,16,1024]{2,1,0:T(8,128)(2,1)}, u32[]{:S(2)}, u32[]{:S(2)}) %all-to-all-start) | async-done | bytes 1048608 | tf_op jit(solution)/shard_map/all_to_all | solution.py:273
  56.7 7.7 %all-to-all-start.1 = ((f32[8,1,18432]{2,1,0:T(1,128)}), f32[8,1,18432]{2,1,0:T(1,128)}, u32[]{:S(2)}, u32[]{:S(2)}) async-start(f32[8,1,18432]{2,1,0:T(1,128)} %reshape.444), calls=%async_computation.1 | async-start | bytes 1179648 | tf_op jit(solution)/shard_map/all_to_all | solution.py:140
  64.4 2.1 %fusion.11 = f32[2,32,128]{2,0,1:T(2,128)S(1)} fusion(bf16[32,256,128]{2,1,0:T(8,128)(2,1)} %gather_fusion.6, pred[32]{0:T(512)(128)(4,1)S(1)} %copy-done.16, bf16[2,32,256]{2,1,0:T(8,128)(2,1)S(1)} %copy-done.8), kind=kOutput, calls=%fused_computation.23 | convolution fusion | flops 5242880 | bytes 2162720 | tf_op jit(solution)/shard_map/srd,rdk->srk/dot_general | solution.py:226
  67.8 3.0 %collective-permute-start.5 = (f32[2,32,128]{2,0,1:T(2,128)S(1)}, f32[2,32,128]{2,0,1:T(2,128)S(1)}, u32[]{:S(2)}, u32[]{:S(2)}) collective-permute-start(f32[2,32,128]{2,0,1:T(2,128)S(1)} %add.130), channel_id=1, source_target_pairs={{0,2},{1,3},{2,0},{3,1},{4,6},{5,7},{6,4},{7,5},{8,10},{9,11},{10,... | collective-permute-start | bytes 98312 | tf_op jit(solution)/shard_map/ppermute | solution.py:159
  71.5 1.8 collective-permute-done.5
  73.3 2.1 %collective-permute-start.6 = (f32[2,32,128]{2,0,1:T(2,128)S(1)}, f32[2,32,128]{2,0,1:T(2,128)S(1)}, u32[]{:S(2)}, u32[]{:S(2)}) collective-permute-start(f32[2,32,128]{2,0,1:T(2,128)S(1)} %add.131), channel_id=1, source_target_pairs={{0,4},{1,5},{2,6},{3,7},{4,0},{5,1},{6,2},{7,3},{8,12},{9,13},{10,... | collective-permute-start | bytes 98312 | tf_op jit(solution)/shard_map/ppermute | solution.py:159
  75.4 2.7 %pad_maximum_fusion = bf16[64,16,1024]{2,1,0:T(8,128)(2,1)} fusion(bf16[32,16,1024]{2,1,0:T(8,128)(2,1)} %all-to-all-done, bf16[32,16,1024]{2,1,0:T(8,128)(2,1)S(1)} %copy-done.3), kind=kLoop, calls=%fused_computation.11 | loop fusion | flops 1048576 | bytes 4194304 | tf_op jit(solution)/shard_map/concatenate | solution.py:274
  78.2 3.2 %gather_fusion.1 = bf16[32,16,1024]{2,1,0:T(8,128)(2,1)} fusion(bf16[64,16,1024]{2,1,0:T(8,128)(2,1)} %pad_maximum_fusion, s32[1024]{0:T(1024)S(1)} %pad_clamp_fusion.2), kind=kCustom, calls=%fused_computation.1 | custom fusion | bytes 2097280 | tf_op jit(solution)/shard_map/jit(_take)/gather | solution.py:275
  81.4 1.5 copy.211
  82.9 2.4 %collective-permute-start.7 = (f32[2,32,128]{2,0,1:T(2,128)S(1)}, f32[2,32,128]{2,0,1:T(2,128)S(1)}, u32[]{:S(2)}, u32[]{:S(2)}) collective-permute-start(f32[2,32,128]{2,0,1:T(2,128)S(1)} %add.132), channel_id=1, source_target_pairs={{0,8},{1,9},{2,10},{3,11},{4,12},{5,13},{6,14},{7,15},{8,0},{9,1},... | collective-permute-start | bytes 98312 | tf_op jit(solution)/shard_map/ppermute | solution.py:159
  85.5 2.4 %collective-permute-done.7 = f32[2,32,128]{2,0,1:T(2,128)S(1)} collective-permute-done((f32[2,32,128]{2,0,1:T(2,128)S(1)}, f32[2,32,128]{2,0,1:T(2,128)S(1)}, u32[]{:S(2)}, u32[]{:S(2)}) %collective-permute-start.7) | collective-permute-done | bytes 32800 | tf_op jit(solution)/shard_map/ppermute | solution.py:159
  87.9 4.6 %collective-permute-start.8 = (f32[2,32,128]{2,0,1:T(2,128)S(1)}, f32[2,32,128]{2,0,1:T(2,128)S(1)}, u32[]{:S(2)}, u32[]{:S(2)}) collective-permute-start(f32[2,32,128]{2,0,1:T(2,128)S(1)} %add.133), channel_id=1, source_target_pairs={{0,16},{1,17},{2,18},{3,19},{4,20},{5,21},{6,22},{7,23},{8,24},{9,... | collective-permute-start | bytes 98312 | tf_op jit(solution)/shard_map/ppermute | solution.py:159
  93.2 1.0 slice.112
  94.2 0.9 reshape.451
  95.1 1.1 copy.229
  96.2 1.2 gather_fusion.7
  97.4 1.4 gather_fusion.5
  98.9 1.3 copy.311
  101.0 2.9 %collective-permute-start.2 = (bf16[8,2,32,256]{3,2,1,0:T(8,128)(2,1)S(1)}, bf16[8,2,32,256]{3,2,1,0:T(8,128)(2,1)}, u32[]{:S(2)}, u32[]{:S(2)}) collective-permute-start(bf16[8,2,32,256]{3,2,1,0:T(8,128)(2,1)S(1)} %bitcast.187), channel_id=1, source_target_pairs={{0,2},{1,3},{2,0},{3,1},{4,6},{5,7},{6,4},{7,5},{8,10},{9,11},{10,... | collective-permute-start | bytes 786440 | tf_op jit(solution)/shard_map/ppermute | solution.py:147
  104.9 4.1 %collective-permute-done.2 = bf16[8,2,32,256]{3,2,1,0:T(8,128)(2,1)} collective-permute-done((bf16[8,2,32,256]{3,2,1,0:T(8,128)(2,1)S(1)}, bf16[8,2,32,256]{3,2,1,0:T(8,128)(2,1)}, u32[]{:S(2)}, u32[]{:S(2)}) %collective-permute-start.2) | collective-permute-done | bytes 262176 | tf_op jit(solution)/shard_map/ppermute | solution.py:147
  109.0 1.9 %maximum_select_fusion.2 = bf16[8,2,2,32,256]{4,3,2,0,1:T(8,128)(2,1)} fusion(bf16[8,1,2,32,256]{4,3,2,0,1:T(8,128)(2,1)} %bitcast.14, bf16[8,1,2,32,256]{4,3,2,0,1:T(8,128)(2,1)S(1)} %bitcast.188, pred[]{:T(512)S(6)} %eq.19), kind=kLoop, calls=%fused_computation.44 | loop fusion | flops 786432 | bytes 1048577 | tf_op jit(solution)/shard_map/jit(_where)/select_n | solution.py:148
  111.0 1.3 fusion.31
  112.3 1.1 maximum_select_fusion.1
  113.5 1.5 maximum_select_fusion
  116.4 5.9 %all-to-all-start.3 = ((f32[2,32,1,144]{3,0,2,1:T(2,128)}), f32[2,32,1,144]{3,0,2,1:T(2,128)S(1)}, u32[]{:S(2)}, u32[]{:S(2)}) async-start(f32[2,32,1,144]{3,0,2,1:T(2,128)} %copy.232), calls=%async_computation.3 | async-start | bytes 131072 | tf_op jit(solution)/shard_map/all_to_all | solution.py:255
  123.2 9.1 %all-to-all-done.3 = f32[2,32,1,144]{3,0,2,1:T(2,128)S(1)} async-done(((f32[2,32,1,144]{3,0,2,1:T(2,128)}), f32[2,32,1,144]{3,0,2,1:T(2,128)S(1)}, u32[]{:S(2)}, u32[]{:S(2)}) %all-to-all-start.3) | async-done | bytes 36896 | tf_op jit(solution)/shard_map/all_to_all | solution.py:255
  133.8 12.7 %all_to_all.42 = bf16[2,1,32,128]{3,0,1,2:T(2,128)(2,1)S(1)} all-to-all(bf16[2,1,32,128]{3,0,1,2:T(2,128)(2,1)S(1)} %copy.243), channel_id=1, replica_groups=mesh['group'=8,'tp'=32] {'tp'}, dimensions={2} | all-to-all | bytes 32768 | tf_op jit(solution)/shard_map/all_to_all | solution.py:279
  146.5 2.0 %fusion = f32[64,32,256]{2,0,1:T(8,128)S(1)} fusion(bf16[64,128,1]{1,0,2:T(8,128)(2,1)S(1)} %bitcast.203, bf16[16,32,8,256]{3,2,1,0:T(8,128)(2,1)} %bitcast.190), kind=kOutput, calls=%fused_computation.8 | convolution fusion | flops 134217728 | bytes 4210688 | tf_op jit(solution)/shard_map/rk,kdc->drc/dot_general | solution.py:281
  148.7 1.5 copy.267
  150.2 2.1 %select_n.250 = f32[16,1,16384]{2,1,0:T(1,128)} reshape(f32[16,1,64,256]{3,2,1,0:T(8,128)S(1)} %get-tuple-element.6) | data formatting | bytes 2097152 | tf_op jit(solution)/shard_map/jit(_where)/select_n | solution.py:87
  152.3 0.9 collective-permute-done.9
  153.2 2.6 %add.139 = f32[16,1,16384]{2,1,0:T(1,128)S(1)} add(f32[16,1,16384]{2,1,0:T(1,128)} %select_n.250, f32[16,1,16384]{2,1,0:T(1,128)} %bitcast.52) | non-fusion elementwise | flops 262144 | bytes 3145728 | tf_op jit(solution)/shard_map/add | solution.py:91
  155.9 33.9 %all_to_all.43 = f32[16,1,16384]{2,1,0:T(1,128)S(1)} all-to-all(f32[16,1,16384]{2,1,0:T(1,128)S(1)} %add.139), channel_id=1, replica_groups={{0,2,4,6,8,10,12,14,16,18,20,22,24,26,28,30},{1,3,5,7,9,11,13,15,17,19,..., dimensions={0} | all-to-all | bytes 2097152 | tf_op jit(solution)/shard_map/all_to_all | solution.py:98
  (124 shorter events, 19.9 us)
Async XLA Ops:
  0.0 115.2 %copy-start = (bf16[8192,128]{1,0:T(8,128)(2,1)S(1)}, bf16[8192,128]{1,0:T(8,128)(2,1)}, u32[]{:S(2)}) copy-start(bf16[8192,128]{1,0:T(8,128)(2,1)} %param.14) | copy-start | bytes 6291460
  0.0 3.2 %copy-start.9 = (s32[8,8,2]{1,2,0:T(2,128)S(1)}, s32[8,8,2]{1,2,0:T(2,128)}, u32[]{:S(2)}) copy-start(s32[8,8,2]{1,2,0:T(2,128)} %param.25) | copy-start | bytes 1540
  0.0 5.6 %copy-start.6 = (bf16[4,64,128]{2,1,0:T(8,128)(2,1)S(1)}, bf16[4,64,128]{2,1,0:T(8,128)(2,1)}, u32[]{:S(2)}) copy-start(bf16[4,64,128]{2,1,0:T(8,128)(2,1)} %param.18) | copy-start | bytes 196612
  0.0 7.1 %copy-start.2 = (bf16[4,256,128]{2,1,0:T(8,128)(2,1)S(1)}, bf16[4,256,128]{2,1,0:T(8,128)(2,1)}, u32[]{:S(2)}) copy-start(bf16[4,256,128]{2,1,0:T(8,128)(2,1)} %param.17) | copy-start | bytes 786436
  3.2 19.8 %collective-permute-start = (f32[16,2,1024]{2,0,1:T(8,128)}, f32[16,2,1024]{2,0,1:T(8,128)}, u32[]{:S(2)}, u32[]{:S(2)}) collective-permute-start(f32[16,2,1024]{2,0,1:T(8,128)} %bitcast.174), channel_id=1, source_target_pairs={{0,1},{1,0},{2,3},{3,2},{4,5},{5,4},{6,7},{7,6},{8,9},{9,8},{10,11... | collective-permute-start | bytes 393224 | tf_op jit(solution)/shard_map/ppermute | solution.py:131
  7.9 1.0 copy-start.7
  8.8 7.0 %copy-start.10 = (s32[1,1,8,4]{2,3,1,0:T(4,128)S(1)}, s32[1,1,8,4]{2,3,1,0:T(4,128)}, u32[]{:S(2)}) copy-start(s32[1,1,8,4]{2,3,1,0:T(4,128)} %param.23) | copy-start | bytes 388
  8.8 7.1 %copy-start.14 = (s32[1,32]{1,0:T(1,128)S(1)}, s32[1,32]{1,0:T(1,128)}, u32[]{:S(2)}) copy-start(s32[1,32]{1,0:T(1,128)} %param.22) | copy-start | bytes 388
  8.8 7.6 %copy-start.15 = (s32[32]{0:T(128)S(1)}, s32[32]{0:T(128)}, u32[]{:S(2)}) copy-start(s32[32]{0:T(128)} %param.24) | copy-start | bytes 388
  10.0 26.1 %all-to-all-start.2 = ((bf16[8,2,328,128]{3,2,1,0:T(8,128)(2,1)}), bf16[8,2,328,128]{3,2,1,0:T(8,128)(2,1)S(1)}, u32[]{:S(2)}, u32[]{:S(2)}) async-start(bf16[8,2,328,128]{3,2,1,0:T(8,128)(2,1)} %pad_maximum_fusion.1), calls=%async_computation.2 | async-start | bytes 2686976 | tf_op jit(solution)/shard_map/all_to_all | solution.py:206
  17.6 5.3 %copy-start.8 = (bf16[2,32,256]{2,1,0:T(8,128)(2,1)S(1)}, bf16[2,32,256]{2,1,0:T(8,128)(2,1)}, u32[]{:S(2)}) copy-start(bf16[2,32,256]{2,1,0:T(8,128)(2,1)} %param.13) | copy-start | bytes 98308
  27.5 8.0 %collective-permute-start.1 = (f32[8,2,1024]{2,0,1:T(8,128)S(1)}, f32[8,2,1024]{2,0,1:T(8,128)S(1)}, u32[]{:S(2)}, u32[]{:S(2)}) collective-permute-start(f32[8,2,1024]{2,0,1:T(8,128)S(1)} %select_bitcast_fusion), channel_id=1, source_target_pairs={{0,2},{1,3},{2,0},{3,1},{4,6},{5,7},{6,4},{7,5},{8,10},{9,11},{10,... | collective-permute-start | bytes 196616 | tf_op jit(solution)/shard_map/ppermute | solution.py:131
  36.1 8.1 %copy-start.1 = (bf16[8,2,328,128]{3,2,1,0:T(8,128)(2,1)}, bf16[8,2,328,128]{3,2,1,0:T(8,128)(2,1)S(1)}, u32[]{:S(2)}) copy-start(bf16[8,2,328,128]{3,2,1,0:T(8,128)(2,1)S(1)} %all-to-all-done.2) | copy-start | bytes 4030468
  36.1 20.6 %all-to-all-start = ((bf16[32,16,1024]{2,1,0:T(8,128)(2,1)}), bf16[32,16,1024]{2,1,0:T(8,128)(2,1)}, u32[]{:S(2)}, u32[]{:S(2)}) async-start(bf16[32,16,1024]{2,1,0:T(8,128)(2,1)} %select_multiply_fusion), calls=%async_computation | async-start | bytes 2097152 | tf_op jit(solution)/shard_map/all_to_all | solution.py:273
  45.5 18.8 %copy-start.16 = (pred[32]{0:T(512)(128)(4,1)S(1)}, pred[32]{0:T(512)(128)(4,1)}, u32[]{:S(2)}) copy-start(pred[32]{0:T(512)(128)(4,1)} %get-tuple-element.20) | copy-start | bytes 100
  56.7 42.2 %all-to-all-start.1 = ((f32[8,1,18432]{2,1,0:T(1,128)}), f32[8,1,18432]{2,1,0:T(1,128)}, u32[]{:S(2)}, u32[]{:S(2)}) async-start(f32[8,1,18432]{2,1,0:T(1,128)} %reshape.444), calls=%async_computation.1 | async-start | bytes 1179648 | tf_op jit(solution)/shard_map/all_to_all | solution.py:140
  64.4 7.0 %copy-start.11 = (pred[32]{0:T(512)(128)(4,1)S(1)}, pred[32]{0:T(512)(128)(4,1)}, u32[]{:S(2)}) copy-start(pred[32]{0:T(512)(128)(4,1)} %get-tuple-element.21) | copy-start | bytes 100
  64.4 11.1 %copy-start.3 = (bf16[32,16,1024]{2,1,0:T(8,128)(2,1)S(1)}, bf16[32,16,1024]{2,1,0:T(8,128)(2,1)}, u32[]{:S(2)}) copy-start(bf16[32,16,1024]{2,1,0:T(8,128)(2,1)} %param.20) | copy-start | bytes 3145732
  66.5 1.3 collective-permute-start.4
  67.8 5.5 %collective-permute-start.5 = (f32[2,32,128]{2,0,1:T(2,128)S(1)}, f32[2,32,128]{2,0,1:T(2,128)S(1)}, u32[]{:S(2)}, u32[]{:S(2)}) collective-permute-start(f32[2,32,128]{2,0,1:T(2,128)S(1)} %add.130), channel_id=1, source_target_pairs={{0,2},{1,3},{2,0},{3,1},{4,6},{5,7},{6,4},{7,5},{8,10},{9,11},{10,... | collective-permute-start | bytes 98312 | tf_op jit(solution)/shard_map/ppermute | solution.py:159
  73.3 9.5 %collective-permute-start.6 = (f32[2,32,128]{2,0,1:T(2,128)S(1)}, f32[2,32,128]{2,0,1:T(2,128)S(1)}, u32[]{:S(2)}, u32[]{:S(2)}) collective-permute-start(f32[2,32,128]{2,0,1:T(2,128)S(1)} %add.131), channel_id=1, source_target_pairs={{0,4},{1,5},{2,6},{3,7},{4,0},{5,1},{6,2},{7,3},{8,12},{9,13},{10,... | collective-permute-start | bytes 98312 | tf_op jit(solution)/shard_map/ppermute | solution.py:159
  82.9 4.9 %collective-permute-start.7 = (f32[2,32,128]{2,0,1:T(2,128)S(1)}, f32[2,32,128]{2,0,1:T(2,128)S(1)}, u32[]{:S(2)}, u32[]{:S(2)}) collective-permute-start(f32[2,32,128]{2,0,1:T(2,128)S(1)} %add.132), channel_id=1, source_target_pairs={{0,8},{1,9},{2,10},{3,11},{4,12},{5,13},{6,14},{7,15},{8,0},{9,1},... | collective-permute-start | bytes 98312 | tf_op jit(solution)/shard_map/ppermute | solution.py:159
  87.9 16.0 %collective-permute-start.8 = (f32[2,32,128]{2,0,1:T(2,128)S(1)}, f32[2,32,128]{2,0,1:T(2,128)S(1)}, u32[]{:S(2)}, u32[]{:S(2)}) collective-permute-start(f32[2,32,128]{2,0,1:T(2,128)S(1)} %add.133), channel_id=1, source_target_pairs={{0,16},{1,17},{2,18},{3,19},{4,20},{5,21},{6,22},{7,23},{8,24},{9,... | collective-permute-start | bytes 98312 | tf_op jit(solution)/shard_map/ppermute | solution.py:159
  98.9 5.0 %copy-start.4 = (bf16[32,64,16]{1,2,0:T(8,128)(2,1)S(1)}, bf16[32,64,16]{1,2,0:T(8,128)(2,1)}, u32[]{:S(2)}) copy-start(bf16[32,64,16]{1,2,0:T(8,128)(2,1)} %gather_fusion.7) | copy-start | bytes 196612
  100.2 0.8 copy-start.5
  101.0 8.0 %collective-permute-start.2 = (bf16[8,2,32,256]{3,2,1,0:T(8,128)(2,1)S(1)}, bf16[8,2,32,256]{3,2,1,0:T(8,128)(2,1)}, u32[]{:S(2)}, u32[]{:S(2)}) collective-permute-start(bf16[8,2,32,256]{3,2,1,0:T(8,128)(2,1)S(1)} %bitcast.187), channel_id=1, source_target_pairs={{0,2},{1,3},{2,0},{3,1},{4,6},{5,7},{6,4},{7,5},{8,10},{9,11},{10,... | collective-permute-start | bytes 786440 | tf_op jit(solution)/shard_map/ppermute | solution.py:147
  110.9 2.6 %collective-permute-start.3 = (bf16[8,2,2,32,256]{4,3,2,0,1:T(8,128)(2,1)}, bf16[8,2,2,32,256]{4,3,2,0,1:T(8,128)(2,1)}, u32[]{:S(2)}, u32[]{:S(2)}) collective-permute-start(bf16[8,2,2,32,256]{4,3,2,0,1:T(8,128)(2,1)} %maximum_select_fusion.2), channel_id=1, source_target_pairs={{0,1},{1,0},{2,3},{3,2},{4,5},{5,4},{6,7},{7,6},{8,9},{9,8},{10,11... | collective-permute-start | bytes 1572872 | tf_op jit(solution)/shard_map/ppermute | solution.py:147
  115.2 17.4 %copy-start.12 = (pred[2,2]{0,1:T(4,128)(4,1)S(1)}, pred[2,2]{0,1:T(4,128)(4,1)}, u32[]{:S(2)}) copy-start(pred[2,2]{0,1:T(4,128)(4,1)} %iota_compare_fusion.1) | copy-start | bytes 16
  115.2 17.5 %copy-start.13 = (pred[512]{0:T(512)(128)(4,1)S(1)}, pred[512]{0:T(512)(128)(4,1)}, u32[]{:S(2)}) copy-start(pred[512]{0:T(512)(128)(4,1)} %iota_compare_fusion) | copy-start | bytes 1540
  116.4 15.9 %all-to-all-start.3 = ((f32[2,32,1,144]{3,0,2,1:T(2,128)}), f32[2,32,1,144]{3,0,2,1:T(2,128)S(1)}, u32[]{:S(2)}, u32[]{:S(2)}) async-start(f32[2,32,1,144]{3,0,2,1:T(2,128)} %copy.232), calls=%async_computation.3 | async-start | bytes 131072 | tf_op jit(solution)/shard_map/all_to_all | solution.py:255
  150.2 3.0 %collective-permute-start.9 = (f32[262144]{0:T(1024)}, f32[262144]{0:T(1024)}, u32[]{:S(2)}, u32[]{:S(2)}) collective-permute-start(f32[262144]{0:T(1024)} %bitcast.97), channel_id=1, source_target_pairs={{0,1},{1,0},{2,3},{3,2},{4,5},{5,4},{6,7},{7,6},{8,9},{9,8},{10,11... | collective-permute-start | bytes 3145736 | tf_op jit(solution)/shard_map/ppermute | solution.py:90

commit v13 on v8

--- a/solution.py
+++ b/solution.py
@@ -84,8 +84,8 @@
     for bit in bits:
         mine = (column_id // bit) % 2
         split = parts.reshape((-1, 2) + parts.shape[1:])
-        keep = jnp.where(mine == 0, split[:, 0], split[:, 1])
-        give = jnp.where(mine == 0, split[:, 1], split[:, 0])
+        keep = lax.dynamic_index_in_dim(split, mine, 1, keepdims=False)
+        give = lax.dynamic_index_in_dim(split, 1 - mine, 1, keepdims=False)
         sent = jnp.concatenate([give.reshape(-1), shared.reshape(-1)])
         got = lax.ppermute(sent, "tp", [(t, t ^ bit) for t in range(n_tp)])
         parts = keep + got[: give.size].reshape(give.shape)

time: 177 us -> 175 us (0.989)
  other arithmetic: 26.6 us -> 24.6 us
    dynamic_slice x0 -> x2, local copies, waits for them, and re-layouts: none -> 2.19 us  [the longest x1 2.02 us: reduce_scatter_tp(): keep = lax.dynamic_index_in_dim(split, mine, 1, keepdims=False)]
    squeeze x0 -> x1, local copies, waits for them, and re-layouts: none -> 2.04 us  [reduce_scatter_tp(): keep = lax.dynamic_index_in_dim(split, mine, 1, keepdims=False)]
    select_n x1 -> x0, local copies, waits for them, and re-layouts: 2.04 us -> none  [reduce_scatter_tp(): keep = jnp.where(mine == 0, split[:, 0], split[:, 1])]
  transfers between devices with their start and end apart: 10 -> 10, of which waited for: 4 -> 4; matrix products, arithmetic and copies ran while one was open for 29% -> 28% of each run, Pallas kernels for 0% -> 0%
where the time goes in v13:
time: 175 us; the launch traced here: 174 us
  blocking collectives  46.6 us (27%)
  starting transfers between devices  42.5 us (24%)
  local copies, waits for them, and re-layouts  32.3 us (18%)
  other arithmetic  24.6 us (14%)
  waiting for transfers between devices  18.6 us (11%)
  matrix products  8.38 us (5%)
    all_to_all x1, blocking collectives, reduce_scatter_tp(): lax.all_to_all(send, 'tp', 0, 0, tiled=True, axis_index_groups=stage_grou...  33.9 us
    all_to_all x1, blocking collectives, per_device(): lax.all_to_all(attended, 'tp', split_axis=2, concat_axis=1, tiled=True)  12.7 us
    all_to_all x1, starting transfers between devices, per_device(): lax.all_to_all(query_send, 'tp', split_axis=1, concat_axis=2, tiled=True)  9.13 us
    all_to_all x1, waiting for transfers between devices, per_device(): lax.all_to_all(query_send, 'tp', split_axis=1, concat_axis=2, tiled=True)  8.69 us
    all_to_all x1, starting transfers between devices, all_gather_tp(): lax.all_to_all(jnp.broadcast_to(block[None], (rest,) + block.shape), 'tp'...  8.47 us
    all_to_all x1, waiting for transfers between devices, per_device(): lax.all_to_all(panel_send, 'group', 0, 0, tiled=True)  6.87 us
    all_to_all x1, starting transfers between devices, reduce_scatter_tp(): lax.all_to_all(send, 'tp', 0, 0, tiled=True, axis_index_groups=stage_grou...  6.57 us
    all_to_all x1, starting transfers between devices, per_device(): lax.all_to_all(outgoing, 'group', split_axis=0, concat_axis=0, tiled=True)  6.06 us
  transfers between devices with their start and end apart: 10, of which 4 were waited for; matrix products, arithmetic and copies ran while one was open for 28% of the time, Pallas kernels for 0%

profile of v13, /device:TPU:2, one launch (start us, length us, event | category | flops | bytes accessed | tf_op | source)
XLA Modules:
  0.0 174.1 jit_solution(12532807121126164388)
XLA Ops:
  0.0 1.6 broadcast_in_dim.136
  1.6 8.5 %all-to-all-start.1 = ((bf16[8,2,32,256]{3,2,1,0:T(8,128)(2,1)}), bf16[8,2,32,256]{3,2,1,0:T(8,128)(2,1)}, u32[]{:S(2)}, u32[]{:S(2)}) async-start(bf16[8,2,32,256]{3,2,1,0:T(8,128)(2,1)} %broadcast_in_dim.136), calls=%async_computation.1 | async-start | bytes 524288 | tf_op jit(solution)/shard_map/all_to_all | solution.py:106
  10.1 1.0 fusion.54
  11.1 0.8 broadcast_compare_fusion
  11.9 1.3 convolution_bitcast_fusion
  13.1 0.9 reshape.473
  14.1 0.9 constant_dynamic-slice_fusion.4
  16.9 1.1 broadcast_select_fusion
  18.7 0.8 broadcast_select_fusion.2
  19.6 2.0 %constant_dynamic-slice_fusion.3 = (f32[16,1,2,1024]{3,1,0,2:T(1,128)}, f32[16,1,2,1024]{3,1,0,2:T(1,128)}) fusion(f32[16,2,2,1024]{3,1,0,2:T(2,128)} %reshape.473, s32[]{:T(128)S(6)} %select_n.187, s32[]{:T(128)S(6)} %select_n.188), kind=kLoop, calls=%fused_computation.103 | loop fusion | bytes 524296 | tf_op jit(solution)/shard_map/jit(dynamic_index_in_dim)/dynamic_slice | solution.py:87
  21.7 2.1 %pad_maximum_fusion.1 = bf16[8,2,328,128]{3,2,1,0:T(8,128)(2,1)} fusion(bf16[8,2,8,128]{3,2,1,0:T(8,128)(2,1)S(1)} %broadcast_select_fusion.3, bf16[8,2,64,128]{3,2,1,0:T(8,128)(2,1)} %broadcast_select_fusion.2, bf16[8,2,256,128]{3,2,1,0:T(8,128)(2,1)S(1)} %copy-done.4), kind=kLoop, calls=%fused_computation.17 | loop fusion | flops 4030464 | bytes 2686976 | tf_op jit(solution)/shard_map/concatenate | solution.py:159
  23.8 5.9 %all-to-all-start.2 = ((bf16[8,2,328,128]{3,2,1,0:T(8,128)(2,1)}), bf16[8,2,328,128]{3,2,1,0:T(8,128)(2,1)S(1)}, u32[]{:S(2)}, u32[]{:S(2)}) async-start(bf16[8,2,328,128]{3,2,1,0:T(8,128)(2,1)} %pad_maximum_fusion.1), calls=%async_computation.2 | async-start | bytes 2686976 | tf_op jit(solution)/shard_map/all_to_all | solution.py:167
  29.7 1.0 copy.316
  32.4 2.9 %gather_fusion = bf16[32,16,1024]{2,1,0:T(8,128)(2,1)} fusion(bf16[32,16,1024]{2,1,0:T(8,128)(2,1)} %param.20, s32[1024]{0:T(1024)S(1)} %pad_clamp_fusion.3), kind=kCustom, calls=%fused_computation | custom fusion | bytes 2097280 | tf_op jit(solution)/shard_map/jit(_take)/gather | solution.py:231
  35.3 2.4 %select_multiply_fusion = bf16[32,16,1024]{2,1,0:T(8,128)(2,1)} fusion(bf16[32,16,1024]{2,1,0:T(8,128)(2,1)} %gather_fusion, pred[32]{0:T(512)(128)(4,1)S(1)} %le.73, bf16[32]{0:T(256)(128)(2,1)S(1)} %reshape.495), kind=kLoop, calls=%fused_computation.34 | loop fusion | flops 1048576 | bytes 2097248 | tf_op jit(solution)/shard_map/mul | solution.py:231
  37.8 2.9 %collective-permute-start = (bf16[8,2,32,256]{3,2,1,0:T(8,128)(2,1)}, bf16[8,2,32,256]{3,2,1,0:T(8,128)(2,1)}, u32[]{:S(2)}, u32[]{:S(2)}) collective-permute-start(bf16[8,2,32,256]{3,2,1,0:T(8,128)(2,1)} %all-to-all-done.1), channel_id=1, source_target_pairs={{0,2},{1,3},{2,0},{3,1},{4,6},{5,7},{6,4},{7,5},{8,10},{9,11},{10,... | collective-permute-start | bytes 786440 | tf_op jit(solution)/shard_map/ppermute | solution.py:116
  40.7 6.9 %all-to-all-done.2 = bf16[8,2,328,128]{3,2,1,0:T(8,128)(2,1)S(1)} async-done(((bf16[8,2,328,128]{3,2,1,0:T(8,128)(2,1)}), bf16[8,2,328,128]{3,2,1,0:T(8,128)(2,1)S(1)}, u32[]{:S(2)}, u32[]{:S(2)}) %all-to-all-start.2) | async-done | bytes 1343520 | tf_op jit(solution)/shard_map/all_to_all | solution.py:167
  47.5 6.1 %all-to-all-start = ((bf16[32,16,1024]{2,1,0:T(8,128)(2,1)}), bf16[32,16,1024]{2,1,0:T(8,128)(2,1)}, u32[]{:S(2)}, u32[]{:S(2)}) async-start(bf16[32,16,1024]{2,1,0:T(8,128)(2,1)} %select_multiply_fusion), calls=%async_computation | async-start | bytes 2097152 | tf_op jit(solution)/shard_map/all_to_all | solution.py:234
  53.6 1.3 slice.149
  54.9 2.1 %gather_fusion.6 = bf16[32,256,128]{2,1,0:T(8,128)(2,1)} fusion(bf16[16,256,128]{2,1,0:T(8,128)(2,1)S(1)} %slice.149, s32[1024]{0:T(1024)S(1)} %pad_clamp_fusion), kind=kCustom, calls=%fused_computation.6 | custom fusion | bytes 4194432 | tf_op jit(solution)/shard_map/jit(_take)/gather | solution.py:175
  57.1 2.1 %fusion.5 = f32[32,128,2]{1,2,0:T(2,128)S(1)} fusion(bf16[32,256,128]{2,1,0:T(8,128)(2,1)} %gather_fusion.6, pred[32]{0:T(512)(128)(4,1)S(1)} %get-tuple-element.19, bf16[2,32,256]{2,1,0:T(8,128)(2,1)S(1)} %copy-done.9), kind=kOutput, calls=%fused_computation.14 | convolution fusion | flops 5242880 | bytes 2162720 | tf_op jit(solution)/shard_map/srd,rdk->srk/dot_general | solution.py:184
  59.5 2.1 %maximum_select_fusion.2 = bf16[8,2,2,32,256]{4,3,2,0,1:T(8,128)(2,1)} fusion(bf16[8,1,2,32,256]{4,3,2,0,1:T(8,128)(2,1)} %bitcast.10, bf16[8,1,2,32,256]{4,3,2,0,1:T(8,128)(2,1)} %bitcast.9, pred[]{:T(512)S(6)} %eq.13), kind=kLoop, calls=%fused_computation.38 | loop fusion | flops 786432 | bytes 1048577 | tf_op jit(solution)/shard_map/jit(_where)/select_n | solution.py:117
  62.4 3.0 %collective-permute-start.3 = (f32[24576]{0:T(1024)S(1)}, f32[24576]{0:T(1024)S(1)}, u32[]{:S(2)}, u32[]{:S(2)}) collective-permute-start(f32[24576]{0:T(1024)S(1)} %pad_maximum_fusion.4), channel_id=1, source_target_pairs={{0,2},{1,3},{2,0},{3,1},{4,6},{5,7},{6,4},{7,5},{8,10},{9,11},{10,... | collective-permute-start | bytes 294920 | tf_op jit(solution)/shard_map/ppermute | solution.py:90
  65.4 2.1 %maximum_select_fusion.1 = bf16[8,2,1,2,32,256]{5,4,3,0,2,1:T(8,128)(2,1)} fusion(bf16[8,1,1,2,32,256]{5,4,3,0,2,1:T(8,128)(2,1)} %bitcast.8, bf16[8,1,1,2,32,256]{5,4,3,0,2,1:T(8,128)(2,1)} %bitcast.7, pred[]{:T(512)S(6)} %eq.13), kind=kLoop, calls=%fused_computation.37 | loop fusion | flops 786432 | bytes 1048577 | tf_op jit(solution)/shard_map/jit(_where)/select_n | solution.py:117
  67.5 2.1 %collective-permute-done.3 = f32[24576]{0:T(1024)S(1)} collective-permute-done((f32[24576]{0:T(1024)S(1)}, f32[24576]{0:T(1024)S(1)}, u32[]{:S(2)}, u32[]{:S(2)}) %collective-permute-start.3) | collective-permute-done | bytes 98336 | tf_op jit(solution)/shard_map/ppermute | solution.py:90
  69.8 0.9 all_to_all.38
  70.7 6.6 %all-to-all-start.3 = ((f32[8,1,10240]{2,1,0:T(1,128)}), f32[8,1,10240]{2,1,0:T(1,128)}, u32[]{:S(2)}, u32[]{:S(2)}) async-start(f32[8,1,10240]{2,1,0:T(1,128)} %all_to_all.38), calls=%async_computation.3 | async-start | bytes 655360 | tf_op jit(solution)/shard_map/all_to_all | solution.py:98
  77.3 2.7 %pad_maximum_fusion = bf16[64,16,1024]{2,1,0:T(8,128)(2,1)} fusion(bf16[32,16,1024]{2,1,0:T(8,128)(2,1)} %all-to-all-done, bf16[32,16,1024]{2,1,0:T(8,128)(2,1)S(1)} %copy-done.3), kind=kLoop, calls=%fused_computation.11 | loop fusion | flops 1048576 | bytes 4194304 | tf_op jit(solution)/shard_map/concatenate | solution.py:235
  80.0 2.2 %gather_fusion.1 = bf16[32,16,1024]{2,1,0:T(8,128)(2,1)S(1)} fusion(bf16[64,16,1024]{2,1,0:T(8,128)(2,1)} %pad_maximum_fusion, s32[1024]{0:T(1024)S(1)} %pad_clamp_fusion.2), kind=kCustom, calls=%fused_computation.1 | custom fusion | bytes 2097280 | tf_op jit(solution)/shard_map/jit(_take)/gather | solution.py:236
  82.2 1.3 copy.223
  83.6 2.3 %broadcast_select_fusion.1 = bf16[1,512,1024]{1,2,0:T(8,128)(2,1)} fusion(bf16[1,512,1024]{1,2,0:T(8,128)(2,1)} %copy.223, pred[512]{0:T(512)(128)(4,1)S(1)} %broadcast_in_dim.131), kind=kLoop, calls=%fused_computation.36 | loop fusion | flops 524288 | bytes 2097664 | tf_op jit(solution)/shard_map/jit(_take)/select_n | solution.py:236
  85.9 1.0 slice.148
  86.9 0.8 slice.156
  87.7 1.4 gather_fusion.5
  90.1 1.6 maximum_select_fusion
  91.8 1.2 reduce_sum.36
  93.6 1.4 fusion.28
  96.1 9.1 %all-to-all-start.4 = ((f32[2,32,1,144]{3,0,2,1:T(2,128)}), f32[2,32,1,144]{3,0,2,1:T(2,128)S(1)}, u32[]{:S(2)}, u32[]{:S(2)}) async-start(f32[2,32,1,144]{3,0,2,1:T(2,128)} %copy.244), calls=%async_computation.4 | async-start | bytes 131072 | tf_op jit(solution)/shard_map/all_to_all | solution.py:216
  105.3 1.3 fusion.64
  106.6 8.7 %all-to-all-done.4 = f32[2,32,1,144]{3,0,2,1:T(2,128)S(1)} async-done(((f32[2,32,1,144]{3,0,2,1:T(2,128)}), f32[2,32,1,144]{3,0,2,1:T(2,128)S(1)}, u32[]{:S(2)}, u32[]{:S(2)}) %all-to-all-start.4) | async-done | bytes 36896 | tf_op jit(solution)/shard_map/all_to_all | solution.py:216
  116.7 12.7 %all_to_all.51 = bf16[2,1,32,128]{3,0,1,2:T(2,128)(2,1)S(1)} all-to-all(bf16[2,1,32,128]{3,0,1,2:T(2,128)(2,1)S(1)} %copy.255), channel_id=1, replica_groups=mesh['group'=8,'tp'=32] {'tp'}, dimensions={2} | all-to-all | bytes 32768 | tf_op jit(solution)/shard_map/all_to_all | solution.py:240
  129.4 2.0 %fusion = f32[64,32,256]{2,0,1:T(8,128)S(1)} fusion(bf16[64,128,1]{1,0,2:T(8,128)(2,1)S(1)} %bitcast.205, bf16[16,32,8,256]{3,2,1,0:T(8,128)(2,1)} %bitcast.186), kind=kOutput, calls=%fused_computation.8 | convolution fusion | flops 134217728 | bytes 4210688 | tf_op jit(solution)/shard_map/rk,kdc->drc/dot_general | solution.py:242
  131.6 1.5 copy.277
  133.2 2.0 %squeeze.19 = f32[16,1,16384]{2,1,0:T(1,128)} reshape(f32[16,1,64,256]{3,2,1,0:T(8,128)S(1)} %get-tuple-element.6) | data formatting | bytes 2097152 | tf_op jit(solution)/shard_map/jit(dynamic_index_in_dim)/squeeze | solution.py:87
  135.2 1.0 collective-permute-done.4
  136.2 2.6 %add.150 = f32[16,1,16384]{2,1,0:T(1,128)S(1)} add(f32[16,1,16384]{2,1,0:T(1,128)} %squeeze.19, f32[16,1,16384]{2,1,0:T(1,128)} %bitcast.59) | non-fusion elementwise | flops 262144 | bytes 3145728 | tf_op jit(solution)/shard_map/add | solution.py:91
  138.8 33.9 %all_to_all.52 = f32[16,1,16384]{2,1,0:T(1,128)S(1)} all-to-all(f32[16,1,16384]{2,1,0:T(1,128)S(1)} %add.150), channel_id=1, replica_groups={{0,2,4,6,8,10,12,14,16,18,20,22,24,26,28,30},{1,3,5,7,9,11,13,15,17,19,..., dimensions={0} | all-to-all | bytes 2097152 | tf_op jit(solution)/shard_map/all_to_all | solution.py:98
  172.6 0.8 reduce_sum.39
  (114 shorter events, 10.0 us)
Async XLA Ops:
  0.0 94.9 %copy-start = (bf16[8192,128]{1,0:T(8,128)(2,1)S(1)}, bf16[8192,128]{1,0:T(8,128)(2,1)}, u32[]{:S(2)}) copy-start(bf16[8192,128]{1,0:T(8,128)(2,1)} %param.14) | copy-start | bytes 6291460
  0.0 16.0 %copy-start.2 = (bf16[4,256,128]{2,1,0:T(8,128)(2,1)S(1)}, bf16[4,256,128]{2,1,0:T(8,128)(2,1)}, u32[]{:S(2)}) copy-start(bf16[4,256,128]{2,1,0:T(8,128)(2,1)} %param.17) | copy-start | bytes 786436
  1.6 22.2 %all-to-all-start.1 = ((bf16[8,2,32,256]{3,2,1,0:T(8,128)(2,1)}), bf16[8,2,32,256]{3,2,1,0:T(8,128)(2,1)}, u32[]{:S(2)}, u32[]{:S(2)}) async-start(bf16[8,2,32,256]{3,2,1,0:T(8,128)(2,1)} %broadcast_in_dim.136), calls=%async_computation.1 | async-start | bytes 524288 | tf_op jit(solution)/shard_map/all_to_all | solution.py:106
  16.0 2.0 %copy-start.6 = (bf16[4,64,128]{2,1,0:T(8,128)(2,1)S(1)}, bf16[4,64,128]{2,1,0:T(8,128)(2,1)}, u32[]{:S(2)}) copy-start(bf16[4,64,128]{2,1,0:T(8,128)(2,1)} %param.18) | copy-start | bytes 196612
  16.8 2.7 %copy-start.10 = (s32[1,1,8,4]{2,3,1,0:T(4,128)S(1)}, s32[1,1,8,4]{2,3,1,0:T(4,128)}, u32[]{:S(2)}) copy-start(s32[1,1,8,4]{2,3,1,0:T(4,128)} %param.23) | copy-start | bytes 388
  18.1 3.6 %copy-start.4 = (bf16[8,2,256,128]{3,2,1,0:T(8,128)(2,1)S(1)}, bf16[8,2,256,128]{3,2,1,0:T(8,128)(2,1)}, u32[]{:S(2)}) copy-start(bf16[8,2,256,128]{3,2,1,0:T(8,128)(2,1)} %broadcast_select_fusion) | copy-start | bytes 3145732
  23.8 11.5 %copy-start.12 = (s32[32]{0:T(128)S(1)}, s32[32]{0:T(128)}, u32[]{:S(2)}) copy-start(s32[32]{0:T(128)} %param.24) | copy-start | bytes 388
  23.8 11.5 %copy-start.11 = (s32[1,32]{1,0:T(1,128)S(1)}, s32[1,32]{1,0:T(1,128)}, u32[]{:S(2)}) copy-start(s32[1,32]{1,0:T(1,128)} %param.22) | copy-start | bytes 388
  23.8 23.7 %all-to-all-start.2 = ((bf16[8,2,328,128]{3,2,1,0:T(8,128)(2,1)}), bf16[8,2,328,128]{3,2,1,0:T(8,128)(2,1)S(1)}, u32[]{:S(2)}, u32[]{:S(2)}) async-start(bf16[8,2,328,128]{3,2,1,0:T(8,128)(2,1)} %pad_maximum_fusion.1), calls=%async_computation.2 | async-start | bytes 2686976 | tf_op jit(solution)/shard_map/all_to_all | solution.py:167
  37.8 21.8 %collective-permute-start = (bf16[8,2,32,256]{3,2,1,0:T(8,128)(2,1)}, bf16[8,2,32,256]{3,2,1,0:T(8,128)(2,1)}, u32[]{:S(2)}, u32[]{:S(2)}) collective-permute-start(bf16[8,2,32,256]{3,2,1,0:T(8,128)(2,1)} %all-to-all-done.1), channel_id=1, source_target_pairs={{0,2},{1,3},{2,0},{3,1},{4,6},{5,7},{6,4},{7,5},{8,10},{9,11},{10,... | collective-permute-start | bytes 786440 | tf_op jit(solution)/shard_map/ppermute | solution.py:116
  47.5 6.1 %copy-start.1 = (bf16[8,2,328,128]{3,2,1,0:T(8,128)(2,1)}, bf16[8,2,328,128]{3,2,1,0:T(8,128)(2,1)S(1)}, u32[]{:S(2)}) copy-start(bf16[8,2,328,128]{3,2,1,0:T(8,128)(2,1)S(1)} %all-to-all-done.2) | copy-start | bytes 4030468
  47.5 23.2 %all-to-all-start = ((bf16[32,16,1024]{2,1,0:T(8,128)(2,1)}), bf16[32,16,1024]{2,1,0:T(8,128)(2,1)}, u32[]{:S(2)}, u32[]{:S(2)}) async-start(bf16[32,16,1024]{2,1,0:T(8,128)(2,1)} %select_multiply_fusion), calls=%async_computation | async-start | bytes 2097152 | tf_op jit(solution)/shard_map/all_to_all | solution.py:234
  54.9 2.2 %copy-start.9 = (bf16[2,32,256]{2,1,0:T(8,128)(2,1)S(1)}, bf16[2,32,256]{2,1,0:T(8,128)(2,1)}, u32[]{:S(2)}) copy-start(bf16[2,32,256]{2,1,0:T(8,128)(2,1)} %param.13) | copy-start | bytes 98308
  57.1 2.1 %copy-start.8 = (f32[16,8,2,128]{3,1,2,0:T(8,128)S(1)}, f32[16,8,2,128]{3,1,2,0:T(8,128)}, u32[]{:S(2)}) copy-start(f32[16,8,2,128]{3,1,2,0:T(8,128)} %copy.274) | copy-start | bytes 393220
  59.1 3.1 %copy-start.7 = (f32[16,1,2,1024]{3,1,0,2:T(1,128)S(1)}, f32[16,1,2,1024]{3,1,0,2:T(1,128)}, u32[]{:S(2)}) copy-start(f32[16,1,2,1024]{3,1,0,2:T(1,128)} %get-tuple-element.9) | copy-start | bytes 393220
  59.2 2.9 %collective-permute-start.2 = (f32[40960]{0:T(1024)S(1)}, f32[40960]{0:T(1024)S(1)}, u32[]{:S(2)}, u32[]{:S(2)}) collective-permute-start(f32[40960]{0:T(1024)S(1)} %pad_maximum_fusion.3), channel_id=1, source_target_pairs={{0,1},{1,0},{2,3},{3,2},{4,5},{5,4},{6,7},{7,6},{8,9},{9,8},{10,11... | collective-permute-start | bytes 491528 | tf_op jit(solution)/shard_map/ppermute | solution.py:90
  61.6 28.4 %collective-permute-start.1 = (bf16[8,2,2,32,256]{4,3,2,0,1:T(8,128)(2,1)}, bf16[8,2,2,32,256]{4,3,2,0,1:T(8,128)(2,1)}, u32[]{:S(2)}, u32[]{:S(2)}) collective-permute-start(bf16[8,2,2,32,256]{4,3,2,0,1:T(8,128)(2,1)} %maximum_select_fusion.2), channel_id=1, source_target_pairs={{0,1},{1,0},{2,3},{3,2},{4,5},{5,4},{6,7},{7,6},{8,9},{9,8},{10,11... | collective-permute-start | bytes 1572872 | tf_op jit(solution)/shard_map/ppermute | solution.py:116
  62.3 14.9 %copy-start.3 = (bf16[32,16,1024]{2,1,0:T(8,128)(2,1)S(1)}, bf16[32,16,1024]{2,1,0:T(8,128)(2,1)}, u32[]{:S(2)}) copy-start(bf16[32,16,1024]{2,1,0:T(8,128)(2,1)} %param.20) | copy-start | bytes 3145732
  62.4 7.2 %collective-permute-start.3 = (f32[24576]{0:T(1024)S(1)}, f32[24576]{0:T(1024)S(1)}, u32[]{:S(2)}, u32[]{:S(2)}) collective-permute-start(f32[24576]{0:T(1024)S(1)} %pad_maximum_fusion.4), channel_id=1, source_target_pairs={{0,2},{1,3},{2,0},{3,1},{4,6},{5,7},{6,4},{7,5},{8,10},{9,11},{10,... | collective-permute-start | bytes 294920 | tf_op jit(solution)/shard_map/ppermute | solution.py:90
  70.7 21.1 %all-to-all-start.3 = ((f32[8,1,10240]{2,1,0:T(1,128)}), f32[8,1,10240]{2,1,0:T(1,128)}, u32[]{:S(2)}, u32[]{:S(2)}) async-start(f32[8,1,10240]{2,1,0:T(1,128)} %all_to_all.38), calls=%async_computation.3 | async-start | bytes 655360 | tf_op jit(solution)/shard_map/all_to_all | solution.py:98
  85.9 4.2 %copy-start.5 = (bf16[8,2,1,2,32,256]{5,4,3,0,2,1:T(8,128)(2,1)S(1)}, bf16[8,2,1,2,32,256]{5,4,3,0,2,1:T(8,128)(2,1)}, u32[]{:S(2)}) copy-start(bf16[8,2,1,2,32,256]{5,4,3,0,2,1:T(8,128)(2,1)} %maximum_select_fusion.1) | copy-start | bytes 1572868
  96.1 19.1 %all-to-all-start.4 = ((f32[2,32,1,144]{3,0,2,1:T(2,128)}), f32[2,32,1,144]{3,0,2,1:T(2,128)S(1)}, u32[]{:S(2)}, u32[]{:S(2)}) async-start(f32[2,32,1,144]{3,0,2,1:T(2,128)} %copy.244), calls=%async_computation.4 | async-start | bytes 131072 | tf_op jit(solution)/shard_map/all_to_all | solution.py:216
  133.1 3.0 %collective-permute-start.4 = (f32[262144]{0:T(1024)}, f32[262144]{0:T(1024)}, u32[]{:S(2)}, u32[]{:S(2)}) collective-permute-start(f32[262144]{0:T(1024)} %bitcast.98), channel_id=1, source_target_pairs={{0,1},{1,0},{2,3},{3,2},{4,5},{5,4},{6,7},{7,6},{8,9},{9,8},{10,11... | collective-permute-start | bytes 3145736 | tf_op jit(solution)/shard_map/ppermute | solution.py:90

commit v14 on v13

--- a/solution.py
+++ b/solution.py
@@ -239,14 +239,29 @@
     attended = attend(query_own, ctx_pages, keyval_new, lengths)
     heads_back = lax.all_to_all(attended, "tp", split_axis=2, concat_axis=1, tiled=True)
     out_cols = output_weight.shape[1] // n_tp
+    core = column_id % 2
     projected = jnp.einsum(
-        "rk,kdc->drc",
+        "rk,kjcl->cjrl",
         heads_back.reshape(step_count * batch_rows, -1),
-        output_weight.reshape(output_weight.shape[0], n_tp, out_cols),
-        preferred_element_type=jnp.float32,
-    )
-    summed, _ = reduce_scatter_tp(
-        projected, jnp.zeros((0,), jnp.float32), column_id, n_tp, SWAP_BITS[:1]
+        output_weight.reshape(output_weight.shape[0], n_tp // 2, 2, out_cols),
+        preferred_element_type=jnp.float32,
+    )
+    got = lax.ppermute(
+        lax.dynamic_index_in_dim(projected, 1 - core, 0, keepdims=False),
+        "tp",
+        [(t, t ^ 1) for t in range(n_tp)],
+    )
+    pair_sum = lax.dynamic_index_in_dim(projected, core, 0, keepdims=False) + got
+    summed = jnp.sum(
+        lax.all_to_all(
+            pair_sum.reshape(n_tp // 2, -1),
+            "tp",
+            0,
+            0,
+            tiled=True,
+            axis_index_groups=stage_groups(n_tp, SWAP_BITS[:1]),
+        ),
+        0,
     )
     return summed.reshape(step_count, batch_rows, out_cols).astype(jnp.bfloat16)
 

time: 175 us -> 177 us (1.011)
  blocking collectives: 46.6 us -> 35 us
  waiting for transfers between devices: 18.6 us -> 25.2 us
  starting transfers between devices: 42.5 us -> 46.6 us
  local copies, waits for them, and re-layouts: 32.3 us -> 35.9 us
  other arithmetic: 24.6 us -> 22.1 us
    all_to_all x2 -> x1, blocking collectives: 46.6 us -> 35 us  [per_device(): lax.all_to_all(pair_sum.reshape(n_tp // 2, -1), 'tp', 0, 0, tiled=True, a...]
    all_to_all x0 -> x1, waiting for transfers between devices: none -> 4.97 us  [per_device(): lax.all_to_all(attended, 'tp', split_axis=2, concat_axis=1, tiled=True)]
    reshape x0 -> x1, local copies, waits for them, and re-layouts: none -> 4.5 us  [per_device(): output_weight.reshape(output_weight.shape[0], n_tp // 2, 2, out_cols)]
    all_to_all x0 -> x1, starting transfers between devices: none -> 4.01 us  [per_device(): lax.all_to_all(attended, 'tp', split_axis=2, concat_axis=1, tiled=True)]
    ppermute x0 -> x1, waiting for transfers between devices: none -> 2.65 us  [per_device(): lax.ppermute(lax.dynamic_index_in_dim(projected, 1 - core, 0, keepdims=Fa...]
    add x2 -> x1, other arithmetic: 2.77 us -> 0.14 us  [reduce_scatter_tp(): parts = keep + got[:give.size].reshape(give.shape)]
    all_to_all x0 -> x1, local copies, waits for them, and re-layouts: none -> 2.04 us  [per_device(): lax.all_to_all(pair_sum.reshape(n_tp // 2, -1), 'tp', 0, 0, tiled=True, a...]
    squeeze x1, local copies, waits for them, and re-layouts: 2.04 us -> 0.1 us  [per_device(): lax.dynamic_index_in_dim(projected, 1 - core, 0, keepdims=False)]
  transfers between devices with their start and end apart: 10 -> 11, of which waited for: 4 -> 5; matrix products, arithmetic and copies ran while one was open for 28% -> 29% of each run, Pallas kernels for 0% -> 0%
where the time goes in v14:
time: 177 us; the launch traced here: 175 us
  starting transfers between devices  46.6 us (26%)
  local copies, waits for them, and re-layouts  35.9 us (20%)
  blocking collectives  35 us (20%)
  waiting for transfers between devices  25.2 us (14%)
  other arithmetic  22.1 us (12%)
  matrix products  9.4 us (5%)
    all_to_all x1, blocking collectives, per_device(): lax.all_to_all(pair_sum.reshape(n_tp // 2, -1), 'tp', 0, 0, tiled=True, a...  35 us
    all_to_all x1, starting transfers between devices, per_device(): lax.all_to_all(query_send, 'tp', split_axis=1, concat_axis=2, tiled=True)  9.13 us
    all_to_all x1, waiting for transfers between devices, per_device(): lax.all_to_all(query_send, 'tp', split_axis=1, concat_axis=2, tiled=True)  8.69 us
    all_to_all x1, starting transfers between devices, all_gather_tp(): lax.all_to_all(jnp.broadcast_to(block[None], (rest,) + block.shape), 'tp'...  8.47 us
    all_to_all x1, waiting for transfers between devices, per_device(): lax.all_to_all(panel_send, 'group', 0, 0, tiled=True)  6.85 us
    all_to_all x1, starting transfers between devices, reduce_scatter_tp(): lax.all_to_all(send, 'tp', 0, 0, tiled=True, axis_index_groups=stage_grou...  6.57 us
    all_to_all x1, starting transfers between devices, per_device(): lax.all_to_all(outgoing, 'group', split_axis=0, concat_axis=0, tiled=True)  6.07 us
    all_to_all x1, starting transfers between devices, per_device(): lax.all_to_all(panel_send, 'group', 0, 0, tiled=True)  5.85 us
  transfers between devices with their start and end apart: 11, of which 5 were waited for; matrix products, arithmetic and copies ran while one was open for 29% of the time, Pallas kernels for 0%

profile of v14, /device:TPU:2, one launch (start us, length us, event | category | flops | bytes accessed | tf_op | source)
XLA Modules:
  0.0 175.4 jit_solution(10779676002338842781)
XLA Ops:
  0.0 1.6 broadcast_in_dim.136
  1.6 8.5 %all-to-all-start.1 = ((bf16[8,2,32,256]{3,2,1,0:T(8,128)(2,1)}), bf16[8,2,32,256]{3,2,1,0:T(8,128)(2,1)}, u32[]{:S(2)}, u32[]{:S(2)}) async-start(bf16[8,2,32,256]{3,2,1,0:T(8,128)(2,1)} %broadcast_in_dim.136), calls=%async_computation.1 | async-start | bytes 524288 | tf_op jit(solution)/shard_map/all_to_all | solution.py:106
  10.1 1.0 fusion.53
  11.1 0.8 broadcast_compare_fusion
  11.9 1.3 convolution_bitcast_fusion
  13.1 0.9 reshape.445
  14.1 0.9 constant_dynamic-slice_fusion.2
  16.9 1.1 broadcast_select_fusion
  18.7 0.8 broadcast_select_fusion.2
  19.6 2.1 %constant_dynamic-slice_fusion.1 = (f32[16,1,2,1024]{3,1,0,2:T(1,128)}, f32[16,1,2,1024]{3,1,0,2:T(1,128)}) fusion(f32[16,2,2,1024]{3,1,0,2:T(2,128)} %reshape.445, s32[]{:T(128)S(6)} %select_n.186, s32[]{:T(128)S(6)} %select_n.187), kind=kLoop, calls=%fused_computation.102 | loop fusion | bytes 524296 | tf_op jit(solution)/shard_map/jit(dynamic_index_in_dim)/dynamic_slice | solution.py:87
  21.7 2.2 %pad_maximum_fusion.1 = bf16[8,2,328,128]{3,2,1,0:T(8,128)(2,1)} fusion(bf16[8,2,8,128]{3,2,1,0:T(8,128)(2,1)S(1)} %broadcast_select_fusion.3, bf16[8,2,64,128]{3,2,1,0:T(8,128)(2,1)} %broadcast_select_fusion.2, bf16[8,2,256,128]{3,2,1,0:T(8,128)(2,1)S(1)} %copy-done.4), kind=kLoop, calls=%fused_computation.16 | loop fusion | flops 4030464 | bytes 2686976 | tf_op jit(solution)/shard_map/concatenate | solution.py:159
  23.9 5.9 %all-to-all-start.2 = ((bf16[8,2,328,128]{3,2,1,0:T(8,128)(2,1)}), bf16[8,2,328,128]{3,2,1,0:T(8,128)(2,1)S(1)}, u32[]{:S(2)}, u32[]{:S(2)}) async-start(bf16[8,2,328,128]{3,2,1,0:T(8,128)(2,1)} %pad_maximum_fusion.1), calls=%async_computation.2 | async-start | bytes 2686976 | tf_op jit(solution)/shard_map/all_to_all | solution.py:167
  29.7 1.0 copy.324
  32.4 2.9 %gather_fusion = bf16[32,16,1024]{2,1,0:T(8,128)(2,1)} fusion(bf16[32,16,1024]{2,1,0:T(8,128)(2,1)} %param.20, s32[1024]{0:T(1024)S(1)} %pad_clamp_fusion.3), kind=kCustom, calls=%fused_computation | custom fusion | bytes 2097280 | tf_op jit(solution)/shard_map/jit(_take)/gather | solution.py:231
  35.4 2.4 %select_multiply_fusion = bf16[32,16,1024]{2,1,0:T(8,128)(2,1)} fusion(bf16[32,16,1024]{2,1,0:T(8,128)(2,1)} %gather_fusion, pred[32]{0:T(512)(128)(4,1)S(1)} %le.73, bf16[32]{0:T(256)(128)(2,1)S(1)} %reshape.464), kind=kLoop, calls=%fused_computation.35 | loop fusion | flops 1048576 | bytes 2097248 | tf_op jit(solution)/shard_map/mul | solution.py:231
  37.8 2.9 %collective-permute-start = (bf16[8,2,32,256]{3,2,1,0:T(8,128)(2,1)}, bf16[8,2,32,256]{3,2,1,0:T(8,128)(2,1)}, u32[]{:S(2)}, u32[]{:S(2)}) collective-permute-start(bf16[8,2,32,256]{3,2,1,0:T(8,128)(2,1)} %all-to-all-done.1), channel_id=1, source_target_pairs={{0,2},{1,3},{2,0},{3,1},{4,6},{5,7},{6,4},{7,5},{8,10},{9,11},{10,... | collective-permute-start | bytes 786440 | tf_op jit(solution)/shard_map/ppermute | solution.py:116
  40.7 6.8 %all-to-all-done.2 = bf16[8,2,328,128]{3,2,1,0:T(8,128)(2,1)S(1)} async-done(((bf16[8,2,328,128]{3,2,1,0:T(8,128)(2,1)}), bf16[8,2,328,128]{3,2,1,0:T(8,128)(2,1)S(1)}, u32[]{:S(2)}, u32[]{:S(2)}) %all-to-all-start.2) | async-done | bytes 1343520 | tf_op jit(solution)/shard_map/all_to_all | solution.py:167
  47.6 6.1 %all-to-all-start = ((bf16[32,16,1024]{2,1,0:T(8,128)(2,1)}), bf16[32,16,1024]{2,1,0:T(8,128)(2,1)}, u32[]{:S(2)}, u32[]{:S(2)}) async-start(bf16[32,16,1024]{2,1,0:T(8,128)(2,1)} %select_multiply_fusion), calls=%async_computation | async-start | bytes 2097152 | tf_op jit(solution)/shard_map/all_to_all | solution.py:234
  53.7 1.3 slice.149
  55.0 2.1 %gather_fusion.6 = bf16[32,256,128]{2,1,0:T(8,128)(2,1)} fusion(bf16[16,256,128]{2,1,0:T(8,128)(2,1)S(1)} %slice.149, s32[1024]{0:T(1024)S(1)} %pad_clamp_fusion), kind=kCustom, calls=%fused_computation.6 | custom fusion | bytes 4194432 | tf_op jit(solution)/shard_map/jit(_take)/gather | solution.py:175
  57.1 2.1 %fusion.4 = f32[32,128,2]{1,2,0:T(2,128)S(1)} fusion(bf16[32,256,128]{2,1,0:T(8,128)(2,1)} %gather_fusion.6, pred[32]{0:T(512)(128)(4,1)S(1)} %get-tuple-element.17, bf16[2,32,256]{2,1,0:T(8,128)(2,1)S(1)} %copy-done.9), kind=kOutput, calls=%fused_computation.13 | convolution fusion | flops 5242880 | bytes 2162720 | tf_op jit(solution)/shard_map/srd,rdk->srk/dot_general | solution.py:184
  59.6 2.1 %maximum_select_fusion.2 = bf16[8,2,2,32,256]{4,3,2,0,1:T(8,128)(2,1)} fusion(bf16[8,1,2,32,256]{4,3,2,0,1:T(8,128)(2,1)} %bitcast.10, bf16[8,1,2,32,256]{4,3,2,0,1:T(8,128)(2,1)} %bitcast.9, pred[]{:T(512)S(6)} %eq.13), kind=kLoop, calls=%fused_computation.39 | loop fusion | flops 786432 | bytes 1048577 | tf_op jit(solution)/shard_map/jit(_where)/select_n | solution.py:117
  62.5 3.0 %collective-permute-start.3 = (f32[24576]{0:T(1024)S(1)}, f32[24576]{0:T(1024)S(1)}, u32[]{:S(2)}, u32[]{:S(2)}) collective-permute-start(f32[24576]{0:T(1024)S(1)} %pad_maximum_fusion.4), channel_id=1, source_target_pairs={{0,2},{1,3},{2,0},{3,1},{4,6},{5,7},{6,4},{7,5},{8,10},{9,11},{10,... | collective-permute-start | bytes 294920 | tf_op jit(solution)/shard_map/ppermute | solution.py:90
  65.4 2.1 %maximum_select_fusion.1 = bf16[8,2,1,2,32,256]{5,4,3,0,2,1:T(8,128)(2,1)} fusion(bf16[8,1,1,2,32,256]{5,4,3,0,2,1:T(8,128)(2,1)} %bitcast.8, bf16[8,1,1,2,32,256]{5,4,3,0,2,1:T(8,128)(2,1)} %bitcast.7, pred[]{:T(512)S(6)} %eq.13), kind=kLoop, calls=%fused_computation.38 | loop fusion | flops 786432 | bytes 1048577 | tf_op jit(solution)/shard_map/jit(_where)/select_n | solution.py:117
  67.6 2.1 %collective-permute-done.3 = f32[24576]{0:T(1024)S(1)} collective-permute-done((f32[24576]{0:T(1024)S(1)}, f32[24576]{0:T(1024)S(1)}, u32[]{:S(2)}, u32[]{:S(2)}) %collective-permute-start.3) | collective-permute-done | bytes 98336 | tf_op jit(solution)/shard_map/ppermute | solution.py:90
  69.8 0.9 all_to_all.40
  70.8 6.6 %all-to-all-start.3 = ((f32[8,1,10240]{2,1,0:T(1,128)}), f32[8,1,10240]{2,1,0:T(1,128)}, u32[]{:S(2)}, u32[]{:S(2)}) async-start(f32[8,1,10240]{2,1,0:T(1,128)} %all_to_all.40), calls=%async_computation.3 | async-start | bytes 655360 | tf_op jit(solution)/shard_map/all_to_all | solution.py:98
  77.4 2.7 %pad_maximum_fusion = bf16[64,16,1024]{2,1,0:T(8,128)(2,1)} fusion(bf16[32,16,1024]{2,1,0:T(8,128)(2,1)} %all-to-all-done, bf16[32,16,1024]{2,1,0:T(8,128)(2,1)S(1)} %copy-done.3), kind=kLoop, calls=%fused_computation.8 | loop fusion | flops 1048576 | bytes 4194304 | tf_op jit(solution)/shard_map/concatenate | solution.py:235
  80.1 2.2 %gather_fusion.1 = bf16[32,16,1024]{2,1,0:T(8,128)(2,1)S(1)} fusion(bf16[64,16,1024]{2,1,0:T(8,128)(2,1)} %pad_maximum_fusion, s32[1024]{0:T(1024)S(1)} %pad_clamp_fusion.2), kind=kCustom, calls=%fused_computation.1 | custom fusion | bytes 2097280 | tf_op jit(solution)/shard_map/jit(_take)/gather | solution.py:236
  82.3 1.3 copy.231
  83.6 2.3 %broadcast_select_fusion.1 = bf16[1,512,1024]{1,2,0:T(8,128)(2,1)} fusion(bf16[1,512,1024]{1,2,0:T(8,128)(2,1)} %copy.231, pred[512]{0:T(512)(128)(4,1)S(1)} %broadcast_in_dim.131), kind=kLoop, calls=%fused_computation.37 | loop fusion | flops 524288 | bytes 2097664 | tf_op jit(solution)/shard_map/jit(_take)/select_n | solution.py:236
  85.9 1.0 slice.148
  87.0 0.8 slice.156
  87.7 1.4 gather_fusion.5
  90.1 1.6 maximum_select_fusion
  91.9 1.2 reduce_sum.36
  93.6 1.4 fusion.27
  96.2 9.1 %all-to-all-start.4 = ((f32[2,32,1,144]{3,0,2,1:T(2,128)}), f32[2,32,1,144]{3,0,2,1:T(2,128)S(1)}, u32[]{:S(2)}, u32[]{:S(2)}) async-start(f32[2,32,1,144]{3,0,2,1:T(2,128)} %copy.252), calls=%async_computation.4 | async-start | bytes 131072 | tf_op jit(solution)/shard_map/all_to_all | solution.py:216
  105.3 1.3 fusion.63
  106.6 8.7 %all-to-all-done.4 = f32[2,32,1,144]{3,0,2,1:T(2,128)S(1)} async-done(((f32[2,32,1,144]{3,0,2,1:T(2,128)}), f32[2,32,1,144]{3,0,2,1:T(2,128)S(1)}, u32[]{:S(2)}, u32[]{:S(2)}) %all-to-all-start.4) | async-done | bytes 36896 | tf_op jit(solution)/shard_map/all_to_all | solution.py:216
  117.4 4.0 %all-to-all-start.5 = ((bf16[2,1,32,128]{3,0,1,2:T(2,128)(2,1)}), bf16[2,1,32,128]{3,0,1,2:T(2,128)(2,1)S(1)}, u32[]{:S(2)}, u32[]{:S(2)}) async-start(bf16[2,1,32,128]{3,0,1,2:T(2,128)(2,1)} %copy.263), calls=%async_computation.5 | async-start | bytes 32768 | tf_op jit(solution)/shard_map/all_to_all | solution.py:240
  121.4 4.5 %reshape.463 = bf16[128,16,2,256]{3,2,1,0:T(2,128)(2,1)} reshape(bf16[128,8192]{1,0:T(8,128)(2,1)} %param.16) | data formatting | bytes 4194304 | tf_op jit(solution)/shard_map/reshape | solution.py:246
  125.9 5.0 %all-to-all-done.5 = bf16[2,1,32,128]{3,0,1,2:T(2,128)(2,1)S(1)} async-done(((bf16[2,1,32,128]{3,0,1,2:T(2,128)(2,1)}), bf16[2,1,32,128]{3,0,1,2:T(2,128)(2,1)S(1)}, u32[]{:S(2)}, u32[]{:S(2)}) %all-to-all-start.5) | async-done | bytes 16416 | tf_op jit(solution)/shard_map/all_to_all | solution.py:240
  130.9 3.0 %fusion.2 = f32[64,16,2,256]{3,0,2,1:T(8,128)S(1)} fusion(bf16[64,128,1,1]{1,0,3,2:T(8,128)(2,1)S(1)} %bitcast.202, bf16[128,16,2,256]{3,2,1,0:T(2,128)(2,1)} %reshape.463), kind=kOutput, calls=%fused_computation.11 | convolution fusion | flops 134217728 | bytes 4210688 | tf_op jit(solution)/shard_map/rk,kjcl->cjrl/dot_general | solution.py:243
  134.1 2.6 %collective-permute-done.4 = f32[16,64,256]{2,1,0:T(8,128)S(1)} collective-permute-done((f32[16,64,256]{2,1,0:T(8,128)S(1)}, f32[16,64,256]{2,1,0:T(8,128)S(1)}, u32[]{:S(2)}, u32[]{:S(2)}) %collective-permute-start.4) | collective-permute-done | bytes 1048608 | tf_op jit(solution)/shard_map/ppermute | solution.py:249
  136.9 2.0 %all_to_all.47 = f32[16,1,16384]{2,1,0:T(1,128)} reshape(f32[16,64,256]{2,1,0:T(8,128)S(1)} %bitcast_add_fusion) | data formatting | bytes 2097152 | tf_op jit(solution)/shard_map/all_to_all | solution.py:256
  138.9 35.0 %all_to_all.55 = f32[16,1,16384]{2,1,0:T(1,128)S(1)} all-to-all(f32[16,1,16384]{2,1,0:T(1,128)} %all_to_all.47), channel_id=1, replica_groups={{0,2,4,6,8,10,12,14,16,18,20,22,24,26,28,30},{1,3,5,7,9,11,13,15,17,19,..., dimensions={0} | all-to-all | bytes 2097152 | tf_op jit(solution)/shard_map/all_to_all | solution.py:256
  174.0 0.8 reduce_sum.39
  (115 shorter events, 10.8 us)
Async XLA Ops:
  0.0 95.0 %copy-start = (bf16[8192,128]{1,0:T(8,128)(2,1)S(1)}, bf16[8192,128]{1,0:T(8,128)(2,1)}, u32[]{:S(2)}) copy-start(bf16[8192,128]{1,0:T(8,128)(2,1)} %param.14) | copy-start | bytes 6291460
  0.0 16.0 %copy-start.2 = (bf16[4,256,128]{2,1,0:T(8,128)(2,1)S(1)}, bf16[4,256,128]{2,1,0:T(8,128)(2,1)}, u32[]{:S(2)}) copy-start(bf16[4,256,128]{2,1,0:T(8,128)(2,1)} %param.17) | copy-start | bytes 786436
  1.6 22.2 %all-to-all-start.1 = ((bf16[8,2,32,256]{3,2,1,0:T(8,128)(2,1)}), bf16[8,2,32,256]{3,2,1,0:T(8,128)(2,1)}, u32[]{:S(2)}, u32[]{:S(2)}) async-start(bf16[8,2,32,256]{3,2,1,0:T(8,128)(2,1)} %broadcast_in_dim.136), calls=%async_computation.1 | async-start | bytes 524288 | tf_op jit(solution)/shard_map/all_to_all | solution.py:106
  16.1 2.0 %copy-start.6 = (bf16[4,64,128]{2,1,0:T(8,128)(2,1)S(1)}, bf16[4,64,128]{2,1,0:T(8,128)(2,1)}, u32[]{:S(2)}) copy-start(bf16[4,64,128]{2,1,0:T(8,128)(2,1)} %param.18) | copy-start | bytes 196612
  16.8 2.6 %copy-start.10 = (s32[1,1,8,4]{2,3,1,0:T(4,128)S(1)}, s32[1,1,8,4]{2,3,1,0:T(4,128)}, u32[]{:S(2)}) copy-start(s32[1,1,8,4]{2,3,1,0:T(4,128)} %param.23) | copy-start | bytes 388
  18.1 3.6 %copy-start.4 = (bf16[8,2,256,128]{3,2,1,0:T(8,128)(2,1)S(1)}, bf16[8,2,256,128]{3,2,1,0:T(8,128)(2,1)}, u32[]{:S(2)}) copy-start(bf16[8,2,256,128]{3,2,1,0:T(8,128)(2,1)} %broadcast_select_fusion) | copy-start | bytes 3145732
  23.9 11.5 %copy-start.12 = (s32[32]{0:T(128)S(1)}, s32[32]{0:T(128)}, u32[]{:S(2)}) copy-start(s32[32]{0:T(128)} %param.24) | copy-start | bytes 388
  23.9 11.5 %copy-start.11 = (s32[1,32]{1,0:T(1,128)S(1)}, s32[1,32]{1,0:T(1,128)}, u32[]{:S(2)}) copy-start(s32[1,32]{1,0:T(1,128)} %param.22) | copy-start | bytes 388
  23.9 23.7 %all-to-all-start.2 = ((bf16[8,2,328,128]{3,2,1,0:T(8,128)(2,1)}), bf16[8,2,328,128]{3,2,1,0:T(8,128)(2,1)S(1)}, u32[]{:S(2)}, u32[]{:S(2)}) async-start(bf16[8,2,328,128]{3,2,1,0:T(8,128)(2,1)} %pad_maximum_fusion.1), calls=%async_computation.2 | async-start | bytes 2686976 | tf_op jit(solution)/shard_map/all_to_all | solution.py:167
  37.8 21.8 %collective-permute-start = (bf16[8,2,32,256]{3,2,1,0:T(8,128)(2,1)}, bf16[8,2,32,256]{3,2,1,0:T(8,128)(2,1)}, u32[]{:S(2)}, u32[]{:S(2)}) collective-permute-start(bf16[8,2,32,256]{3,2,1,0:T(8,128)(2,1)} %all-to-all-done.1), channel_id=1, source_target_pairs={{0,2},{1,3},{2,0},{3,1},{4,6},{5,7},{6,4},{7,5},{8,10},{9,11},{10,... | collective-permute-start | bytes 786440 | tf_op jit(solution)/shard_map/ppermute | solution.py:116
  47.6 6.1 %copy-start.1 = (bf16[8,2,328,128]{3,2,1,0:T(8,128)(2,1)}, bf16[8,2,328,128]{3,2,1,0:T(8,128)(2,1)S(1)}, u32[]{:S(2)}) copy-start(bf16[8,2,328,128]{3,2,1,0:T(8,128)(2,1)S(1)} %all-to-all-done.2) | copy-start | bytes 4030468
  47.6 23.2 %all-to-all-start = ((bf16[32,16,1024]{2,1,0:T(8,128)(2,1)}), bf16[32,16,1024]{2,1,0:T(8,128)(2,1)}, u32[]{:S(2)}, u32[]{:S(2)}) async-start(bf16[32,16,1024]{2,1,0:T(8,128)(2,1)} %select_multiply_fusion), calls=%async_computation | async-start | bytes 2097152 | tf_op jit(solution)/shard_map/all_to_all | solution.py:234
  55.0 2.2 %copy-start.9 = (bf16[2,32,256]{2,1,0:T(8,128)(2,1)S(1)}, bf16[2,32,256]{2,1,0:T(8,128)(2,1)}, u32[]{:S(2)}) copy-start(bf16[2,32,256]{2,1,0:T(8,128)(2,1)} %param.13) | copy-start | bytes 98308
  57.1 2.1 %copy-start.8 = (f32[16,8,2,128]{3,1,2,0:T(8,128)S(1)}, f32[16,8,2,128]{3,1,2,0:T(8,128)}, u32[]{:S(2)}) copy-start(f32[16,8,2,128]{3,1,2,0:T(8,128)} %copy.285) | copy-start | bytes 393220
  59.2 3.1 %copy-start.7 = (f32[16,1,2,1024]{3,1,0,2:T(1,128)S(1)}, f32[16,1,2,1024]{3,1,0,2:T(1,128)}, u32[]{:S(2)}) copy-start(f32[16,1,2,1024]{3,1,0,2:T(1,128)} %get-tuple-element.7) | copy-start | bytes 393220
  59.2 2.9 %collective-permute-start.2 = (f32[40960]{0:T(1024)S(1)}, f32[40960]{0:T(1024)S(1)}, u32[]{:S(2)}, u32[]{:S(2)}) collective-permute-start(f32[40960]{0:T(1024)S(1)} %pad_maximum_fusion.3), channel_id=1, source_target_pairs={{0,1},{1,0},{2,3},{3,2},{4,5},{5,4},{6,7},{7,6},{8,9},{9,8},{10,11... | collective-permute-start | bytes 491528 | tf_op jit(solution)/shard_map/ppermute | solution.py:90
  61.7 28.4 %collective-permute-start.1 = (bf16[8,2,2,32,256]{4,3,2,0,1:T(8,128)(2,1)}, bf16[8,2,2,32,256]{4,3,2,0,1:T(8,128)(2,1)}, u32[]{:S(2)}, u32[]{:S(2)}) collective-permute-start(bf16[8,2,2,32,256]{4,3,2,0,1:T(8,128)(2,1)} %maximum_select_fusion.2), channel_id=1, source_target_pairs={{0,1},{1,0},{2,3},{3,2},{4,5},{5,4},{6,7},{7,6},{8,9},{9,8},{10,11... | collective-permute-start | bytes 1572872 | tf_op jit(solution)/shard_map/ppermute | solution.py:116
  62.4 14.9 %copy-start.3 = (bf16[32,16,1024]{2,1,0:T(8,128)(2,1)S(1)}, bf16[32,16,1024]{2,1,0:T(8,128)(2,1)}, u32[]{:S(2)}) copy-start(bf16[32,16,1024]{2,1,0:T(8,128)(2,1)} %param.20) | copy-start | bytes 3145732
  62.5 7.2 %collective-permute-start.3 = (f32[24576]{0:T(1024)S(1)}, f32[24576]{0:T(1024)S(1)}, u32[]{:S(2)}, u32[]{:S(2)}) collective-permute-start(f32[24576]{0:T(1024)S(1)} %pad_maximum_fusion.4), channel_id=1, source_target_pairs={{0,2},{1,3},{2,0},{3,1},{4,6},{5,7},{6,4},{7,5},{8,10},{9,11},{10,... | collective-permute-start | bytes 294920 | tf_op jit(solution)/shard_map/ppermute | solution.py:90
  70.8 21.1 %all-to-all-start.3 = ((f32[8,1,10240]{2,1,0:T(1,128)}), f32[8,1,10240]{2,1,0:T(1,128)}, u32[]{:S(2)}, u32[]{:S(2)}) async-start(f32[8,1,10240]{2,1,0:T(1,128)} %all_to_all.40), calls=%async_computation.3 | async-start | bytes 655360 | tf_op jit(solution)/shard_map/all_to_all | solution.py:98
  85.9 4.2 %copy-start.5 = (bf16[8,2,1,2,32,256]{5,4,3,0,2,1:T(8,128)(2,1)S(1)}, bf16[8,2,1,2,32,256]{5,4,3,0,2,1:T(8,128)(2,1)}, u32[]{:S(2)}) copy-start(bf16[8,2,1,2,32,256]{5,4,3,0,2,1:T(8,128)(2,1)} %maximum_select_fusion.1) | copy-start | bytes 1572868
  96.2 19.1 %all-to-all-start.4 = ((f32[2,32,1,144]{3,0,2,1:T(2,128)}), f32[2,32,1,144]{3,0,2,1:T(2,128)S(1)}, u32[]{:S(2)}, u32[]{:S(2)}) async-start(f32[2,32,1,144]{3,0,2,1:T(2,128)} %copy.252), calls=%async_computation.4 | async-start | bytes 131072 | tf_op jit(solution)/shard_map/all_to_all | solution.py:216
  117.4 13.5 %all-to-all-start.5 = ((bf16[2,1,32,128]{3,0,1,2:T(2,128)(2,1)}), bf16[2,1,32,128]{3,0,1,2:T(2,128)(2,1)S(1)}, u32[]{:S(2)}, u32[]{:S(2)}) async-start(bf16[2,1,32,128]{3,0,1,2:T(2,128)(2,1)} %copy.263), calls=%async_computation.5 | async-start | bytes 32768 | tf_op jit(solution)/shard_map/all_to_all | solution.py:240
  134.0 2.7 %collective-permute-start.4 = (f32[16,64,256]{2,1,0:T(8,128)S(1)}, f32[16,64,256]{2,1,0:T(8,128)S(1)}, u32[]{:S(2)}, u32[]{:S(2)}) collective-permute-start(f32[16,64,256]{2,1,0:T(8,128)S(1)} %dynamic-slice_bitcast_fusion), channel_id=1, source_target_pairs={{0,1},{1,0},{2,3},{3,2},{4,5},{5,4},{6,7},{7,6},{8,9},{9,8},{10,11... | collective-permute-start | bytes 3145736 | tf_op jit(solution)/shard_map/ppermute | solution.py:249

commit v15 on v13

--- a/solution.py
+++ b/solution.py
@@ -101,17 +101,17 @@
     return total[: flat.shape[1]], total[flat.shape[1] :].reshape(shared.shape)
 
 
-def all_gather_tp(block, column_id, n_tp):
-    rest = n_tp >> len(SWAP_BITS)
+def all_gather_tp(block, column_id, n_tp, bits=SWAP_BITS):
+    rest = n_tp >> len(bits)
     gathered = lax.all_to_all(
         jnp.broadcast_to(block[None], (rest,) + block.shape),
         "tp",
         0,
         0,
         tiled=True,
-        axis_index_groups=stage_groups(n_tp, SWAP_BITS),
-    )
-    for done, bit in enumerate(reversed(SWAP_BITS)):
+        axis_index_groups=stage_groups(n_tp, bits),
+    )
+    for done, bit in enumerate(reversed(bits)):
         mine = (column_id // bit) % 2
         other = lax.ppermute(gathered, "tp", [(t, t ^ bit) for t in range(n_tp)])
         gathered = jnp.where(
@@ -176,7 +176,7 @@
     upq_rows = jnp.take(upq_recv, request_adapter_entry, axis=0)
     upv_rows = jnp.take(upv_recv, request_adapter_entry, axis=0)
 
-    hidden_sent = all_gather_tp(hidden, column_id, n_tp)
+    hidden_sent = all_gather_tp(hidden, column_id, n_tp, SWAP_BITS[:1])
     hidden_full = jnp.transpose(hidden_sent, (1, 2, 0, 3)).reshape(
         step_count, batch_rows, n_tp * width_local
     )

time: 175 us -> 184 us (1.051)
  waiting for transfers between devices: 18.6 us -> 33.2 us
  other arithmetic: 24.6 us -> 20.7 us
  starting transfers between devices: 42.5 us -> 38.6 us
    all_to_all x1, waiting for transfers between devices: 0.01 us -> 10.4 us  [per_device(): lax.all_to_all(outgoing, 'group', split_axis=0, concat_axis=0, tiled=True)]
    all_to_all x1, waiting for transfers between devices: 0.01 us -> 6.79 us  [all_gather_tp(): lax.all_to_all(jnp.broadcast_to(block[None], (rest,) + block.shape), 'tp'...]
    select_n x3 -> x1, other arithmetic: 5.79 us -> 1.7 us  [all_gather_tp(): jnp.where(mine == 0, jnp.stack([gathered, other], 1 + done), jnp.stack([o...]
    ppermute x2 -> x1, starting transfers between devices: 3.35 us -> 0.01 us  [all_gather_tp(): other = lax.ppermute(gathered, 'tp', [(t, t ^ bit) for t in range(n_tp)])]
    all_to_all x1, starting transfers between devices: 8.47 us -> 11 us  [all_gather_tp(): lax.all_to_all(jnp.broadcast_to(block[None], (rest,) + block.shape), 'tp'...]
    all_to_all x1, starting transfers between devices: 6.57 us -> 4.34 us  [reduce_scatter_tp(): lax.all_to_all(send, 'tp', 0, 0, tiled=True, axis_index_groups=stage_grou...]
  transfers between devices with their start and end apart: 10 -> 9, of which waited for: 4 -> 6; matrix products, arithmetic and copies ran while one was open for 28% -> 20% of each run, Pallas kernels for 0% -> 0%
where the time goes in v15:
time: 184 us; the launch traced here: 182 us
  blocking collectives  46.6 us (25%)
  starting transfers between devices  38.6 us (21%)
  waiting for transfers between devices  33.2 us (18%)
  local copies, waits for them, and re-layouts  32.5 us (18%)
  other arithmetic  20.7 us (11%)
  matrix products  9.08 us (5%)
    all_to_all x1, blocking collectives, reduce_scatter_tp(): lax.all_to_all(send, 'tp', 0, 0, tiled=True, axis_index_groups=stage_grou...  33.9 us
    all_to_all x1, blocking collectives, per_device(): lax.all_to_all(attended, 'tp', split_axis=2, concat_axis=1, tiled=True)  12.7 us
    all_to_all x1, starting transfers between devices, all_gather_tp(): lax.all_to_all(jnp.broadcast_to(block[None], (rest,) + block.shape), 'tp'...  11 us
    all_to_all x1, waiting for transfers between devices, per_device(): lax.all_to_all(outgoing, 'group', split_axis=0, concat_axis=0, tiled=True)  10.4 us
    all_to_all x1, waiting for transfers between devices, per_device(): lax.all_to_all(query_send, 'tp', split_axis=1, concat_axis=2, tiled=True)  8.69 us
    all_to_all x1, starting transfers between devices, per_device(): lax.all_to_all(query_send, 'tp', split_axis=1, concat_axis=2, tiled=True)  7.64 us
    all_to_all x1, waiting for transfers between devices, all_gather_tp(): lax.all_to_all(jnp.broadcast_to(block[None], (rest,) + block.shape), 'tp'...  6.79 us
    all_to_all x1, starting transfers between devices, per_device(): lax.all_to_all(outgoing, 'group', split_axis=0, concat_axis=0, tiled=True)  6.28 us
  transfers between devices with their start and end apart: 9, of which 6 were waited for; matrix products, arithmetic and copies ran while one was open for 20% of the time, Pallas kernels for 0%

profile of v15, /device:TPU:2, one launch (start us, length us, event | category | flops | bytes accessed | tf_op | source)
XLA Modules:
  0.0 182.0 jit_solution(6893274216469049258)
XLA Ops:
  0.0 1.1 fusion.54
  1.1 0.8 broadcast_compare_fusion
  2.0 0.9 constant_dynamic-slice_fusion.4
  4.0 1.7 gather_fusion.2
  5.8 1.1 broadcast_select_fusion
  7.7 2.4 %pad_maximum_fusion.1 = bf16[8,2,328,128]{3,2,1,0:T(8,128)(2,1)} fusion(bf16[8,2,8,128]{3,2,1,0:T(8,128)(2,1)S(1)} %broadcast_select_fusion.3, bf16[8,2,64,128]{3,2,1,0:T(8,128)(2,1)S(1)} %broadcast_select_fusion.2, bf16[8,2,256,128]{3,2,1,0:T(8,128)(2,1)} %broadcast_select_fusion), kind=kLoop, calls=%fused_computation.17 | loop fusion | flops 4030464 | bytes 2686976 | tf_op jit(solution)/shard_map/concatenate | solution.py:159
  10.1 5.8 %all-to-all-start.2 = ((bf16[8,2,328,128]{3,2,1,0:T(8,128)(2,1)}), bf16[8,2,328,128]{3,2,1,0:T(8,128)(2,1)S(1)}, u32[]{:S(2)}, u32[]{:S(2)}) async-start(bf16[8,2,328,128]{3,2,1,0:T(8,128)(2,1)} %pad_maximum_fusion.1), calls=%async_computation.2 | async-start | bytes 2686976 | tf_op jit(solution)/shard_map/all_to_all | solution.py:167
  16.0 2.0 %convolution_bitcast_fusion = f32[32,2,1024]{2,0,1:T(8,128)} fusion(bf16[2,32,256]{2,1,0:T(8,128)(2,1)S(1)} %copy-done.6, bf16[256,1024]{1,0:T(8,128)(2,1)} %param.15), kind=kOutput, calls=%fused_computation.18 | convolution fusion | flops 33554432 | bytes 819200 | tf_op jit(solution)/shard_map/srd,dc->rsc/dot_general | solution.py:185
  17.9 1.8 reshape.414
  19.7 2.0 %constant_dynamic-slice_fusion.3 = (f32[16,1,2,1024]{3,1,0,2:T(1,128)}, f32[16,1,2,1024]{3,1,0,2:T(1,128)S(1)}) fusion(f32[16,2,2,1024]{3,1,0,2:T(2,128)} %reshape.414, s32[]{:T(128)S(6)} %select_n.159, s32[]{:T(128)S(6)} %select_n.160), kind=kLoop, calls=%fused_computation.100 | loop fusion | bytes 524296 | tf_op jit(solution)/shard_map/jit(dynamic_index_in_dim)/dynamic_slice | solution.py:87
  21.8 0.7 copy.254
  23.0 2.9 %gather_fusion = bf16[32,16,1024]{2,1,0:T(8,128)(2,1)} fusion(bf16[32,16,1024]{2,1,0:T(8,128)(2,1)} %param.20, s32[1024]{0:T(1024)S(1)} %pad_clamp_fusion.3), kind=kCustom, calls=%fused_computation | custom fusion | bytes 2097280 | tf_op jit(solution)/shard_map/jit(_take)/gather | solution.py:231
  25.9 2.4 %select_multiply_fusion = bf16[32,16,1024]{2,1,0:T(8,128)(2,1)} fusion(bf16[32,16,1024]{2,1,0:T(8,128)(2,1)} %gather_fusion, pred[32]{0:T(512)(128)(4,1)S(1)} %le.73, bf16[32]{0:T(256)(128)(2,1)S(1)} %reshape.436), kind=kLoop, calls=%fused_computation.34 | loop fusion | flops 1048576 | bytes 2097248 | tf_op jit(solution)/shard_map/mul | solution.py:231
  28.3 5.9 %all-to-all-done.2 = bf16[8,2,328,128]{3,2,1,0:T(8,128)(2,1)S(1)} async-done(((bf16[8,2,328,128]{3,2,1,0:T(8,128)(2,1)}), bf16[8,2,328,128]{3,2,1,0:T(8,128)(2,1)S(1)}, u32[]{:S(2)}, u32[]{:S(2)}) %all-to-all-start.2) | async-done | bytes 1343520 | tf_op jit(solution)/shard_map/all_to_all | solution.py:167
  34.2 0.9 broadcast_in_dim.136
  35.2 11.0 %all-to-all-start.1 = ((bf16[16,2,32,256]{3,2,1,0:T(8,128)(2,1)}), bf16[16,2,32,256]{3,2,1,0:T(8,128)(2,1)}, u32[]{:S(2)}, u32[]{:S(2)}) async-start(bf16[16,2,32,256]{3,2,1,0:T(8,128)(2,1)} %broadcast_in_dim.136), calls=%async_computation.1 | async-start | bytes 1048576 | tf_op jit(solution)/shard_map/all_to_all | solution.py:106
  46.1 1.3 slice.149
  47.5 2.2 %gather_fusion.6 = bf16[32,256,128]{2,1,0:T(8,128)(2,1)} fusion(bf16[16,256,128]{2,1,0:T(8,128)(2,1)S(1)} %slice.149, s32[1024]{0:T(1024)S(1)} %pad_clamp_fusion), kind=kCustom, calls=%fused_computation.6 | custom fusion | bytes 4194432 | tf_op jit(solution)/shard_map/jit(_take)/gather | solution.py:175
  49.6 2.1 %fusion.5 = f32[32,128,2]{1,2,0:T(2,128)S(1)} fusion(bf16[32,256,128]{2,1,0:T(8,128)(2,1)} %gather_fusion.6, pred[32]{0:T(512)(128)(4,1)S(1)} %get-tuple-element.19, bf16[2,32,256]{2,1,0:T(8,128)(2,1)S(1)} %copy-done.6), kind=kOutput, calls=%fused_computation.14 | convolution fusion | flops 5242880 | bytes 2162720 | tf_op jit(solution)/shard_map/srd,rdk->srk/dot_general | solution.py:184
  53.5 3.5 %collective-permute-start.2 = (f32[24576]{0:T(1024)S(1)}, f32[24576]{0:T(1024)S(1)}, u32[]{:S(2)}, u32[]{:S(2)}) collective-permute-start(f32[24576]{0:T(1024)S(1)} %pad_maximum_fusion.4), channel_id=1, source_target_pairs={{0,2},{1,3},{2,0},{3,1},{4,6},{5,7},{6,4},{7,5},{8,10},{9,11},{10,... | collective-permute-start | bytes 294920 | tf_op jit(solution)/shard_map/ppermute | solution.py:90
  57.6 6.8 %all-to-all-done.1 = bf16[16,2,32,256]{3,2,1,0:T(8,128)(2,1)} async-done(((bf16[16,2,32,256]{3,2,1,0:T(8,128)(2,1)}), bf16[16,2,32,256]{3,2,1,0:T(8,128)(2,1)}, u32[]{:S(2)}, u32[]{:S(2)}) %all-to-all-start.1) | async-done | bytes 524320 | tf_op jit(solution)/shard_map/all_to_all | solution.py:106
  64.3 6.3 %all-to-all-start = ((bf16[32,16,1024]{2,1,0:T(8,128)(2,1)}), bf16[32,16,1024]{2,1,0:T(8,128)(2,1)}, u32[]{:S(2)}, u32[]{:S(2)}) async-start(bf16[32,16,1024]{2,1,0:T(8,128)(2,1)} %select_multiply_fusion), calls=%async_computation | async-start | bytes 2097152 | tf_op jit(solution)/shard_map/all_to_all | solution.py:234
  70.8 1.0 all_to_all.38
  71.8 10.4 %all-to-all-done = bf16[32,16,1024]{2,1,0:T(8,128)(2,1)} async-done(((bf16[32,16,1024]{2,1,0:T(8,128)(2,1)}), bf16[32,16,1024]{2,1,0:T(8,128)(2,1)}, u32[]{:S(2)}, u32[]{:S(2)}) %all-to-all-start) | async-done | bytes 1048608 | tf_op jit(solution)/shard_map/all_to_all | solution.py:234
  82.2 4.3 %all-to-all-start.3 = ((f32[8,1,10240]{2,1,0:T(1,128)}), f32[8,1,10240]{2,1,0:T(1,128)}, u32[]{:S(2)}, u32[]{:S(2)}) async-start(f32[8,1,10240]{2,1,0:T(1,128)} %all_to_all.38), calls=%async_computation.3 | async-start | bytes 655360 | tf_op jit(solution)/shard_map/all_to_all | solution.py:98
  86.5 2.7 %pad_maximum_fusion = bf16[64,16,1024]{2,1,0:T(8,128)(2,1)} fusion(bf16[32,16,1024]{2,1,0:T(8,128)(2,1)} %all-to-all-done, bf16[32,16,1024]{2,1,0:T(8,128)(2,1)S(1)} %copy-done.2), kind=kLoop, calls=%fused_computation.11 | loop fusion | flops 1048576 | bytes 4194304 | tf_op jit(solution)/shard_map/concatenate | solution.py:235
  89.3 2.2 %gather_fusion.1 = bf16[32,16,1024]{2,1,0:T(8,128)(2,1)S(1)} fusion(bf16[64,16,1024]{2,1,0:T(8,128)(2,1)} %pad_maximum_fusion, s32[1024]{0:T(1024)S(1)} %pad_clamp_fusion.2), kind=kCustom, calls=%fused_computation.1 | custom fusion | bytes 2097280 | tf_op jit(solution)/shard_map/jit(_take)/gather | solution.py:236
  91.5 1.3 copy.206
  92.8 2.3 %broadcast_select_fusion.1 = bf16[1,512,1024]{1,2,0:T(8,128)(2,1)} fusion(bf16[1,512,1024]{1,2,0:T(8,128)(2,1)} %copy.206, pred[512]{0:T(512)(128)(4,1)S(1)} %broadcast_in_dim.131), kind=kLoop, calls=%fused_computation.36 | loop fusion | flops 524288 | bytes 2097664 | tf_op jit(solution)/shard_map/jit(_take)/select_n | solution.py:236
  95.1 1.0 slice.148
  96.1 0.8 slice.156
  96.8 1.4 gather_fusion.5
  99.2 1.7 maximum_select_fusion
  101.2 1.2 reduce_sum.36
  102.9 1.4 fusion.28
  104.8 0.7 copy.224
  105.5 7.6 %all-to-all-start.4 = ((f32[2,32,1,144]{3,0,2,1:T(2,128)}), f32[2,32,1,144]{3,0,2,1:T(2,128)S(1)}, u32[]{:S(2)}, u32[]{:S(2)}) async-start(f32[2,32,1,144]{3,0,2,1:T(2,128)} %copy.224), calls=%async_computation.4 | async-start | bytes 131072 | tf_op jit(solution)/shard_map/all_to_all | solution.py:216
  113.1 1.3 fusion.64
  114.4 8.7 %all-to-all-done.4 = f32[2,32,1,144]{3,0,2,1:T(2,128)S(1)} async-done(((f32[2,32,1,144]{3,0,2,1:T(2,128)}), f32[2,32,1,144]{3,0,2,1:T(2,128)S(1)}, u32[]{:S(2)}, u32[]{:S(2)}) %all-to-all-start.4) | async-done | bytes 36896 | tf_op jit(solution)/shard_map/all_to_all | solution.py:216
  124.6 12.7 %all_to_all.51 = bf16[2,1,32,128]{3,0,1,2:T(2,128)(2,1)S(1)} all-to-all(bf16[2,1,32,128]{3,0,1,2:T(2,128)(2,1)S(1)} %copy.235), channel_id=1, replica_groups=mesh['group'=8,'tp'=32] {'tp'}, dimensions={2} | all-to-all | bytes 32768 | tf_op jit(solution)/shard_map/all_to_all | solution.py:240
  137.3 2.0 %fusion = f32[64,32,256]{2,0,1:T(8,128)S(1)} fusion(bf16[64,128,1]{1,0,2:T(8,128)(2,1)S(1)} %bitcast.199, bf16[16,32,8,256]{3,2,1,0:T(8,128)(2,1)} %bitcast.180), kind=kOutput, calls=%fused_computation.8 | convolution fusion | flops 134217728 | bytes 4210688 | tf_op jit(solution)/shard_map/rk,kdc->drc/dot_general | solution.py:242
  139.5 1.5 copy.257
  141.0 2.0 %squeeze.19 = f32[16,1,16384]{2,1,0:T(1,128)} reshape(f32[16,1,64,256]{3,2,1,0:T(8,128)S(1)} %get-tuple-element.6) | data formatting | bytes 2097152 | tf_op jit(solution)/shard_map/jit(dynamic_index_in_dim)/squeeze | solution.py:87
  143.1 1.0 collective-permute-done.3
  144.0 2.6 %add.149 = f32[16,1,16384]{2,1,0:T(1,128)S(1)} add(f32[16,1,16384]{2,1,0:T(1,128)} %squeeze.19, f32[16,1,16384]{2,1,0:T(1,128)} %bitcast.56) | non-fusion elementwise | flops 262144 | bytes 3145728 | tf_op jit(solution)/shard_map/add | solution.py:91
  146.6 33.9 %all_to_all.52 = f32[16,1,16384]{2,1,0:T(1,128)S(1)} all-to-all(f32[16,1,16384]{2,1,0:T(1,128)S(1)} %add.149), channel_id=1, replica_groups={{0,2,4,6,8,10,12,14,16,18,20,22,24,26,28,30},{1,3,5,7,9,11,13,15,17,19,..., dimensions={0} | all-to-all | bytes 2097152 | tf_op jit(solution)/shard_map/all_to_all | solution.py:98
  180.5 0.8 reduce_sum.39
  181.4 0.6 convert_element_type.71
  (110 shorter events, 8.1 us)
Async XLA Ops:
  0.0 104.2 %copy-start = (bf16[8192,128]{1,0:T(8,128)(2,1)S(1)}, bf16[8192,128]{1,0:T(8,128)(2,1)}, u32[]{:S(2)}) copy-start(bf16[8192,128]{1,0:T(8,128)(2,1)} %param.14) | copy-start | bytes 6291460
  4.0 3.0 %copy-start.3 = (bf16[4,64,128]{2,1,0:T(8,128)(2,1)S(1)}, bf16[4,64,128]{2,1,0:T(8,128)(2,1)}, u32[]{:S(2)}) copy-start(bf16[4,64,128]{2,1,0:T(8,128)(2,1)} %param.18) | copy-start | bytes 196612
  7.6 8.3 %copy-start.7 = (s32[1,1,8,4]{2,3,1,0:T(4,128)S(1)}, s32[1,1,8,4]{2,3,1,0:T(4,128)}, u32[]{:S(2)}) copy-start(s32[1,1,8,4]{2,3,1,0:T(4,128)} %param.23) | copy-start | bytes 388
  7.7 8.3 %copy-start.6 = (bf16[2,32,256]{2,1,0:T(8,128)(2,1)S(1)}, bf16[2,32,256]{2,1,0:T(8,128)(2,1)}, u32[]{:S(2)}) copy-start(bf16[2,32,256]{2,1,0:T(8,128)(2,1)} %param.13) | copy-start | bytes 98308
  10.1 24.2 %all-to-all-start.2 = ((bf16[8,2,328,128]{3,2,1,0:T(8,128)(2,1)}), bf16[8,2,328,128]{3,2,1,0:T(8,128)(2,1)S(1)}, u32[]{:S(2)}, u32[]{:S(2)}) async-start(bf16[8,2,328,128]{3,2,1,0:T(8,128)(2,1)} %pad_maximum_fusion.1), calls=%async_computation.2 | async-start | bytes 2686976 | tf_op jit(solution)/shard_map/all_to_all | solution.py:167
  16.0 9.9 %copy-start.10 = (s32[32]{0:T(128)S(1)}, s32[32]{0:T(128)}, u32[]{:S(2)}) copy-start(s32[32]{0:T(128)} %param.24) | copy-start | bytes 388
  16.0 9.9 %copy-start.9 = (s32[1,32]{1,0:T(1,128)S(1)}, s32[1,32]{1,0:T(1,128)}, u32[]{:S(2)}) copy-start(s32[1,32]{1,0:T(1,128)} %param.22) | copy-start | bytes 388
  25.9 23.7 %copy-start.11 = (pred[32]{0:T(512)(128)(4,1)}, pred[32]{0:T(512)(128)(4,1)S(1)}, u32[]{:S(2)}) copy-start(pred[32]{0:T(512)(128)(4,1)S(1)} %get-tuple-element.19) | copy-start | bytes 100
  34.2 11.9 %copy-start.1 = (bf16[8,2,328,128]{3,2,1,0:T(8,128)(2,1)}, bf16[8,2,328,128]{3,2,1,0:T(8,128)(2,1)S(1)}, u32[]{:S(2)}) copy-start(bf16[8,2,328,128]{3,2,1,0:T(8,128)(2,1)S(1)} %all-to-all-done.2) | copy-start | bytes 4030468
  35.2 29.2 %all-to-all-start.1 = ((bf16[16,2,32,256]{3,2,1,0:T(8,128)(2,1)}), bf16[16,2,32,256]{3,2,1,0:T(8,128)(2,1)}, u32[]{:S(2)}, u32[]{:S(2)}) async-start(bf16[16,2,32,256]{3,2,1,0:T(8,128)(2,1)} %broadcast_in_dim.136), calls=%async_computation.1 | async-start | bytes 1048576 | tf_op jit(solution)/shard_map/all_to_all | solution.py:106
  49.6 2.1 %copy-start.5 = (f32[16,8,2,128]{3,1,2,0:T(8,128)S(1)}, f32[16,8,2,128]{3,1,2,0:T(8,128)}, u32[]{:S(2)}) copy-start(f32[16,8,2,128]{3,1,2,0:T(8,128)} %copy.254) | copy-start | bytes 393220
  49.6 3.7 %copy-start.4 = (f32[16,1,2,1024]{3,1,0,2:T(1,128)S(1)}, f32[16,1,2,1024]{3,1,0,2:T(1,128)}, u32[]{:S(2)}) copy-start(f32[16,1,2,1024]{3,1,0,2:T(1,128)} %get-tuple-element.9) | copy-start | bytes 393220
  51.7 1.5 collective-permute-start.1
  53.5 17.1 %collective-permute-start.2 = (f32[24576]{0:T(1024)S(1)}, f32[24576]{0:T(1024)S(1)}, u32[]{:S(2)}, u32[]{:S(2)}) collective-permute-start(f32[24576]{0:T(1024)S(1)} %pad_maximum_fusion.4), channel_id=1, source_target_pairs={{0,2},{1,3},{2,0},{3,1},{4,6},{5,7},{6,4},{7,5},{8,10},{9,11},{10,... | collective-permute-start | bytes 294920 | tf_op jit(solution)/shard_map/ppermute | solution.py:90
  57.6 29.0 %copy-start.2 = (bf16[32,16,1024]{2,1,0:T(8,128)(2,1)S(1)}, bf16[32,16,1024]{2,1,0:T(8,128)(2,1)}, u32[]{:S(2)}) copy-start(bf16[32,16,1024]{2,1,0:T(8,128)(2,1)} %param.20) | copy-start | bytes 3145732
  64.3 17.8 %all-to-all-start = ((bf16[32,16,1024]{2,1,0:T(8,128)(2,1)}), bf16[32,16,1024]{2,1,0:T(8,128)(2,1)}, u32[]{:S(2)}, u32[]{:S(2)}) async-start(bf16[32,16,1024]{2,1,0:T(8,128)(2,1)} %select_multiply_fusion), calls=%async_computation | async-start | bytes 2097152 | tf_op jit(solution)/shard_map/all_to_all | solution.py:234
  70.6 28.6 %collective-permute-start = (bf16[16,2,32,256]{3,2,1,0:T(8,128)(2,1)}, bf16[16,2,32,256]{3,2,1,0:T(8,128)(2,1)}, u32[]{:S(2)}, u32[]{:S(2)}) collective-permute-start(bf16[16,2,32,256]{3,2,1,0:T(8,128)(2,1)} %all-to-all-done.1), channel_id=1, source_target_pairs={{0,1},{1,0},{2,3},{3,2},{4,5},{5,4},{6,7},{7,6},{8,9},{9,8},{10,11... | collective-permute-start | bytes 1572872 | tf_op jit(solution)/shard_map/ppermute | solution.py:116
  82.2 19.0 %all-to-all-start.3 = ((f32[8,1,10240]{2,1,0:T(1,128)}), f32[8,1,10240]{2,1,0:T(1,128)}, u32[]{:S(2)}, u32[]{:S(2)}) async-start(f32[8,1,10240]{2,1,0:T(1,128)} %all_to_all.38), calls=%async_computation.3 | async-start | bytes 655360 | tf_op jit(solution)/shard_map/all_to_all | solution.py:98
  101.0 1.5 copy-start.12
  104.8 18.6 %copy-start.8 = (pred[512]{0:T(512)(128)(4,1)S(1)}, pred[512]{0:T(512)(128)(4,1)}, u32[]{:S(2)}) copy-start(pred[512]{0:T(512)(128)(4,1)} %iota_compare_fusion) | copy-start | bytes 1540
  105.5 17.6 %all-to-all-start.4 = ((f32[2,32,1,144]{3,0,2,1:T(2,128)}), f32[2,32,1,144]{3,0,2,1:T(2,128)S(1)}, u32[]{:S(2)}, u32[]{:S(2)}) async-start(f32[2,32,1,144]{3,0,2,1:T(2,128)} %copy.224), calls=%async_computation.4 | async-start | bytes 131072 | tf_op jit(solution)/shard_map/all_to_all | solution.py:216
  141.0 3.0 %collective-permute-start.3 = (f32[262144]{0:T(1024)}, f32[262144]{0:T(1024)}, u32[]{:S(2)}, u32[]{:S(2)}) collective-permute-start(f32[262144]{0:T(1024)} %bitcast.95), channel_id=1, source_target_pairs={{0,1},{1,0},{2,3},{3,2},{4,5},{5,4},{6,7},{7,6},{8,9},{9,8},{10,11... | collective-permute-start | bytes 3145736 | tf_op jit(solution)/shard_map/ppermute | solution.py:90

commit v16 on v13

--- a/solution.py
+++ b/solution.py
@@ -205,19 +205,22 @@
         upv_rows,
         preferred_element_type=jnp.float32,
     )
-    heads_local = query_rows.shape[2] // HEAD_SIZE
+    value_row = jnp.transpose(value_adapter_term, (1, 0, 2)).reshape(batch_rows, 1, -1)
     query_send = jnp.concatenate(
         [
-            query_rows.astype(jnp.float32).reshape(step_count, batch_rows, heads_local, HEAD_SIZE),
-            value_adapter_term.reshape(step_count, batch_rows, heads_local, value_cols),
+            jnp.transpose(query_rows.astype(jnp.float32), (1, 0, 2)),
+            jnp.pad(value_row, ((0, 0), (0, 0), (0, HEAD_SIZE - value_row.shape[2]))),
         ],
-        -1,
-    )
-    query_recv = lax.all_to_all(query_send, "tp", split_axis=1, concat_axis=2, tiled=True)
-    query_own = query_recv[..., :HEAD_SIZE].astype(jnp.bfloat16)
-    value_own = jnp.transpose(query_recv[..., HEAD_SIZE:], (1, 0, 2, 3)).reshape(
-        batch_own, step_count, -1
-    )
+        1,
+    )
+    query_recv = lax.all_to_all(query_send, "tp", 0, 0, tiled=True)
+    query_own = jnp.transpose(query_recv[:, :step_count], (1, 0, 2))[:, None].astype(
+        jnp.bfloat16
+    )
+    value_own = jnp.transpose(
+        query_recv[:, step_count, : step_count * value_cols].reshape(n_tp, step_count, value_cols),
+        (1, 0, 2),
+    ).reshape(batch_own, step_count, -1)
     keyval_new = jnp.concatenate(
         [
             key_value_plain[..., :key_span_width],

time: 175 us -> 176 us (level)
  no operation moved by 1% of the time
where the time goes in v16:
time: 176 us; the launch traced here: 174 us
  blocking collectives  46.6 us (26%)
  starting transfers between devices  42.5 us (24%)
  local copies, waits for them, and re-layouts  32.5 us (18%)
  other arithmetic  24.6 us (14%)
  waiting for transfers between devices  18.6 us (11%)
  matrix products  8.39 us (5%)
    all_to_all x1, blocking collectives, reduce_scatter_tp(): lax.all_to_all(send, 'tp', 0, 0, tiled=True, axis_index_groups=stage_grou...  33.9 us
    all_to_all x1, blocking collectives, per_device(): lax.all_to_all(attended, 'tp', split_axis=2, concat_axis=1, tiled=True)  12.7 us
    all_to_all x1, starting transfers between devices, per_device(): query_recv = lax.all_to_all(query_send, 'tp', 0, 0, tiled=True)  9.13 us
    all_to_all x1, waiting for transfers between devices, per_device(): query_recv = lax.all_to_all(query_send, 'tp', 0, 0, tiled=True)  8.69 us
    all_to_all x1, starting transfers between devices, all_gather_tp(): lax.all_to_all(jnp.broadcast_to(block[None], (rest,) + block.shape), 'tp'...  8.47 us
    all_to_all x1, waiting for transfers between devices, per_device(): lax.all_to_all(panel_send, 'group', 0, 0, tiled=True)  6.87 us
    all_to_all x1, starting transfers between devices, reduce_scatter_tp(): lax.all_to_all(send, 'tp', 0, 0, tiled=True, axis_index_groups=stage_grou...  6.57 us
    all_to_all x1, starting transfers between devices, per_device(): lax.all_to_all(outgoing, 'group', split_axis=0, concat_axis=0, tiled=True)  6.06 us
  transfers between devices with their start and end apart: 10, of which 4 were waited for; matrix products, arithmetic and copies ran while one was open for 28% of the time, Pallas kernels for 0%

profile of v16, /device:TPU:2, one launch (start us, length us, event | category | flops | bytes accessed | tf_op | source)
XLA Modules:
  0.0 174.3 jit_solution(16513153922224604631)
XLA Ops:
  0.0 1.6 broadcast_in_dim.137
  1.6 8.5 %all-to-all-start.1 = ((bf16[8,2,32,256]{3,2,1,0:T(8,128)(2,1)}), bf16[8,2,32,256]{3,2,1,0:T(8,128)(2,1)}, u32[]{:S(2)}, u32[]{:S(2)}) async-start(bf16[8,2,32,256]{3,2,1,0:T(8,128)(2,1)} %broadcast_in_dim.137), calls=%async_computation.1 | async-start | bytes 524288 | tf_op jit(solution)/shard_map/all_to_all | solution.py:106
  10.1 1.0 fusion.53
  11.1 0.8 broadcast_compare_fusion
  11.9 1.3 convolution_bitcast_fusion
  13.1 0.9 reshape.468
  14.1 0.9 constant_dynamic-slice_fusion.2
  16.9 1.1 broadcast_select_fusion
  18.7 0.8 broadcast_select_fusion.2
  19.6 2.0 %constant_dynamic-slice_fusion.4 = (f32[16,1,2,1024]{3,1,0,2:T(1,128)}, f32[16,1,2,1024]{3,1,0,2:T(1,128)}) fusion(f32[16,2,2,1024]{3,1,0,2:T(2,128)} %reshape.468, s32[]{:T(128)S(6)} %select_n.180, s32[]{:T(128)S(6)} %select_n.181), kind=kLoop, calls=%fused_computation.103 | loop fusion | bytes 524296 | tf_op jit(solution)/shard_map/jit(dynamic_index_in_dim)/dynamic_slice | solution.py:87
  21.7 2.1 %pad_maximum_fusion.1 = bf16[8,2,328,128]{3,2,1,0:T(8,128)(2,1)} fusion(bf16[8,2,8,128]{3,2,1,0:T(8,128)(2,1)S(1)} %broadcast_select_fusion.3, bf16[8,2,64,128]{3,2,1,0:T(8,128)(2,1)} %broadcast_select_fusion.2, bf16[8,2,256,128]{3,2,1,0:T(8,128)(2,1)S(1)} %copy-done.4), kind=kLoop, calls=%fused_computation.17 | loop fusion | flops 4030464 | bytes 2686976 | tf_op jit(solution)/shard_map/concatenate | solution.py:159
  23.8 5.9 %all-to-all-start.2 = ((bf16[8,2,328,128]{3,2,1,0:T(8,128)(2,1)}), bf16[8,2,328,128]{3,2,1,0:T(8,128)(2,1)S(1)}, u32[]{:S(2)}, u32[]{:S(2)}) async-start(bf16[8,2,328,128]{3,2,1,0:T(8,128)(2,1)} %pad_maximum_fusion.1), calls=%async_computation.2 | async-start | bytes 2686976 | tf_op jit(solution)/shard_map/all_to_all | solution.py:167
  29.7 1.0 copy.339
  32.4 2.9 %gather_fusion = bf16[32,16,1024]{2,1,0:T(8,128)(2,1)} fusion(bf16[32,16,1024]{2,1,0:T(8,128)(2,1)} %param.20, s32[1024]{0:T(1024)S(1)} %pad_clamp_fusion.3), kind=kCustom, calls=%fused_computation | custom fusion | bytes 2097280 | tf_op jit(solution)/shard_map/jit(_take)/gather | solution.py:234
  35.3 2.4 %select_multiply_fusion = bf16[32,16,1024]{2,1,0:T(8,128)(2,1)} fusion(bf16[32,16,1024]{2,1,0:T(8,128)(2,1)} %gather_fusion, pred[32]{0:T(512)(128)(4,1)S(1)} %le.73, bf16[32]{0:T(256)(128)(2,1)S(1)} %reshape.490), kind=kLoop, calls=%fused_computation.35 | loop fusion | flops 1048576 | bytes 2097248 | tf_op jit(solution)/shard_map/mul | solution.py:234
  37.8 2.9 %collective-permute-start = (bf16[8,2,32,256]{3,2,1,0:T(8,128)(2,1)}, bf16[8,2,32,256]{3,2,1,0:T(8,128)(2,1)}, u32[]{:S(2)}, u32[]{:S(2)}) collective-permute-start(bf16[8,2,32,256]{3,2,1,0:T(8,128)(2,1)} %all-to-all-done.1), channel_id=1, source_target_pairs={{0,2},{1,3},{2,0},{3,1},{4,6},{5,7},{6,4},{7,5},{8,10},{9,11},{10,... | collective-permute-start | bytes 786440 | tf_op jit(solution)/shard_map/ppermute | solution.py:116
  40.7 6.9 %all-to-all-done.2 = bf16[8,2,328,128]{3,2,1,0:T(8,128)(2,1)S(1)} async-done(((bf16[8,2,328,128]{3,2,1,0:T(8,128)(2,1)}), bf16[8,2,328,128]{3,2,1,0:T(8,128)(2,1)S(1)}, u32[]{:S(2)}, u32[]{:S(2)}) %all-to-all-start.2) | async-done | bytes 1343520 | tf_op jit(solution)/shard_map/all_to_all | solution.py:167
  47.5 6.1 %all-to-all-start = ((bf16[32,16,1024]{2,1,0:T(8,128)(2,1)}), bf16[32,16,1024]{2,1,0:T(8,128)(2,1)}, u32[]{:S(2)}, u32[]{:S(2)}) async-start(bf16[32,16,1024]{2,1,0:T(8,128)(2,1)} %select_multiply_fusion), calls=%async_computation | async-start | bytes 2097152 | tf_op jit(solution)/shard_map/all_to_all | solution.py:237
  53.6 1.3 slice.148
  54.9 2.1 %gather_fusion.5 = bf16[32,256,128]{2,1,0:T(8,128)(2,1)} fusion(bf16[16,256,128]{2,1,0:T(8,128)(2,1)S(1)} %slice.148, s32[1024]{0:T(1024)S(1)} %pad_clamp_fusion), kind=kCustom, calls=%fused_computation.5 | custom fusion | bytes 4194432 | tf_op jit(solution)/shard_map/jit(_take)/gather | solution.py:175
  57.1 2.1 %fusion.5 = f32[32,128,2]{1,2,0:T(2,128)S(1)} fusion(bf16[32,256,128]{2,1,0:T(8,128)(2,1)} %gather_fusion.5, pred[32]{0:T(512)(128)(4,1)S(1)} %get-tuple-element.19, bf16[2,32,256]{2,1,0:T(8,128)(2,1)S(1)} %copy-done.9), kind=kOutput, calls=%fused_computation.14 | convolution fusion | flops 5242880 | bytes 2162720 | tf_op jit(solution)/shard_map/srd,rdk->srk/dot_general | solution.py:184
  59.5 2.1 %maximum_select_fusion.2 = bf16[8,2,2,32,256]{4,3,2,0,1:T(8,128)(2,1)} fusion(bf16[8,1,2,32,256]{4,3,2,0,1:T(8,128)(2,1)} %bitcast.10, bf16[8,1,2,32,256]{4,3,2,0,1:T(8,128)(2,1)} %bitcast.9, pred[]{:T(512)S(6)} %eq.13), kind=kLoop, calls=%fused_computation.39 | loop fusion | flops 786432 | bytes 1048577 | tf_op jit(solution)/shard_map/jit(_where)/select_n | solution.py:117
  62.4 3.0 %collective-permute-start.3 = (f32[24576]{0:T(1024)S(1)}, f32[24576]{0:T(1024)S(1)}, u32[]{:S(2)}, u32[]{:S(2)}) collective-permute-start(f32[24576]{0:T(1024)S(1)} %pad_maximum_fusion.4), channel_id=1, source_target_pairs={{0,2},{1,3},{2,0},{3,1},{4,6},{5,7},{6,4},{7,5},{8,10},{9,11},{10,... | collective-permute-start | bytes 294920 | tf_op jit(solution)/shard_map/ppermute | solution.py:90
  65.4 2.1 %maximum_select_fusion.1 = bf16[8,2,1,2,32,256]{5,4,3,0,2,1:T(8,128)(2,1)} fusion(bf16[8,1,1,2,32,256]{5,4,3,0,2,1:T(8,128)(2,1)} %bitcast.8, bf16[8,1,1,2,32,256]{5,4,3,0,2,1:T(8,128)(2,1)} %bitcast.7, pred[]{:T(512)S(6)} %eq.13), kind=kLoop, calls=%fused_computation.38 | loop fusion | flops 786432 | bytes 1048577 | tf_op jit(solution)/shard_map/jit(_where)/select_n | solution.py:117
  67.5 2.1 %collective-permute-done.3 = f32[24576]{0:T(1024)S(1)} collective-permute-done((f32[24576]{0:T(1024)S(1)}, f32[24576]{0:T(1024)S(1)}, u32[]{:S(2)}, u32[]{:S(2)}) %collective-permute-start.3) | collective-permute-done | bytes 98336 | tf_op jit(solution)/shard_map/ppermute | solution.py:90
  69.8 0.9 all_to_all.32
  70.7 6.6 %all-to-all-start.3 = ((f32[8,1,10240]{2,1,0:T(1,128)}), f32[8,1,10240]{2,1,0:T(1,128)}, u32[]{:S(2)}, u32[]{:S(2)}) async-start(f32[8,1,10240]{2,1,0:T(1,128)} %all_to_all.32), calls=%async_computation.3 | async-start | bytes 655360 | tf_op jit(solution)/shard_map/all_to_all | solution.py:98
  77.3 2.7 %pad_maximum_fusion = bf16[64,16,1024]{2,1,0:T(8,128)(2,1)} fusion(bf16[32,16,1024]{2,1,0:T(8,128)(2,1)} %all-to-all-done, bf16[32,16,1024]{2,1,0:T(8,128)(2,1)S(1)} %copy-done.3), kind=kLoop, calls=%fused_computation.11 | loop fusion | flops 1048576 | bytes 4194304 | tf_op jit(solution)/shard_map/concatenate | solution.py:238
  80.0 2.2 %gather_fusion.1 = bf16[32,16,1024]{2,1,0:T(8,128)(2,1)S(1)} fusion(bf16[64,16,1024]{2,1,0:T(8,128)(2,1)} %pad_maximum_fusion, s32[1024]{0:T(1024)S(1)} %pad_clamp_fusion.2), kind=kCustom, calls=%fused_computation.1 | custom fusion | bytes 2097280 | tf_op jit(solution)/shard_map/jit(_take)/gather | solution.py:239
  82.2 1.3 copy.236
  83.6 2.3 %broadcast_select_fusion.1 = bf16[1,512,1024]{1,2,0:T(8,128)(2,1)} fusion(bf16[1,512,1024]{1,2,0:T(8,128)(2,1)} %copy.236, pred[512]{0:T(512)(128)(4,1)S(1)} %broadcast_in_dim.132), kind=kLoop, calls=%fused_computation.37 | loop fusion | flops 524288 | bytes 2097664 | tf_op jit(solution)/shard_map/jit(_take)/select_n | solution.py:239
  85.9 1.0 slice.155
  86.9 0.8 slice.157
  87.7 1.4 gather_fusion.6
  90.1 1.6 maximum_select_fusion
  91.8 1.2 reduce_sum.36
  93.6 1.4 fusion.28
  96.1 9.1 %all-to-all-start.4 = ((f32[32,3,128]{2,1,0:T(4,128)}), f32[32,3,128]{2,1,0:T(4,128)S(1)}, u32[]{:S(2)}, u32[]{:S(2)}) async-start(f32[32,3,128]{2,1,0:T(4,128)} %copy.257), calls=%async_computation.4 | async-start | bytes 131072 | tf_op jit(solution)/shard_map/all_to_all | solution.py:216
  105.2 1.3 fusion.63
  106.5 8.7 %all-to-all-done.4 = f32[32,3,128]{2,1,0:T(4,128)S(1)} async-done(((f32[32,3,128]{2,1,0:T(4,128)}), f32[32,3,128]{2,1,0:T(4,128)S(1)}, u32[]{:S(2)}, u32[]{:S(2)}) %all-to-all-start.4) | async-done | bytes 49184 | tf_op jit(solution)/shard_map/all_to_all | solution.py:216
  116.9 12.7 %all_to_all.44 = bf16[2,1,32,128]{3,0,1,2:T(2,128)(2,1)S(1)} all-to-all(bf16[2,1,32,128]{3,0,1,2:T(2,128)(2,1)S(1)} %copy.270), channel_id=1, replica_groups=mesh['group'=8,'tp'=32] {'tp'}, dimensions={2} | all-to-all | bytes 32768 | tf_op jit(solution)/shard_map/all_to_all | solution.py:243
  129.6 2.0 %fusion = f32[64,32,256]{2,0,1:T(8,128)S(1)} fusion(bf16[64,128,1]{1,0,2:T(8,128)(2,1)S(1)} %bitcast.198, bf16[16,32,8,256]{3,2,1,0:T(8,128)(2,1)} %bitcast.182), kind=kOutput, calls=%fused_computation.8 | convolution fusion | flops 134217728 | bytes 4210688 | tf_op jit(solution)/shard_map/rk,kdc->drc/dot_general | solution.py:245
  131.8 1.5 copy.294
  133.3 2.0 %squeeze.19 = f32[16,1,16384]{2,1,0:T(1,128)} reshape(f32[16,1,64,256]{3,2,1,0:T(8,128)S(1)} %get-tuple-element.6) | data formatting | bytes 2097152 | tf_op jit(solution)/shard_map/jit(dynamic_index_in_dim)/squeeze | solution.py:87
  135.4 1.0 collective-permute-done.4
  136.3 2.6 %add.153 = f32[16,1,16384]{2,1,0:T(1,128)S(1)} add(f32[16,1,16384]{2,1,0:T(1,128)} %squeeze.19, f32[16,1,16384]{2,1,0:T(1,128)} %bitcast.60) | non-fusion elementwise | flops 262144 | bytes 3145728 | tf_op jit(solution)/shard_map/add | solution.py:91
  138.9 33.9 %all_to_all.45 = f32[16,1,16384]{2,1,0:T(1,128)S(1)} all-to-all(f32[16,1,16384]{2,1,0:T(1,128)S(1)} %add.153), channel_id=1, replica_groups={{0,2,4,6,8,10,12,14,16,18,20,22,24,26,28,30},{1,3,5,7,9,11,13,15,17,19,..., dimensions={0} | all-to-all | bytes 2097152 | tf_op jit(solution)/shard_map/all_to_all | solution.py:98
  172.8 0.8 reduce_sum.39
  (115 shorter events, 10.2 us)
Async XLA Ops:
  0.0 94.9 %copy-start = (bf16[8192,128]{1,0:T(8,128)(2,1)S(1)}, bf16[8192,128]{1,0:T(8,128)(2,1)}, u32[]{:S(2)}) copy-start(bf16[8192,128]{1,0:T(8,128)(2,1)} %param.14) | copy-start | bytes 6291460
  0.0 16.0 %copy-start.2 = (bf16[4,256,128]{2,1,0:T(8,128)(2,1)S(1)}, bf16[4,256,128]{2,1,0:T(8,128)(2,1)}, u32[]{:S(2)}) copy-start(bf16[4,256,128]{2,1,0:T(8,128)(2,1)} %param.17) | copy-start | bytes 786436
  1.6 22.2 %all-to-all-start.1 = ((bf16[8,2,32,256]{3,2,1,0:T(8,128)(2,1)}), bf16[8,2,32,256]{3,2,1,0:T(8,128)(2,1)}, u32[]{:S(2)}, u32[]{:S(2)}) async-start(bf16[8,2,32,256]{3,2,1,0:T(8,128)(2,1)} %broadcast_in_dim.137), calls=%async_computation.1 | async-start | bytes 524288 | tf_op jit(solution)/shard_map/all_to_all | solution.py:106
  16.0 2.0 %copy-start.6 = (bf16[4,64,128]{2,1,0:T(8,128)(2,1)S(1)}, bf16[4,64,128]{2,1,0:T(8,128)(2,1)}, u32[]{:S(2)}) copy-start(bf16[4,64,128]{2,1,0:T(8,128)(2,1)} %param.18) | copy-start | bytes 196612
  16.8 2.7 %copy-start.10 = (s32[1,1,8,4]{2,3,1,0:T(4,128)S(1)}, s32[1,1,8,4]{2,3,1,0:T(4,128)}, u32[]{:S(2)}) copy-start(s32[1,1,8,4]{2,3,1,0:T(4,128)} %param.23) | copy-start | bytes 388
  18.1 3.6 %copy-start.4 = (bf16[8,2,256,128]{3,2,1,0:T(8,128)(2,1)S(1)}, bf16[8,2,256,128]{3,2,1,0:T(8,128)(2,1)}, u32[]{:S(2)}) copy-start(bf16[8,2,256,128]{3,2,1,0:T(8,128)(2,1)} %broadcast_select_fusion) | copy-start | bytes 3145732
  23.8 11.5 %copy-start.12 = (s32[32]{0:T(128)S(1)}, s32[32]{0:T(128)}, u32[]{:S(2)}) copy-start(s32[32]{0:T(128)} %param.24) | copy-start | bytes 388
  23.8 11.5 %copy-start.11 = (s32[1,32]{1,0:T(1,128)S(1)}, s32[1,32]{1,0:T(1,128)}, u32[]{:S(2)}) copy-start(s32[1,32]{1,0:T(1,128)} %param.22) | copy-start | bytes 388
  23.8 23.7 %all-to-all-start.2 = ((bf16[8,2,328,128]{3,2,1,0:T(8,128)(2,1)}), bf16[8,2,328,128]{3,2,1,0:T(8,128)(2,1)S(1)}, u32[]{:S(2)}, u32[]{:S(2)}) async-start(bf16[8,2,328,128]{3,2,1,0:T(8,128)(2,1)} %pad_maximum_fusion.1), calls=%async_computation.2 | async-start | bytes 2686976 | tf_op jit(solution)/shard_map/all_to_all | solution.py:167
  37.8 21.8 %collective-permute-start = (bf16[8,2,32,256]{3,2,1,0:T(8,128)(2,1)}, bf16[8,2,32,256]{3,2,1,0:T(8,128)(2,1)}, u32[]{:S(2)}, u32[]{:S(2)}) collective-permute-start(bf16[8,2,32,256]{3,2,1,0:T(8,128)(2,1)} %all-to-all-done.1), channel_id=1, source_target_pairs={{0,2},{1,3},{2,0},{3,1},{4,6},{5,7},{6,4},{7,5},{8,10},{9,11},{10,... | collective-permute-start | bytes 786440 | tf_op jit(solution)/shard_map/ppermute | solution.py:116
  47.5 6.1 %copy-start.1 = (bf16[8,2,328,128]{3,2,1,0:T(8,128)(2,1)}, bf16[8,2,328,128]{3,2,1,0:T(8,128)(2,1)S(1)}, u32[]{:S(2)}) copy-start(bf16[8,2,328,128]{3,2,1,0:T(8,128)(2,1)S(1)} %all-to-all-done.2) | copy-start | bytes 4030468
  47.5 23.2 %all-to-all-start = ((bf16[32,16,1024]{2,1,0:T(8,128)(2,1)}), bf16[32,16,1024]{2,1,0:T(8,128)(2,1)}, u32[]{:S(2)}, u32[]{:S(2)}) async-start(bf16[32,16,1024]{2,1,0:T(8,128)(2,1)} %select_multiply_fusion), calls=%async_computation | async-start | bytes 2097152 | tf_op jit(solution)/shard_map/all_to_all | solution.py:237
  54.9 2.2 %copy-start.9 = (bf16[2,32,256]{2,1,0:T(8,128)(2,1)S(1)}, bf16[2,32,256]{2,1,0:T(8,128)(2,1)}, u32[]{:S(2)}) copy-start(bf16[2,32,256]{2,1,0:T(8,128)(2,1)} %param.13) | copy-start | bytes 98308
  57.1 2.1 %copy-start.8 = (f32[16,8,2,128]{3,1,2,0:T(8,128)S(1)}, f32[16,8,2,128]{3,1,2,0:T(8,128)}, u32[]{:S(2)}) copy-start(f32[16,8,2,128]{3,1,2,0:T(8,128)} %copy.291) | copy-start | bytes 393220
  59.1 3.1 %copy-start.7 = (f32[16,1,2,1024]{3,1,0,2:T(1,128)S(1)}, f32[16,1,2,1024]{3,1,0,2:T(1,128)}, u32[]{:S(2)}) copy-start(f32[16,1,2,1024]{3,1,0,2:T(1,128)} %get-tuple-element.9) | copy-start | bytes 393220
  59.2 2.9 %collective-permute-start.2 = (f32[40960]{0:T(1024)S(1)}, f32[40960]{0:T(1024)S(1)}, u32[]{:S(2)}, u32[]{:S(2)}) collective-permute-start(f32[40960]{0:T(1024)S(1)} %pad_maximum_fusion.3), channel_id=1, source_target_pairs={{0,1},{1,0},{2,3},{3,2},{4,5},{5,4},{6,7},{7,6},{8,9},{9,8},{10,11... | collective-permute-start | bytes 491528 | tf_op jit(solution)/shard_map/ppermute | solution.py:90
  61.6 28.4 %collective-permute-start.1 = (bf16[8,2,2,32,256]{4,3,2,0,1:T(8,128)(2,1)}, bf16[8,2,2,32,256]{4,3,2,0,1:T(8,128)(2,1)}, u32[]{:S(2)}, u32[]{:S(2)}) collective-permute-start(bf16[8,2,2,32,256]{4,3,2,0,1:T(8,128)(2,1)} %maximum_select_fusion.2), channel_id=1, source_target_pairs={{0,1},{1,0},{2,3},{3,2},{4,5},{5,4},{6,7},{7,6},{8,9},{9,8},{10,11... | collective-permute-start | bytes 1572872 | tf_op jit(solution)/shard_map/ppermute | solution.py:116
  62.3 14.9 %copy-start.3 = (bf16[32,16,1024]{2,1,0:T(8,128)(2,1)S(1)}, bf16[32,16,1024]{2,1,0:T(8,128)(2,1)}, u32[]{:S(2)}) copy-start(bf16[32,16,1024]{2,1,0:T(8,128)(2,1)} %param.20) | copy-start | bytes 3145732
  62.4 7.2 %collective-permute-start.3 = (f32[24576]{0:T(1024)S(1)}, f32[24576]{0:T(1024)S(1)}, u32[]{:S(2)}, u32[]{:S(2)}) collective-permute-start(f32[24576]{0:T(1024)S(1)} %pad_maximum_fusion.4), channel_id=1, source_target_pairs={{0,2},{1,3},{2,0},{3,1},{4,6},{5,7},{6,4},{7,5},{8,10},{9,11},{10,... | collective-permute-start | bytes 294920 | tf_op jit(solution)/shard_map/ppermute | solution.py:90
  70.7 21.1 %all-to-all-start.3 = ((f32[8,1,10240]{2,1,0:T(1,128)}), f32[8,1,10240]{2,1,0:T(1,128)}, u32[]{:S(2)}, u32[]{:S(2)}) async-start(f32[8,1,10240]{2,1,0:T(1,128)} %all_to_all.32), calls=%async_computation.3 | async-start | bytes 655360 | tf_op jit(solution)/shard_map/all_to_all | solution.py:98
  85.9 4.2 %copy-start.5 = (bf16[8,2,1,2,32,256]{5,4,3,0,2,1:T(8,128)(2,1)S(1)}, bf16[8,2,1,2,32,256]{5,4,3,0,2,1:T(8,128)(2,1)}, u32[]{:S(2)}) copy-start(bf16[8,2,1,2,32,256]{5,4,3,0,2,1:T(8,128)(2,1)} %maximum_select_fusion.1) | copy-start | bytes 1572868
  96.1 19.1 %all-to-all-start.4 = ((f32[32,3,128]{2,1,0:T(4,128)}), f32[32,3,128]{2,1,0:T(4,128)S(1)}, u32[]{:S(2)}, u32[]{:S(2)}) async-start(f32[32,3,128]{2,1,0:T(4,128)} %copy.257), calls=%async_computation.4 | async-start | bytes 131072 | tf_op jit(solution)/shard_map/all_to_all | solution.py:216
  133.3 3.0 %collective-permute-start.4 = (f32[262144]{0:T(1024)}, f32[262144]{0:T(1024)}, u32[]{:S(2)}, u32[]{:S(2)}) collective-permute-start(f32[262144]{0:T(1024)} %bitcast.96), channel_id=1, source_target_pairs={{0,1},{1,0},{2,3},{3,2},{4,5},{5,4},{6,7},{7,6},{8,9},{9,8},{10,11... | collective-permute-start | bytes 3145736 | tf_op jit(solution)/shard_map/ppermute | solution.py:90
